TPU v7x, 32 devices: a whole 2x2x4 slice. The times are simulated.
32 devices in a mesh: grp: 2 (over y), shot: 4 (over z), freq: 2 (over x), sub: 2 (over core).
Axes of the slice: x: 2, y: 2, z: 4, core: 2. Of those that a mesh axis runs over, the one named last changes fastest.
Arguments:
- downgoing: bfloat16 [2, 2, 6144, 1024], P(None, 'freq', ('grp', 'shot')), parts along dimension 2
- upgoing: bfloat16 [2, 2, 6144, 512], P(None, 'freq', ('grp', 'shot')), parts along dimension 2, may hold values from -448 to 448
- source_order: int32 [1024], P('grp'), parts along dimension 0, may hold values from 0 to 511, each once
Outputs:
- response: float32 [2, 2, 1024, 1024], P(None, 'freq', ('grp', 'shot', 'sub')), parts along dimension 2
There are 2 independent parts, one for each index of `grp`. A program takes and returns all parts, laid end to end along the dimension named above; each array names one. Nothing has to cross between parts.
Inputs may be any that keep to these rules, and one draw needn't show every extreme that they name: `source_order`: each of the 512 columns appears exactly once.
All inputs are finite; a program needn't handle non-finite values.
Results may differ from a plain program's by a relative error of at most 0.012.
Values may be sent and summed in bfloat16 or wider, within the bound.
No kernel may reach another device: no remote copies, remote signals or barrier semaphores. Data moves between devices by JAX's collectives and lax.ppermute only.
A program may use at most 64 MiB of HBM per device.

v0:
```python
import jax
import jax.numpy as jnp
from jax import lax
from jax.sharding import PartitionSpec as P

SWEEPS = 6


relaxation = 0.125
damping = 1.0


def shot_terms(left_factor, recorded_trace):
    leading_operand = jnp.einsum(
        "qtu,qto->uqo", left_factor[0], recorded_trace[0], preferred_element_type=jnp.float32
    )
    following_operand = jnp.einsum(
        "qtu,qto->uqo", left_factor[1], recorded_trace[1], preferred_element_type=jnp.float32
    )
    middle_operand = jnp.einsum(
        "qtu,qto->uqo", left_factor[1], recorded_trace[0], preferred_element_type=jnp.float32
    )
    trailing_operand = jnp.einsum(
        "qtu,qto->uqo", left_factor[0], recorded_trace[1], preferred_element_type=jnp.float32
    )
    return jnp.stack(
        [leading_operand + following_operand, middle_operand - trailing_operand], axis=2
    )


def add_product(slender_portion, gram_portion):
    real_real = jnp.einsum(
        "mad,dax->max",
        slender_portion[:, :, 0],
        gram_portion[:, :, 0],
        preferred_element_type=jnp.float32,
    )
    imag_imag = jnp.einsum(
        "mad,dax->max",
        slender_portion[:, :, 1],
        gram_portion[:, :, 1],
        preferred_element_type=jnp.float32,
    )
    real_imag = jnp.einsum(
        "mad,dax->max",
        slender_portion[:, :, 0],
        gram_portion[:, :, 1],
        preferred_element_type=jnp.float32,
    )
    imag_real = jnp.einsum(
        "mad,dax->max",
        slender_portion[:, :, 1],
        gram_portion[:, :, 0],
        preferred_element_type=jnp.float32,
    )
    return (real_real - imag_imag, real_imag + imag_real)


def sweep_whole(whole, solution, target):
    for sweep in range(SWEEPS):
        narrow = solution.astype(jnp.bfloat16)
        image_real, image_imag = add_product(narrow, whole)
        image = jnp.stack([image_real, image_imag], axis=2)
        solution = solution + relaxation * (target - image - damping * solution)
    return solution


def per_device(downgoing, upgoing, source_order):
    shot_count = lax.axis_size("shot")
    core_count = lax.axis_size("sub")
    core_index = lax.axis_index("sub")
    receivers = downgoing.shape[3]
    freq_local = downgoing.shape[1]
    shot_local = downgoing.shape[2]
    sources = source_order.shape[0]
    source_local = sources // (shot_count * core_count)
    local_power = jnp.sum(jnp.square(downgoing.astype(jnp.float32)), axis=(0, 2, 3))
    power = lax.psum(local_power, "shot") / receivers
    power_wide = power[None, :, None, None]
    order_table = source_order.reshape(shot_count, core_count, source_local)
    own_order = lax.dynamic_slice_in_dim(order_table, core_index, 1, 1).reshape(-1)
    chosen = jnp.take(upgoing, own_order, axis=3)
    left_factor = chosen
    corr = lax.psum_scatter(
        shot_terms(left_factor, downgoing).astype(jnp.bfloat16),
        "shot",
        scatter_dimension=0,
        tiled=True,
    ).astype(jnp.float32)
    target = corr / power_wide
    solution = jnp.zeros((source_local, freq_local, 2, receivers), jnp.float32)
    columns = downgoing.reshape(2, freq_local, shot_local, receivers // core_count, core_count)
    own_columns = lax.dynamic_slice_in_dim(columns, core_index, 1, 4)[..., 0]
    left_factor = own_columns
    gram_rows = lax.psum_scatter(
        shot_terms(left_factor, downgoing).astype(jnp.bfloat16),
        "shot",
        scatter_dimension=0,
        tiled=True,
    ).astype(jnp.float32)
    scaled = (gram_rows / power_wide).astype(jnp.bfloat16)
    across = lax.all_gather(scaled[:, None], "shot", axis=0, tiled=True)
    whole = lax.all_gather(across, "sub", axis=1, tiled=True)
    whole = whole.reshape(receivers, freq_local, 2, receivers)
    solution = sweep_whole(whole, solution, target)
    return jnp.transpose(solution, (2, 1, 0, 3))


def solution(mesh):
    return jax.shard_map(
        per_device,
        mesh=mesh,
        in_specs=(
            P(None, "freq", ("grp", "shot"), None),
            P(None, "freq", ("grp", "shot"), None),
            P("grp"),
        ),
        out_specs=P(None, "freq", ("grp", "shot", "sub"), None),
        check_vma=False,
    )
```

profile of v0, /device:TPU:0, one launch (start us, length us, event | category | flops | bytes accessed | tf_op | source)
XLA Modules:
  0.0 206.0 jit_solution(8275821068163915679)
XLA Ops:
  6.5 8.8 %copy.22 = bf16[2,1,768,1024]{2,0,3,1:T(2,128)(2,1)} copy(bf16[2,1,768,1024]{3,2,1,0:T(8,128)(2,1)} %param.3) | data formatting | bytes 6291456 | tf_op args[0]
  15.3 6.2 %constant_dynamic-slice_fusion = (bf16[1,1,768,512,1]{2,0,4,3,1:T(2,128)(2,1)}, bf16[1,1,768,512,1]{2,0,4,3,1:T(2,128)(2,1)}) fusion(bf16[2,1,768,512,2]{2,0,4,3,1:T(2,128)(2,1)} %bitcast.302, s32[]{:T(128)S(6)} %select_n.32, s32[]{:T(128)S(6)} %add.164), kind=kLoop, calls=%fused_computation.155 | loop fusion | bytes 3145736 | tf_op jit(solution)/shard_map/slice | solution.py:15
  21.5 4.6 %copy.23 = bf16[1,1,768,512,1]{3,2,4,1,0:T(8,128)(2,1)} copy(bf16[1,1,768,512,1]{2,0,4,3,1:T(2,128)(2,1)} %get-tuple-element.13) | data formatting | bytes 1572864 | tf_op jit(solution)/shard_map/slice | solution.py:15
  26.2 3.5 %fusion.52 = f32[512,1024]{1,0:T(8,128)} fusion(bf16[2,1,768,1024]{3,2,1,0:T(8,128)(2,1)S(1)} %copy-done.2, bf16[1,1,768,512,1]{3,2,4,1,0:T(8,128)(2,1)} %copy.23), kind=kOutput, calls=%fused_computation.57 | convolution fusion | flops 805306368 | bytes 4456448 | tf_op jit(solution)/shard_map/qtu,qto->uqo/dot_general | solution.py:14
  29.6 4.6 %copy.24 = bf16[1,1,768,512,1]{3,2,4,1,0:T(8,128)(2,1)} copy(bf16[1,1,768,512,1]{2,0,4,3,1:T(2,128)(2,1)} %get-tuple-element.14) | data formatting | bytes 1572864 | tf_op jit(solution)/shard_map/slice | solution.py:18
  34.3 2.3 %fusion.50 = f32[512,1024]{1,0:T(8,128)S(1)} fusion(bf16[2,1,768,1024]{3,2,1,0:T(8,128)(2,1)S(1)} %copy-done.2, bf16[1,1,768,512,1]{3,2,4,1,0:T(8,128)(2,1)} %copy.24), kind=kOutput, calls=%fused_computation.55 | convolution fusion | flops 805306368 | bytes 4456448 | tf_op jit(solution)/shard_map/qtu,qto->uqo/dot_general | solution.py:20
  38.8 1.5 pad_maximum_fusion
  40.3 2.2 %multiply_reduce_fusion = f32[]{:T(128)} fusion(bf16[2,1,768,1024]{3,2,1,0:T(8,128)(2,1)S(1)} %copy-done.2), kind=kLoop, calls=%fused_computation.1 | loop fusion | flops 4718591 | bytes 3145732 | tf_op jit(solution)/shard_map/reduce_sum | solution.py:77
  42.6 14.3 %psum.7 = f32[1]{0:T(128)} all-reduce(f32[1]{0:T(128)} %bitcast.16), channel_id=1, replica_groups=mesh['grp'=2,'shot'=4,'freq'=2,'sub'=2] {'shot'}, use_global_device_ids=true, to_apply=%region_2.3 | all-reduce | flops 1 | bytes 8 | tf_op jit(solution)/shard_map/psum | solution.py:78
  57.5 29.5 %reduce-scatter.5.cloned.1.call-done = bf16[128,1,2,1024]{3,0,2,1:T(8,128)(2,1)} async-done(((bf16[512,1,2,1024]{3,0,2,1:T(8,128)(2,1)}), bf16[128,1,2,1024]{3,0,2,1:T(8,128)(2,1)}) %reduce-scatter.5.cloned.1.call-update) | async-done | bytes 524304 | tf_op jit(solution)/shard_map/reduce_scatter | solution.py:95
  87.1 1.9 divide_convert_fusion
  89.1 45.4 %all-gather.5.cloned.1.call-done = bf16[512,1,2,1024]{3,0,2,1:T(8,128)(2,1)} async-done(((bf16[128,1,2,1024]{3,0,2,1:T(8,128)(2,1)}), bf16[512,1,2,1024]{3,0,2,1:T(8,128)(2,1)}) %all-gather.5.cloned.1.call-update) | async-done | bytes 2097168 | tf_op jit(solution)/shard_map/all_gather | solution.py:102
  136.1 5.0 %copy.19 = bf16[2,1,768,512]{2,0,3,1:T(2,128)(2,1)} copy(bf16[2,1,768,512]{3,2,1,0:T(8,128)(2,1)} %param.4) | data formatting | bytes 3145728 | tf_op args[1]
  141.2 4.8 %gather_fusion = bf16[256,2,768]{2,1,0:T(2,128)(2,1)} fusion(bf16[2,768,512]{1,0,2:T(2,128)(2,1)} %bitcast.303, s32[1024]{0:T(1024)S(1)} %pad_clamp_fusion), kind=kCustom, calls=%fused_computation | custom fusion | bytes 1573888 | tf_op jit(solution)/shard_map/jit(_take)/gather | solution.py:82
  146.0 2.2 %broadcast_select_fusion = bf16[2,1,768,256]{2,0,3,1:T(2,128)(2,1)S(1)} fusion(pred[256]{0:T(512)(128)(4,1)S(1)} %compare_and_fusion, bf16[256,2,768]{2,1,0:T(2,128)(2,1)} %gather_fusion), kind=kLoop, calls=%fused_computation.63 | loop fusion | flops 393216 | bytes 1573120 | tf_op jit(solution)/shard_map/jit(_take)/select_n | solution.py:82
  148.3 2.2 %fusion.188 = (bf16[1,1,768,256]{2,0,3,1:T(2,128)(2,1)}, bf16[1,1,768,256]{2,0,3,1:T(2,128)(2,1)}) fusion(bf16[2,1,768,256]{2,0,3,1:T(2,128)(2,1)S(1)} %broadcast_select_fusion), kind=kLoop, calls=%fused_computation.164 | loop fusion | bytes 1572864 | tf_op jit(solution)/shard_map/slice | solution.py:18
  150.5 2.2 %copy.21 = bf16[1,1,768,256]{3,2,1,0:T(8,128)(2,1)S(1)} copy(bf16[1,1,768,256]{2,0,3,1:T(2,128)(2,1)} %get-tuple-element.15) | data formatting | bytes 786432 | tf_op jit(solution)/shard_map/slice | solution.py:18
  152.7 2.9 %copy.20 = bf16[1,1,768,256]{3,2,1,0:T(8,128)(2,1)} copy(bf16[1,1,768,256]{2,0,3,1:T(2,128)(2,1)} %get-tuple-element.16) | data formatting | bytes 786432 | tf_op jit(solution)/shard_map/slice | solution.py:15
  158.3 1.1 pad_maximum_fusion.1
  159.5 6.5 %copy.25 = bf16[512,2,2,1024]{3,2,1,0:T(2,128)(2,1)S(1)} copy(bf16[512,2,2,1024]{3,0,2,1:T(8,128)(2,1)} %all-gather.7.cloned.1.call-done) | data formatting | bytes 8388608 | tf_op jit(solution)/shard_map/all_gather | solution.py:103
  166.0 6.2 %fusion.187 = (bf16[1024,1,1,1024]{3,2,0,1:T(2,128)(2,1)S(1)}, bf16[1024,1,1,1024]{3,2,0,1:T(2,128)(2,1)S(1)}) fusion(bf16[1024,1,2,1024]{3,2,0,1:T(2,128)(2,1)S(1)} %bitcast.301), kind=kLoop, calls=%fused_computation.163 | loop fusion | bytes 8388608 | tf_op jit(solution)/shard_map/slice | solution.py:35
  175.3 10.0 %reduce-scatter.3.cloned.1.call-done = bf16[64,1,2,1024]{3,0,2,1:T(8,128)(2,1)} async-done(((bf16[256,1,2,1024]{3,0,2,1:T(8,128)(2,1)}), bf16[64,1,2,1024]{3,0,2,1:T(8,128)(2,1)}) %reduce-scatter.3.cloned.1.call-update) | async-done | bytes 262160 | tf_op jit(solution)/shard_map/reduce_scatter | solution.py:84
  185.3 1.2 fusion.175
  186.5 2.1 %fusion.2 = f32[1024,64]{0,1:T(8,128)S(1)} fusion(bf16[1024,1,1,1024]{3,0,2,1:T(8,128)(2,1)} %copy-done, bf16[64,1,2,1024]{3,0,2,1:T(8,128)(2,1)S(1)} %fusion.175), kind=kOutput, calls=%fused_computation.5 | convolution fusion | flops 134217728 | bytes 2490368 | tf_op jit(solution)/shard_map/mad,dax->max/dot_general | solution.py:38
  (69 shorter events, 20.6 us)
Async XLA Ops:
  6.5 80.6 %reduce-scatter.5.cloned.1.call-start = ((), (), s32[]{:S(2)}) async-start(), calls=%async_computation.3 | async-start | bytes 2621440 | tf_op jit(solution)/shard_map/reduce_scatter | solution.py:95
  15.3 10.9 %copy-start.2 = (bf16[2,1,768,1024]{3,2,1,0:T(8,128)(2,1)S(1)}, bf16[2,1,768,1024]{3,2,1,0:T(8,128)(2,1)}, u32[]{:S(2)}) copy-start(bf16[2,1,768,1024]{3,2,1,0:T(8,128)(2,1)} %param.3) | copy-start | bytes 9437188
  34.3 2.3 %copy-start.6 = (bf16[1,1,768,512,1]{3,2,4,1,0:T(8,128)(2,1)S(1)}, bf16[1,1,768,512,1]{3,2,4,1,0:T(8,128)(2,1)}, u32[]{:S(2)}) copy-start(bf16[1,1,768,512,1]{3,2,4,1,0:T(8,128)(2,1)} %copy.24) | copy-start | bytes 2359300
  34.3 2.3 %copy-start.8 = (f32[512,1024]{1,0:T(8,128)S(1)}, f32[512,1024]{1,0:T(8,128)}, u32[]{:S(2)}) copy-start(f32[512,1024]{1,0:T(8,128)} %fusion.52) | copy-start | bytes 6291460
  36.6 1.1 copy-start.5
  40.3 94.2 %all-gather.5.cloned.1.call-start = ((), (), s32[]{:S(2)}) async-start(), calls=%async_computation.4 | async-start | bytes 2621440 | tf_op jit(solution)/shard_map/all_gather | solution.py:102
  42.6 92.2 %copy-start.7 = (s32[512]{0:T(512)S(1)}, s32[512]{0:T(512)}, u32[]{:S(2)}) copy-start(s32[512]{0:T(512)} %param.5) | copy-start | bytes 6148
  89.1 70.4 %all-gather.7.cloned.1.call-start = ((), (), s32[]{:S(2)}) async-start(), calls=%async_computation.5 | async-start | bytes 6291456 | tf_op jit(solution)/shard_map/all_gather | solution.py:103
  134.5 50.8 %reduce-scatter.3.cloned.1.call-start = ((), (), s32[]{:S(2)}) async-start(), calls=%async_computation.2 | async-start | bytes 1310720 | tf_op jit(solution)/shard_map/reduce_scatter | solution.py:84
  155.5 1.0 copy-start.4
  173.0 1.4 copy-start
  185.3 3.3 %copy-start.1 = (bf16[1024,1,1,1024]{3,0,2,1:T(8,128)(2,1)S(1)}, bf16[1024,1,1,1024]{3,0,2,1:T(8,128)(2,1)}, u32[]{:S(2)}) copy-start(bf16[1024,1,1,1024]{3,0,2,1:T(8,128)(2,1)} %copy-done) | copy-start | bytes 6291460
  189.1 1.0 copy-start.3
Sparse Core Ops, SparseCore 0:
  40.4 46.6 reduce-scatter.4
  89.2 45.2 all-gather.4
  136.1 12.3 all-gather.6
  159.6 25.6 reduce-scatter.2
where the time goes:
time: 207 us; the launch traced here: 206 us
  waiting for transfers between devices  85 us (41%)
  local copies, waits for them, and re-layouts  58.2 us (28%)
  matrix products  22.3 us (11%)
  blocking collectives  14.3 us (7%)
  between operations  14.1 us (7%)
  other arithmetic  11.8 us (6%)
    all_gather x1, waiting for transfers between devices, per_device(): across = lax.all_gather(scaled[:, None], 'shot', axis=0, tiled=True)  45.4 us
    reduce_scatter x2, waiting for transfers between devices, per_device(): lax.psum_scatter(shot_terms(left_factor, downgoing).astype(jnp.bfloat16),...  39.5 us
    unnamed x22, local copies, waits for them, and re-layouts  16.5 us
    psum x1, blocking collectives, per_device(): power = lax.psum(local_power, 'shot') / receivers  14.3 us
    slice x3, local copies, waits for them, and re-layouts, shot_terms(): left_factor[0]  13.7 us
    slice x3, local copies, waits for them, and re-layouts, shot_terms(): left_factor[1]  9.05 us
    all_gather x1, local copies, waits for them, and re-layouts, per_device(): whole = lax.all_gather(across, 'sub', axis=1, tiled=True)  6.5 us
    slice x1, local copies, waits for them, and re-layouts, add_product(): gram_portion[:, :, 0]  6.18 us
  transfers between devices with their start and end apart: 4, of which 3 were waited for; matrix products, arithmetic and copies ran while one was open for 20% of the time, Pallas kernels for 0%

commit v1 on v0

v1 whole, which is shorter than its diff:
```python
import jax
import jax.numpy as jnp
from jax import lax
from jax.sharding import PartitionSpec as P

SWEEPS = 6


relaxation = 0.125
damping = 1.0


def stacked_left(factor):
    real_left = jnp.concatenate([factor[0], factor[1]], axis=1)
    imag_left = jnp.concatenate([factor[1], -factor[0]], axis=1)
    return jnp.stack([real_left, imag_left], axis=2)


def stacked_right(trace):
    return jnp.concatenate([trace[0], trace[1]], axis=1)


def sweep_whole(scaled, solution, target):
    for sweep in range(SWEEPS):
        narrow = solution.astype(jnp.bfloat16)
        real_real = jnp.einsum("qjc,qcr->qjr", narrow[0], scaled[0], preferred_element_type=jnp.float32)
        imag_imag = jnp.einsum("qjc,qcr->qjr", narrow[1], scaled[1], preferred_element_type=jnp.float32)
        real_imag = jnp.einsum("qjc,qcr->qjr", narrow[0], scaled[1], preferred_element_type=jnp.float32)
        imag_real = jnp.einsum("qjc,qcr->qjr", narrow[1], scaled[0], preferred_element_type=jnp.float32)
        image = jnp.stack([real_real - imag_imag, real_imag + imag_real])
        solution = solution + relaxation * (target - image - damping * solution)
    return solution


def per_device(downgoing, upgoing, source_order):
    shot_count = lax.axis_size("shot")
    core_count = lax.axis_size("sub")
    core_index = lax.axis_index("sub")
    receivers = downgoing.shape[3]
    freq_local = downgoing.shape[1]
    shot_local = downgoing.shape[2]
    sources = source_order.shape[0]
    source_local = sources // (shot_count * core_count)
    block = receivers // (shot_count * core_count)

    right = stacked_right(downgoing)

    columns = downgoing.reshape(2, freq_local, shot_local, shot_count, core_count, block)
    own_columns = lax.dynamic_slice_in_dim(columns, core_index, 1, 4)[:, :, :, :, 0]
    own_columns = own_columns.reshape(2, freq_local, shot_local, shot_count * block)
    gram_part = jnp.einsum(
        "qtpu,qto->qpuo", stacked_left(own_columns), right, preferred_element_type=jnp.float32
    )
    gram_part = gram_part.reshape(freq_local, 2, shot_count, block, receivers)
    gram_part = jnp.transpose(gram_part, (2, 0, 1, 3, 4)).astype(jnp.bfloat16)
    gram_rows = lax.psum_scatter(gram_part, "shot", scatter_dimension=0, tiled=True)
    across = lax.all_gather(gram_rows, "shot", axis=0, tiled=True)
    whole = lax.all_gather(across, "sub", axis=1, tiled=False)
    whole = jnp.transpose(whole, (3, 2, 0, 1, 4, 5)).reshape(2, freq_local, receivers, receivers)

    local_power = jnp.sum(jnp.square(downgoing.astype(jnp.float32)), axis=(0, 2, 3))
    power = jnp.sum(lax.all_gather(local_power, "shot", axis=0), axis=0) / receivers
    power_wide = power[None, :, None, None]

    corr_all = jnp.einsum(
        "qtpu,qto->uqpo", stacked_left(upgoing), right, preferred_element_type=jnp.float32
    )
    order_table = source_order.reshape(shot_count, core_count, source_local)
    own_order = lax.dynamic_slice_in_dim(order_table, core_index, 1, 1).reshape(-1)
    corr_part = jnp.take(corr_all, own_order, axis=0).astype(jnp.bfloat16)
    corr = lax.psum_scatter(corr_part, "shot", scatter_dimension=0, tiled=True).astype(jnp.float32)
    target = jnp.transpose(corr, (2, 1, 0, 3)) / power_wide

    scaled = (whole.astype(jnp.float32) / power_wide).astype(jnp.bfloat16)
    solution = jnp.zeros((2, freq_local, source_local, receivers), jnp.float32)
    return sweep_whole(scaled, solution, target)


def solution(mesh):
    return jax.shard_map(
        per_device,
        mesh=mesh,
        in_specs=(
            P(None, "freq", ("grp", "shot"), None),
            P(None, "freq", ("grp", "shot"), None),
            P("grp"),
        ),
        out_specs=P(None, "freq", ("grp", "shot", "sub"), None),
        check_vma=False,
    )
```

time: 207 us -> 258 us (1.25)
  waiting for transfers between devices: 85 us -> 139 us
  other arithmetic: 11.8 us -> 17.5 us
  blocking collectives: 14.3 us -> 9.71 us
    unnamed x4 -> x5, waiting for transfers between devices: 0.07 us -> 88.1 us
    reduce_scatter x2 -> x1, waiting for transfers between devices: 39.5 us -> 5.76 us  [per_device(): lax.psum_scatter(corr_part, 'shot', scatter_dimension=0, tiled=True)]
    psum x1 -> x0, blocking collectives: 14.3 us -> none  [per_device(): power = lax.psum(local_power, 'shot') / receivers]
    slice x7 -> x5, local copies, waits for them, and re-layouts: 28.9 us -> 18.5 us  [the longest x3 16.1 us: stacked_left(): real_left = jnp.concatenate([factor[0], factor[1]], axis=1)]
    unnamed x0 -> x1, blocking collectives: none -> 9.71 us
    transpose x0 -> x1, local copies, waits for them, and re-layouts: none -> 6.27 us  [per_device(): jnp.einsum('qtpu,qto->uqpo', stacked_left(upgoing), right, preferred_elem...]
    reshape x0 -> x1, local copies, waits for them, and re-layouts: none -> 6.23 us  [per_device(): downgoing.reshape(2, freq_local, shot_local, shot_count, core_count, block)]
    convert_element_type x1 -> x2, other arithmetic: 1.94 us -> 5.87 us  [the longest x1 3.36 us: per_device(): scaled = (whole.astype(jnp.float32) / power_wide).astype(jnp.bfloat16)]
  transfers between devices with their start and end apart: 4 -> 4, of which waited for: 3 -> 3; matrix products, arithmetic and copies ran while one was open for 20% -> 12% of each run, Pallas kernels for 0% -> 0%
where the time goes in v1:
time: 258 us; the launch traced here: 257 us
  waiting for transfers between devices  139 us (54%)
  local copies, waits for them, and re-layouts  56.5 us (22%)
  matrix products  19.8 us (8%)
  other arithmetic  17.5 us (7%)
  between operations  14.1 us (5%)
  blocking collectives  9.71 us (4%)
    unnamed x5, waiting for transfers between devices  88.1 us
    all_gather x1, waiting for transfers between devices, per_device(): across = lax.all_gather(gram_rows, 'shot', axis=0, tiled=True)  45 us
    slice x3, local copies, waits for them, and re-layouts, stacked_left(): real_left = jnp.concatenate([factor[0], factor[1]], axis=1)  16.1 us
    unnamed x28, local copies, waits for them, and re-layouts  15.5 us
    unnamed x1, blocking collectives  9.71 us
    transpose x1, local copies, waits for them, and re-layouts, per_device(): jnp.einsum('qtpu,qto->uqpo', stacked_left(upgoing), right, preferred_elem...  6.27 us
    reshape x1, local copies, waits for them, and re-layouts, per_device(): downgoing.reshape(2, freq_local, shot_local, shot_count, core_count, block)  6.23 us
    reduce_scatter x1, waiting for transfers between devices, per_device(): lax.psum_scatter(corr_part, 'shot', scatter_dimension=0, tiled=True)  5.76 us
  transfers between devices with their start and end apart: 4, of which 3 were waited for; matrix products, arithmetic and copies ran while one was open for 12% of the time, Pallas kernels for 0%

profile of v1, /device:TPU:0, one launch (start us, length us, event | category | flops | bytes accessed | tf_op | source)
XLA Modules:
  0.0 256.9 jit_solution(16034828763522613362)
XLA Ops:
  6.5 6.2 %reshape.314 = bf16[2,1,768,4,2,128]{5,4,3,2,0,1:T(2,128)(2,1)} reshape(bf16[2,1,768,1024]{3,2,1,0:T(8,128)(2,1)} %param.3) | data formatting | bytes 6291456 | tf_op jit(solution)/shard_map/reshape | solution.py:48
  12.8 2.0 fusion.67
  14.7 6.8 %constant_dynamic-slice_fusion.1 = (bf16[1,1,768,4,1,128]{5,4,3,2,0,1:T(2,128)(2,1)}, bf16[1,1,768,4,1,128]{5,4,3,2,0,1:T(2,128)(2,1)}) fusion(bf16[2,1,768,4,2,128]{5,4,3,2,0,1:T(2,128)(2,1)} %reshape.314, s32[]{:T(128)S(6)} %add.92, s32[]{:T(128)S(6)} %select_n.32), kind=kLoop, calls=%fused_computation.100 | loop fusion | bytes 3145736 | tf_op jit(solution)/shard_map/slice | solution.py:14
  21.5 4.6 %copy.48 = bf16[1,1,768,4,1,128]{2,5,3,4,1,0:T(8,128)(2,1)} copy(bf16[1,1,768,4,1,128]{5,4,3,2,0,1:T(2,128)(2,1)} %get-tuple-element.15) | data formatting | bytes 1572864 | tf_op jit(solution)/shard_map/slice | solution.py:14
  26.2 4.7 %copy.47 = bf16[1,1,768,4,1,128]{2,5,3,4,1,0:T(8,128)(2,1)} copy(bf16[1,1,768,4,1,128]{5,4,3,2,0,1:T(2,128)(2,1)} %get-tuple-element.16) | data formatting | bytes 1572864 | tf_op jit(solution)/shard_map/slice | solution.py:14
  30.8 2.1 bitcast_negate_fusion
  32.9 2.6 %copy.56 = bf16[1,1,768,1024]{2,3,1,0:T(8,128)(2,1)} copy(bf16[1,1,768,1024]{3,2,1,0:T(8,128)(2,1)} %get-tuple-element.13) | data formatting | bytes 3145728
  35.5 2.7 %copy.57 = bf16[1,1,768,1024]{2,3,1,0:T(8,128)(2,1)} copy(bf16[1,1,768,1024]{3,2,1,0:T(8,128)(2,1)} %get-tuple-element.14) | data formatting | bytes 3145728
  38.1 2.1 maximum_bitcast_fusion.6
  42.1 4.7 %convert_bitcast_fusion = bf16[4,1,2,128,1024]{4,3,0,2,1:T(8,128)(2,1)} fusion(bf16[2,4,128,1536]{3,2,1,0:T(8,128)(2,1)S(1)} %bitcast.205, bf16[1,768,1024]{1,2,0:T(8,128)(2,1)S(1)} %bitcast.209, bf16[1,768,1024]{1,2,0:T(8,128)(2,1)S(1)} %bitcast.207), kind=kOutput, calls=%fused_computation.16 | convolution fusion | flops 3228565504 | bytes 8388608 | tf_op jit(solution)/shard_map/qtpu,qto->qpuo/dot_general | solution.py:51
  48.1 88.1 %all-reduce.4.cloned.1.call-done = bf16[4,1,2,128,1024]{4,3,0,2,1:T(8,128)(2,1)} async-done(((bf16[4,1,2,128,1024]{4,3,0,2,1:T(8,128)(2,1)}), bf16[4,1,2,128,1024]{4,3,0,2,1:T(8,128)(2,1)}) %all-reduce.4.cloned.1.call-update) | async-done | bytes 2097168
  136.1 2.5 constant_dynamic-slice_fusion.3
  138.7 45.0 %all-gather.4.cloned.1.call-done = bf16[4,1,2,128,1024]{4,3,0,2,1:T(8,128)(2,1)} async-done(((bf16[1,1,2,128,1024]{4,3,0,2,1:T(8,128)(2,1)}), bf16[4,1,2,128,1024]{4,3,0,2,1:T(8,128)(2,1)}) %all-gather.4.cloned.1.call-update) | async-done | bytes 2097168 | tf_op jit(solution)/shard_map/all_gather | solution.py:57
  183.7 3.1 %copy.50 = bf16[4,1,2,128,1024]{4,3,2,0,1:T(8,128)(2,1)} copy(bf16[4,1,2,128,1024]{4,3,0,2,1:T(8,128)(2,1)} %all-gather.4.cloned.1.call-done) | data formatting | bytes 4194304 | tf_op jit(solution)/shard_map/all_gather | solution.py:57
  188.9 1.3 fusion.60
  193.0 4.6 %fusion.7 = bf16[512,2,1024]{0,2,1:T(8,128)(2,1)} fusion(bf16[1,1536,1,512]{3,1,2,0:T(8,128)(2,1)S(1)} %get-tuple-element.20, bf16[1,1536,1,512]{3,1,2,0:T(8,128)(2,1)S(1)} %get-tuple-element.19, bf16[1,768,1024]{1,2,0:T(8,128)(2,1)S(1)} %bitcast.210, bf16[1,768,1024]{1,2,0:T(8,128)(2,1)S(1)} %bitcast.208), kind=kOutput, calls=%fused_computation.13 | convolution fusion | flops 3233808384 | bytes 8388608 | tf_op jit(solution)/shard_map/qtpu,qto->uqpo/dot_general | solution.py:65
  197.5 6.3 %copy.45 = bf16[512,2,1024]{2,1,0:T(2,128)(2,1)} copy(bf16[512,2,1024]{0,2,1:T(8,128)(2,1)} %fusion.7) | data formatting | bytes 4194304 | tf_op jit(solution)/shard_map/qtpu,qto->uqpo/transpose | solution.py:65
  203.8 5.3 %gather_fusion = bf16[256,2,1024]{2,1,0:T(2,128)(2,1)} fusion(bf16[512,2,1024]{2,1,0:T(2,128)(2,1)} %copy.45, s32[1024]{0:T(1024)S(1)} %pad_clamp_fusion), kind=kCustom, calls=%fused_computation | custom fusion | bytes 2098176 | tf_op jit(solution)/shard_map/jit(_take)/gather | solution.py:70
  209.2 2.5 fusion.10
  211.7 2.2 multiply_reduce_fusion
  213.9 1.4 dynamic-update-slice
  215.4 9.7 %all-reduce = f32[4]{0:T(128)S(1)} all-reduce(f32[4]{0:T(128)S(1)} %dynamic-update-slice), channel_id=1, replica_groups=mesh['grp'=2,'shot'=4,'freq'=2,'sub'=2] {'shot'}, use_global_device_ids=true, to_apply=%add | all-reduce | flops 4 | bytes 32
  226.4 3.4 %fusion = bf16[2,1,4,2,128,1024]{5,4,3,2,1,0:T(8,128)(2,1)S(1)} fusion(bf16[4,2,2,128,1024]{4,3,2,0,1:T(8,128)(2,1)} %all-gather.6.cloned.1.call-done, f32[]{:T(128)S(6)} %div.32), kind=kLoop, calls=%fused_computation.3 | loop fusion | flops 6291456 | bytes 8388612 | tf_op jit(solution)/shard_map/convert_element_type | solution.py:74
  232.0 5.8 %reduce-scatter.5.cloned.1.call-done = bf16[64,1,2,1024]{3,0,1,2:T(8,128)(2,1)} async-done(((bf16[256,1,2,1024]{3,0,1,2:T(8,128)(2,1)}), bf16[64,1,2,1024]{3,0,1,2:T(8,128)(2,1)}) %reduce-scatter.5.cloned.1.call-update) | async-done | bytes 262160 | tf_op jit(solution)/shard_map/reduce_scatter | solution.py:71
  (74 shorter events, 23.3 us)
Async XLA Ops:
  6.5 129.6 %all-reduce.4.cloned.1.call-start = ((), (), s32[]{:S(2)}) async-start(), calls=%async_computation.4 | async-start | bytes 4194304
  6.5 6.2 %copy-start.2 = (bf16[2,1,768,1024]{3,2,1,0:T(8,128)(2,1)S(1)}, bf16[2,1,768,1024]{3,2,1,0:T(8,128)(2,1)}, u32[]{:S(2)}) copy-start(bf16[2,1,768,1024]{3,2,1,0:T(8,128)(2,1)} %param.3) | copy-start | bytes 9437188
  40.2 1.4 copy-start.5
  40.2 1.9 copy-start.7
  46.8 0.7 copy-start.10
  46.8 136.9 %all-gather.4.cloned.1.call-start = ((), (), s32[]{:S(2)}) async-start(), calls=%async_computation.2 | async-start | bytes 2621440 | tf_op jit(solution)/shard_map/all_gather | solution.py:57
  138.7 87.7 %all-gather.6.cloned.1.call-start = ((), (), s32[]{:S(2)}) async-start(), calls=%async_computation.3 | async-start | bytes 6291456 | tf_op jit(solution)/shard_map/all_gather | solution.py:58
  186.8 0.7 copy-start.9
  186.9 50.9 %reduce-scatter.5.cloned.1.call-start = ((), (), s32[]{:S(2)}) async-start(), calls=%async_computation.1 | async-start | bytes 1310720 | tf_op jit(solution)/shard_map/reduce_scatter | solution.py:71
  188.9 1.6 copy-start.4
  190.7 1.6 copy-start.6
  190.7 2.3 copy-start.8
  230.2 1.3 copy-start
  237.8 1.7 copy-start.1
  239.9 1.0 copy-start.3
Sparse Core Ops, SparseCore 0:
  46.9 89.1 all-reduce.3
  138.8 44.8 all-gather.3
  187.0 12.3 all-gather.5
  211.8 25.8 reduce-scatter.4

commit v2 on v1

--- a/solution.py
+++ b/solution.py
@@ -38,29 +38,22 @@
     core_index = lax.axis_index("sub")
     receivers = downgoing.shape[3]
     freq_local = downgoing.shape[1]
-    shot_local = downgoing.shape[2]
     sources = source_order.shape[0]
     source_local = sources // (shot_count * core_count)
     block = receivers // (shot_count * core_count)
 
     right = stacked_right(downgoing)
 
-    columns = downgoing.reshape(2, freq_local, shot_local, shot_count, core_count, block)
-    own_columns = lax.dynamic_slice_in_dim(columns, core_index, 1, 4)[:, :, :, :, 0]
-    own_columns = own_columns.reshape(2, freq_local, shot_local, shot_count * block)
-    gram_part = jnp.einsum(
-        "qtpu,qto->qpuo", stacked_left(own_columns), right, preferred_element_type=jnp.float32
+    gram_full = jnp.einsum(
+        "qtpu,qto->uqpo", stacked_left(downgoing), right, preferred_element_type=jnp.float32
     )
-    gram_part = gram_part.reshape(freq_local, 2, shot_count, block, receivers)
-    gram_part = jnp.transpose(gram_part, (2, 0, 1, 3, 4)).astype(jnp.bfloat16)
+    gram_full = gram_full.reshape(shot_count, core_count, block, freq_local, 2, receivers)
+    gram_part = lax.dynamic_slice_in_dim(gram_full, core_index, 1, 1)
+    gram_part = gram_part.reshape(shot_count * block, freq_local, 2, receivers).astype(jnp.bfloat16)
     gram_rows = lax.psum_scatter(gram_part, "shot", scatter_dimension=0, tiled=True)
-    across = lax.all_gather(gram_rows, "shot", axis=0, tiled=True)
-    whole = lax.all_gather(across, "sub", axis=1, tiled=False)
-    whole = jnp.transpose(whole, (3, 2, 0, 1, 4, 5)).reshape(2, freq_local, receivers, receivers)
 
     local_power = jnp.sum(jnp.square(downgoing.astype(jnp.float32)), axis=(0, 2, 3))
-    power = jnp.sum(lax.all_gather(local_power, "shot", axis=0), axis=0) / receivers
-    power_wide = power[None, :, None, None]
+    power = lax.psum(local_power, "shot") / receivers
 
     corr_all = jnp.einsum(
         "qtpu,qto->uqpo", stacked_left(upgoing), right, preferred_element_type=jnp.float32
@@ -68,6 +61,16 @@
     order_table = source_order.reshape(shot_count, core_count, source_local)
     own_order = lax.dynamic_slice_in_dim(order_table, core_index, 1, 1).reshape(-1)
     corr_part = jnp.take(corr_all, own_order, axis=0).astype(jnp.bfloat16)
+
+    gram_rows, corr_part, power = lax.optimization_barrier((gram_rows, corr_part, power))
+    power_wide = power[None, :, None, None]
+
+    across = lax.all_gather(gram_rows, "shot", axis=0, tiled=True)
+    across = across.reshape(shot_count, block, freq_local, 2, receivers)
+    whole = lax.all_gather(across, "sub", axis=1, tiled=False)
+    whole = whole.reshape(receivers, freq_local, 2, receivers)
+    whole = jnp.transpose(whole, (2, 1, 0, 3))
+
     corr = lax.psum_scatter(corr_part, "shot", scatter_dimension=0, tiled=True).astype(jnp.float32)
     target = jnp.transpose(corr, (2, 1, 0, 3)) / power_wide
 

time: 258 us -> 190 us (0.74)
  waiting for transfers between devices: 139 us -> 95.3 us
  local copies, waits for them, and re-layouts: 56.5 us -> 22.6 us
  matrix products: 19.8 us -> 26.6 us
  blocking collectives: 9.71 us -> 14.3 us
    unnamed x5 -> x4, waiting for transfers between devices: 88.1 us -> 0.39 us
    reduce_scatter x1, waiting for transfers between devices: 5.76 us -> 24.8 us  [per_device(): lax.psum_scatter(corr_part, 'shot', scatter_dimension=0, tiled=True)]
    slice x4 -> x0, local copies, waits for them, and re-layouts: 16.5 us -> none  [the longest x3 16.1 us: stacked_left(): real_left = jnp.concatenate([factor[0], factor[1]], axis=1)]
    psum x0 -> x1, blocking collectives: none -> 14.3 us  [per_device(): power = lax.psum(local_power, 'shot') / receivers]
    all_gather x1, waiting for transfers between devices: 0.02 us -> 13.4 us  [per_device(): whole = lax.all_gather(across, 'sub', axis=1, tiled=False)]
    unnamed x28 -> x12, local copies, waits for them, and re-layouts: 15.5 us -> 5.5 us
    unnamed x1 -> x0, blocking collectives: 9.71 us -> none
    reduce_scatter x0 -> x1, waiting for transfers between devices: none -> 9.67 us  [per_device(): lax.psum_scatter(gram_part, 'shot', scatter_dimension=0, tiled=True)]
  transfers between devices with their start and end apart: 4 -> 4, of which waited for: 3 -> 4; matrix products, arithmetic and copies ran while one was open for 12% -> 14% of each run, Pallas kernels for 0% -> 0%
where the time goes in v2:
time: 190 us; the launch traced here: 189 us
  waiting for transfers between devices  95.3 us (50%)
  matrix products  26.6 us (14%)
  local copies, waits for them, and re-layouts  22.6 us (12%)
  other arithmetic  15.9 us (8%)
  blocking collectives  14.3 us (8%)
  between operations  14.1 us (7%)
    all_gather x1, waiting for transfers between devices, per_device(): across = lax.all_gather(gram_rows, 'shot', axis=0, tiled=True)  47 us
    reduce_scatter x1, waiting for transfers between devices, per_device(): lax.psum_scatter(corr_part, 'shot', scatter_dimension=0, tiled=True)  24.8 us
    psum x1, blocking collectives, per_device(): power = lax.psum(local_power, 'shot') / receivers  14.3 us
    all_gather x1, waiting for transfers between devices, per_device(): whole = lax.all_gather(across, 'sub', axis=1, tiled=False)  13.4 us
    reduce_scatter x1, waiting for transfers between devices, per_device(): lax.psum_scatter(gram_part, 'shot', scatter_dimension=0, tiled=True)  9.67 us
    dot_general x1, matrix products, per_device(): jnp.einsum('qtpu,qto->uqpo', stacked_left(downgoing), right, preferred_el...  8.21 us
    unnamed x12, local copies, waits for them, and re-layouts  5.5 us
    transpose x1, local copies, waits for them, and re-layouts, per_device(): jnp.einsum('qtpu,qto->uqpo', stacked_left(upgoing), right, preferred_elem...  5.05 us
  transfers between devices with their start and end apart: 4, of which 4 were waited for; matrix products, arithmetic and copies ran while one was open for 14% of the time, Pallas kernels for 0%

profile of v2, /device:TPU:0, one launch (start us, length us, event | category | flops | bytes accessed | tf_op | source)
XLA Modules:
  0.0 189.1 jit_solution(12423138623566420429)
XLA Ops:
  6.5 3.3 %fusion.66 = (bf16[1,1,768,1024]{3,2,1,0:T(8,128)(2,1)S(1)}, bf16[1,1,768,1024]{3,2,1,0:T(8,128)(2,1)}) fusion(bf16[2,1,768,1024]{3,2,1,0:T(8,128)(2,1)} %param.3), kind=kLoop, calls=%fused_computation.112 | loop fusion | bytes 6291456 | tf_op jit(solution)/shard_map/slice | solution.py:20
  9.9 1.7 copy.39
  11.6 1.6 copy.40
  13.2 1.3 bitcast_negate_fusion
  15.2 1.7 fusion.22
  16.9 8.2 %fusion = bf16[1024,2,1024]{0,2,1:T(8,128)(2,1)} fusion(bf16[1,1536,1,1024]{1,3,2,0:T(8,128)(2,1)S(1)} %get-tuple-element.22, bf16[1,1536,1,1024]{1,3,2,0:T(8,128)(2,1)S(1)} %get-tuple-element.21, bf16[1,768,1024]{1,2,0:T(8,128)(2,1)S(1)} %bitcast.199, bf16[1,768,1024]{1,2,0:T(8,128)(2,1)S(1)} %bitcast.195), kind=kOutput, calls=%fused_computation.3 | convolution fusion | flops 6461325312 | bytes 13631488 | tf_op jit(solution)/shard_map/qtpu,qto->uqpo/dot_general | solution.py:47
  25.1 3.1 %dynamic-slice_convert_fusion = bf16[4,1,128,1,2,1024]{5,2,1,0,4,3:T(8,128)(2,1)} fusion(bf16[4,2,128,1,2,1024]{5,2,1,0,4,3:T(8,128)(2,1)} %bitcast.202, s32[]{:T(128)S(6)} %select_n.32), kind=kLoop, calls=%fused_computation.7 | loop fusion | bytes 4194308 | tf_op jit(solution)/shard_map/convert_element_type | solution.py:52
  28.2 4.1 %multiply_reduce_fusion = f32[]{:T(128)} fusion(bf16[2,1,768,1024]{3,2,1,0:T(8,128)(2,1)} %param.3), kind=kLoop, calls=%fused_computation.6 | loop fusion | flops 4718591 | bytes 3145732 | tf_op jit(solution)/shard_map/reduce_sum | solution.py:55
  32.3 14.3 %psum.7 = f32[1]{0:T(128)} all-reduce(f32[1]{0:T(128)} %bitcast.22), channel_id=1, replica_groups=mesh['grp'=2,'shot'=4,'freq'=2,'sub'=2] {'shot'}, use_global_device_ids=true, to_apply=%region_2.0 | all-reduce | flops 1 | bytes 8 | tf_op jit(solution)/shard_map/psum | solution.py:56
  46.6 1.2 fusion.60
  47.8 1.5 slice_bitcast_fusion.3
  49.6 4.6 %fusion.8 = bf16[512,2,1024]{0,2,1:T(8,128)(2,1)} fusion(bf16[1,1536,1,512]{3,1,2,0:T(8,128)(2,1)S(1)} %get-tuple-element.24, bf16[1,1536,1,512]{3,1,2,0:T(8,128)(2,1)S(1)} %get-tuple-element.23, bf16[1,768,1024]{1,2,0:T(8,128)(2,1)S(1)} %bitcast.200, bf16[1,768,1024]{1,2,0:T(8,128)(2,1)S(1)} %bitcast.196), kind=kOutput, calls=%fused_computation.16 | convolution fusion | flops 3233808384 | bytes 8388608 | tf_op jit(solution)/shard_map/qtpu,qto->uqpo/dot_general | solution.py:58
  54.2 5.0 %copy.35 = bf16[512,2,1024]{2,1,0:T(2,128)(2,1)S(1)} copy(bf16[512,2,1024]{0,2,1:T(8,128)(2,1)} %fusion.8) | data formatting | bytes 4194304 | tf_op jit(solution)/shard_map/qtpu,qto->uqpo/transpose | solution.py:58
  60.6 2.8 %gather_fusion = bf16[256,2,1024]{2,1,0:T(2,128)(2,1)S(1)} fusion(bf16[512,2,1024]{2,1,0:T(2,128)(2,1)S(1)} %copy.35, s32[1024]{0:T(1024)S(1)} %pad_clamp_fusion), kind=kCustom, calls=%fused_computation | custom fusion | bytes 2098176 | tf_op jit(solution)/shard_map/jit(_take)/gather | solution.py:63
  64.0 1.3 fusion.11
  65.3 9.7 %reduce-scatter.3.cloned.1.call-done = bf16[128,1,2,1024]{3,0,2,1:T(8,128)(2,1)} async-done(((bf16[512,1,2,1024]{3,0,2,1:T(8,128)(2,1)}), bf16[128,1,2,1024]{3,0,2,1:T(8,128)(2,1)}) %reduce-scatter.3.cloned.1.call-update) | async-done | bytes 524304 | tf_op jit(solution)/shard_map/reduce_scatter | solution.py:53
  75.1 47.0 %all-gather.3.cloned.1.call-done = bf16[512,1,2,1024]{3,0,2,1:T(8,128)(2,1)} async-done(((bf16[128,1,2,1024]{3,0,2,1:T(8,128)(2,1)}), bf16[512,1,2,1024]{3,0,2,1:T(8,128)(2,1)}) %all-gather.3.cloned.1.call-update) | async-done | bytes 2097168 | tf_op jit(solution)/shard_map/all_gather | solution.py:68
  122.6 13.4 %all-gather.5.cloned.1.call-done = bf16[4,2,128,1,2,1024]{5,2,1,0,4,3:T(8,128)(2,1)} async-done(((bf16[4,1,128,1,2,1024]{5,2,1,0,4,3:T(8,128)(2,1)}), bf16[4,2,128,1,2,1024]{5,2,1,0,4,3:T(8,128)(2,1)}) %all-gather.5.cloned.1.call-update) | async-done | bytes 4194320 | tf_op jit(solution)/shard_map/all_gather | solution.py:70
  136.1 3.3 %divide_convert_fusion = bf16[4,2,128,1,2,1024]{5,2,1,0,4,3:T(8,128)(2,1)S(1)} fusion(bf16[4,2,128,1,2,1024]{5,2,1,0,4,3:T(8,128)(2,1)} %all-gather.5.cloned.1.call-done, f32[]{:T(128)} %bitcast.23), kind=kLoop, calls=%fused_computation.1 | loop fusion | flops 6291456 | bytes 8388612 | tf_op jit(solution)/shard_map/convert_element_type | solution.py:77
  139.9 1.5 copy-done
  141.9 24.8 %reduce-scatter.5.cloned.1.call-done = bf16[64,1,2,1024]{3,0,1,2:T(8,128)(2,1)} async-done(((bf16[256,1,2,1024]{3,0,1,2:T(8,128)(2,1)}), bf16[64,1,2,1024]{3,0,1,2:T(8,128)(2,1)}) %reduce-scatter.5.cloned.1.call-update) | async-done | bytes 262160 | tf_op jit(solution)/shard_map/reduce_scatter | solution.py:74
  166.7 1.2 fusion.39
  167.9 2.2 %fusion.41 = f32[64,1024]{1,0:T(8,128)S(1)} fusion(bf16[2,1,64,1024]{3,2,1,0:T(8,128)(2,1)S(1)} %fusion.39, bf16[2,1,1024,1024]{3,2,0,1:T(8,128)(2,1)} %bitcast.174), kind=kOutput, calls=%fused_computation.83 | convolution fusion | flops 134217728 | bytes 2490368 | tf_op jit(solution)/shard_map/qjc,qcr->qjr/dot_general | solution.py:26
  170.1 2.1 %fusion.40 = f32[64,1024]{1,0:T(8,128)S(1)} fusion(bf16[2,1,64,1024]{3,2,1,0:T(8,128)(2,1)S(1)} %fusion.39, bf16[2,1,1024,1024]{3,2,0,1:T(8,128)(2,1)} %bitcast.175), kind=kOutput, calls=%fused_computation.82 | convolution fusion | flops 134217728 | bytes 2490368 | tf_op jit(solution)/shard_map/qjc,qcr->qjr/dot_general | solution.py:28
  (51 shorter events, 14.3 us)
Async XLA Ops:
  6.5 68.5 %reduce-scatter.3.cloned.1.call-start = ((), (), s32[]{:S(2)}) async-start(), calls=%async_computation.2 | async-start | bytes 2621440 | tf_op jit(solution)/shard_map/reduce_scatter | solution.py:53
  13.2 2.0 %copy-start.3 = (bf16[1,1,768,1024]{2,3,1,0:T(8,128)(2,1)S(1)}, bf16[1,1,768,1024]{2,3,1,0:T(8,128)(2,1)}, u32[]{:S(2)}) copy-start(bf16[1,1,768,1024]{2,3,1,0:T(8,128)(2,1)} %copy.40) | copy-start | bytes 4718596
  28.2 93.8 %all-gather.3.cloned.1.call-start = ((), (), s32[]{:S(2)}) async-start(), calls=%async_computation.4 | async-start | bytes 2621440 | tf_op jit(solution)/shard_map/all_gather | solution.py:68
  54.2 5.1 %copy-start.4 = (s32[512]{0:T(512)S(1)}, s32[512]{0:T(512)}, u32[]{:S(2)}) copy-start(s32[512]{0:T(512)} %param.5) | copy-start | bytes 6148
  75.0 61.1 %all-gather.5.cloned.1.call-start = ((), (), s32[]{:S(2)}) async-start(), calls=%async_computation.5 | async-start | bytes 6291456 | tf_op jit(solution)/shard_map/all_gather | solution.py:70
  122.1 44.6 %reduce-scatter.5.cloned.1.call-start = ((), (), s32[]{:S(2)}) async-start(), calls=%async_computation.3 | async-start | bytes 1310720 | tf_op jit(solution)/shard_map/reduce_scatter | solution.py:74
  139.4 1.9 %copy-start = (bf16[4,2,128,1,2,1024]{5,2,1,0,4,3:T(8,128)(2,1)}, bf16[4,2,128,1,2,1024]{5,2,1,0,4,3:T(8,128)(2,1)S(1)}, u32[]{:S(2)}) copy-start(bf16[4,2,128,1,2,1024]{5,2,1,0,4,3:T(8,128)(2,1)S(1)} %divide_convert_fusion) | copy-start | bytes 12582916
  166.7 5.5 %copy-start.1 = (bf16[4,2,128,1,2,1024]{5,2,1,0,4,3:T(8,128)(2,1)S(1)}, bf16[4,2,128,1,2,1024]{5,2,1,0,4,3:T(8,128)(2,1)}, u32[]{:S(2)}) copy-start(bf16[4,2,128,1,2,1024]{5,2,1,0,4,3:T(8,128)(2,1)} %copy-done) | copy-start | bytes 12582916
  172.2 1.0 copy-start.2
Sparse Core Ops, SparseCore 0:
  28.3 46.6 reduce-scatter.2
  76.6 45.3 all-gather.2
  123.7 12.3 all-gather.4
  138.3 28.2 reduce-scatter.4

commit v3 on v2

--- a/solution.py
+++ b/solution.py
@@ -32,6 +32,39 @@
     return solution
 
 
+def strip_partials(gram_full, shot_count, core_count, core_index, rows_each, tile, span):
+    receivers = gram_full.shape[0]
+    rows = gram_full.reshape(shot_count, core_count, rows_each, *gram_full.shape[1:])
+    rows = lax.dynamic_slice_in_dim(rows, core_index, 1, 1)[:, 0].astype(jnp.bfloat16)
+    doubled = jnp.concatenate([rows, rows], axis=-1)
+    windows = []
+    for k in range(shot_count):
+        start = ((k * core_count + core_index) * rows_each // tile) * tile
+        windows.append(lax.dynamic_slice_in_dim(doubled[k], start, span, axis=-1))
+    return jnp.stack(windows).reshape(shot_count * rows_each, *gram_full.shape[1:3], span)
+
+
+def rebuild_gram(strips, groups, block):
+    half = groups // 2
+    freq_local = strips.shape[2]
+    pieces = strips.reshape(groups, block, freq_local, 2, half + 1, block)
+    direct = [pieces[:, :, :, :, offset, :] for offset in range(half + 1)]
+    mirrored = []
+    for offset in range(half + 1, groups):
+        back = groups - offset
+        source = pieces[:, :, :, :, back, :]
+        flipped = jnp.transpose(source, (0, 4, 2, 3, 1))
+        flipped = jnp.stack([flipped[:, :, :, 0], -flipped[:, :, :, 1]], axis=3)
+        mirrored.append(jnp.roll(flipped, back, axis=0))
+    cyclic = jnp.stack(direct + mirrored, axis=1)
+    doubled = jnp.concatenate([cyclic, cyclic], axis=1)
+    flat = doubled.reshape(2 * groups * groups, *doubled.shape[2:])
+    skewed = flat[groups : groups + groups * (2 * groups - 1)]
+    blocks = skewed.reshape(groups, 2 * groups - 1, *doubled.shape[2:])[:, :groups]
+    blocks = jnp.transpose(blocks, (4, 3, 0, 2, 1, 5))
+    return blocks.reshape(2, freq_local, groups * block, groups * block)
+
+
 def per_device(downgoing, upgoing, source_order):
     shot_count = lax.axis_size("shot")
     core_count = lax.axis_size("sub")
@@ -39,18 +72,20 @@
     receivers = downgoing.shape[3]
     freq_local = downgoing.shape[1]
     sources = source_order.shape[0]
-    source_local = sources // (shot_count * core_count)
-    block = receivers // (shot_count * core_count)
+    groups = shot_count * core_count
+    source_local = sources // groups
+    rows_each = receivers // groups
+    tiles = 8 if groups % 8 == 0 else groups
+    tile = receivers // tiles
+    span = (tiles // 2 + 1) * tile
 
     right = stacked_right(downgoing)
 
     gram_full = jnp.einsum(
         "qtpu,qto->uqpo", stacked_left(downgoing), right, preferred_element_type=jnp.float32
     )
-    gram_full = gram_full.reshape(shot_count, core_count, block, freq_local, 2, receivers)
-    gram_part = lax.dynamic_slice_in_dim(gram_full, core_index, 1, 1)
-    gram_part = gram_part.reshape(shot_count * block, freq_local, 2, receivers).astype(jnp.bfloat16)
-    gram_rows = lax.psum_scatter(gram_part, "shot", scatter_dimension=0, tiled=True)
+    gram_part = strip_partials(gram_full, shot_count, core_count, core_index, rows_each, tile, span)
+    gram_strip = lax.psum_scatter(gram_part, "shot", scatter_dimension=0, tiled=True)
 
     local_power = jnp.sum(jnp.square(downgoing.astype(jnp.float32)), axis=(0, 2, 3))
     power = lax.psum(local_power, "shot") / receivers
@@ -62,14 +97,20 @@
     own_order = lax.dynamic_slice_in_dim(order_table, core_index, 1, 1).reshape(-1)
     corr_part = jnp.take(corr_all, own_order, axis=0).astype(jnp.bfloat16)
 
-    gram_rows, corr_part, power = lax.optimization_barrier((gram_rows, corr_part, power))
+    gram_strip, corr_part, power = lax.optimization_barrier((gram_strip, corr_part, power))
     power_wide = power[None, :, None, None]
 
-    across = lax.all_gather(gram_rows, "shot", axis=0, tiled=True)
-    across = across.reshape(shot_count, block, freq_local, 2, receivers)
-    whole = lax.all_gather(across, "sub", axis=1, tiled=False)
-    whole = whole.reshape(receivers, freq_local, 2, receivers)
-    whole = jnp.transpose(whole, (2, 1, 0, 3))
+    across = lax.all_gather(gram_strip, "shot", axis=0, tiled=True)
+    across = across.reshape(shot_count, rows_each, freq_local, 2, span)
+    if core_count == 2:
+        other = lax.ppermute(across, "sub", perm=[(0, 1), (1, 0)])
+        first = jnp.where(core_index == 0, across, other)
+        second = jnp.where(core_index == 0, other, across)
+        strips = jnp.stack([first, second], axis=1)
+    else:
+        strips = lax.all_gather(across, "sub", axis=1, tiled=False)
+    strips = strips.reshape(tiles, tile, freq_local, 2, span)
+    whole = rebuild_gram(strips, tiles, tile)
 
     corr = lax.psum_scatter(corr_part, "shot", scatter_dimension=0, tiled=True).astype(jnp.float32)
     target = jnp.transpose(corr, (2, 1, 0, 3)) / power_wide

time: 190 us -> 170 us (0.89)
  waiting for transfers between devices: 95.3 us -> 34.3 us
  local copies, waits for them, and re-layouts: 22.6 us -> 55.7 us
  other arithmetic: 15.9 us -> 26.6 us
  matrix products: 26.6 us -> 23.8 us
    all_gather x2 -> x1, waiting for transfers between devices: 60.4 us -> 31 us  [per_device(): across = lax.all_gather(gram_strip, 'shot', axis=0, tiled=True)]
    reduce_scatter x1, waiting for transfers between devices: 24.8 us -> 0.02 us  [per_device(): lax.psum_scatter(corr_part, 'shot', scatter_dimension=0, tiled=True)]
    unnamed x12 -> x37, local copies, waits for them, and re-layouts: 5.5 us -> 16.3 us
    concatenate x0 -> x1, local copies, waits for them, and re-layouts: none -> 10.3 us  [rebuild_gram(): doubled = jnp.concatenate([cyclic, cyclic], axis=1)]
    slice x0 -> x6, local copies, waits for them, and re-layouts: none -> 9.91 us  [the longest x1 4.99 us: rebuild_gram(): skewed = flat[groups:groups + groups * (2 * groups - 1)]]
    reduce_scatter x1, waiting for transfers between devices: 9.67 us -> 0.01 us  [per_device(): lax.psum_scatter(gram_part, 'shot', scatter_dimension=0, tiled=True)]
    another operation x0 -> x3, local copies, waits for them, and re-layouts: none -> 5.17 us  [the longest x1 3.49 us: per_device(): strips = jnp.stack([first, second], axis=1)]
    another operation x0 -> x3, other arithmetic: none -> 4.62 us  [the longest x2 3.34 us: per_device(): strips = jnp.stack([first, second], axis=1)]
  transfers between devices with their start and end apart: 4 -> 4, of which waited for: 4 -> 2; matrix products, arithmetic and copies ran while one was open for 14% -> 40% of each run, Pallas kernels for 0% -> 0%
where the time goes in v3:
time: 170 us; the launch traced here: 169 us
  local copies, waits for them, and re-layouts  55.7 us (33%)
  waiting for transfers between devices  34.3 us (20%)
  other arithmetic  26.6 us (16%)
  matrix products  23.8 us (14%)
  blocking collectives  14.3 us (8%)
  between operations  14.3 us (8%)
    all_gather x1, waiting for transfers between devices, per_device(): across = lax.all_gather(gram_strip, 'shot', axis=0, tiled=True)  31 us
    unnamed x37, local copies, waits for them, and re-layouts  16.3 us
    psum x1, blocking collectives, per_device(): power = lax.psum(local_power, 'shot') / receivers  14.3 us
    concatenate x1, local copies, waits for them, and re-layouts, rebuild_gram(): doubled = jnp.concatenate([cyclic, cyclic], axis=1)  10.3 us
    dot_general x1, matrix products, per_device(): jnp.einsum('qtpu,qto->uqpo', stacked_left(downgoing), right, preferred_el...  6.91 us
    transpose x1, local copies, waits for them, and re-layouts, per_device(): jnp.einsum('qtpu,qto->uqpo', stacked_left(upgoing), right, preferred_elem...  5.03 us
    slice x1, local copies, waits for them, and re-layouts, rebuild_gram(): skewed = flat[groups:groups + groups * (2 * groups - 1)]  4.99 us
    dot_general x1, matrix products, per_device(): jnp.einsum('qtpu,qto->uqpo', stacked_left(upgoing), right, preferred_elem...  4.58 us
  transfers between devices with their start and end apart: 4, of which 2 were waited for; matrix products, arithmetic and copies ran while one was open for 40% of the time, Pallas kernels for 0%

profile of v3, /device:TPU:0, one launch (start us, length us, event | category | flops | bytes accessed | tf_op | source)
XLA Modules:
  0.0 169.1 jit_solution(11296097143568283349)
XLA Ops:
  6.5 2.2 %fusion.186 = (bf16[1,1,768,1024]{3,2,1,0:T(8,128)(2,1)S(1)}, bf16[1,1,768,1024]{3,2,1,0:T(8,128)(2,1)S(1)}) fusion(bf16[2,1,768,1024]{3,2,1,0:T(8,128)(2,1)} %param.3), kind=kLoop, calls=%fused_computation.219 | loop fusion | bytes 6291456 | tf_op jit(solution)/shard_map/slice | solution.py:20
  8.7 1.6 copy.84
  11.2 1.9 %copy-done.4 = bf16[1,1,768,1024]{2,3,1,0:T(8,128)(2,1)S(1)} copy-done((bf16[1,1,768,1024]{2,3,1,0:T(8,128)(2,1)S(1)}, bf16[1,1,768,1024]{2,3,1,0:T(8,128)(2,1)}, u32[]{:S(2)}) %copy-start.4) | copy-done | bytes 1572888
  13.5 6.9 %fusion = bf16[1024,2,1024]{0,2,1:T(8,128)(2,1)S(1)} fusion(bf16[1,1536,1,1024]{1,3,2,0:T(8,128)(2,1)S(1)} %get-tuple-element.40, bf16[1,1536,1,1024]{1,3,2,0:T(8,128)(2,1)S(1)} %get-tuple-element.39, bf16[1,768,1024]{1,2,0:T(8,128)(2,1)S(1)} %bitcast.317, bf16[1,768,1024]{1,2,0:T(8,128)(2,1)S(1)} %bitcast.313), kind=kOutput, calls=%fused_computation.3 | convolution fusion | flops 6461325312 | bytes 13631488 | tf_op jit(solution)/shard_map/qtpu,qto->uqpo/dot_general | solution.py:84
  20.8 2.5 %pad_slice_fusion.4 = (bf16[1,128,1,2,2048]{4,1,0,3,2:T(8,128)(2,1)}, bf16[1,128,1,2,2048]{4,1,0,3,2:T(8,128)(2,1)S(1)}, bf16[1,128,1,2,2048]{4,1,0,3,2:T(8,128)...) fusion(bf16[4,128,1,2,1024]{4,1,0,3,2:T(8,128)(2,1)S(1)} %fusion.12), kind=kLoop, calls=%fused_computation.11 | loop fusion | bytes 8388608 | tf_op jit(solution)/shard_map/slice | solution.py:43
  23.3 1.3 fusion.148
  24.6 1.4 dynamic-slice_maximum_fusion
  28.3 2.2 %multiply_reduce_fusion = f32[]{:T(128)} fusion(bf16[2,1,768,1024]{3,2,1,0:T(8,128)(2,1)S(1)} %copy-done.2), kind=kLoop, calls=%fused_computation.6 | loop fusion | flops 4718591 | bytes 3145732 | tf_op jit(solution)/shard_map/reduce_sum | solution.py:90
  30.6 14.3 %psum.7 = f32[1]{0:T(128)} all-reduce(f32[1]{0:T(128)} %bitcast.23), channel_id=1, replica_groups=mesh['grp'=2,'shot'=4,'freq'=2,'sub'=2] {'shot'}, use_global_device_ids=true, to_apply=%region_2.3 | all-reduce | flops 1 | bytes 8 | tf_op jit(solution)/shard_map/psum | solution.py:91
  49.5 4.6 %fusion.9 = bf16[512,2,1024]{0,2,1:T(8,128)(2,1)} fusion(bf16[1,1536,1,512]{3,1,2,0:T(8,128)(2,1)S(1)} %get-tuple-element.42, bf16[1,1536,1,512]{3,1,2,0:T(8,128)(2,1)S(1)} %get-tuple-element.41, bf16[1,768,1024]{1,2,0:T(8,128)(2,1)S(1)} %bitcast.318, bf16[1,768,1024]{1,2,0:T(8,128)(2,1)S(1)} %bitcast.314), kind=kOutput, calls=%fused_computation.24 | convolution fusion | flops 3233808384 | bytes 8388608 | tf_op jit(solution)/shard_map/qtpu,qto->uqpo/dot_general | solution.py:93
  54.1 5.0 %copy.63 = bf16[512,2,1024]{2,1,0:T(2,128)(2,1)S(1)} copy(bf16[512,2,1024]{0,2,1:T(8,128)(2,1)} %fusion.9) | data formatting | bytes 4194304 | tf_op jit(solution)/shard_map/qtpu,qto->uqpo/transpose | solution.py:93
  59.8 2.8 %gather_fusion = bf16[256,2,1024]{2,1,0:T(2,128)(2,1)S(1)} fusion(bf16[512,2,1024]{2,1,0:T(2,128)(2,1)S(1)} %copy.63, s32[1024]{0:T(1024)S(1)} %pad_clamp_fusion), kind=kCustom, calls=%fused_computation | custom fusion | bytes 2098176 | tf_op jit(solution)/shard_map/jit(_take)/gather | solution.py:98
  64.0 31.0 %all-gather.2.cloned.1.call-done = bf16[512,1,2,640]{3,0,2,1:T(8,128)(2,1)} async-done(((bf16[128,1,2,640]{3,0,2,1:T(8,128)(2,1)}), bf16[512,1,2,640]{3,0,2,1:T(8,128)(2,1)}) %all-gather.2.cloned.1.call-update) | async-done | bytes 1310736 | tf_op jit(solution)/shard_map/all_gather | solution.py:103
  95.0 3.2 %collective-permute-done = bf16[4,128,1,2,640]{4,1,0,3,2:T(8,128)(2,1)S(1)} collective-permute-done((bf16[4,128,1,2,640]{4,1,0,3,2:T(8,128)(2,1)}, bf16[4,128,1,2,640]{4,1,0,3,2:T(8,128)(2,1)S(1)}, u32[]{:S(2)}, u32[]{:S(2)}) %collective-permute-start) | collective-permute-done | bytes 1310752 | tf_op jit(solution)/shard_map/ppermute | solution.py:106
  98.2 1.6 select_bitcast_fusion.1
  99.8 1.8 %pad_maximum_fusion.1 = bf16[4,2,128,1,2,640]{5,2,0,4,3,1:T(8,128)(2,1)} fusion(bf16[4,1,128,1,2,640]{5,2,0,4,3,1:T(8,128)(2,1)S(1)} %get-tuple-element.30, bf16[4,1,128,1,2,640]{5,2,0,4,3,1:T(8,128)(2,1)S(1)} %get-tuple-element.29), kind=kLoop, calls=%fused_computation.23 | loop fusion | flops 1310720 | bytes 5242880 | tf_op jit(solution)/shard_map/stack | solution.py:109
  101.5 3.5 %copy.65 = bf16[4,2,128,1,2,640]{2,5,4,1,0,3:T(8,128)(2,1)S(1)} copy(bf16[4,2,128,1,2,640]{5,2,0,4,3,1:T(8,128)(2,1)} %pad_maximum_fusion.1) | data formatting | bytes 5242880 | tf_op jit(solution)/shard_map/stack | solution.py:109
  105.0 2.1 %slice_bitcast_fusion.5 = (bf16[8,128,1,2,128]{4,1,3,0,2:T(8,128)(2,1)S(1)}, bf16[8,128,1,2,128]{4,1,3,0,2:T(8,128)(2,1)}, bf16[8,1,128,1,2,128]{2,5,4,0,3,1:T(8...) fusion(bf16[8,128,1,2,5,128]{1,5,4,3,0,2:T(8,128)(2,1)S(1)} %bi, ...), kind=kLoop, calls=%fused_computation.146 | loop fusion | bytes 6815744 | tf_op jit(solution)/shard_map/transpose | solution.py:56
  107.2 1.4 copy.71
  109.5 1.3 copy.70
  126.5 10.3 %copy.79 = bf16[8,16,128,1,2,128]{5,2,4,3,1,0:T(8,128)(2,1)} copy(bf16[8,16,128,1,2,128]{5,2,4,0,3,1:T(8,128)(2,1)} %fusion.147) | data formatting | bytes 16777216 | tf_op jit(solution)/shard_map/concatenate | solution.py:60
  136.8 5.0 %slice.228 = bf16[120,128,1,2,128]{4,1,3,2,0:T(8,128)(2,1)S(1)} slice(bf16[128,128,1,2,128]{4,1,3,2,0:T(8,128)(2,1)} %bitcast.310), slice={[8:128], [0:128], [0:1], [0:2], [0:128]} | slice | bytes 15728640 | tf_op jit(solution)/shard_map/slice | solution.py:62
  142.4 3.6 %fusion.3 = bf16[2,1,8,128,8,128]{5,4,3,2,1,0:T(8,128)(2,1)S(1)} fusion(bf16[8,8,128,1,2,128]{5,2,4,1,0,3:T(8,128)(2,1)S(1)} %slice.229, f32[]{:T(128)} %bitcast.24), kind=kLoop, calls=%fused_computation.13 | loop fusion | flops 6291456 | bytes 8388612 | tf_op jit(solution)/shard_map/convert_element_type | solution.py:118
  149.3 2.1 %fusion.29 = f32[64,1024]{1,0:T(8,128)S(1)} fusion(bf16[2,1,64,1024]{3,2,1,0:T(8,128)(2,1)S(1)} %fusion.141, bf16[128,8,8,128]{3,2,1,0:T(8,128)(2,1)} %bitcast.321), kind=kOutput, calls=%fused_computation.42 | convolution fusion | flops 134217728 | bytes 2490368 | tf_op jit(solution)/shard_map/qjc,qcr->qjr/dot_general | solution.py:28
  (100 shorter events, 41.2 us)
Async XLA Ops:
  6.5 57.4 %reduce-scatter.3.cloned.1.call-start = ((), (), s32[]{:S(2)}) async-start(), calls=%async_computation.2 | async-start | bytes 1638400 | tf_op jit(solution)/shard_map/reduce_scatter | solution.py:88
  11.0 2.5 %copy-start = (bf16[1,1,768,1024]{2,3,1,0:T(8,128)(2,1)}, bf16[1,1,768,1024]{2,3,1,0:T(8,128)(2,1)S(1)}, u32[]{:S(2)}) copy-start(bf16[1,1,768,1024]{2,3,1,0:T(8,128)(2,1)S(1)} %copy.83) | copy-start | bytes 4718596
  11.0 2.0 %copy-start.4 = (bf16[1,1,768,1024]{2,3,1,0:T(8,128)(2,1)S(1)}, bf16[1,1,768,1024]{2,3,1,0:T(8,128)(2,1)}, u32[]{:S(2)}) copy-start(bf16[1,1,768,1024]{2,3,1,0:T(8,128)(2,1)} %copy.84) | copy-start | bytes 4718596
  26.0 2.4 %copy-start.2 = (bf16[2,1,768,1024]{3,2,1,0:T(8,128)(2,1)S(1)}, bf16[2,1,768,1024]{3,2,1,0:T(8,128)(2,1)}, u32[]{:S(2)}) copy-start(bf16[2,1,768,1024]{3,2,1,0:T(8,128)(2,1)} %param.3) | copy-start | bytes 9437188
  27.3 17.6 %copy-start.11 = (s32[512]{0:T(512)S(1)}, s32[512]{0:T(512)}, u32[]{:S(2)}) copy-start(s32[512]{0:T(512)} %param.5) | copy-start | bytes 6148
  27.3 67.7 %all-gather.2.cloned.1.call-start = ((), (), s32[]{:S(2)}) async-start(), calls=%async_computation.4 | async-start | bytes 1638400 | tf_op jit(solution)/shard_map/all_gather | solution.py:103
  30.6 17.0 %copy-start.6 = (bf16[2,1,768,512]{3,2,1,0:T(8,128)(2,1)S(1)}, bf16[2,1,768,512]{3,2,1,0:T(8,128)(2,1)}, u32[]{:S(2)}) copy-start(bf16[2,1,768,512]{3,2,1,0:T(8,128)(2,1)} %param.4) | copy-start | bytes 4718596
  47.7 1.4 copy-start.1
  47.7 1.9 %copy-start.5 = (bf16[1,1,768,1024]{2,3,1,0:T(8,128)(2,1)S(1)}, bf16[1,1,768,1024]{2,3,1,0:T(8,128)(2,1)}, u32[]{:S(2)}) copy-start(bf16[1,1,768,1024]{2,3,1,0:T(8,128)(2,1)} %copy.84) | copy-start | bytes 4718596
  63.9 84.2 %reduce-scatter.5.cloned.1.call-start = ((), (), s32[]{:S(2)}) async-start(), calls=%async_computation.3 | async-start | bytes 1310720 | tf_op jit(solution)/shard_map/reduce_scatter | solution.py:115
  95.0 3.2 %collective-permute-start = (bf16[4,128,1,2,640]{4,1,0,3,2:T(8,128)(2,1)}, bf16[4,128,1,2,640]{4,1,0,3,2:T(8,128)(2,1)S(1)}, u32[]{:S(2)}, u32[]{:S(2)}) collective-permute-start(bf16[4,128,1,2,640]{4,1,0,3,2:T(8,128)(2,1)} %bitcast.331), channel_id=1, source_target_pairs={{0,1},{1,0},{2,3},{3,2},{4,5},{5,4},{6,7},{7,6},{8,9},{9,8},{10,11... | collective-permute-start | bytes 3932168 | tf_op jit(solution)/shard_map/ppermute | solution.py:106
  107.2 1.8 %copy-start.10 = (bf16[8,128,1,2,1,128]{1,5,4,3,0,2:T(8,128)(2,1)S(1)}, bf16[8,128,1,2,1,128]{1,5,4,3,0,2:T(8,128)(2,1)}, u32[]{:S(2)}) copy-start(bf16[8,128,1,2,1,128]{1,5,4,3,0,2:T(8,128)(2,1)} %get-tuple-element.25) | copy-start | bytes 1572868
  107.2 2.0 %copy-start.9 = (bf16[8,128,1,2,1,128]{1,5,4,3,0,2:T(8,128)(2,1)S(1)}, bf16[8,128,1,2,1,128]{1,5,4,3,0,2:T(8,128)(2,1)}, u32[]{:S(2)}) copy-start(bf16[8,128,1,2,1,128]{1,5,4,3,0,2:T(8,128)(2,1)} %get-tuple-element.26) | copy-start | bytes 1572868
  146.3 1.3 copy-start.7
  148.1 3.3 %copy-start.8 = (bf16[1,1,8,128,8,128]{5,4,3,2,1,0:T(8,128)(2,1)S(1)}, bf16[1,1,8,128,8,128]{5,4,3,2,1,0:T(8,128)(2,1)}, u32[]{:S(2)}) copy-start(bf16[1,1,8,128,8,128]{5,4,3,2,1,0:T(8,128)(2,1)} %copy-done.7) | copy-start | bytes 6291460
  152.1 1.0 copy-start.3
Sparse Core Ops, SparseCore 0:
  27.4 34.0 reduce-scatter.2
  64.0 30.8 all-gather.1
  97.3 26.1 reduce-scatter.4

commit v4 on v3

--- a/solution.py
+++ b/solution.py
@@ -44,25 +44,20 @@
     return jnp.stack(windows).reshape(shot_count * rows_each, *gram_full.shape[1:3], span)
 
 
-def rebuild_gram(strips, groups, block):
-    half = groups // 2
-    freq_local = strips.shape[2]
-    pieces = strips.reshape(groups, block, freq_local, 2, half + 1, block)
-    direct = [pieces[:, :, :, :, offset, :] for offset in range(half + 1)]
-    mirrored = []
-    for offset in range(half + 1, groups):
-        back = groups - offset
-        source = pieces[:, :, :, :, back, :]
-        flipped = jnp.transpose(source, (0, 4, 2, 3, 1))
-        flipped = jnp.stack([flipped[:, :, :, 0], -flipped[:, :, :, 1]], axis=3)
-        mirrored.append(jnp.roll(flipped, back, axis=0))
-    cyclic = jnp.stack(direct + mirrored, axis=1)
-    doubled = jnp.concatenate([cyclic, cyclic], axis=1)
-    flat = doubled.reshape(2 * groups * groups, *doubled.shape[2:])
-    skewed = flat[groups : groups + groups * (2 * groups - 1)]
-    blocks = skewed.reshape(groups, 2 * groups - 1, *doubled.shape[2:])[:, :groups]
-    blocks = jnp.transpose(blocks, (4, 3, 0, 2, 1, 5))
-    return blocks.reshape(2, freq_local, groups * block, groups * block)
+def rebuild_gram(strips, tiles, tile):
+    freq_local = strips.shape[1]
+    receivers = tiles * tile
+    span = strips.shape[-1]
+    padded = jnp.pad(strips, [(0, 0)] * 3 + [(0, receivers - span)])
+    padded = padded.reshape(tiles, tile, freq_local, 2, receivers)
+    upper = jnp.stack([jnp.roll(padded[a], a * tile, axis=-1) for a in range(tiles)])
+    upper = jnp.transpose(upper, (3, 2, 0, 1, 4)).reshape(2, freq_local, receivers, receivers)
+    mirror = jnp.swapaxes(upper, 2, 3)
+    mirror = jnp.stack([mirror[0], -mirror[1]])
+    row_tile = lax.broadcasted_iota(jnp.int32, (receivers, receivers), 0) // tile
+    col_tile = lax.broadcasted_iota(jnp.int32, (receivers, receivers), 1) // tile
+    direct = (col_tile - row_tile) % tiles <= tiles // 2
+    return jnp.where(direct, upper, mirror)
 
 
 def per_device(downgoing, upgoing, source_order):
@@ -109,7 +104,7 @@
         strips = jnp.stack([first, second], axis=1)
     else:
         strips = lax.all_gather(across, "sub", axis=1, tiled=False)
-    strips = strips.reshape(tiles, tile, freq_local, 2, span)
+    strips = strips.reshape(receivers, freq_local, 2, span)
     whole = rebuild_gram(strips, tiles, tile)
 
     corr = lax.psum_scatter(corr_part, "shot", scatter_dimension=0, tiled=True).astype(jnp.float32)

time: 170 us -> 152 us (0.89)
  local copies, waits for them, and re-layouts: 55.7 us -> 33.9 us
  waiting for transfers between devices: 34.3 us -> 37.7 us
    concatenate x1 -> x0, local copies, waits for them, and re-layouts: 10.3 us -> none  [rebuild_gram(): doubled = jnp.concatenate([cyclic, cyclic], axis=1)]
    unnamed x37 -> x26, local copies, waits for them, and re-layouts: 16.3 us -> 8.16 us
    slice x5 -> x7, local copies, waits for them, and re-layouts: 7.38 us -> 0.25 us  [rebuild_gram(): jnp.roll(padded[a], a * tile, axis=-1)]
    reduce_scatter x1, waiting for transfers between devices: 0.02 us -> 6.73 us  [per_device(): lax.psum_scatter(corr_part, 'shot', scatter_dimension=0, tiled=True)]
    reshape x0 -> x1, local copies, waits for them, and re-layouts: none -> 6.24 us  [rebuild_gram(): jnp.transpose(upper, (3, 2, 0, 1, 4))]
    another operation x3 -> x0, local copies, waits for them, and re-layouts: 5.17 us -> none  [the longest x1 3.49 us: per_device(): strips = jnp.stack([first, second], axis=1)]
    unnamed x5 -> x3, other arithmetic: 4.19 us -> 0.17 us
    le x0 -> x1, other arithmetic: none -> 3.56 us  [rebuild_gram(): direct = (col_tile - row_tile) % tiles <= tiles // 2]
  transfers between devices with their start and end apart: 4 -> 4, of which waited for: 2 -> 2; matrix products, arithmetic and copies ran while one was open for 40% -> 27% of each run, Pallas kernels for 0% -> 0%
where the time goes in v4:
time: 152 us; the launch traced here: 151 us
  waiting for transfers between devices  37.7 us (25%)
  local copies, waits for them, and re-layouts  33.9 us (22%)
  other arithmetic  25.7 us (17%)
  matrix products  25.3 us (17%)
  between operations  14.3 us (9%)
  blocking collectives  14.2 us (9%)
    all_gather x1, waiting for transfers between devices, per_device(): across = lax.all_gather(gram_strip, 'shot', axis=0, tiled=True)  30.9 us
    psum x1, blocking collectives, per_device(): power = lax.psum(local_power, 'shot') / receivers  14.2 us
    unnamed x26, local copies, waits for them, and re-layouts  8.16 us
    dot_general x1, matrix products, per_device(): jnp.einsum('qtpu,qto->uqpo', stacked_left(downgoing), right, preferred_el...  6.91 us
    reduce_scatter x1, waiting for transfers between devices, per_device(): lax.psum_scatter(corr_part, 'shot', scatter_dimension=0, tiled=True)  6.73 us
    reshape x1, local copies, waits for them, and re-layouts, rebuild_gram(): jnp.transpose(upper, (3, 2, 0, 1, 4))  6.24 us
    transpose x1, local copies, waits for them, and re-layouts, per_device(): jnp.einsum('qtpu,qto->uqpo', stacked_left(upgoing), right, preferred_elem...  5.03 us
    dot_general x6, matrix products, sweep_whole(): jnp.einsum('qjc,qcr->qjr', narrow[0], scaled[0], preferred_element_type=j...  4.6 us
  transfers between devices with their start and end apart: 4, of which 2 were waited for; matrix products, arithmetic and copies ran while one was open for 27% of the time, Pallas kernels for 0%

profile of v4, /device:TPU:0, one launch (start us, length us, event | category | flops | bytes accessed | tf_op | source)
XLA Modules:
  0.0 151.3 jit_solution(8449359261265592852)
XLA Ops:
  6.5 3.3 %fusion.80 = (bf16[1,1,768,1024]{3,2,1,0:T(8,128)(2,1)S(1)}, bf16[1,1,768,1024]{3,2,1,0:T(8,128)(2,1)}) fusion(bf16[2,1,768,1024]{3,2,1,0:T(8,128)(2,1)} %param.3), kind=kLoop, calls=%fused_computation.164 | loop fusion | bytes 6291456 | tf_op jit(solution)/shard_map/slice | solution.py:20
  9.9 1.7 %copy.57 = bf16[1,1,768,1024]{2,3,1,0:T(8,128)(2,1)S(1)} copy(bf16[1,1,768,1024]{3,2,1,0:T(8,128)(2,1)} %get-tuple-element.20) | data formatting | bytes 3145728
  11.6 1.6 %copy.58 = bf16[1,1,768,1024]{2,3,1,0:T(8,128)(2,1)} copy(bf16[1,1,768,1024]{3,2,1,0:T(8,128)(2,1)S(1)} %get-tuple-element.19) | data formatting | bytes 3145728
  15.2 1.7 %fusion.25 = (bf16[1,1536,1,1024]{1,3,2,0:T(8,128)(2,1)S(1)}, bf16[1,1536,1,1024]{1,3,2,0:T(8,128)(2,1)S(1)}) fusion(bf16[1,768,1024]{1,2,0:T(8,128)(2,1)S(1)} %bitcast.221, bf16[1,768,1024]{1,2,0:T(8,128)(2,1)S(1)} %bitcast.218, bf16[1,768,1024]{1,2,0:T(8,128)(2,1)} %bitcast_negate_fusion), kind=kLoop, calls=%fused_computation.70 | loop fusion | flops 12582912 | bytes 11010048 | tf_op jit(solution)/shard_map/stack | solution.py:16
  16.9 6.9 %fusion = bf16[1024,2,1024]{0,2,1:T(8,128)(2,1)S(1)} fusion(bf16[1,1536,1,1024]{1,3,2,0:T(8,128)(2,1)S(1)} %get-tuple-element.40, bf16[1,1536,1,1024]{1,3,2,0:T(8,128)(2,1)S(1)} %get-tuple-element.39, bf16[1,768,1024]{1,2,0:T(8,128)(2,1)S(1)} %bitcast.222, bf16[1,768,1024]{1,2,0:T(8,128)(2,1)S(1)} %bitcast.219), kind=kOutput, calls=%fused_computation.3 | convolution fusion | flops 6461325312 | bytes 13631488 | tf_op jit(solution)/shard_map/qtpu,qto->uqpo/dot_general | solution.py:79
  24.1 2.5 %pad_slice_fusion.11 = (bf16[1,128,1,2,2048]{4,1,0,3,2:T(8,128)(2,1)S(1)}, bf16[1,128,1,2,2048]{4,1,0,3,2:T(8,128)(2,1)}, bf16[1,128,1,2,2048]{4,1,0,3,2:T(8,128...) fusion(bf16[4,128,1,2,1024]{4,1,0,3,2:T(8,128)(2,1)S(1)} %fusion.13), kind=kLoop, calls=%fused_computation.21 | loop fusion | bytes 8388608 | tf_op jit(solution)/shard_map/slice | solution.py:43
  27.9 1.6 %dynamic-slice_maximum_fusion = (bf16[1,128,1,2,640]{4,1,0,3,2:T(8,128)(2,1)S(1)}, bf16[1,128,1,2,640]{4,1,0,3,2:T(8,128)(2,1)S(1)}) fusion(bf16[1,128,1,2,2048]{4,1,0,3,2:T(8,128)(2,1)} %get-tuple-element.36, s32[]{:T(128)S(6)} %select_n.102, bf16[1,128,1,2,2048]{4,1,0,3,2:T(8,128)(2,1)} %get-tuple-element.35, ...), kind=kLoop, calls=%fused_computation.111 | loop fusion | flops 1310720 | bytes 1966088 | tf_op jit(solution)/shard_map/concatenate | solution.py:39
  30.9 2.2 %multiply_reduce_fusion = f32[]{:T(128)} fusion(bf16[2,1,768,1024]{3,2,1,0:T(8,128)(2,1)S(1)} %copy-done.5), kind=kLoop, calls=%fused_computation.9 | loop fusion | flops 4718591 | bytes 3145732 | tf_op jit(solution)/shard_map/reduce_sum | solution.py:85
  33.1 14.2 %psum.7 = f32[1]{0:T(128)} all-reduce(f32[1]{0:T(128)} %bitcast.23), channel_id=1, replica_groups=mesh['grp'=2,'shot'=4,'freq'=2,'sub'=2] {'shot'}, use_global_device_ids=true, to_apply=%region_2.3 | all-reduce | flops 1 | bytes 8 | tf_op jit(solution)/shard_map/psum | solution.py:86
  49.8 1.5 slice_bitcast_fusion.3
  53.2 4.5 %fusion.10 = bf16[512,2,1024]{0,2,1:T(8,128)(2,1)} fusion(bf16[1,1536,1,512]{3,1,2,0:T(8,128)(2,1)S(1)} %get-tuple-element.42, bf16[1,1536,1,512]{3,1,2,0:T(8,128)(2,1)S(1)} %get-tuple-element.41, bf16[1,768,1024]{1,2,0:T(8,128)(2,1)S(1)} %bitcast.223, bf16[1,768,1024]{1,2,0:T(8,128)(2,1)S(1)} %bitcast.220), kind=kOutput, calls=%fused_computation.36 | convolution fusion | flops 3233808384 | bytes 8388608 | tf_op jit(solution)/shard_map/qtpu,qto->uqpo/dot_general | solution.py:88
  57.7 5.0 %copy.50 = bf16[512,2,1024]{2,1,0:T(2,128)(2,1)S(1)} copy(bf16[512,2,1024]{0,2,1:T(8,128)(2,1)} %fusion.10) | data formatting | bytes 4194304 | tf_op jit(solution)/shard_map/qtpu,qto->uqpo/transpose | solution.py:88
  62.9 2.8 %gather_fusion = bf16[256,2,1024]{2,1,0:T(2,128)(2,1)S(1)} fusion(bf16[512,2,1024]{2,1,0:T(2,128)(2,1)S(1)} %copy.50, s32[1024]{0:T(1024)S(1)} %pad_clamp_fusion), kind=kCustom, calls=%fused_computation | custom fusion | bytes 2098176 | tf_op jit(solution)/shard_map/jit(_take)/gather | solution.py:93
  67.9 30.9 %all-gather.2.cloned.1.call-done = bf16[512,1,2,640]{3,0,2,1:T(8,128)(2,1)} async-done(((bf16[128,1,2,640]{3,0,2,1:T(8,128)(2,1)}), bf16[512,1,2,640]{3,0,2,1:T(8,128)(2,1)}) %all-gather.2.cloned.1.call-update) | async-done | bytes 1310736 | tf_op jit(solution)/shard_map/all_gather | solution.py:98
  98.8 3.6 %fusion.4 = pred[1024,1024]{1,0:T(8,128)(4,1)S(1)} fusion(s32[1024]{0:T(1024)S(1)} %get-tuple-element.49, s32[1024]{0:T(1024)S(1)} %get-tuple-element.50, pred[1024]{0:T(1024)(128)(4,1)S(1)} %fusion.68), kind=kLoop, calls=%fused_computation.24 | loop fusion | flops 15728640 | bytes 1057792 | tf_op jit(solution)/shard_map/le | solution.py:59
  102.4 1.6 %select_bitcast_fusion.1 = (bf16[4,1,128,1,2,640]{5,2,1,0,4,3:T(8,128)(2,1)S(1)}, bf16[4,1,128,1,2,640]{5,2,1,0,4,3:T(8,128)(2,1)S(1)}) fusion(bf16[4,128,1,2,640]{4,1,0,3,2:T(8,128)(2,1)} %bitcast.227, bf16[4,128,1,2,640]{4,1,0,3,2:T(8,128)(2,1)S(1)} %collective-permute-done, pred[]{:T(512)S(6)} %eq.6), kind=kLoop, calls=%fused_computation.47 | loop fusion | flops 1310720 | bytes 5242881 | tf_op jit(solution)/shard_map/stack | solution.py:104
  105.1 2.4 %copy.53 = bf16[2,1,8,128,1024]{4,3,2,0,1:T(8,128)(2,1)} copy(bf16[2,1,8,128,1024]{4,3,0,1,2:T(8,128)(2,1)S(1)} %bitcast.224) | data formatting | bytes 8388608 | tf_op jit(solution)/shard_map/transpose | solution.py:54
  107.5 6.2 %copy.54 = bf16[2,1,1024,1024]{2,3,0,1:T(8,128)(2,1)} copy(bf16[2,1,1024,1024]{3,2,0,1:T(8,128)(2,1)} %bitcast.216) | data formatting | bytes 8388608 | tf_op jit(solution)/shard_map/reshape | solution.py:54
  113.7 2.7 %fusion.79 = (bf16[1,1,1024,1024]{3,2,0,1:T(8,128)(2,1)S(1)}, bf16[1,1,1024,1024]{3,2,0,1:T(8,128)(2,1)S(1)}) fusion(bf16[2,1,1024,1024]{3,2,0,1:T(8,128)(2,1)} %bitcast.217), kind=kLoop, calls=%fused_computation.163 | loop fusion | flops 1048576 | bytes 8388608 | tf_op jit(solution)/shard_map/slice | solution.py:56
  117.2 2.5 %divide_convert_fusion = bf16[2,1,1024,1024]{3,2,0,1:T(8,128)(2,1)S(1)} fusion(bf16[1,1,1024,1024]{3,2,0,1:T(8,128)(2,1)S(1)} %get-tuple-element.18, bf16[1,1,1024,1024]{3,2,0,1:T(8,128)(2,1)S(1)} %get-tuple-element.17, f32[]{:T(128)} %bitcast.24, pred[1024,1024]{1,0:T(8,128)(4,1)S(1)} %fusion.4, bf16[2,1,8,128,1024]{4,3,2,0,1:T(8,128)(2,1)S(1)} %copy-done.2), kind=kLoop, calls=%fused_computation.1 | loop fusion | flops 10485760 | bytes 13631492 | tf_op jit(solution)/shard_map/convert_element_type | solution.py:113
  120.2 1.4 copy-done
  122.1 6.7 %reduce-scatter.5.cloned.1.call-done = bf16[64,1,2,1024]{3,0,1,2:T(8,128)(2,1)} async-done(((bf16[256,1,2,1024]{3,0,1,2:T(8,128)(2,1)}), bf16[64,1,2,1024]{3,0,1,2:T(8,128)(2,1)}) %reduce-scatter.5.cloned.1.call-update) | async-done | bytes 262160 | tf_op jit(solution)/shard_map/reduce_scatter | solution.py:110
  130.0 2.2 %fusion.51 = f32[64,1024]{1,0:T(8,128)S(1)} fusion(bf16[2,1,64,1024]{3,2,1,0:T(8,128)(2,1)S(1)} %fusion.48, bf16[2,1,1024,1024]{3,2,0,1:T(8,128)(2,1)} %copy-done), kind=kOutput, calls=%fused_computation.127 | convolution fusion | flops 134217728 | bytes 2490368 | tf_op jit(solution)/shard_map/qjc,qcr->qjr/dot_general | solution.py:26
  132.2 2.1 %fusion.50 = f32[64,1024]{1,0:T(8,128)S(1)} fusion(bf16[2,1,64,1024]{3,2,1,0:T(8,128)(2,1)S(1)} %fusion.48, bf16[2,1,1024,1024]{3,2,0,1:T(8,128)(2,1)} %copy-done), kind=kOutput, calls=%fused_computation.126 | convolution fusion | flops 134217728 | bytes 2490368 | tf_op jit(solution)/shard_map/qjc,qcr->qjr/dot_general | solution.py:28
  (87 shorter events, 25.2 us)
Async XLA Ops:
  6.5 61.1 %reduce-scatter.3.cloned.1.call-start = ((), (), s32[]{:S(2)}) async-start(), calls=%async_computation.2 | async-start | bytes 1638400 | tf_op jit(solution)/shard_map/reduce_scatter | solution.py:83
  11.6 5.3 %copy-start.3 = (bf16[1,1,768,1024]{2,3,1,0:T(8,128)(2,1)}, bf16[1,1,768,1024]{2,3,1,0:T(8,128)(2,1)S(1)}, u32[]{:S(2)}) copy-start(bf16[1,1,768,1024]{2,3,1,0:T(8,128)(2,1)S(1)} %copy.57) | copy-start | bytes 4718596
  13.3 2.0 %copy-start.7 = (bf16[1,1,768,1024]{2,3,1,0:T(8,128)(2,1)S(1)}, bf16[1,1,768,1024]{2,3,1,0:T(8,128)(2,1)}, u32[]{:S(2)}) copy-start(bf16[1,1,768,1024]{2,3,1,0:T(8,128)(2,1)} %copy.58) | copy-start | bytes 4718596
  27.9 3.0 %copy-start.5 = (bf16[2,1,768,1024]{3,2,1,0:T(8,128)(2,1)S(1)}, bf16[2,1,768,1024]{3,2,1,0:T(8,128)(2,1)}, u32[]{:S(2)}) copy-start(bf16[2,1,768,1024]{3,2,1,0:T(8,128)(2,1)} %param.3) | copy-start | bytes 9437188
  29.5 17.7 %copy-start.9 = (s32[512]{0:T(512)S(1)}, s32[512]{0:T(512)}, u32[]{:S(2)}) copy-start(s32[512]{0:T(512)} %param.5) | copy-start | bytes 6148
  30.8 68.0 %all-gather.2.cloned.1.call-start = ((), (), s32[]{:S(2)}) async-start(), calls=%async_computation.4 | async-start | bytes 1638400 | tf_op jit(solution)/shard_map/all_gather | solution.py:98
  51.3 1.4 copy-start.4
  51.3 1.9 %copy-start.8 = (bf16[1,1,768,1024]{2,3,1,0:T(8,128)(2,1)S(1)}, bf16[1,1,768,1024]{2,3,1,0:T(8,128)(2,1)}, u32[]{:S(2)}) copy-start(bf16[1,1,768,1024]{2,3,1,0:T(8,128)(2,1)} %copy.58) | copy-start | bytes 4718596
  67.6 61.2 %reduce-scatter.5.cloned.1.call-start = ((), (), s32[]{:S(2)}) async-start(), calls=%async_computation.3 | async-start | bytes 1310720 | tf_op jit(solution)/shard_map/reduce_scatter | solution.py:110
  98.8 3.6 %collective-permute-start = (bf16[4,128,1,2,640]{4,1,0,3,2:T(8,128)(2,1)}, bf16[4,128,1,2,640]{4,1,0,3,2:T(8,128)(2,1)S(1)}, u32[]{:S(2)}, u32[]{:S(2)}) collective-permute-start(bf16[4,128,1,2,640]{4,1,0,3,2:T(8,128)(2,1)} %bitcast.226), channel_id=1, source_target_pairs={{0,1},{1,0},{2,3},{3,2},{4,5},{5,4},{6,7},{7,6},{8,9},{9,8},{10,11... | collective-permute-start | bytes 3932168 | tf_op jit(solution)/shard_map/ppermute | solution.py:101
  113.7 3.5 %copy-start.2 = (bf16[2,1,8,128,1024]{4,3,2,0,1:T(8,128)(2,1)S(1)}, bf16[2,1,8,128,1024]{4,3,2,0,1:T(8,128)(2,1)}, u32[]{:S(2)}) copy-start(bf16[2,1,8,128,1024]{4,3,2,0,1:T(8,128)(2,1)} %copy.53) | copy-start | bytes 12582916
  119.7 1.9 %copy-start = (bf16[2,1,1024,1024]{3,2,0,1:T(8,128)(2,1)}, bf16[2,1,1024,1024]{3,2,0,1:T(8,128)(2,1)S(1)}, u32[]{:S(2)}) copy-start(bf16[2,1,1024,1024]{3,2,0,1:T(8,128)(2,1)S(1)} %divide_convert_fusion) | copy-start | bytes 12582916
  128.8 5.5 %copy-start.1 = (bf16[2,1,1024,1024]{3,2,0,1:T(8,128)(2,1)S(1)}, bf16[2,1,1024,1024]{3,2,0,1:T(8,128)(2,1)}, u32[]{:S(2)}) copy-start(bf16[2,1,1024,1024]{3,2,0,1:T(8,128)(2,1)} %copy-done) | copy-start | bytes 12582916
  134.3 1.0 copy-start.6
Sparse Core Ops, SparseCore 0:
  30.9 34.0 reduce-scatter.2
  67.8 30.9 all-gather.1
  102.5 26.2 reduce-scatter.4

commit v5 on v4

--- a/solution.py
+++ b/solution.py
@@ -1,6 +1,7 @@
 import jax
 import jax.numpy as jnp
 from jax import lax
+from jax.experimental import pallas as pl
 from jax.sharding import PartitionSpec as P
 
 SWEEPS = 6
@@ -20,16 +21,31 @@
     return jnp.concatenate([trace[0], trace[1]], axis=1)
 
 
-def sweep_whole(scaled, solution, target):
+def sweep_kernel(weight_ref, target_ref, out_ref):
+    target = target_ref[...]
+    solution = jnp.zeros_like(target)
     for sweep in range(SWEEPS):
         narrow = solution.astype(jnp.bfloat16)
-        real_real = jnp.einsum("qjc,qcr->qjr", narrow[0], scaled[0], preferred_element_type=jnp.float32)
-        imag_imag = jnp.einsum("qjc,qcr->qjr", narrow[1], scaled[1], preferred_element_type=jnp.float32)
-        real_imag = jnp.einsum("qjc,qcr->qjr", narrow[0], scaled[1], preferred_element_type=jnp.float32)
-        imag_real = jnp.einsum("qjc,qcr->qjr", narrow[1], scaled[0], preferred_element_type=jnp.float32)
-        image = jnp.stack([real_real - imag_imag, real_imag + imag_real])
+        image = jnp.dot(narrow, weight_ref[...], preferred_element_type=jnp.float32)
         solution = solution + relaxation * (target - image - damping * solution)
-    return solution
+    out_ref[...] = solution
+
+
+def sweep_whole(scaled, target):
+    receivers = target.shape[-1]
+    results = []
+    for freq in range(target.shape[1]):
+        real, imag = scaled[0, freq], scaled[1, freq]
+        weight = jnp.concatenate(
+            [jnp.concatenate([real, imag], axis=1), jnp.concatenate([-imag, real], axis=1)], axis=0
+        )
+        stacked = jnp.concatenate([target[0, freq], target[1, freq]], axis=1)
+        response = pl.pallas_call(
+            sweep_kernel,
+            out_shape=jax.ShapeDtypeStruct(stacked.shape, jnp.float32),
+        )(weight, stacked)
+        results.append(jnp.stack([response[:, :receivers], response[:, receivers:]]))
+    return jnp.stack(results, axis=1)
 
 
 def strip_partials(gram_full, shot_count, core_count, core_index, rows_each, tile, span):
@@ -111,8 +127,7 @@
     target = jnp.transpose(corr, (2, 1, 0, 3)) / power_wide
 
     scaled = (whole.astype(jnp.float32) / power_wide).astype(jnp.bfloat16)
-    solution = jnp.zeros((2, freq_local, source_local, receivers), jnp.float32)
-    return sweep_whole(scaled, solution, target)
+    return sweep_whole(scaled, target)
 
 
 def solution(mesh):

time: 152 us -> 225 us (1.48)
  other arithmetic: 25.7 us -> 65.6 us
  waiting for transfers between devices: 37.7 us -> 55.8 us
  local copies, waits for them, and re-layouts: 33.9 us -> 49.2 us
  matrix products: 25.3 us -> 11.5 us
  Pallas kernels: 0 us -> 13.2 us
    concatenate x0 -> x2, other arithmetic: none -> 37.7 us  [the longest x1 36.9 us: sweep_whole(): jnp.concatenate([jnp.concatenate([real, imag], axis=1), jnp.concatenate([...]
    reduce_scatter x1, waiting for transfers between devices: 6.73 us -> 24.9 us  [per_device(): lax.psum_scatter(corr_part, 'shot', scatter_dimension=0, tiled=True)]
    dot_general x22 -> x0, matrix products: 13.9 us -> none  [the longest x6 4.6 us: sweep_whole(): jnp.einsum('qjc,qcr->qjr', narrow[0], scaled[0], preferred_element_type=j...]
    pallas_call x0 -> x1, Pallas kernels: none -> 13.2 us  [sweep_whole(): pl.pallas_call(sweep_kernel, out_shape=jax.ShapeDtypeStruct(stacked.shape...]
    reshape x1 -> x2, local copies, waits for them, and re-layouts: 6.24 us -> 13.5 us  [rebuild_gram(): jnp.transpose(upper, (3, 2, 0, 1, 4))]
    transpose x1, local copies, waits for them, and re-layouts: 2.38 us -> 6.74 us  [rebuild_gram(): jnp.transpose(upper, (3, 2, 0, 1, 4))]
    unnamed x3, other arithmetic: 0.17 us -> 2.6 us
    unnamed x26 -> x22, local copies, waits for them, and re-layouts: 8.16 us -> 9.95 us
  transfers between devices with their start and end apart: 4 -> 4, of which waited for: 2 -> 2; matrix products, arithmetic and copies ran while one was open for 27% -> 11% of each run, Pallas kernels for 0% -> 0%
where the time goes in v5:
time: 225 us; the launch traced here: 224 us
  other arithmetic  65.6 us (29%)
  waiting for transfers between devices  55.8 us (25%)
  local copies, waits for them, and re-layouts  49.2 us (22%)
  blocking collectives  14.2 us (6%)
  between operations  14 us (6%)
  Pallas kernels  13.2 us (6%)
  matrix products  11.5 us (5%)
    concatenate x1, other arithmetic, sweep_whole(): jnp.concatenate([jnp.concatenate([real, imag], axis=1), jnp.concatenate([...  36.9 us
    all_gather x1, waiting for transfers between devices, per_device(): across = lax.all_gather(gram_strip, 'shot', axis=0, tiled=True)  30.4 us
    reduce_scatter x1, waiting for transfers between devices, per_device(): lax.psum_scatter(corr_part, 'shot', scatter_dimension=0, tiled=True)  24.9 us
    psum x1, blocking collectives, per_device(): power = lax.psum(local_power, 'shot') / receivers  14.2 us
    reshape x2, local copies, waits for them, and re-layouts, rebuild_gram(): jnp.transpose(upper, (3, 2, 0, 1, 4))  13.5 us
    pallas_call x1, Pallas kernels, sweep_whole(): pl.pallas_call(sweep_kernel, out_shape=jax.ShapeDtypeStruct(stacked.shape...  13.2 us
    unnamed x22, local copies, waits for them, and re-layouts  9.95 us
    dot_general x1, matrix products, per_device(): jnp.einsum('qtpu,qto->uqpo', stacked_left(downgoing), right, preferred_el...  6.91 us
  transfers between devices with their start and end apart: 4, of which 2 were waited for; matrix products, arithmetic and copies ran while one was open for 11% of the time, Pallas kernels for 0%

profile of v5, /device:TPU:0, one launch (start us, length us, event | category | flops | bytes accessed | tf_op | source)
XLA Modules:
  0.0 223.8 jit_solution(13497397282641073275)
XLA Ops:
  6.5 3.4 %fusion.32 = (bf16[1,1,768,1024]{3,2,1,0:T(8,128)(2,1)S(1)}, bf16[1,1,768,1024]{3,2,1,0:T(8,128)(2,1)}) fusion(bf16[2,1,768,1024]{3,2,1,0:T(8,128)(2,1)} %param.3), kind=kLoop, calls=%fused_computation.97 | loop fusion | bytes 6291456 | tf_op jit(solution)/shard_map/slice | solution.py:21
  9.9 1.7 copy.40
  11.6 1.7 copy.41
  15.2 1.7 fusion.15
  16.9 6.9 %fusion = bf16[1024,2,1024]{0,2,1:T(8,128)(2,1)S(1)} fusion(bf16[1,1536,1,1024]{1,3,2,0:T(8,128)(2,1)S(1)} %get-tuple-element.38, bf16[1,1536,1,1024]{1,3,2,0:T(8,128)(2,1)S(1)} %get-tuple-element.37, bf16[1,768,1024]{1,2,0:T(8,128)(2,1)S(1)} %bitcast.128, bf16[1,768,1024]{1,2,0:T(8,128)(2,1)S(1)} %bitcast.125), kind=kOutput, calls=%fused_computation.4 | convolution fusion | flops 6461325312 | bytes 13631488 | tf_op jit(solution)/shard_map/qtpu,qto->uqpo/dot_general | solution.py:95
  24.1 2.5 %pad_slice_fusion.11 = (bf16[1,128,1,2,2048]{4,1,0,3,2:T(8,128)(2,1)S(1)}, bf16[1,128,1,2,2048]{4,1,0,3,2:T(8,128)(2,1)}, bf16[1,128,1,2,2048]{4,1,0,3,2:T(8,128...) fusion(bf16[4,128,1,2,1024]{4,1,0,3,2:T(8,128)(2,1)S(1)} %fusion.13), kind=kLoop, calls=%fused_computation.22 | loop fusion | bytes 8388608 | tf_op jit(solution)/shard_map/slice | solution.py:59
  27.9 1.6 dynamic-slice_maximum_fusion
  30.9 2.2 multiply_reduce_fusion
  33.1 14.2 %psum.7 = f32[1]{0:T(128)} all-reduce(f32[1]{0:T(128)} %bitcast.23), channel_id=1, replica_groups=mesh['grp'=2,'shot'=4,'freq'=2,'sub'=2] {'shot'}, use_global_device_ids=true, to_apply=%region_2.3 | all-reduce | flops 1 | bytes 8 | tf_op jit(solution)/shard_map/psum | solution.py:102
  49.8 1.5 slice_bitcast_fusion.3
  53.2 4.6 %fusion.10 = bf16[512,2,1024]{0,2,1:T(8,128)(2,1)} fusion(bf16[1,1536,1,512]{3,1,2,0:T(8,128)(2,1)S(1)} %get-tuple-element.40, bf16[1,1536,1,512]{3,1,2,0:T(8,128)(2,1)S(1)} %get-tuple-element.39, bf16[1,768,1024]{1,2,0:T(8,128)(2,1)S(1)} %bitcast.129, bf16[1,768,1024]{1,2,0:T(8,128)(2,1)S(1)} %bitcast.126), kind=kOutput, calls=%fused_computation.37 | convolution fusion | flops 3233808384 | bytes 8388608 | tf_op jit(solution)/shard_map/qtpu,qto->uqpo/dot_general | solution.py:104
  57.7 5.0 %copy.29 = bf16[512,2,1024]{2,1,0:T(2,128)(2,1)S(1)} copy(bf16[512,2,1024]{0,2,1:T(8,128)(2,1)} %fusion.10) | data formatting | bytes 4194304 | tf_op jit(solution)/shard_map/qtpu,qto->uqpo/transpose | solution.py:104
  62.9 2.8 %gather_fusion = bf16[256,2,1024]{2,1,0:T(2,128)(2,1)S(1)} fusion(bf16[512,2,1024]{2,1,0:T(2,128)(2,1)S(1)} %copy.29, s32[1024]{0:T(1024)S(1)} %pad_clamp_fusion), kind=kCustom, calls=%fused_computation | custom fusion | bytes 2098176 | tf_op jit(solution)/shard_map/jit(_take)/gather | solution.py:109
  68.4 30.4 %all-gather.2.cloned.1.call-done = bf16[512,1,2,640]{3,0,2,1:T(8,128)(2,1)} async-done(((bf16[128,1,2,640]{3,0,2,1:T(8,128)(2,1)}), bf16[512,1,2,640]{3,0,2,1:T(8,128)(2,1)}) %all-gather.2.cloned.1.call-update) | async-done | bytes 1310736 | tf_op jit(solution)/shard_map/all_gather | solution.py:114
  98.8 3.5 %fusion.4 = pred[1024,1024]{1,0:T(8,128)(4,1)S(1)} fusion(s32[1024]{0:T(1024)S(1)} %get-tuple-element.49, s32[1024]{0:T(1024)S(1)} %get-tuple-element.50, pred[1024]{0:T(1024)(128)(4,1)S(1)} %fusion.25), kind=kLoop, calls=%fused_computation.25 | loop fusion | flops 15728640 | bytes 1057792 | tf_op jit(solution)/shard_map/le | solution.py:75
  102.3 24.9 %reduce-scatter.5.cloned.1.call-done = bf16[64,1,2,1024]{3,0,1,2:T(8,128)(2,1)} async-done(((bf16[256,1,2,1024]{3,0,1,2:T(8,128)(2,1)}), bf16[64,1,2,1024]{3,0,1,2:T(8,128)(2,1)}) %reduce-scatter.5.cloned.1.call-update) | async-done | bytes 262160 | tf_op jit(solution)/shard_map/reduce_scatter | solution.py:126
  129.1 1.6 select_bitcast_fusion.1
  138.6 6.7 %copy.34 = bf16[2,1,8,128,1024]{3,2,4,0,1:T(8,128)(2,1)} copy(bf16[2,1,8,128,1024]{4,3,0,1,2:T(8,128)(2,1)} %bitcast.36) | data formatting | bytes 8388608 | tf_op jit(solution)/shard_map/transpose | solution.py:70
  145.3 7.3 %reshape.208 = bf16[2,1,1024,1024]{2,3,1,0:T(8,128)(2,1)} reshape(bf16[2,1,8,128,1024]{3,2,4,0,1:T(8,128)(2,1)} %copy.34) | data formatting | bytes 8388608 | tf_op jit(solution)/shard_map/reshape | solution.py:70
  152.7 6.2 %copy.35 = bf16[2,1,1024,1024]{3,2,1,0:T(8,128)(2,1)} copy(bf16[2,1,1024,1024]{2,3,1,0:T(8,128)(2,1)} %reshape.208) | data formatting | bytes 8388608 | tf_op jit(solution)/shard_map/reshape | solution.py:70
  158.8 2.6 %fusion.31 = (bf16[1,1,1024,1024]{3,2,1,0:T(8,128)(2,1)S(1)}, bf16[1,1,1024,1024]{3,2,1,0:T(8,128)(2,1)S(1)}) fusion(bf16[2,1,1024,1024]{3,2,1,0:T(8,128)(2,1)} %bitcast.123), kind=kLoop, calls=%fused_computation.96 | loop fusion | flops 1048576 | bytes 8388608 | tf_op jit(solution)/shard_map/slice | solution.py:72
  162.3 2.3 %divide_convert_fusion = bf16[2,1,1024,1024]{3,2,1,0:T(8,128)(2,1)S(1)} fusion(bf16[2,1,1024,1024]{3,2,1,0:T(8,128)(2,1)S(1)} %copy-done, bf16[1,1,1024,1024]{3,2,1,0:T(8,128)(2,1)S(1)} %get-tuple-element.16, bf16[1,1,1024,1024]{3,2,1,0:T(8,128)(2,1)S(1)} %get-tuple-element.15, f32[]{:T(128)} %bitcast.38, pred[1024,1024]{1,0:T(8,128)(4,1)S(1)} %fusion.4), kind=kLoop, calls=%fused_computation.2 | loop fusion | flops 10485760 | bytes 13631492 | tf_op jit(solution)/shard_map/convert_element_type | solution.py:129
  165.2 36.9 %maximum_maximum_fusion.weight_ref = bf16[2048,2048]{1,0:T(8,128)(2,1)} fusion(bf16[1024,1024]{1,0:T(8,128)(2,1)S(1)} %get-tuple-element.14, bf16[1024,1024]{1,0:T(8,128)(2,1)S(1)} %fusion.29, bf16[1024,1024]{1,0:T(8,128)(2,1)S(1)} %get-tuple-element.13), kind=kLoop, calls=%fused_computation.1 | loop fusion | flops 33554432 | bytes 14680064 | tf_op jit(solution)/shard_map/concatenate | solution.py:39
  202.1 13.2 %shard_map.37 = f32[64,2048]{1,0:T(8,128)} custom-call(bf16[2048,2048]{1,0:T(8,128)(2,1)} %maximum_maximum_fusion.weight_ref, f32[64,2048]{1,0:T(8,128)} %pad_maximum_fusion.5.target_ref), custom_call_target="tpu_custom_call" | custom-call | tf_op jit(solution)/shard_map/pallas_call | solution.py:43
  (66 shorter events, 24.4 us)
Async XLA Ops:
  6.5 61.1 %reduce-scatter.3.cloned.1.call-start = ((), (), s32[]{:S(2)}) async-start(), calls=%async_computation.2 | async-start | bytes 1638400 | tf_op jit(solution)/shard_map/reduce_scatter | solution.py:99
  11.6 5.3 %copy-start.1 = (bf16[1,1,768,1024]{2,3,1,0:T(8,128)(2,1)}, bf16[1,1,768,1024]{2,3,1,0:T(8,128)(2,1)S(1)}, u32[]{:S(2)}) copy-start(bf16[1,1,768,1024]{2,3,1,0:T(8,128)(2,1)S(1)} %copy.40) | copy-start | bytes 4718596
  13.3 2.0 copy-start.4
  27.9 3.0 %copy-start.3 = (bf16[2,1,768,1024]{3,2,1,0:T(8,128)(2,1)S(1)}, bf16[2,1,768,1024]{3,2,1,0:T(8,128)(2,1)}, u32[]{:S(2)}) copy-start(bf16[2,1,768,1024]{3,2,1,0:T(8,128)(2,1)} %param.3) | copy-start | bytes 9437188
  29.5 17.7 %copy-start.7 = (s32[512]{0:T(512)S(1)}, s32[512]{0:T(512)}, u32[]{:S(2)}) copy-start(s32[512]{0:T(512)} %param.5) | copy-start | bytes 6148
  30.8 68.0 %all-gather.2.cloned.1.call-start = ((), (), s32[]{:S(2)}) async-start(), calls=%async_computation.3 | async-start | bytes 1638400 | tf_op jit(solution)/shard_map/all_gather | solution.py:114
  51.3 1.4 copy-start.2
  51.3 1.9 copy-start.5
  67.6 59.6 %reduce-scatter.5.cloned.1.call-start = ((), (), s32[]{:S(2)}) async-start(), calls=%async_computation.4 | async-start | bytes 1310720 | tf_op jit(solution)/shard_map/reduce_scatter | solution.py:126
  98.8 30.4 %copy-start.6 = (bf16[512,1,2,640]{3,0,2,1:T(8,128)(2,1)S(1)}, bf16[512,1,2,640]{3,0,2,1:T(8,128)(2,1)}, u32[]{:S(2)}) copy-start(bf16[512,1,2,640]{3,0,2,1:T(8,128)(2,1)} %all-gather.2.cloned.1.call-done) | copy-start | bytes 3932164
  98.8 30.4 %collective-permute-start = (bf16[4,128,1,2,640]{4,1,0,3,2:T(8,128)(2,1)}, bf16[4,128,1,2,640]{4,1,0,3,2:T(8,128)(2,1)}, u32[]{:S(2)}, u32[]{:S(2)}) collective-permute-start(bf16[4,128,1,2,640]{4,1,0,3,2:T(8,128)(2,1)} %bitcast.131), channel_id=1, source_target_pairs={{0,1},{1,0},{2,3},{3,2},{4,5},{5,4},{6,7},{7,6},{8,9},{9,8},{10,11... | collective-permute-start | bytes 3932168 | tf_op jit(solution)/shard_map/ppermute | solution.py:117
  158.8 3.4 %copy-start = (bf16[2,1,1024,1024]{3,2,1,0:T(8,128)(2,1)S(1)}, bf16[2,1,1024,1024]{3,2,1,0:T(8,128)(2,1)}, u32[]{:S(2)}) copy-start(bf16[2,1,1024,1024]{3,2,1,0:T(8,128)(2,1)} %copy.35) | copy-start | bytes 12582916
Sparse Core Ops, SparseCore 0:
  30.9 34.0 reduce-scatter.2
  67.8 30.9 all-gather.1
  101.1 26.1 reduce-scatter.4

commit v6 on v4

--- a/solution.py
+++ b/solution.py
@@ -8,6 +8,12 @@
 
 relaxation = 0.125
 damping = 1.0
+
+
+def stacked_rows(factor):
+    real_left = jnp.concatenate([factor[0], factor[1]], axis=1)
+    imag_left = jnp.concatenate([factor[1], -factor[0]], axis=1)
+    return jnp.swapaxes(jnp.stack([real_left, imag_left], axis=1), 2, 3)
 
 
 def stacked_left(factor):
@@ -32,16 +38,14 @@
     return solution
 
 
-def strip_partials(gram_full, shot_count, core_count, core_index, rows_each, tile, span):
-    receivers = gram_full.shape[0]
-    rows = gram_full.reshape(shot_count, core_count, rows_each, *gram_full.shape[1:])
-    rows = lax.dynamic_slice_in_dim(rows, core_index, 1, 1)[:, 0].astype(jnp.bfloat16)
+def strip_partials(rows, shot_count, core_count, core_index, rows_each, tile, span):
+    rows = rows.astype(jnp.bfloat16)
     doubled = jnp.concatenate([rows, rows], axis=-1)
     windows = []
     for k in range(shot_count):
         start = ((k * core_count + core_index) * rows_each // tile) * tile
         windows.append(lax.dynamic_slice_in_dim(doubled[k], start, span, axis=-1))
-    return jnp.stack(windows).reshape(shot_count * rows_each, *gram_full.shape[1:3], span)
+    return jnp.stack(windows).reshape(shot_count * rows_each, *rows.shape[2:4], span)
 
 
 def rebuild_gram(strips, tiles, tile):
@@ -76,14 +80,19 @@
 
     right = stacked_right(downgoing)
 
-    gram_full = jnp.einsum(
-        "qtpu,qto->uqpo", stacked_left(downgoing), right, preferred_element_type=jnp.float32
-    )
-    gram_part = strip_partials(gram_full, shot_count, core_count, core_index, rows_each, tile, span)
+    left = stacked_rows(downgoing).reshape(freq_local, 2, shot_count, core_count, rows_each, -1)
+    left = lax.dynamic_slice_in_dim(left, core_index, 1, 3)[:, :, :, 0]
+    gram_rows = jnp.einsum("qpkit,qto->kiqpo", left, right, preferred_element_type=jnp.float32)
+    gram_part = strip_partials(gram_rows, shot_count, core_count, core_index, rows_each, tile, span)
     gram_strip = lax.psum_scatter(gram_part, "shot", scatter_dimension=0, tiled=True)
 
     local_power = jnp.sum(jnp.square(downgoing.astype(jnp.float32)), axis=(0, 2, 3))
     power = lax.psum(local_power, "shot") / receivers
+    gram_strip, power = lax.optimization_barrier((gram_strip, power))
+    power_wide = power[None, :, None, None]
+
+    across = lax.all_gather(gram_strip, "shot", axis=0, tiled=True)
+    across = across.reshape(shot_count, rows_each, freq_local, 2, span)
 
     corr_all = jnp.einsum(
         "qtpu,qto->uqpo", stacked_left(upgoing), right, preferred_element_type=jnp.float32
@@ -91,12 +100,8 @@
     order_table = source_order.reshape(shot_count, core_count, source_local)
     own_order = lax.dynamic_slice_in_dim(order_table, core_index, 1, 1).reshape(-1)
     corr_part = jnp.take(corr_all, own_order, axis=0).astype(jnp.bfloat16)
+    across, corr_part = lax.optimization_barrier((across, corr_part))
 
-    gram_strip, corr_part, power = lax.optimization_barrier((gram_strip, corr_part, power))
-    power_wide = power[None, :, None, None]
-
-    across = lax.all_gather(gram_strip, "shot", axis=0, tiled=True)
-    across = across.reshape(shot_count, rows_each, freq_local, 2, span)
     if core_count == 2:
         other = lax.ppermute(across, "sub", perm=[(0, 1), (1, 0)])
         first = jnp.where(core_index == 0, across, other)

time: 152 us -> 150 us (0.987)
  other arithmetic: 25.7 us -> 30 us
  waiting for transfers between devices: 37.7 us -> 33.6 us
  matrix products: 25.3 us -> 22.1 us
    all_gather x1, waiting for transfers between devices: 30.9 us -> 14.7 us  [per_device(): across = lax.all_gather(gram_strip, 'shot', axis=0, tiled=True)]
    reduce_scatter x1, waiting for transfers between devices: 0.01 us -> 12.3 us  [per_device(): lax.psum_scatter(gram_part, 'shot', scatter_dimension=0, tiled=True)]
    dot_general x1, matrix products: 6.91 us -> 3.69 us  [per_device(): jnp.einsum('qpkit,qto->kiqpo', left, right, preferred_element_type=jnp.fl...]
    another operation x0 -> x1, local copies, waits for them, and re-layouts: none -> 2.44 us  [strip_partials(): jnp.stack(windows).reshape(shot_count * rows_each, *rows.shape[2:4], span)]
    another operation x1 -> x3, other arithmetic: 1.27 us -> 3.47 us  [the longest x2 2.24 us: stacked_rows(): return jnp.swapaxes(jnp.stack([real_left, imag_left], axis=1), 2, 3)]
    reduce_sum x1, other arithmetic: 2.22 us -> 4.11 us  [per_device(): jnp.sum(jnp.square(downgoing.astype(jnp.float32)), axis=(0, 2, 3))]
    unnamed x26 -> x20, local copies, waits for them, and re-layouts: 8.16 us -> 6.87 us
  transfers between devices with their start and end apart: 4 -> 4, of which waited for: 2 -> 3; matrix products, arithmetic and copies ran while one was open for 27% -> 31% of each run, Pallas kernels for 0% -> 0%
where the time goes in v6:
time: 150 us
  local copies, waits for them, and re-layouts  35.1 us (23%)
  waiting for transfers between devices  33.6 us (22%)
  other arithmetic  30 us (20%)
  matrix products  22.1 us (15%)
  blocking collectives  14.4 us (10%)
  between operations  14.3 us (10%)
    all_gather x1, waiting for transfers between devices, per_device(): across = lax.all_gather(gram_strip, 'shot', axis=0, tiled=True)  14.7 us
    psum x1, blocking collectives, per_device(): power = lax.psum(local_power, 'shot') / receivers  14.4 us
    reduce_scatter x1, waiting for transfers between devices, per_device(): lax.psum_scatter(gram_part, 'shot', scatter_dimension=0, tiled=True)  12.3 us
    unnamed x20, local copies, waits for them, and re-layouts  6.87 us
    reduce_scatter x1, waiting for transfers between devices, per_device(): lax.psum_scatter(corr_part, 'shot', scatter_dimension=0, tiled=True)  6.46 us
    reshape x1, local copies, waits for them, and re-layouts, rebuild_gram(): jnp.transpose(upper, (3, 2, 0, 1, 4))  6.25 us
    transpose x1, local copies, waits for them, and re-layouts, per_device(): jnp.einsum('qtpu,qto->uqpo', stacked_left(upgoing), right, preferred_elem...  5.05 us
    dot_general x1, matrix products, per_device(): jnp.einsum('qtpu,qto->uqpo', stacked_left(upgoing), right, preferred_elem...  4.58 us
  transfers between devices with their start and end apart: 4, of which 3 were waited for; matrix products, arithmetic and copies ran while one was open for 31% of the time, Pallas kernels for 0%

profile of v6, /device:TPU:0, one launch (start us, length us, event | category | flops | bytes accessed | tf_op | source)
XLA Modules:
  0.0 149.6 jit_solution(5643038475918416033)
XLA Ops:
  6.5 2.2 %fusion.84 = (bf16[1,1,768,1024]{3,2,1,0:T(8,128)(2,1)S(1)}, bf16[1,1,768,1024]{3,2,1,0:T(8,128)(2,1)S(1)}) fusion(bf16[2,1,768,1024]{3,2,1,0:T(8,128)(2,1)} %param.3), kind=kLoop, calls=%fused_computation.164 | loop fusion | bytes 6291456 | tf_op jit(solution)/shard_map/slice | solution.py:26
  8.7 1.6 %copy.59 = bf16[1,1,768,1024]{2,3,1,0:T(8,128)(2,1)} copy(bf16[1,1,768,1024]{3,2,1,0:T(8,128)(2,1)S(1)} %get-tuple-element.21) | data formatting | bytes 3145728
  13.0 1.7 %fusion.28 = (bf16[1,1,1536,1024]{2,3,1,0:T(8,128)(2,1)S(1)}, bf16[1,1,1536,1024]{2,3,1,0:T(8,128)(2,1)S(1)}) fusion(bf16[1,768,1024]{1,2,0:T(8,128)(2,1)S(1)} %bitcast.230, bf16[1,768,1024]{1,2,0:T(8,128)(2,1)S(1)} %bitcast.226, bf16[1,768,1024]{1,2,0:T(8,128)(2,1)} %bitcast_negate_fusion), kind=kLoop, calls=%fused_computation.69 | loop fusion | flops 12582912 | bytes 11010048 | tf_op jit(solution)/shard_map/stack | solution.py:16
  15.3 3.7 %convert_bitcast_fusion = bf16[4,128,1,2,1024]{1,4,0,3,2:T(8,128)(2,1)S(1)} fusion(bf16[1,2,4,2,128,1536]{5,4,3,2,1,0:T(8,128)(2,1)S(1)} %bitcast.229, s32[]{:T(128)S(6)} %select_n.96, bf16[1,768,1024]{1,2,0:T(8,128)(2,1)S(1)} %bitcast.231, bf16[1,768,1024]{1,2,0:T(8,128)(2,1)S(1)} %bitcast.227), kind=kOutput, calls=%fused_computation.41 | convolution fusion | flops 3228565504 | bytes 8388612 | tf_op jit(solution)/shard_map/qpkit,qto->kiqpo/dot_general | solution.py:85
  20.3 2.8 %pad_slice_fusion.11 = (bf16[1,128,1,2,2048]{1,4,0,3,2:T(8,128)(2,1)}, bf16[1,128,1,2,2048]{1,4,0,3,2:T(8,128)(2,1)}, bf16[1,128,1,2,2048]{1,4,0,3,2:T(8,128)(2,...) fusion(bf16[4,128,1,2,1024]{1,4,0,3,2:T(8,128)(2,1)S(1)} %conve, ...), kind=kLoop, calls=%fused_computation.18 | loop fusion | bytes 8388608 | tf_op jit(solution)/shard_map/slice | solution.py:47
  27.3 2.4 %copy.51 = bf16[4,128,1,2,640]{4,1,0,3,2:T(8,128)(2,1)} copy(bf16[4,128,1,2,640]{1,4,0,3,2:T(8,128)(2,1)} %pad_maximum_fusion.3) | data formatting | bytes 2621440 | tf_op jit(solution)/shard_map/stack | solution.py:48
  29.8 4.1 %multiply_reduce_fusion = f32[]{:T(128)} fusion(bf16[2,1,768,1024]{3,2,1,0:T(8,128)(2,1)} %param.3), kind=kLoop, calls=%fused_computation.6 | loop fusion | flops 4718591 | bytes 3145732 | tf_op jit(solution)/shard_map/reduce_sum | solution.py:89
  33.9 14.4 %psum.7 = f32[1]{0:T(128)} all-reduce(f32[1]{0:T(128)} %bitcast.13), channel_id=1, replica_groups=mesh['grp'=2,'shot'=4,'freq'=2,'sub'=2] {'shot'}, use_global_device_ids=true, to_apply=%region_2.3 | all-reduce | flops 1 | bytes 8 | tf_op jit(solution)/shard_map/psum | solution.py:90
  49.0 2.6 %slice_bitcast_fusion.3 = (bf16[1,768,512]{2,1,0:T(8,128)(2,1)}, bf16[1,768,512]{2,1,0:T(8,128)(2,1)}) fusion(bf16[2,1,768,512]{3,2,1,0:T(8,128)(2,1)} %param.4), kind=kLoop, calls=%fused_computation.71 | loop fusion | bytes 3145728 | tf_op jit(solution)/shard_map/squeeze | solution.py:20
  51.6 12.3 %reduce-scatter.3.cloned.1.call-done = bf16[128,1,2,640]{3,0,2,1:T(8,128)(2,1)} async-done(((bf16[512,1,2,640]{3,0,2,1:T(8,128)(2,1)}), bf16[128,1,2,640]{3,0,2,1:T(8,128)(2,1)}) %reduce-scatter.3.cloned.1.call-update) | async-done | bytes 327696 | tf_op jit(solution)/shard_map/reduce_scatter | solution.py:87
  65.4 1.8 %maximum_bitcast_fusion.5 = (bf16[1,1536,1,512]{3,1,2,0:T(8,128)(2,1)S(1)}, bf16[1,1536,1,512]{3,1,2,0:T(8,128)(2,1)S(1)}) fusion(bf16[1,768,512]{2,1,0:T(8,128)(2,1)} %get-tuple-element.40, bf16[1,768,512]{2,1,0:T(8,128)(2,1)} %get-tuple-element.39, bf16[1,768,512]{2,1,0:T(8,128)(2,1)S(1)} %fusion.77), kind=kLoop, calls=%fused_computation.42 | loop fusion | flops 6291456 | bytes 5505024 | tf_op jit(solution)/shard_map/stack | solution.py:22
  67.2 4.6 %fusion.10 = bf16[512,2,1024]{0,2,1:T(8,128)(2,1)} fusion(bf16[1,1536,1,512]{3,1,2,0:T(8,128)(2,1)S(1)} %get-tuple-element.44, bf16[1,1536,1,512]{3,1,2,0:T(8,128)(2,1)S(1)} %get-tuple-element.43, bf16[1,768,1024]{1,2,0:T(8,128)(2,1)S(1)} %bitcast.232, bf16[1,768,1024]{1,2,0:T(8,128)(2,1)S(1)} %bitcast.228), kind=kOutput, calls=%fused_computation.35 | convolution fusion | flops 3233808384 | bytes 8388608 | tf_op jit(solution)/shard_map/qtpu,qto->uqpo/dot_general | solution.py:97
  71.8 5.0 %copy.52 = bf16[512,2,1024]{2,1,0:T(2,128)(2,1)S(1)} copy(bf16[512,2,1024]{0,2,1:T(8,128)(2,1)} %fusion.10) | data formatting | bytes 4194304 | tf_op jit(solution)/shard_map/qtpu,qto->uqpo/transpose | solution.py:97
  78.3 2.8 %gather_fusion = bf16[256,2,1024]{2,1,0:T(2,128)(2,1)S(1)} fusion(bf16[512,2,1024]{2,1,0:T(2,128)(2,1)S(1)} %copy.52, s32[1024]{0:T(1024)S(1)} %pad_clamp_fusion), kind=kCustom, calls=%fused_computation | custom fusion | bytes 2098176 | tf_op jit(solution)/shard_map/jit(_take)/gather | solution.py:102
  82.4 14.7 %all-gather.2.cloned.1.call-done = bf16[512,1,2,640]{3,0,2,1:T(8,128)(2,1)} async-done(((bf16[128,1,2,640]{3,0,2,1:T(8,128)(2,1)}), bf16[512,1,2,640]{3,0,2,1:T(8,128)(2,1)}) %all-gather.2.cloned.1.call-update) | async-done | bytes 1310736 | tf_op jit(solution)/shard_map/all_gather | solution.py:94
  97.2 3.6 %fusion.1 = pred[1024,1024]{1,0:T(8,128)(4,1)S(1)} fusion(s32[1024]{0:T(1024)S(1)} %get-tuple-element.51, s32[1024]{0:T(1024)S(1)} %get-tuple-element.52, pred[1024]{0:T(1024)(128)(4,1)S(1)} %fusion.71), kind=kLoop, calls=%fused_computation.21 | loop fusion | flops 15728640 | bytes 1057792 | tf_op jit(solution)/shard_map/le | solution.py:63
  100.8 1.6 %select_bitcast_fusion.1 = (bf16[4,1,128,1,2,640]{5,2,1,0,4,3:T(8,128)(2,1)S(1)}, bf16[4,1,128,1,2,640]{5,2,1,0,4,3:T(8,128)(2,1)S(1)}) fusion(bf16[4,128,1,2,640]{4,1,0,3,2:T(8,128)(2,1)} %bitcast.236, bf16[4,128,1,2,640]{4,1,0,3,2:T(8,128)(2,1)S(1)} %collective-permute-done, pred[]{:T(512)S(6)} %eq.6), kind=kLoop, calls=%fused_computation.46 | loop fusion | flops 1310720 | bytes 5242881 | tf_op jit(solution)/shard_map/stack | solution.py:109
  103.5 2.4 %copy.55 = bf16[2,1,8,128,1024]{4,3,2,0,1:T(8,128)(2,1)} copy(bf16[2,1,8,128,1024]{4,3,0,1,2:T(8,128)(2,1)S(1)} %bitcast.233) | data formatting | bytes 8388608 | tf_op jit(solution)/shard_map/transpose | solution.py:58
  105.8 6.2 %copy.56 = bf16[2,1,1024,1024]{2,3,0,1:T(8,128)(2,1)} copy(bf16[2,1,1024,1024]{3,2,0,1:T(8,128)(2,1)} %bitcast.224) | data formatting | bytes 8388608 | tf_op jit(solution)/shard_map/reshape | solution.py:58
  112.1 2.7 %fusion.83 = (bf16[1,1,1024,1024]{3,2,0,1:T(8,128)(2,1)S(1)}, bf16[1,1,1024,1024]{3,2,0,1:T(8,128)(2,1)S(1)}) fusion(bf16[2,1,1024,1024]{3,2,0,1:T(8,128)(2,1)} %bitcast.225), kind=kLoop, calls=%fused_computation.163 | loop fusion | flops 1048576 | bytes 8388608 | tf_op jit(solution)/shard_map/slice | solution.py:60
  115.6 2.7 %divide_convert_fusion = bf16[2,1,1024,1024]{3,2,0,1:T(8,128)(2,1)S(1)} fusion(bf16[1,1,1024,1024]{3,2,0,1:T(8,128)(2,1)S(1)} %get-tuple-element.20, bf16[1,1,1024,1024]{3,2,0,1:T(8,128)(2,1)S(1)} %get-tuple-element.19, f32[]{:T(128)} %bitcast.26, pred[1024,1024]{1,0:T(8,128)(4,1)S(1)} %fusion.1, bf16[2,1,8,128,1024]{4,3,2,0,1:T(8,128)(2,1)S(1)} %copy-done.2), kind=kLoop, calls=%fused_computation.1 | loop fusion | flops 10485760 | bytes 13631492 | tf_op jit(solution)/shard_map/convert_element_type | solution.py:118
  120.7 6.5 %reduce-scatter.5.cloned.1.call-done = bf16[64,1,2,1024]{3,0,1,2:T(8,128)(2,1)} async-done(((bf16[256,1,2,1024]{3,0,1,2:T(8,128)(2,1)}), bf16[64,1,2,1024]{3,0,1,2:T(8,128)(2,1)}) %reduce-scatter.5.cloned.1.call-update) | async-done | bytes 262160 | tf_op jit(solution)/shard_map/reduce_scatter | solution.py:115
  128.4 2.2 %fusion.53 = f32[64,1024]{1,0:T(8,128)S(1)} fusion(bf16[2,1,64,1024]{3,2,1,0:T(8,128)(2,1)S(1)} %fusion.51, bf16[2,1,1024,1024]{3,2,0,1:T(8,128)(2,1)} %copy-done), kind=kOutput, calls=%fused_computation.125 | convolution fusion | flops 134217728 | bytes 2490368 | tf_op jit(solution)/shard_map/qjc,qcr->qjr/dot_general | solution.py:34
  130.6 2.1 %fusion.54 = f32[64,1024]{1,0:T(8,128)S(1)} fusion(bf16[2,1,64,1024]{3,2,1,0:T(8,128)(2,1)S(1)} %fusion.51, bf16[2,1,1024,1024]{3,2,0,1:T(8,128)(2,1)} %copy-done), kind=kOutput, calls=%fused_computation.126 | convolution fusion | flops 134217728 | bytes 2490368 | tf_op jit(solution)/shard_map/qjc,qcr->qjr/dot_general | solution.py:32
  (82 shorter events, 28.7 us)
Async XLA Ops:
  6.5 57.4 %reduce-scatter.3.cloned.1.call-start = ((), (), s32[]{:S(2)}) async-start(), calls=%async_computation.2 | async-start | bytes 1638400 | tf_op jit(solution)/shard_map/reduce_scatter | solution.py:87
  11.0 2.0 %copy-start.5 = (bf16[1,1,768,1024]{2,3,1,0:T(8,128)(2,1)S(1)}, bf16[1,1,768,1024]{2,3,1,0:T(8,128)(2,1)}, u32[]{:S(2)}) copy-start(bf16[1,1,768,1024]{2,3,1,0:T(8,128)(2,1)} %copy.59) | copy-start | bytes 4718596
  19.0 1.3 copy-start.4
  29.8 67.4 %all-gather.2.cloned.1.call-start = ((), (), s32[]{:S(2)}) async-start(), calls=%async_computation.3 | async-start | bytes 1638400 | tf_op jit(solution)/shard_map/all_gather | solution.py:94
  64.0 63.2 %reduce-scatter.5.cloned.1.call-start = ((), (), s32[]{:S(2)}) async-start(), calls=%async_computation.4 | async-start | bytes 1310720 | tf_op jit(solution)/shard_map/reduce_scatter | solution.py:115
  71.8 5.1 %copy-start.6 = (s32[512]{0:T(512)S(1)}, s32[512]{0:T(512)}, u32[]{:S(2)}) copy-start(s32[512]{0:T(512)} %param.5) | copy-start | bytes 6148
  97.1 3.6 %collective-permute-start = (bf16[4,128,1,2,640]{4,1,0,3,2:T(8,128)(2,1)}, bf16[4,128,1,2,640]{4,1,0,3,2:T(8,128)(2,1)S(1)}, u32[]{:S(2)}, u32[]{:S(2)}) collective-permute-start(bf16[4,128,1,2,640]{4,1,0,3,2:T(8,128)(2,1)} %bitcast.235), channel_id=1, source_target_pairs={{0,1},{1,0},{2,3},{3,2},{4,5},{5,4},{6,7},{7,6},{8,9},{9,8},{10,11... | collective-permute-start | bytes 3932168 | tf_op jit(solution)/shard_map/ppermute | solution.py:106
  112.1 3.5 %copy-start.2 = (bf16[2,1,8,128,1024]{4,3,2,0,1:T(8,128)(2,1)S(1)}, bf16[2,1,8,128,1024]{4,3,2,0,1:T(8,128)(2,1)}, u32[]{:S(2)}) copy-start(bf16[2,1,8,128,1024]{4,3,2,0,1:T(8,128)(2,1)} %copy.55) | copy-start | bytes 12582916
  118.3 1.9 %copy-start = (bf16[2,1,1024,1024]{3,2,0,1:T(8,128)(2,1)}, bf16[2,1,1024,1024]{3,2,0,1:T(8,128)(2,1)S(1)}, u32[]{:S(2)}) copy-start(bf16[2,1,1024,1024]{3,2,0,1:T(8,128)(2,1)S(1)} %divide_convert_fusion) | copy-start | bytes 12582916
  127.2 5.5 %copy-start.1 = (bf16[2,1,1024,1024]{3,2,0,1:T(8,128)(2,1)S(1)}, bf16[2,1,1024,1024]{3,2,0,1:T(8,128)(2,1)}, u32[]{:S(2)}) copy-start(bf16[2,1,1024,1024]{3,2,0,1:T(8,128)(2,1)} %copy-done) | copy-start | bytes 12582916
  132.7 1.0 copy-start.3
Sparse Core Ops, SparseCore 0:
  29.9 34.0 reduce-scatter.2
  65.5 31.5 all-gather.1
  100.9 26.2 reduce-scatter.4

commit v7 on v6

--- a/solution.py
+++ b/solution.py
@@ -88,11 +88,6 @@
 
     local_power = jnp.sum(jnp.square(downgoing.astype(jnp.float32)), axis=(0, 2, 3))
     power = lax.psum(local_power, "shot") / receivers
-    gram_strip, power = lax.optimization_barrier((gram_strip, power))
-    power_wide = power[None, :, None, None]
-
-    across = lax.all_gather(gram_strip, "shot", axis=0, tiled=True)
-    across = across.reshape(shot_count, rows_each, freq_local, 2, span)
 
     corr_all = jnp.einsum(
         "qtpu,qto->uqpo", stacked_left(upgoing), right, preferred_element_type=jnp.float32
@@ -100,7 +95,20 @@
     order_table = source_order.reshape(shot_count, core_count, source_local)
     own_order = lax.dynamic_slice_in_dim(order_table, core_index, 1, 1).reshape(-1)
     corr_part = jnp.take(corr_all, own_order, axis=0).astype(jnp.bfloat16)
-    across, corr_part = lax.optimization_barrier((across, corr_part))
+
+    gram_strip, power, corr_part = lax.optimization_barrier((gram_strip, power, corr_part))
+    power_wide = power[None, :, None, None]
+
+    shot_index = lax.axis_index("shot")
+    corr_blocks = corr_part.reshape(shot_count, source_local, *corr_part.shape[1:])
+    corr = lax.dynamic_index_in_dim(corr_blocks, shot_index, 0, keepdims=False).astype(jnp.float32)
+    for shift in range(1, shot_count):
+        outgoing = lax.dynamic_index_in_dim(corr_blocks, (shot_index + shift) % shot_count, 0, keepdims=False)
+        pairs = [(k, (k + shift) % shot_count) for k in range(shot_count)]
+        corr = corr + lax.ppermute(outgoing, "shot", perm=pairs).astype(jnp.float32)
+
+    across = lax.all_gather(gram_strip, "shot", axis=0, tiled=True)
+    across = across.reshape(shot_count, rows_each, freq_local, 2, span)
 
     if core_count == 2:
         other = lax.ppermute(across, "sub", perm=[(0, 1), (1, 0)])
@@ -112,7 +120,6 @@
     strips = strips.reshape(receivers, freq_local, 2, span)
     whole = rebuild_gram(strips, tiles, tile)
 
-    corr = lax.psum_scatter(corr_part, "shot", scatter_dimension=0, tiled=True).astype(jnp.float32)
     target = jnp.transpose(corr, (2, 1, 0, 3)) / power_wide
 
     scaled = (whole.astype(jnp.float32) / power_wide).astype(jnp.bfloat16)

time: 150 us -> 149 us (level)
  starting transfers between devices: 0.27 us -> 3.49 us
  matrix products: 22.1 us -> 18.9 us
  other arithmetic: 30 us -> 27.6 us
  waiting for transfers between devices: 33.6 us -> 35.4 us
  local copies, waits for them, and re-layouts: 35.1 us -> 33.5 us
    all_gather x1, waiting for transfers between devices: 14.7 us -> 31.1 us  [per_device(): across = lax.all_gather(gram_strip, 'shot', axis=0, tiled=True)]
    reduce_scatter x1, waiting for transfers between devices: 12.3 us -> 0.02 us  [per_device(): lax.psum_scatter(gram_part, 'shot', scatter_dimension=0, tiled=True)]
    reduce_scatter x1 -> x0, waiting for transfers between devices: 6.46 us -> none  [per_device(): lax.psum_scatter(corr_part, 'shot', scatter_dimension=0, tiled=True)]
    ppermute x0 -> x3, waiting for transfers between devices: none -> 4.31 us  [per_device(): corr = corr + lax.ppermute(outgoing, 'shot', perm=pairs).astype(jnp.float32)]
    ppermute x0 -> x3, starting transfers between devices: none -> 3.44 us  [per_device(): corr = corr + lax.ppermute(outgoing, 'shot', perm=pairs).astype(jnp.float32)]
    dot_general x5, matrix products: 4.12 us -> 2.39 us  [sweep_whole(): jnp.einsum('qjc,qcr->qjr', narrow[0], scaled[1], preferred_element_type=j...]
    dot_general x6, matrix products: 4.46 us -> 2.88 us  [sweep_whole(): jnp.einsum('qjc,qcr->qjr', narrow[0], scaled[0], preferred_element_type=j...]
    another operation x1, other arithmetic: 1.81 us -> 0.29 us  [stacked_left(): return jnp.stack([real_left, imag_left], axis=2)]
  transfers between devices with their start and end apart: 4 -> 6, of which waited for: 3 -> 2; matrix products, arithmetic and copies ran while one was open for 31% -> 30% of each run, Pallas kernels for 0% -> 0%
where the time goes in v7:
time: 149 us; the launch traced here: 148 us
  waiting for transfers between devices  35.4 us (24%)
  local copies, waits for them, and re-layouts  33.5 us (22%)
  other arithmetic  27.6 us (19%)
  matrix products  18.9 us (13%)
  between operations  14.6 us (10%)
  blocking collectives  14.5 us (10%)
  starting transfers between devices  3.49 us (2%)
    all_gather x1, waiting for transfers between devices, per_device(): across = lax.all_gather(gram_strip, 'shot', axis=0, tiled=True)  31.1 us
    psum x1, blocking collectives, per_device(): power = lax.psum(local_power, 'shot') / receivers  14.5 us
    reshape x1, local copies, waits for them, and re-layouts, rebuild_gram(): jnp.transpose(upper, (3, 2, 0, 1, 4))  6.24 us
    unnamed x16, local copies, waits for them, and re-layouts  5.37 us
    transpose x1, local copies, waits for them, and re-layouts, per_device(): jnp.einsum('qtpu,qto->uqpo', stacked_left(upgoing), right, preferred_elem...  5.05 us
    dot_general x1, matrix products, per_device(): jnp.einsum('qtpu,qto->uqpo', stacked_left(upgoing), right, preferred_elem...  4.58 us
    ppermute x3, waiting for transfers between devices, per_device(): corr = corr + lax.ppermute(outgoing, 'shot', perm=pairs).astype(jnp.float32)  4.31 us
    reduce_sum x1, other arithmetic, per_device(): jnp.sum(jnp.square(downgoing.astype(jnp.float32)), axis=(0, 2, 3))  4.11 us
  transfers between devices with their start and end apart: 6, of which 2 were waited for; matrix products, arithmetic and copies ran while one was open for 30% of the time, Pallas kernels for 0%

profile of v7, /device:TPU:0, one launch (start us, length us, event | category | flops | bytes accessed | tf_op | source)
XLA Modules:
  0.0 148.0 jit_solution(4417088098574541034)
XLA Ops:
  6.5 2.2 %fusion.88 = (bf16[1,1,768,1024]{3,2,1,0:T(8,128)(2,1)S(1)}, bf16[1,1,768,1024]{3,2,1,0:T(8,128)(2,1)S(1)}) fusion(bf16[2,1,768,1024]{3,2,1,0:T(8,128)(2,1)} %param.3), kind=kLoop, calls=%fused_computation.171 | loop fusion | bytes 6291456 | tf_op jit(solution)/shard_map/slice | solution.py:26
  8.7 1.6 %copy.40 = bf16[1,1,768,1024]{2,3,1,0:T(8,128)(2,1)} copy(bf16[1,1,768,1024]{3,2,1,0:T(8,128)(2,1)S(1)} %get-tuple-element.19) | data formatting | bytes 3145728
  13.0 1.7 %fusion.28 = (bf16[1,1,1536,1024]{2,3,1,0:T(8,128)(2,1)S(1)}, bf16[1,1,1536,1024]{2,3,1,0:T(8,128)(2,1)S(1)}) fusion(bf16[1,768,1024]{1,2,0:T(8,128)(2,1)S(1)} %bitcast.225, bf16[1,768,1024]{1,2,0:T(8,128)(2,1)S(1)} %bitcast.221, bf16[1,768,1024]{1,2,0:T(8,128)(2,1)} %bitcast_negate_fusion), kind=kLoop, calls=%fused_computation.69 | loop fusion | flops 12582912 | bytes 11010048 | tf_op jit(solution)/shard_map/stack | solution.py:16
  15.3 3.7 %convert_bitcast_fusion = bf16[4,128,1,2,1024]{1,4,0,3,2:T(8,128)(2,1)S(1)} fusion(bf16[1,2,4,2,128,1536]{5,4,3,2,1,0:T(8,128)(2,1)S(1)} %bitcast.224, s32[]{:T(128)S(6)} %select_n.123, bf16[1,768,1024]{1,2,0:T(8,128)(2,1)S(1)} %bitcast.226, bf16[1,768,1024]{1,2,0:T(8,128)(2,1)S(1)} %bitcast.222), kind=kOutput, calls=%fused_computation.41 | convolution fusion | flops 3228565504 | bytes 8388612 | tf_op jit(solution)/shard_map/qpkit,qto->kiqpo/dot_general | solution.py:85
  20.3 2.8 %pad_slice_fusion.11 = (bf16[1,128,1,2,2048]{1,4,0,3,2:T(8,128)(2,1)}, bf16[1,128,1,2,2048]{1,4,0,3,2:T(8,128)(2,1)}, bf16[1,128,1,2,2048]{1,4,0,3,2:T(8,128)(2,...) fusion(bf16[4,128,1,2,1024]{1,4,0,3,2:T(8,128)(2,1)S(1)} %conve, ...), kind=kLoop, calls=%fused_computation.18 | loop fusion | bytes 8388608 | tf_op jit(solution)/shard_map/slice | solution.py:47
  23.1 1.5 %fusion.56 = (bf16[1,128,1,2,640]{1,4,0,3,2:T(8,128)(2,1)S(1)}, bf16[1,128,1,2,640]{1,4,0,3,2:T(8,128)(2,1)S(1)}) fusion(s32[]{:T(128)S(6)} %select_n.131, bf16[4,128,1,2,1024]{1,4,0,3,2:T(8,128)(2,1)} %copy-done.1, bf16[1,128,1,2,2048]{1,4,0,3,2:T(8,128)(2,1)} %get-tuple-element.33, s32[]{:T(128)S(6)} %select_n.125, ...), kind=kLoop, calls=%fused_computation.113 | loop fusion | flops 1310720 | bytes 3407880 | tf_op jit(solution)/shard_map/concatenate | solution.py:43
  24.6 1.5 dynamic-slice_maximum_fusion
  27.3 2.4 %copy.31 = bf16[4,128,1,2,640]{4,1,0,3,2:T(8,128)(2,1)} copy(bf16[4,128,1,2,640]{1,4,0,3,2:T(8,128)(2,1)} %pad_maximum_fusion.3) | data formatting | bytes 2621440 | tf_op jit(solution)/shard_map/stack | solution.py:48
  29.8 4.1 %multiply_reduce_fusion = f32[]{:T(128)} fusion(bf16[2,1,768,1024]{3,2,1,0:T(8,128)(2,1)} %param.3), kind=kLoop, calls=%fused_computation.6 | loop fusion | flops 4718591 | bytes 3145732 | tf_op jit(solution)/shard_map/reduce_sum | solution.py:89
  33.9 14.5 %psum.7 = f32[1]{0:T(128)} all-reduce(f32[1]{0:T(128)} %bitcast.13), channel_id=1, replica_groups=mesh['grp'=2,'shot'=4,'freq'=2,'sub'=2] {'shot'}, use_global_device_ids=true, to_apply=%region_2.3 | all-reduce | flops 1 | bytes 8 | tf_op jit(solution)/shard_map/psum | solution.py:90
  49.7 1.5 %slice_bitcast_fusion.3 = (bf16[1,768,512]{2,1,0:T(8,128)(2,1)S(1)}, bf16[1,768,512]{2,1,0:T(8,128)(2,1)S(1)}) fusion(bf16[2,1,768,512]{3,2,1,0:T(8,128)(2,1)} %param.4), kind=kLoop, calls=%fused_computation.71 | loop fusion | bytes 3145728 | tf_op jit(solution)/shard_map/squeeze | solution.py:20
  51.5 4.6 %fusion.10 = bf16[512,2,1024]{0,2,1:T(8,128)(2,1)} fusion(bf16[1,1536,1,512]{3,1,2,0:T(8,128)(2,1)S(1)} %get-tuple-element.45, bf16[1,1536,1,512]{3,1,2,0:T(8,128)(2,1)S(1)} %get-tuple-element.44, bf16[1,768,1024]{1,2,0:T(8,128)(2,1)S(1)} %bitcast.227, bf16[1,768,1024]{1,2,0:T(8,128)(2,1)S(1)} %bitcast.223), kind=kOutput, calls=%fused_computation.35 | convolution fusion | flops 3233808384 | bytes 8388608 | tf_op jit(solution)/shard_map/qtpu,qto->uqpo/dot_general | solution.py:92
  56.0 5.0 %copy.32 = bf16[512,2,1024]{2,1,0:T(2,128)(2,1)S(1)} copy(bf16[512,2,1024]{0,2,1:T(8,128)(2,1)} %fusion.10) | data formatting | bytes 4194304 | tf_op jit(solution)/shard_map/qtpu,qto->uqpo/transpose | solution.py:92
  63.2 2.8 %gather_fusion = bf16[256,2,1024]{2,1,0:T(2,128)(2,1)S(1)} fusion(bf16[512,2,1024]{2,1,0:T(2,128)(2,1)S(1)} %copy.32, s32[1024]{0:T(1024)S(1)} %pad_clamp_fusion), kind=kCustom, calls=%fused_computation | custom fusion | bytes 2098176 | tf_op jit(solution)/shard_map/jit(_take)/gather | solution.py:97
  66.0 1.5 %fusion.13 = bf16[256,1,2,1024]{3,2,0,1:T(2,128)(2,1)S(1)} fusion(bf16[256,2,1024]{2,1,0:T(2,128)(2,1)S(1)} %gather_fusion, pred[256]{0:T(512)(128)(4,1)S(1)} %compare_and_fusion), kind=kLoop, calls=%fused_computation.40 | loop fusion | flops 524288 | bytes 2097408 | tf_op jit(solution)/shard_map/convert_element_type | solution.py:97
  67.6 31.1 %all-gather.2.cloned.1.call-done = bf16[512,1,2,640]{3,0,2,1:T(8,128)(2,1)} async-done(((bf16[128,1,2,640]{3,0,2,1:T(8,128)(2,1)}), bf16[512,1,2,640]{3,0,2,1:T(8,128)(2,1)}) %all-gather.2.cloned.1.call-update) | async-done | bytes 1310736 | tf_op jit(solution)/shard_map/all_gather | solution.py:110
  98.6 3.6 %fusion.1 = pred[1024,1024]{1,0:T(8,128)(4,1)S(1)} fusion(s32[1024]{0:T(1024)S(1)} %get-tuple-element.52, s32[1024]{0:T(1024)S(1)} %get-tuple-element.53, pred[1024]{0:T(1024)(128)(4,1)S(1)} %fusion.75), kind=kLoop, calls=%fused_computation.21 | loop fusion | flops 15728640 | bytes 1057792 | tf_op jit(solution)/shard_map/le | solution.py:63
  103.3 1.4 collective-permute-start.2
  106.7 1.6 %select_bitcast_fusion.1 = (bf16[4,1,128,1,2,640]{5,2,1,0,4,3:T(8,128)(2,1)S(1)}, bf16[4,1,128,1,2,640]{5,2,1,0,4,3:T(8,128)(2,1)S(1)}) fusion(bf16[4,128,1,2,640]{4,1,0,3,2:T(8,128)(2,1)S(1)} %bitcast.233, bf16[4,128,1,2,640]{4,1,0,3,2:T(8,128)(2,1)} %collective-permute-done.3, pred[]{:T(512)S(6)} %eq.10), kind=kLoop, calls=%fused_computation.46 | loop fusion | flops 1310720 | bytes 5242881 | tf_op jit(solution)/shard_map/stack | solution.py:117
  109.4 2.4 %copy.36 = bf16[2,1,8,128,1024]{4,3,2,0,1:T(8,128)(2,1)} copy(bf16[2,1,8,128,1024]{4,3,0,1,2:T(8,128)(2,1)S(1)} %bitcast.228) | data formatting | bytes 8388608 | tf_op jit(solution)/shard_map/transpose | solution.py:58
  111.8 6.2 %copy.37 = bf16[2,1,1024,1024]{2,3,0,1:T(8,128)(2,1)} copy(bf16[2,1,1024,1024]{3,2,0,1:T(8,128)(2,1)} %bitcast.219) | data formatting | bytes 8388608 | tf_op jit(solution)/shard_map/reshape | solution.py:58
  118.0 2.6 %fusion.87 = (bf16[1,1,1024,1024]{3,2,0,1:T(8,128)(2,1)S(1)}, bf16[1,1,1024,1024]{3,2,0,1:T(8,128)(2,1)S(1)}) fusion(bf16[2,1,1024,1024]{3,2,0,1:T(8,128)(2,1)} %bitcast.220), kind=kLoop, calls=%fused_computation.170 | loop fusion | flops 1048576 | bytes 8388608 | tf_op jit(solution)/shard_map/slice | solution.py:60
  121.5 2.5 %divide_convert_fusion = bf16[2,1,1024,1024]{3,2,0,1:T(8,128)(2,1)S(1)} fusion(bf16[1,1,1024,1024]{3,2,0,1:T(8,128)(2,1)S(1)} %get-tuple-element.18, bf16[1,1,1024,1024]{3,2,0,1:T(8,128)(2,1)S(1)} %get-tuple-element.17, f32[]{:T(128)} %bitcast.30, pred[1024,1024]{1,0:T(8,128)(4,1)S(1)} %fusion.1, bf16[2,1,8,128,1024]{4,3,2,0,1:T(8,128)(2,1)S(1)} %copy-done), kind=kLoop, calls=%fused_computation.1 | loop fusion | flops 10485760 | bytes 13631492 | tf_op jit(solution)/shard_map/convert_element_type | solution.py:125
  125.0 4.3 %collective-permute-done.1 = bf16[64,1,2,1024]{3,0,1,2:T(8,128)(2,1)S(1)} collective-permute-done((bf16[64,1,2,1024]{3,0,1,2:T(8,128)(2,1)S(1)}, bf16[64,1,2,1024]{3,0,1,2:T(8,128)(2,1)S(1)}, u32[]{:S(2)}, u32[]{:S(2)}) %collective-permute-start.1) | collective-permute-done | bytes 262176 | tf_op jit(solution)/shard_map/ppermute | solution.py:108
  (83 shorter events, 26.4 us)
Async XLA Ops:
  6.5 61.0 %reduce-scatter.2.cloned.1.call-start = ((), (), s32[]{:S(2)}) async-start(), calls=%async_computation.1 | async-start | bytes 1638400 | tf_op jit(solution)/shard_map/reduce_scatter | solution.py:87
  11.0 2.0 %copy-start.2 = (bf16[1,1,768,1024]{2,3,1,0:T(8,128)(2,1)S(1)}, bf16[1,1,768,1024]{2,3,1,0:T(8,128)(2,1)}, u32[]{:S(2)}) copy-start(bf16[1,1,768,1024]{2,3,1,0:T(8,128)(2,1)} %copy.40) | copy-start | bytes 4718596
  19.0 1.3 copy-start.1
  29.8 68.8 %all-gather.2.cloned.1.call-start = ((), (), s32[]{:S(2)}) async-start(), calls=%async_computation.2 | async-start | bytes 1638400 | tf_op jit(solution)/shard_map/all_gather | solution.py:110
  56.0 5.1 %copy-start.4 = (s32[512]{0:T(512)S(1)}, s32[512]{0:T(512)}, u32[]{:S(2)}) copy-start(s32[512]{0:T(512)} %param.5) | copy-start | bytes 6148
  98.6 8.1 %collective-permute-start.3 = (bf16[4,128,1,2,640]{4,1,0,3,2:T(8,128)(2,1)}, bf16[4,128,1,2,640]{4,1,0,3,2:T(8,128)(2,1)}, u32[]{:S(2)}, u32[]{:S(2)}) collective-permute-start(bf16[4,128,1,2,640]{4,1,0,3,2:T(8,128)(2,1)} %bitcast.232), channel_id=1, source_target_pairs={{0,1},{1,0},{2,3},{3,2},{4,5},{5,4},{6,7},{7,6},{8,9},{9,8},{10,11... | collective-permute-start | bytes 3932168 | tf_op jit(solution)/shard_map/ppermute | solution.py:114
  98.6 8.1 %copy-start.3 = (bf16[512,1,2,640]{3,0,2,1:T(8,128)(2,1)S(1)}, bf16[512,1,2,640]{3,0,2,1:T(8,128)(2,1)}, u32[]{:S(2)}) copy-start(bf16[512,1,2,640]{3,0,2,1:T(8,128)(2,1)} %all-gather.2.cloned.1.call-done) | copy-start | bytes 3932164
  103.3 21.7 %collective-permute-start.2 = (bf16[64,1,2,1024]{3,0,1,2:T(8,128)(2,1)}, bf16[64,1,2,1024]{3,0,1,2:T(8,128)(2,1)S(1)}, u32[]{:S(2)}, u32[]{:S(2)}) collective-permute-start(bf16[64,1,2,1024]{3,0,1,2:T(8,128)(2,1)} %get-tuple-element.42), channel_id=1, source_target_pairs={{0,12},{4,0},{8,4},{12,8},{1,13},{5,1},{9,5},{13,9},{2,14},{6,2},{... | collective-permute-start | bytes 786440 | tf_op jit(solution)/shard_map/ppermute | solution.py:108
  104.7 24.6 %collective-permute-start.1 = (bf16[64,1,2,1024]{3,0,1,2:T(8,128)(2,1)S(1)}, bf16[64,1,2,1024]{3,0,1,2:T(8,128)(2,1)S(1)}, u32[]{:S(2)}, u32[]{:S(2)}) collective-permute-start(bf16[64,1,2,1024]{3,0,1,2:T(8,128)(2,1)S(1)} %get-tuple-element.43), channel_id=1, source_target_pairs={{0,8},{4,12},{8,0},{12,4},{1,9},{5,13},{9,1},{13,5},{2,10},{6,14},... | collective-permute-start | bytes 786440 | tf_op jit(solution)/shard_map/ppermute | solution.py:108
  105.5 23.8 %collective-permute-start = (bf16[64,1,2,1024]{3,0,1,2:T(8,128)(2,1)S(1)}, bf16[64,1,2,1024]{3,0,1,2:T(8,128)(2,1)S(1)}, u32[]{:S(2)}, u32[]{:S(2)}) collective-permute-start(bf16[64,1,2,1024]{3,0,1,2:T(8,128)(2,1)S(1)} %get-tuple-element.41), channel_id=1, source_target_pairs={{0,4},{4,8},{8,12},{12,0},{1,5},{5,9},{9,13},{13,1},{2,6},{6,10},{... | collective-permute-start | bytes 786440 | tf_op jit(solution)/shard_map/ppermute | solution.py:108
  118.0 3.4 %copy-start = (bf16[2,1,8,128,1024]{4,3,2,0,1:T(8,128)(2,1)S(1)}, bf16[2,1,8,128,1024]{4,3,2,0,1:T(8,128)(2,1)}, u32[]{:S(2)}) copy-start(bf16[2,1,8,128,1024]{4,3,2,0,1:T(8,128)(2,1)} %copy.36) | copy-start | bytes 12582916
Sparse Core Ops, SparseCore 0:
  29.9 34.0 reduce-scatter.1
  67.7 30.8 all-gather.1

commit v8 on v7

--- a/solution.py
+++ b/solution.py
@@ -48,7 +48,14 @@
     return jnp.stack(windows).reshape(shot_count * rows_each, *rows.shape[2:4], span)
 
 
-def rebuild_gram(strips, tiles, tile):
+def offset_mask(tiles, tile):
+    receivers = tiles * tile
+    row_tile = lax.broadcasted_iota(jnp.int32, (receivers, receivers), 0) // tile
+    col_tile = lax.broadcasted_iota(jnp.int32, (receivers, receivers), 1) // tile
+    return (col_tile - row_tile) % tiles <= tiles // 2
+
+
+def rebuild_gram(strips, tiles, tile, direct):
     freq_local = strips.shape[1]
     receivers = tiles * tile
     span = strips.shape[-1]
@@ -58,9 +65,6 @@
     upper = jnp.transpose(upper, (3, 2, 0, 1, 4)).reshape(2, freq_local, receivers, receivers)
     mirror = jnp.swapaxes(upper, 2, 3)
     mirror = jnp.stack([mirror[0], -mirror[1]])
-    row_tile = lax.broadcasted_iota(jnp.int32, (receivers, receivers), 0) // tile
-    col_tile = lax.broadcasted_iota(jnp.int32, (receivers, receivers), 1) // tile
-    direct = (col_tile - row_tile) % tiles <= tiles // 2
     return jnp.where(direct, upper, mirror)
 
 
@@ -96,7 +100,8 @@
     own_order = lax.dynamic_slice_in_dim(order_table, core_index, 1, 1).reshape(-1)
     corr_part = jnp.take(corr_all, own_order, axis=0).astype(jnp.bfloat16)
 
-    gram_strip, power, corr_part = lax.optimization_barrier((gram_strip, power, corr_part))
+    direct = offset_mask(tiles, tile)
+    gram_strip, power, corr_part, direct = lax.optimization_barrier((gram_strip, power, corr_part, direct))
     power_wide = power[None, :, None, None]
 
     shot_index = lax.axis_index("shot")
@@ -109,6 +114,7 @@
 
     across = lax.all_gather(gram_strip, "shot", axis=0, tiled=True)
     across = across.reshape(shot_count, rows_each, freq_local, 2, span)
+    across, corr = lax.optimization_barrier((across, corr))
 
     if core_count == 2:
         other = lax.ppermute(across, "sub", perm=[(0, 1), (1, 0)])
@@ -118,7 +124,7 @@
     else:
         strips = lax.all_gather(across, "sub", axis=1, tiled=False)
     strips = strips.reshape(receivers, freq_local, 2, span)
-    whole = rebuild_gram(strips, tiles, tile)
+    whole = rebuild_gram(strips, tiles, tile, direct)
 
     target = jnp.transpose(corr, (2, 1, 0, 3)) / power_wide
 

time: 149 us -> 157 us (1.054)
  waiting for transfers between devices: 35.4 us -> 43.1 us
  matrix products: 18.9 us -> 20.7 us
    ppermute x3, waiting for transfers between devices: 4.31 us -> 36.9 us  [per_device(): corr = corr + lax.ppermute(outgoing, 'shot', perm=pairs).astype(jnp.float32)]
    all_gather x1, waiting for transfers between devices: 31.1 us -> 2.93 us  [per_device(): across = lax.all_gather(gram_strip, 'shot', axis=0, tiled=True)]
    ppermute x1, waiting for transfers between devices: 0.01 us -> 3.18 us  [per_device(): other = lax.ppermute(across, 'sub', perm=[(0, 1), (1, 0)])]
    reduce_sum x1, other arithmetic: 4.11 us -> 2.22 us  [per_device(): jnp.sum(jnp.square(downgoing.astype(jnp.float32)), axis=(0, 2, 3))]
    dot_general x1, matrix products: 4.58 us -> 6.46 us  [per_device(): jnp.einsum('qtpu,qto->uqpo', stacked_left(upgoing), right, preferred_elem...]
    another operation x1, other arithmetic: 0.29 us -> 1.91 us  [stacked_left(): return jnp.stack([real_left, imag_left], axis=2)]
    unnamed x16 -> x18, local copies, waits for them, and re-layouts: 5.37 us -> 6.76 us
  transfers between devices with their start and end apart: 6 -> 6, of which waited for: 2 -> 4; matrix products, arithmetic and copies ran while one was open for 30% -> 18% of each run, Pallas kernels for 0% -> 0%
where the time goes in v8:
time: 157 us
  waiting for transfers between devices  43.1 us (27%)
  local copies, waits for them, and re-layouts  34.3 us (22%)
  other arithmetic  27.2 us (17%)
  matrix products  20.7 us (13%)
  blocking collectives  14.7 us (9%)
  between operations  14.6 us (9%)
  starting transfers between devices  2.21 us (1%)
    ppermute x3, waiting for transfers between devices, per_device(): corr = corr + lax.ppermute(outgoing, 'shot', perm=pairs).astype(jnp.float32)  36.9 us
    psum x1, blocking collectives, per_device(): power = lax.psum(local_power, 'shot') / receivers  14.7 us
    unnamed x18, local copies, waits for them, and re-layouts  6.76 us
    dot_general x1, matrix products, per_device(): jnp.einsum('qtpu,qto->uqpo', stacked_left(upgoing), right, preferred_elem...  6.46 us
    reshape x1, local copies, waits for them, and re-layouts, rebuild_gram(): jnp.transpose(upper, (3, 2, 0, 1, 4))  6.24 us
    transpose x1, local copies, waits for them, and re-layouts, per_device(): jnp.einsum('qtpu,qto->uqpo', stacked_left(upgoing), right, preferred_elem...  5.05 us
    dot_general x1, matrix products, per_device(): jnp.einsum('qpkit,qto->kiqpo', left, right, preferred_element_type=jnp.fl...  3.69 us
    le x1, other arithmetic, offset_mask(): return (col_tile - row_tile) % tiles <= tiles // 2  3.56 us
  transfers between devices with their start and end apart: 6, of which 4 were waited for; matrix products, arithmetic and copies ran while one was open for 18% of the time, Pallas kernels for 0%

profile of v8, /device:TPU:0, one launch (start us, length us, event | category | flops | bytes accessed | tf_op | source)
XLA Modules:
  0.0 156.8 jit_solution(3015441080072410486)
XLA Ops:
  6.5 2.2 %fusion.85 = (bf16[1,1,768,1024]{3,2,1,0:T(8,128)(2,1)S(1)}, bf16[1,1,768,1024]{3,2,1,0:T(8,128)(2,1)S(1)}) fusion(bf16[2,1,768,1024]{3,2,1,0:T(8,128)(2,1)} %param.3), kind=kLoop, calls=%fused_computation.170 | loop fusion | bytes 6291456 | tf_op jit(solution)/shard_map/slice | solution.py:26
  8.7 1.6 %copy.40 = bf16[1,1,768,1024]{2,3,1,0:T(8,128)(2,1)} copy(bf16[1,1,768,1024]{3,2,1,0:T(8,128)(2,1)S(1)} %get-tuple-element.23) | data formatting | bytes 3145728
  13.0 1.7 %fusion.28 = (bf16[1,1,1536,1024]{2,3,1,0:T(8,128)(2,1)S(1)}, bf16[1,1,1536,1024]{2,3,1,0:T(8,128)(2,1)S(1)}) fusion(bf16[1,768,1024]{1,2,0:T(8,128)(2,1)S(1)} %bitcast.247, bf16[1,768,1024]{1,2,0:T(8,128)(2,1)S(1)} %bitcast.243, bf16[1,768,1024]{1,2,0:T(8,128)(2,1)} %bitcast_negate_fusion), kind=kLoop, calls=%fused_computation.69 | loop fusion | flops 12582912 | bytes 11010048 | tf_op jit(solution)/shard_map/stack | solution.py:16
  15.3 3.7 %convert_bitcast_fusion = bf16[4,128,1,2,1024]{1,4,0,3,2:T(8,128)(2,1)S(1)} fusion(bf16[1,2,4,2,128,1536]{5,4,3,2,1,0:T(8,128)(2,1)S(1)} %bitcast.246, s32[]{:T(128)S(6)} %select_n.123, bf16[1,768,1024]{1,2,0:T(8,128)(2,1)S(1)} %bitcast.248, bf16[1,768,1024]{1,2,0:T(8,128)(2,1)S(1)} %bitcast.244), kind=kOutput, calls=%fused_computation.41 | convolution fusion | flops 3228565504 | bytes 8388612 | tf_op jit(solution)/shard_map/qpkit,qto->kiqpo/dot_general | solution.py:89
  20.3 2.8 %pad_slice_fusion.11 = (bf16[1,128,1,2,2048]{1,4,0,3,2:T(8,128)(2,1)}, bf16[1,128,1,2,2048]{1,4,0,3,2:T(8,128)(2,1)}, bf16[1,128,1,2,2048]{1,4,0,3,2:T(8,128)(2,...) fusion(bf16[4,128,1,2,1024]{1,4,0,3,2:T(8,128)(2,1)S(1)} %conve, ...), kind=kLoop, calls=%fused_computation.18 | loop fusion | bytes 8388608 | tf_op jit(solution)/shard_map/slice | solution.py:47
  27.3 2.4 %copy.31 = bf16[4,128,1,2,640]{4,1,0,3,2:T(8,128)(2,1)} copy(bf16[4,128,1,2,640]{1,4,0,3,2:T(8,128)(2,1)} %pad_maximum_fusion.3) | data formatting | bytes 2621440 | tf_op jit(solution)/shard_map/stack | solution.py:48
  29.9 1.6 %slice_bitcast_fusion.3 = (bf16[1,768,512]{2,1,0:T(8,128)(2,1)S(1)}, bf16[1,768,512]{2,1,0:T(8,128)(2,1)S(1)}) fusion(bf16[2,1,768,512]{3,2,1,0:T(8,128)(2,1)} %param.4), kind=kLoop, calls=%fused_computation.71 | loop fusion | bytes 3145728 | tf_op jit(solution)/shard_map/squeeze | solution.py:20
  31.8 1.9 %maximum_bitcast_fusion.5 = (bf16[1,1536,1,512]{3,1,2,0:T(8,128)(2,1)}, bf16[1,1536,1,512]{3,1,2,0:T(8,128)(2,1)}) fusion(bf16[1,768,512]{2,1,0:T(8,128)(2,1)S(1)} %get-tuple-element.42, bf16[1,768,512]{2,1,0:T(8,128)(2,1)S(1)} %get-tuple-element.41, bf16[1,768,512]{2,1,0:T(8,128)(2,1)S(1)} %fusion.79), kind=kLoop, calls=%fused_computation.42 | loop fusion | flops 6291456 | bytes 5505024 | tf_op jit(solution)/shard_map/stack | solution.py:22
  34.8 2.2 %multiply_reduce_fusion = f32[]{:T(128)} fusion(bf16[2,1,768,1024]{3,2,1,0:T(8,128)(2,1)S(1)} %copy-done.1), kind=kLoop, calls=%fused_computation.6 | loop fusion | flops 4718591 | bytes 3145732 | tf_op jit(solution)/shard_map/reduce_sum | solution.py:93
  37.0 14.7 %psum.7 = f32[1]{0:T(128)} all-reduce(f32[1]{0:T(128)} %bitcast.13), channel_id=1, replica_groups=mesh['grp'=2,'shot'=4,'freq'=2,'sub'=2] {'shot'}, use_global_device_ids=true, to_apply=%region_2.3 | all-reduce | flops 1 | bytes 8 | tf_op jit(solution)/shard_map/psum | solution.py:94
  51.7 6.5 %fusion.10 = bf16[512,2,1024]{0,2,1:T(8,128)(2,1)} fusion(bf16[1,1536,1,512]{3,1,2,0:T(8,128)(2,1)} %get-tuple-element.49, bf16[1,1536,1,512]{3,1,2,0:T(8,128)(2,1)} %get-tuple-element.48, bf16[1,768,1024]{1,2,0:T(8,128)(2,1)S(1)} %bitcast.249, bf16[1,768,1024]{1,2,0:T(8,128)(2,1)S(1)} %bitcast.245), kind=kOutput, calls=%fused_computation.35 | convolution fusion | flops 3233808384 | bytes 8388608 | tf_op jit(solution)/shard_map/qtpu,qto->uqpo/dot_general | solution.py:96
  58.2 5.1 %copy.32 = bf16[512,2,1024]{2,1,0:T(2,128)(2,1)S(1)} copy(bf16[512,2,1024]{0,2,1:T(8,128)(2,1)} %fusion.10) | data formatting | bytes 4194304 | tf_op jit(solution)/shard_map/qtpu,qto->uqpo/transpose | solution.py:96
  65.4 2.8 %gather_fusion = bf16[256,2,1024]{2,1,0:T(2,128)(2,1)S(1)} fusion(bf16[512,2,1024]{2,1,0:T(2,128)(2,1)S(1)} %copy.32, s32[1024]{0:T(1024)S(1)} %pad_clamp_fusion), kind=kCustom, calls=%fused_computation | custom fusion | bytes 2098176 | tf_op jit(solution)/shard_map/jit(_take)/gather | solution.py:101
  69.7 3.6 %fusion.1 = pred[1024,1024]{1,0:T(8,128)(4,1)S(1)} fusion(s32[1024]{0:T(1024)S(1)} %get-tuple-element.56, s32[1024]{0:T(1024)S(1)} %get-tuple-element.57, pred[1024]{0:T(1024)(128)(4,1)S(1)} %fusion.73), kind=kLoop, calls=%fused_computation.21 | loop fusion | flops 15728640 | bytes 1057792 | tf_op jit(solution)/shard_map/le | solution.py:55
  73.9 1.9 %collective-permute-start = (bf16[64,1,2,1024]{3,0,1,2:T(8,128)(2,1)S(1)}, bf16[64,1,2,1024]{3,0,1,2:T(8,128)(2,1)}, u32[]{:S(2)}, u32[]{:S(2)}) collective-permute-start(bf16[64,1,2,1024]{3,0,1,2:T(8,128)(2,1)S(1)} %get-tuple-element.45), channel_id=1, source_target_pairs={{0,4},{4,8},{8,12},{12,0},{1,5},{5,9},{9,13},{13,1},{2,6},{6,10},{... | collective-permute-start | bytes 786440 | tf_op jit(solution)/shard_map/ppermute | solution.py:113
  75.8 6.0 %collective-permute-done.2 = bf16[64,1,2,1024]{3,0,1,2:T(8,128)(2,1)S(1)} collective-permute-done((bf16[64,1,2,1024]{3,0,1,2:T(8,128)(2,1)S(1)}, bf16[64,1,2,1024]{3,0,1,2:T(8,128)(2,1)S(1)}, u32[]{:S(2)}, u32[]{:S(2)}) %collective-permute-start.2) | collective-permute-done | bytes 262176 | tf_op jit(solution)/shard_map/ppermute | solution.py:113
  81.8 30.9 %collective-permute-done.1 = bf16[64,1,2,1024]{3,0,1,2:T(8,128)(2,1)S(1)} collective-permute-done((bf16[64,1,2,1024]{3,0,1,2:T(8,128)(2,1)S(1)}, bf16[64,1,2,1024]{3,0,1,2:T(8,128)(2,1)S(1)}, u32[]{:S(2)}, u32[]{:S(2)}) %collective-permute-start.1) | collective-permute-done | bytes 262176 | tf_op jit(solution)/shard_map/ppermute | solution.py:113
  113.8 2.9 %all-gather.2.cloned.1.call-done = bf16[512,1,2,640]{3,0,2,1:T(8,128)(2,1)} async-done(((bf16[128,1,2,640]{3,0,2,1:T(8,128)(2,1)}), bf16[512,1,2,640]{3,0,2,1:T(8,128)(2,1)}) %all-gather.2.cloned.1.call-update) | async-done | bytes 1310736 | tf_op jit(solution)/shard_map/all_gather | solution.py:115
  116.8 3.2 %collective-permute-done.3 = bf16[4,128,1,2,640]{4,1,0,3,2:T(8,128)(2,1)S(1)} collective-permute-done((bf16[4,128,1,2,640]{4,1,0,3,2:T(8,128)(2,1)}, bf16[4,128,1,2,640]{4,1,0,3,2:T(8,128)(2,1)S(1)}, u32[]{:S(2)}, u32[]{:S(2)}) %collective-permute-start.3) | collective-permute-done | bytes 1310752 | tf_op jit(solution)/shard_map/ppermute | solution.py:120
  120.0 1.6 select_bitcast_fusion.1
  122.7 2.4 %copy.36 = bf16[2,1,8,128,1024]{4,3,2,0,1:T(8,128)(2,1)} copy(bf16[2,1,8,128,1024]{4,3,0,1,2:T(8,128)(2,1)S(1)} %bitcast.250) | data formatting | bytes 8388608 | tf_op jit(solution)/shard_map/transpose | solution.py:65
  125.0 6.2 %copy.37 = bf16[2,1,1024,1024]{2,3,0,1:T(8,128)(2,1)} copy(bf16[2,1,1024,1024]{3,2,0,1:T(8,128)(2,1)} %bitcast.241) | data formatting | bytes 8388608 | tf_op jit(solution)/shard_map/reshape | solution.py:65
  131.3 2.6 %fusion.84 = (bf16[1,1,1024,1024]{3,2,0,1:T(8,128)(2,1)S(1)}, bf16[1,1,1024,1024]{3,2,0,1:T(8,128)(2,1)S(1)}) fusion(bf16[2,1,1024,1024]{3,2,0,1:T(8,128)(2,1)} %bitcast.242), kind=kLoop, calls=%fused_computation.169 | loop fusion | flops 1048576 | bytes 8388608 | tf_op jit(solution)/shard_map/slice | solution.py:67
  134.7 2.5 %divide_convert_fusion = bf16[2,1,1024,1024]{3,2,0,1:T(8,128)(2,1)S(1)} fusion(bf16[1,1,1024,1024]{3,2,0,1:T(8,128)(2,1)S(1)} %get-tuple-element.22, bf16[1,1,1024,1024]{3,2,0,1:T(8,128)(2,1)S(1)} %get-tuple-element.21, f32[]{:T(128)} %bitcast.31, pred[1024,1024]{1,0:T(8,128)(4,1)S(1)} %fusion.1, bf16[2,1,8,128,1024]{4,3,2,0,1:T(8,128)(2,1)S(1)} %copy-done), kind=kLoop, calls=%fused_computation.1 | loop fusion | flops 10485760 | bytes 13631492 | tf_op jit(solution)/shard_map/convert_element_type | solution.py:131
  (86 shorter events, 29.3 us)
Async XLA Ops:
  6.5 66.7 %reduce-scatter.2.cloned.1.call-start = ((), (), s32[]{:S(2)}) async-start(), calls=%async_computation.1 | async-start | bytes 1638400 | tf_op jit(solution)/shard_map/reduce_scatter | solution.py:91
  11.0 2.0 %copy-start.3 = (bf16[1,1,768,1024]{2,3,1,0:T(8,128)(2,1)S(1)}, bf16[1,1,768,1024]{2,3,1,0:T(8,128)(2,1)}, u32[]{:S(2)}) copy-start(bf16[1,1,768,1024]{2,3,1,0:T(8,128)(2,1)} %copy.40) | copy-start | bytes 4718596
  19.0 1.3 copy-start.2
  29.8 87.0 %all-gather.2.cloned.1.call-start = ((), (), s32[]{:S(2)}) async-start(), calls=%async_computation.2 | async-start | bytes 1638400 | tf_op jit(solution)/shard_map/all_gather | solution.py:115
  29.8 1.9 %copy-start.4 = (bf16[2,1,768,512]{3,2,1,0:T(8,128)(2,1)S(1)}, bf16[2,1,768,512]{3,2,1,0:T(8,128)(2,1)}, u32[]{:S(2)}) copy-start(bf16[2,1,768,512]{3,2,1,0:T(8,128)(2,1)} %param.4) | copy-start | bytes 4718596
  31.8 3.0 %copy-start.1 = (bf16[2,1,768,1024]{3,2,1,0:T(8,128)(2,1)S(1)}, bf16[2,1,768,1024]{3,2,1,0:T(8,128)(2,1)}, u32[]{:S(2)}) copy-start(bf16[2,1,768,1024]{3,2,1,0:T(8,128)(2,1)} %param.3) | copy-start | bytes 9437188
  58.2 5.1 %copy-start.5 = (s32[512]{0:T(512)S(1)}, s32[512]{0:T(512)}, u32[]{:S(2)}) copy-start(s32[512]{0:T(512)} %param.5) | copy-start | bytes 6148
  73.7 8.1 %collective-permute-start.2 = (bf16[64,1,2,1024]{3,0,1,2:T(8,128)(2,1)S(1)}, bf16[64,1,2,1024]{3,0,1,2:T(8,128)(2,1)S(1)}, u32[]{:S(2)}, u32[]{:S(2)}) collective-permute-start(bf16[64,1,2,1024]{3,0,1,2:T(8,128)(2,1)S(1)} %get-tuple-element.46), channel_id=1, source_target_pairs={{0,12},{4,0},{8,4},{12,8},{1,13},{5,1},{9,5},{13,9},{2,14},{6,2},{... | collective-permute-start | bytes 786440 | tf_op jit(solution)/shard_map/ppermute | solution.py:113
  73.8 38.9 %collective-permute-start.1 = (bf16[64,1,2,1024]{3,0,1,2:T(8,128)(2,1)S(1)}, bf16[64,1,2,1024]{3,0,1,2:T(8,128)(2,1)S(1)}, u32[]{:S(2)}, u32[]{:S(2)}) collective-permute-start(bf16[64,1,2,1024]{3,0,1,2:T(8,128)(2,1)S(1)} %get-tuple-element.47), channel_id=1, source_target_pairs={{0,8},{4,12},{8,0},{12,4},{1,9},{5,13},{9,1},{13,5},{2,10},{6,14},... | collective-permute-start | bytes 786440 | tf_op jit(solution)/shard_map/ppermute | solution.py:113
  73.9 38.8 %collective-permute-start = (bf16[64,1,2,1024]{3,0,1,2:T(8,128)(2,1)S(1)}, bf16[64,1,2,1024]{3,0,1,2:T(8,128)(2,1)}, u32[]{:S(2)}, u32[]{:S(2)}) collective-permute-start(bf16[64,1,2,1024]{3,0,1,2:T(8,128)(2,1)S(1)} %get-tuple-element.45), channel_id=1, source_target_pairs={{0,4},{4,8},{8,12},{12,0},{1,5},{5,9},{9,13},{13,1},{2,6},{6,10},{... | collective-permute-start | bytes 786440 | tf_op jit(solution)/shard_map/ppermute | solution.py:113
  116.7 3.2 %collective-permute-start.3 = (bf16[4,128,1,2,640]{4,1,0,3,2:T(8,128)(2,1)}, bf16[4,128,1,2,640]{4,1,0,3,2:T(8,128)(2,1)S(1)}, u32[]{:S(2)}, u32[]{:S(2)}) collective-permute-start(bf16[4,128,1,2,640]{4,1,0,3,2:T(8,128)(2,1)} %bitcast.254), channel_id=1, source_target_pairs={{0,1},{1,0},{2,3},{3,2},{4,5},{5,4},{6,7},{7,6},{8,9},{9,8},{10,11... | collective-permute-start | bytes 3932168 | tf_op jit(solution)/shard_map/ppermute | solution.py:120
  131.3 3.4 %copy-start = (bf16[2,1,8,128,1024]{4,3,2,0,1:T(8,128)(2,1)S(1)}, bf16[2,1,8,128,1024]{4,3,2,0,1:T(8,128)(2,1)}, u32[]{:S(2)}) copy-start(bf16[2,1,8,128,1024]{4,3,2,0,1:T(8,128)(2,1)} %copy.36) | copy-start | bytes 12582916
Sparse Core Ops, SparseCore 0:
  29.9 34.1 reduce-scatter.1
  73.4 43.2 all-gather.1

commit v9 on v7

--- a/solution.py
+++ b/solution.py
@@ -23,7 +23,8 @@
 
 
 def stacked_right(trace):
-    return jnp.concatenate([trace[0], trace[1]], axis=1)
+    parts, freq_local, shots, width = trace.shape
+    return jnp.swapaxes(trace, 0, 1).reshape(freq_local, parts * shots, width)
 
 
 def sweep_whole(scaled, solution, target):
@@ -38,14 +39,17 @@
     return solution
 
 
-def strip_partials(rows, shot_count, core_count, core_index, rows_each, tile, span):
-    rows = rows.astype(jnp.bfloat16)
-    doubled = jnp.concatenate([rows, rows], axis=-1)
+def strip_partials(rows, shot_count, core_count, rows_each, tile, span):
+    receivers = rows.shape[-1]
     windows = []
     for k in range(shot_count):
-        start = ((k * core_count + core_index) * rows_each // tile) * tile
-        windows.append(lax.dynamic_slice_in_dim(doubled[k], start, span, axis=-1))
-    return jnp.stack(windows).reshape(shot_count * rows_each, *rows.shape[2:4], span)
+        start = (k * core_count * rows_each // tile) * tile
+        if start + span <= receivers:
+            window = rows[k, ..., start : start + span]
+        else:
+            window = jnp.concatenate([rows[k, ..., start:], rows[k, ..., : start + span - receivers]], axis=-1)
+        windows.append(window)
+    return jnp.stack(windows).astype(jnp.bfloat16).reshape(shot_count * rows_each, *rows.shape[2:4], span)
 
 
 def rebuild_gram(strips, tiles, tile):
@@ -82,8 +86,10 @@
 
     left = stacked_rows(downgoing).reshape(freq_local, 2, shot_count, core_count, rows_each, -1)
     left = lax.dynamic_slice_in_dim(left, core_index, 1, 3)[:, :, :, 0]
-    gram_rows = jnp.einsum("qpkit,qto->kiqpo", left, right, preferred_element_type=jnp.float32)
-    gram_part = strip_partials(gram_rows, shot_count, core_count, core_index, rows_each, tile, span)
+    shift = (core_index * rows_each // tile) * tile
+    rolled = lax.dynamic_slice_in_dim(jnp.concatenate([right, right], axis=-1), shift, receivers, axis=-1)
+    gram_rows = jnp.einsum("qpkit,qto->kiqpo", left, rolled, preferred_element_type=jnp.float32)
+    gram_part = strip_partials(gram_rows, shot_count, core_count, rows_each, tile, span)
     gram_strip = lax.psum_scatter(gram_part, "shot", scatter_dimension=0, tiled=True)
 
     local_power = jnp.sum(jnp.square(downgoing.astype(jnp.float32)), axis=(0, 2, 3))

time: 149 us -> 180 us (1.21); the launches traced: 148 us -> 177 us
  local copies, waits for them, and re-layouts: 33.5 us -> 64.8 us
  waiting for transfers between devices: 35.4 us -> 31.1 us
    unnamed x16, local copies, waits for them, and re-layouts: 5.37 us -> 21 us
    reshape x0 -> x1, local copies, waits for them, and re-layouts: none -> 11 us  [per_device(): stacked_rows(downgoing)]
    dynamic_slice x0 -> x1, local copies, waits for them, and re-layouts: none -> 8.59 us  [per_device(): left = lax.dynamic_slice_in_dim(left, core_index, 1, 3)[:, :, :, 0]]
    ppermute x3, waiting for transfers between devices: 4.31 us -> 0.01 us  [per_device(): corr = corr + lax.ppermute(outgoing, 'shot', perm=pairs).astype(jnp.float32)]
    transpose x0 -> x1, other arithmetic: none -> 3.16 us  [stacked_rows(): return jnp.swapaxes(jnp.stack([real_left, imag_left], axis=1), 2, 3)]
    concatenate x2 -> x0, other arithmetic: 2.95 us -> none  [strip_partials(): doubled = jnp.concatenate([rows, rows], axis=-1)]
    transpose x1, local copies, waits for them, and re-layouts: 5.05 us -> 2.16 us  [per_device(): jnp.einsum('qtpu,qto->uqpo', stacked_left(upgoing), right, preferred_elem...]
    squeeze x1 -> x5, local copies, waits for them, and re-layouts: 1.49 us -> 4.08 us  [the longest x1 4 us: stacked_rows(): real_left = jnp.concatenate([factor[0], factor[1]], axis=1)]
  transfers between devices with their start and end apart: 6 -> 6, of which waited for: 2 -> 1; matrix products, arithmetic and copies ran while one was open for 30% -> 26% of each run, Pallas kernels for 0% -> 0%
where the time goes in v9:
time: 180 us; the launch traced here: 177 us
  local copies, waits for them, and re-layouts  64.8 us (36%)
  waiting for transfers between devices  31.1 us (17%)
  other arithmetic  27.6 us (15%)
  matrix products  19.9 us (11%)
  between operations  14.6 us (8%)
  blocking collectives  14.4 us (8%)
  starting transfers between devices  4.38 us (2%)
    all_gather x1, waiting for transfers between devices, per_device(): across = lax.all_gather(gram_strip, 'shot', axis=0, tiled=True)  31 us
    unnamed x16, local copies, waits for them, and re-layouts  21 us
    psum x1, blocking collectives, per_device(): power = lax.psum(local_power, 'shot') / receivers  14.4 us
    reshape x1, local copies, waits for them, and re-layouts, per_device(): stacked_rows(downgoing)  11 us
    dynamic_slice x1, local copies, waits for them, and re-layouts, per_device(): left = lax.dynamic_slice_in_dim(left, core_index, 1, 3)[:, :, :, 0]  8.59 us
    reshape x1, local copies, waits for them, and re-layouts, rebuild_gram(): jnp.transpose(upper, (3, 2, 0, 1, 4))  6.24 us
    dot_general x1, matrix products, per_device(): jnp.einsum('qpkit,qto->kiqpo', left, rolled, preferred_element_type=jnp.f...  5.69 us
    ppermute x3, starting transfers between devices, per_device(): corr = corr + lax.ppermute(outgoing, 'shot', perm=pairs).astype(jnp.float32)  4.34 us
  transfers between devices with their start and end apart: 6, of which 1 were waited for; matrix products, arithmetic and copies ran while one was open for 26% of the time, Pallas kernels for 0%

profile of v9, /device:TPU:0, one launch (start us, length us, event | category | flops | bytes accessed | tf_op | source)
XLA Modules:
  0.0 176.8 jit_solution(10580970471554688799)
XLA Ops:
  6.5 4.0 %slice_bitcast_fusion.3 = (bf16[1,768,1024]{2,1,0:T(8,128)(2,1)}, bf16[1,768,1024]{2,1,0:T(8,128)(2,1)}) fusion(bf16[2,1,768,1024]{3,2,1,0:T(8,128)(2,1)} %param.3), kind=kLoop, calls=%fused_computation.40 | loop fusion | bytes 6291456 | tf_op jit(solution)/shard_map/squeeze | solution.py:14
  11.8 3.3 %maximum_bitcast_fusion.1 = (bf16[1,1,1536,1024]{3,2,1,0:T(8,128)(2,1)S(1)}, bf16[1,1,1536,1024]{3,2,1,0:T(8,128)(2,1)S(1)}) fusion(bf16[1,768,1024]{2,1,0:T(8,128)(2,1)} %get-tuple-element.20, bf16[1,768,1024]{2,1,0:T(8,128)(2,1)} %get-tuple-element.19, bf16[1,768,1024]{2,1,0:T(8,128)(2,1)} %fusion.77), kind=kLoop, calls=%fused_computation.22 | loop fusion | flops 12582912 | bytes 11010048 | tf_op jit(solution)/shard_map/stack | solution.py:16
  15.1 3.2 %maximum_bitcast_fusion = bf16[1,2,1024,1536]{2,3,1,0:T(8,128)(2,1)} fusion(bf16[1,1,1536,1024]{3,2,1,0:T(8,128)(2,1)S(1)} %get-tuple-element.36, bf16[1,1,1536,1024]{3,2,1,0:T(8,128)(2,1)S(1)} %get-tuple-element.35), kind=kLoop, calls=%fused_computation.4 | loop fusion | flops 3145728 | bytes 12582912 | tf_op jit(solution)/shard_map/transpose | solution.py:16
  18.3 11.0 %reshape.389 = bf16[1,2,4,2,128,1536]{4,3,2,5,1,0:T(2,128)(2,1)} reshape(bf16[1,2,1024,1536]{2,3,1,0:T(8,128)(2,1)} %maximum_bitcast_fusion) | data formatting | bytes 12582912 | tf_op jit(solution)/shard_map/reshape | solution.py:87
  29.2 8.6 %constant_dynamic-slice_fusion.1 = bf16[1,2,4,1,128,1536]{4,3,2,5,1,0:T(2,128)(2,1)} fusion(bf16[1,2,4,2,128,1536]{4,3,2,5,1,0:T(2,128)(2,1)} %reshape.389, s32[]{:T(128)S(6)} %select_n.107), kind=kLoop, calls=%fused_computation.156 | loop fusion | bytes 6291460 | tf_op jit(solution)/shard_map/dynamic_slice | solution.py:88
  37.8 15.3 %copy.49 = bf16[1,2,4,1,128,1536]{5,4,2,1,3,0:T(8,128)(2,1)} copy(bf16[1,2,4,1,128,1536]{4,3,2,5,1,0:T(2,128)(2,1)} %constant_dynamic-slice_fusion.1) | data formatting | bytes 6291456
  53.1 5.7 %convert_bitcast_fusion = bf16[4,128,1,2,1024]{4,1,0,3,2:T(8,128)(2,1)S(1)} fusion(bf16[1,2,4,1,128,1536]{5,4,2,1,3,0:T(8,128)(2,1)} %copy.49, s32[]{:T(128)S(6)} %select_n.106, bf16[1,1536,1024]{2,1,0:T(8,128)(2,1)S(1)} %bitcast.245), kind=kOutput, calls=%fused_computation.36 | convolution fusion | flops 3228565504 | bytes 8388612 | tf_op jit(solution)/shard_map/qpkit,qto->kiqpo/dot_general | solution.py:91
  60.6 2.2 %multiply_reduce_fusion = f32[]{:T(128)} fusion(bf16[2,1,768,1024]{3,2,1,0:T(8,128)(2,1)S(1)} %copy-done.1), kind=kLoop, calls=%fused_computation.8 | loop fusion | flops 4718591 | bytes 3145732 | tf_op jit(solution)/shard_map/reduce_sum | solution.py:95
  62.8 14.4 %psum.7 = f32[1]{0:T(128)} all-reduce(f32[1]{0:T(128)} %bitcast.20), channel_id=1, replica_groups=mesh['grp'=2,'shot'=4,'freq'=2,'sub'=2] {'shot'}, use_global_device_ids=true, to_apply=%region_2.3 | all-reduce | flops 1 | bytes 8 | tf_op jit(solution)/shard_map/psum | solution.py:96
  78.6 2.6 %fusion.84 = (bf16[1,1,768,512]{3,2,1,0:T(8,128)(2,1)}, bf16[1,1,768,512]{3,2,1,0:T(8,128)(2,1)}) fusion(bf16[2,1,768,512]{3,2,1,0:T(8,128)(2,1)} %param.4), kind=kLoop, calls=%fused_computation.168 | loop fusion | bytes 3145728 | tf_op jit(solution)/shard_map/slice | solution.py:20
  81.2 2.3 %copy.55 = bf16[1,1,768,512]{2,3,1,0:T(8,128)(2,1)} copy(bf16[1,1,768,512]{3,2,1,0:T(8,128)(2,1)} %get-tuple-element.34) | data formatting | bytes 1572864
  83.5 2.3 %copy.56 = bf16[1,1,768,512]{2,3,1,0:T(8,128)(2,1)} copy(bf16[1,1,768,512]{3,2,1,0:T(8,128)(2,1)} %get-tuple-element.33) | data formatting | bytes 1572864
  87.0 1.9 %maximum_bitcast_fusion.7 = (bf16[1,1536,1,512]{1,3,2,0:T(8,128)(2,1)S(1)}, bf16[1,1536,1,512]{1,3,2,0:T(8,128)(2,1)S(1)}) fusion(bf16[1,768,512]{1,2,0:T(8,128)(2,1)} %bitcast.253, bf16[1,768,512]{1,2,0:T(8,128)(2,1)} %bitcast.248, bf16[1,768,512]{1,2,0:T(8,128)(2,1)S(1)} %bitcast_negate_fusion), kind=kLoop, calls=%fused_computation.37 | loop fusion | flops 6291456 | bytes 5505024 | tf_op jit(solution)/shard_map/stack | solution.py:22
  88.9 3.6 %fusion.10 = bf16[512,2,1024]{2,0,1:T(8,128)(2,1)S(1)} fusion(bf16[1536,1024,1]{1,0,2:T(8,128)(2,1)S(1)} %bitcast.246, bf16[1,1536,1,512]{1,3,2,0:T(8,128)(2,1)S(1)} %get-tuple-element.41, bf16[1,1536,1,512]{1,3,2,0:T(8,128)(2,1)S(1)} %get-tuple-element.40), kind=kOutput, calls=%fused_computation.30 | convolution fusion | flops 3222798336 | bytes 8388608 | tf_op jit(solution)/shard_map/qtpu,qto->uqpo/dot_general | solution.py:98
  92.5 2.2 %copy.42 = bf16[512,2,1024]{2,1,0:T(2,128)(2,1)S(1)} copy(bf16[512,2,1024]{2,0,1:T(8,128)(2,1)S(1)} %fusion.10) | data formatting | bytes 4194304 | tf_op jit(solution)/shard_map/qtpu,qto->uqpo/transpose | solution.py:98
  94.8 2.8 %gather_fusion = bf16[256,2,1024]{2,1,0:T(2,128)(2,1)S(1)} fusion(bf16[512,2,1024]{2,1,0:T(2,128)(2,1)S(1)} %copy.42, s32[1024]{0:T(1024)S(1)} %pad_clamp_fusion), kind=kCustom, calls=%fused_computation | custom fusion | bytes 2098176 | tf_op jit(solution)/shard_map/jit(_take)/gather | solution.py:103
  99.7 31.0 %all-gather.2.cloned.1.call-done = bf16[512,1,2,640]{3,0,2,1:T(8,128)(2,1)} async-done(((bf16[128,1,2,640]{3,0,2,1:T(8,128)(2,1)}), bf16[512,1,2,640]{3,0,2,1:T(8,128)(2,1)}) %all-gather.2.cloned.1.call-update) | async-done | bytes 1310736 | tf_op jit(solution)/shard_map/all_gather | solution.py:116
  130.8 3.6 %fusion.1 = pred[1024,1024]{1,0:T(8,128)(4,1)S(1)} fusion(s32[1024]{0:T(1024)S(1)} %get-tuple-element.46, s32[1024]{0:T(1024)S(1)} %get-tuple-element.47, pred[1024]{0:T(1024)(128)(4,1)S(1)} %fusion.71), kind=kLoop, calls=%fused_computation.17 | loop fusion | flops 15728640 | bytes 1057792 | tf_op jit(solution)/shard_map/le | solution.py:67
  137.4 2.4 %collective-permute-start.2 = (bf16[64,1,2,1024]{3,0,1,2:T(8,128)(2,1)S(1)}, bf16[64,1,2,1024]{3,0,1,2:T(8,128)(2,1)S(1)}, u32[]{:S(2)}, u32[]{:S(2)}) collective-permute-start(bf16[64,1,2,1024]{3,0,1,2:T(8,128)(2,1)S(1)} %get-tuple-element.38), channel_id=1, source_target_pairs={{0,12},{4,0},{8,4},{12,8},{1,13},{5,1},{9,5},{13,9},{2,14},{6,2},{... | collective-permute-start | bytes 786440 | tf_op jit(solution)/shard_map/ppermute | solution.py:114
  139.8 1.6 select_bitcast_fusion.1
  142.5 2.4 %copy.46 = bf16[2,1,8,128,1024]{4,3,2,0,1:T(8,128)(2,1)} copy(bf16[2,1,8,128,1024]{4,3,0,1,2:T(8,128)(2,1)S(1)} %bitcast.249) | data formatting | bytes 8388608 | tf_op jit(solution)/shard_map/transpose | solution.py:62
  144.9 6.2 %copy.47 = bf16[2,1,1024,1024]{2,3,0,1:T(8,128)(2,1)} copy(bf16[2,1,1024,1024]{3,2,0,1:T(8,128)(2,1)} %bitcast.244) | data formatting | bytes 8388608 | tf_op jit(solution)/shard_map/reshape | solution.py:62
  151.1 2.6 %fusion.83 = (bf16[1,1,1024,1024]{3,2,0,1:T(8,128)(2,1)S(1)}, bf16[1,1,1024,1024]{3,2,0,1:T(8,128)(2,1)S(1)}) fusion(bf16[2,1,1024,1024]{3,2,0,1:T(8,128)(2,1)} %bitcast.247), kind=kLoop, calls=%fused_computation.167 | loop fusion | flops 1048576 | bytes 8388608 | tf_op jit(solution)/shard_map/slice | solution.py:64
  154.6 2.5 %divide_convert_fusion = bf16[2,1,1024,1024]{3,2,0,1:T(8,128)(2,1)S(1)} fusion(bf16[1,1,1024,1024]{3,2,0,1:T(8,128)(2,1)S(1)} %get-tuple-element.18, bf16[1,1,1024,1024]{3,2,0,1:T(8,128)(2,1)S(1)} %get-tuple-element.17, f32[]{:T(128)} %bitcast.39, pred[1024,1024]{1,0:T(8,128)(4,1)S(1)} %fusion.1, bf16[2,1,8,128,1024]{4,3,2,0,1:T(8,128)(2,1)S(1)} %copy-done), kind=kLoop, calls=%fused_computation.1 | loop fusion | flops 10485760 | bytes 13631492 | tf_op jit(solution)/shard_map/convert_element_type | solution.py:131
  (87 shorter events, 24.7 us)
Async XLA Ops:
  6.5 93.2 %reduce-scatter.2.cloned.1.call-start = ((), (), s32[]{:S(2)}) async-start(), calls=%async_computation.1 | async-start | bytes 1638400 | tf_op jit(solution)/shard_map/reduce_scatter | solution.py:93
  6.5 4.0 %copy-start.1 = (bf16[2,1,768,1024]{3,2,1,0:T(8,128)(2,1)S(1)}, bf16[2,1,768,1024]{3,2,1,0:T(8,128)(2,1)}, u32[]{:S(2)}) copy-start(bf16[2,1,768,1024]{3,2,1,0:T(8,128)(2,1)} %param.3) | copy-start | bytes 9437188
  59.3 17.9 %copy-start.3 = (s32[512]{0:T(512)S(1)}, s32[512]{0:T(512)}, u32[]{:S(2)}) copy-start(s32[512]{0:T(512)} %param.5) | copy-start | bytes 6148
  60.5 70.3 %all-gather.2.cloned.1.call-start = ((), (), s32[]{:S(2)}) async-start(), calls=%async_computation.2 | async-start | bytes 1638400 | tf_op jit(solution)/shard_map/all_gather | solution.py:116
  130.8 9.0 %collective-permute-start.3 = (bf16[4,128,1,2,640]{4,1,0,3,2:T(8,128)(2,1)}, bf16[4,128,1,2,640]{4,1,0,3,2:T(8,128)(2,1)}, u32[]{:S(2)}, u32[]{:S(2)}) collective-permute-start(bf16[4,128,1,2,640]{4,1,0,3,2:T(8,128)(2,1)} %bitcast.254), channel_id=1, source_target_pairs={{0,1},{1,0},{2,3},{3,2},{4,5},{5,4},{6,7},{7,6},{8,9},{9,8},{10,11... | collective-permute-start | bytes 3932168 | tf_op jit(solution)/shard_map/ppermute | solution.py:120
  130.8 9.0 %copy-start.2 = (bf16[512,1,2,640]{3,0,2,1:T(8,128)(2,1)S(1)}, bf16[512,1,2,640]{3,0,2,1:T(8,128)(2,1)}, u32[]{:S(2)}) copy-start(bf16[512,1,2,640]{3,0,2,1:T(8,128)(2,1)} %all-gather.2.cloned.1.call-done) | copy-start | bytes 3932164
  135.4 22.6 %collective-permute-start = (bf16[64,1,2,1024]{3,0,1,2:T(8,128)(2,1)}, bf16[64,1,2,1024]{3,0,1,2:T(8,128)(2,1)S(1)}, u32[]{:S(2)}, u32[]{:S(2)}) collective-permute-start(bf16[64,1,2,1024]{3,0,1,2:T(8,128)(2,1)} %get-tuple-element.37), channel_id=1, source_target_pairs={{0,4},{4,8},{8,12},{12,0},{1,5},{5,9},{9,13},{13,1},{2,6},{6,10},{... | collective-permute-start | bytes 786440 | tf_op jit(solution)/shard_map/ppermute | solution.py:114
  136.2 21.8 %collective-permute-start.1 = (bf16[64,1,2,1024]{3,0,1,2:T(8,128)(2,1)S(1)}, bf16[64,1,2,1024]{3,0,1,2:T(8,128)(2,1)S(1)}, u32[]{:S(2)}, u32[]{:S(2)}) collective-permute-start(bf16[64,1,2,1024]{3,0,1,2:T(8,128)(2,1)S(1)} %get-tuple-element.39), channel_id=1, source_target_pairs={{0,8},{4,12},{8,0},{12,4},{1,9},{5,13},{9,1},{13,5},{2,10},{6,14},... | collective-permute-start | bytes 786440 | tf_op jit(solution)/shard_map/ppermute | solution.py:114
  137.4 20.6 %collective-permute-start.2 = (bf16[64,1,2,1024]{3,0,1,2:T(8,128)(2,1)S(1)}, bf16[64,1,2,1024]{3,0,1,2:T(8,128)(2,1)S(1)}, u32[]{:S(2)}, u32[]{:S(2)}) collective-permute-start(bf16[64,1,2,1024]{3,0,1,2:T(8,128)(2,1)S(1)} %get-tuple-element.38), channel_id=1, source_target_pairs={{0,12},{4,0},{8,4},{12,8},{1,13},{5,1},{9,5},{13,9},{2,14},{6,2},{... | collective-permute-start | bytes 786440 | tf_op jit(solution)/shard_map/ppermute | solution.py:114
  151.1 3.4 %copy-start = (bf16[2,1,8,128,1024]{4,3,2,0,1:T(8,128)(2,1)S(1)}, bf16[2,1,8,128,1024]{4,3,2,0,1:T(8,128)(2,1)}, u32[]{:S(2)}) copy-start(bf16[2,1,8,128,1024]{4,3,2,0,1:T(8,128)(2,1)} %copy.46) | copy-start | bytes 12582916
Sparse Core Ops, SparseCore 0:
  60.6 34.0 reduce-scatter.1
  99.9 30.8 all-gather.1

commit v10 on v7

--- a/solution.py
+++ b/solution.py
@@ -64,6 +64,16 @@
     return jnp.where(direct, upper, mirror)
 
 
+def exchange_sum(partials, shot_count, shot_index):
+    blocks = partials.reshape(shot_count, partials.shape[0] // shot_count, *partials.shape[1:])
+    total = lax.dynamic_index_in_dim(blocks, shot_index, 0, keepdims=False).astype(jnp.float32)
+    for shift in range(1, shot_count):
+        outgoing = lax.dynamic_index_in_dim(blocks, (shot_index + shift) % shot_count, 0, keepdims=False)
+        pairs = [(k, (k + shift) % shot_count) for k in range(shot_count)]
+        total = total + lax.ppermute(outgoing, "shot", perm=pairs).astype(jnp.float32)
+    return total
+
+
 def per_device(downgoing, upgoing, source_order):
     shot_count = lax.axis_size("shot")
     core_count = lax.axis_size("sub")
@@ -84,7 +94,8 @@
     left = lax.dynamic_slice_in_dim(left, core_index, 1, 3)[:, :, :, 0]
     gram_rows = jnp.einsum("qpkit,qto->kiqpo", left, right, preferred_element_type=jnp.float32)
     gram_part = strip_partials(gram_rows, shot_count, core_count, core_index, rows_each, tile, span)
-    gram_strip = lax.psum_scatter(gram_part, "shot", scatter_dimension=0, tiled=True)
+    shot_index = lax.axis_index("shot")
+    gram_strip = exchange_sum(gram_part, shot_count, shot_index).astype(jnp.bfloat16)
 
     local_power = jnp.sum(jnp.square(downgoing.astype(jnp.float32)), axis=(0, 2, 3))
     power = lax.psum(local_power, "shot") / receivers
@@ -99,13 +110,7 @@
     gram_strip, power, corr_part = lax.optimization_barrier((gram_strip, power, corr_part))
     power_wide = power[None, :, None, None]
 
-    shot_index = lax.axis_index("shot")
-    corr_blocks = corr_part.reshape(shot_count, source_local, *corr_part.shape[1:])
-    corr = lax.dynamic_index_in_dim(corr_blocks, shot_index, 0, keepdims=False).astype(jnp.float32)
-    for shift in range(1, shot_count):
-        outgoing = lax.dynamic_index_in_dim(corr_blocks, (shot_index + shift) % shot_count, 0, keepdims=False)
-        pairs = [(k, (k + shift) % shot_count) for k in range(shot_count)]
-        corr = corr + lax.ppermute(outgoing, "shot", perm=pairs).astype(jnp.float32)
+    corr = exchange_sum(corr_part, shot_count, shot_index)
 
     across = lax.all_gather(gram_strip, "shot", axis=0, tiled=True)
     across = across.reshape(shot_count, rows_each, freq_local, 2, span)

time: 149 us -> 168 us (1.13)
  waiting for transfers between devices: 35.4 us -> 43.2 us
  starting transfers between devices: 3.49 us -> 8.97 us
  other arithmetic: 27.6 us -> 31.2 us
  local copies, waits for them, and re-layouts: 33.5 us -> 36.1 us
    all_gather x1, waiting for transfers between devices: 31.1 us -> 38 us  [per_device(): across = lax.all_gather(gram_strip, 'shot', axis=0, tiled=True)]
    ppermute x3 -> x6, starting transfers between devices: 3.44 us -> 8.9 us  [exchange_sum(): lax.ppermute(outgoing, 'shot', perm=pairs).astype(jnp.float32)]
    another operation x1 -> x0, local copies, waits for them, and re-layouts: 2.43 us -> none  [strip_partials(): jnp.stack(windows).reshape(shot_count * rows_each, *rows.shape[2:4], span)]
    convert_element_type x0 -> x1, other arithmetic: none -> 2.17 us  [per_device(): exchange_sum(gram_part, shot_count, shot_index).astype(jnp.bfloat16)]
    reduce_sum x1, other arithmetic: 4.11 us -> 2.28 us  [per_device(): jnp.sum(jnp.square(downgoing.astype(jnp.float32)), axis=(0, 2, 3))]
    another operation x1, other arithmetic: 0.29 us -> 2.06 us  [stacked_left(): return jnp.stack([real_left, imag_left], axis=2)]
    reshape x0 -> x1, local copies, waits for them, and re-layouts: none -> 1.7 us  [per_device(): across = across.reshape(shot_count, rows_each, freq_local, 2, span)]
    unnamed x16 -> x22, local copies, waits for them, and re-layouts: 5.37 us -> 6.8 us
  transfers between devices with their start and end apart: 6 -> 8, of which waited for: 2 -> 2; matrix products, arithmetic and copies ran while one was open for 30% -> 28% of each run, Pallas kernels for 0% -> 0%
where the time goes in v10:
time: 168 us; the launch traced here: 167 us
  waiting for transfers between devices  43.2 us (26%)
  local copies, waits for them, and re-layouts  36.1 us (21%)
  other arithmetic  31.2 us (19%)
  matrix products  18.9 us (11%)
  between operations  14.6 us (9%)
  blocking collectives  14.4 us (9%)
  starting transfers between devices  8.97 us (5%)
    all_gather x1, waiting for transfers between devices, per_device(): across = lax.all_gather(gram_strip, 'shot', axis=0, tiled=True)  38 us
    psum x1, blocking collectives, per_device(): power = lax.psum(local_power, 'shot') / receivers  14.4 us
    ppermute x6, starting transfers between devices, exchange_sum(): lax.ppermute(outgoing, 'shot', perm=pairs).astype(jnp.float32)  8.9 us
    unnamed x22, local copies, waits for them, and re-layouts  6.8 us
    reshape x1, local copies, waits for them, and re-layouts, rebuild_gram(): jnp.transpose(upper, (3, 2, 0, 1, 4))  6.25 us
    ppermute x6, waiting for transfers between devices, exchange_sum(): lax.ppermute(outgoing, 'shot', perm=pairs).astype(jnp.float32)  5.17 us
    transpose x1, local copies, waits for them, and re-layouts, per_device(): jnp.einsum('qtpu,qto->uqpo', stacked_left(upgoing), right, preferred_elem...  5.03 us
    dot_general x1, matrix products, per_device(): jnp.einsum('qtpu,qto->uqpo', stacked_left(upgoing), right, preferred_elem...  4.59 us
  transfers between devices with their start and end apart: 8, of which 2 were waited for; matrix products, arithmetic and copies ran while one was open for 28% of the time, Pallas kernels for 0%

profile of v10, /device:TPU:0, one launch (start us, length us, event | category | flops | bytes accessed | tf_op | source)
XLA Modules:
  0.0 167.2 jit_solution(12487072946792440386)
XLA Ops:
  6.5 2.2 %fusion.91 = (bf16[1,1,768,1024]{3,2,1,0:T(8,128)(2,1)S(1)}, bf16[1,1,768,1024]{3,2,1,0:T(8,128)(2,1)S(1)}) fusion(bf16[2,1,768,1024]{3,2,1,0:T(8,128)(2,1)} %param.3), kind=kLoop, calls=%fused_computation.178 | loop fusion | bytes 6291456 | tf_op jit(solution)/shard_map/slice | solution.py:26
  8.7 1.6 copy.45
  13.0 1.7 fusion.28
  15.3 3.7 %convert_bitcast_fusion = bf16[4,128,1,2,1024]{1,4,0,3,2:T(8,128)(2,1)S(1)} fusion(bf16[1,2,4,2,128,1536]{5,4,3,2,1,0:T(8,128)(2,1)S(1)} %bitcast.232, s32[]{:T(128)S(6)} %select_n.134, bf16[1,768,1024]{1,2,0:T(8,128)(2,1)S(1)} %bitcast.234, bf16[1,768,1024]{1,2,0:T(8,128)(2,1)S(1)} %bitcast.230), kind=kOutput, calls=%fused_computation.41 | convolution fusion | flops 3228565504 | bytes 8388612 | tf_op jit(solution)/shard_map/qpkit,qto->kiqpo/dot_general | solution.py:95
  20.3 2.9 %pad_slice_fusion.11 = (bf16[1,128,1,2,2048]{1,4,0,3,2:T(8,128)(2,1)}, bf16[1,128,1,2,2048]{1,4,0,3,2:T(8,128)(2,1)}, bf16[1,128,1,2,2048]{1,4,0,3,2:T(8,128)(2,...) fusion(bf16[4,128,1,2,1024]{1,4,0,3,2:T(8,128)(2,1)S(1)} %conve, ...), kind=kLoop, calls=%fused_computation.18 | loop fusion | bytes 8388608 | tf_op jit(solution)/shard_map/slice | solution.py:47
  24.8 1.6 dynamic-slice_maximum_fusion
  28.6 5.1 %collective-permute-start.2 = (bf16[128,1,2,640]{0,3,2,1:T(8,128)(2,1)}, bf16[128,1,2,640]{0,3,2,1:T(8,128)(2,1)}, u32[]{:S(2)}, u32[]{:S(2)}) collective-permute-start(bf16[128,1,2,640]{0,3,2,1:T(8,128)(2,1)} %get-tuple-element.42), channel_id=1, source_target_pairs={{0,12},{4,0},{8,4},{12,8},{1,13},{5,1},{9,5},{13,9},{2,14},{6,2},{... | collective-permute-start | bytes 983048 | tf_op jit(solution)/shard_map/ppermute | solution.py:73
  34.7 2.3 %multiply_reduce_fusion = f32[]{:T(128)} fusion(bf16[2,1,768,1024]{3,2,1,0:T(8,128)(2,1)S(1)} %copy-done.1), kind=kLoop, calls=%fused_computation.6 | loop fusion | flops 4718591 | bytes 3145732 | tf_op jit(solution)/shard_map/reduce_sum | solution.py:100
  40.8 2.1 %maximum_bitcast_fusion.5 = (bf16[1,1536,1,512]{3,1,2,0:T(8,128)(2,1)S(1)}, bf16[1,1536,1,512]{3,1,2,0:T(8,128)(2,1)S(1)}) fusion(bf16[1,768,512]{2,1,0:T(8,128)(2,1)} %get-tuple-element.38, bf16[1,768,512]{2,1,0:T(8,128)(2,1)} %get-tuple-element.37, bf16[1,768,512]{2,1,0:T(8,128)(2,1)} %fusion.84), kind=kLoop, calls=%fused_computation.42 | loop fusion | flops 6291456 | bytes 5505024 | tf_op jit(solution)/shard_map/stack | solution.py:22
  42.8 4.6 %fusion.10 = bf16[512,2,1024]{0,2,1:T(8,128)(2,1)} fusion(bf16[1,1536,1,512]{3,1,2,0:T(8,128)(2,1)S(1)} %get-tuple-element.48, bf16[1,1536,1,512]{3,1,2,0:T(8,128)(2,1)S(1)} %get-tuple-element.47, bf16[1,768,1024]{1,2,0:T(8,128)(2,1)S(1)} %bitcast.235, bf16[1,768,1024]{1,2,0:T(8,128)(2,1)S(1)} %bitcast.231), kind=kOutput, calls=%fused_computation.35 | convolution fusion | flops 3233808384 | bytes 8388608 | tf_op jit(solution)/shard_map/qtpu,qto->uqpo/dot_general | solution.py:103
  47.4 14.4 %psum.7 = f32[1]{0:T(128)} all-reduce(f32[1]{0:T(128)} %bitcast.16), channel_id=1, replica_groups=mesh['grp'=2,'shot'=4,'freq'=2,'sub'=2] {'shot'}, use_global_device_ids=true, to_apply=%region_1.2 | all-reduce | flops 1 | bytes 8 | tf_op jit(solution)/shard_map/psum | solution.py:101
  61.8 5.0 %copy.33 = bf16[512,2,1024]{2,1,0:T(2,128)(2,1)S(1)} copy(bf16[512,2,1024]{0,2,1:T(8,128)(2,1)} %fusion.10) | data formatting | bytes 4194304 | tf_op jit(solution)/shard_map/qtpu,qto->uqpo/transpose | solution.py:103
  67.4 3.7 %gather_fusion = bf16[256,2,1024]{2,1,0:T(2,128)(2,1)} fusion(bf16[512,2,1024]{2,1,0:T(2,128)(2,1)S(1)} %copy.33, s32[1024]{0:T(1024)S(1)} %pad_clamp_fusion), kind=kCustom, calls=%fused_computation | custom fusion | bytes 2098176 | tf_op jit(solution)/shard_map/jit(_take)/gather | solution.py:108
  71.1 2.5 %fusion.13 = bf16[256,1,2,1024]{3,2,0,1:T(2,128)(2,1)S(1)} fusion(bf16[256,2,1024]{2,1,0:T(2,128)(2,1)} %gather_fusion, pred[256]{0:T(512)(128)(4,1)S(1)} %compare_and_fusion), kind=kLoop, calls=%fused_computation.40 | loop fusion | flops 524288 | bytes 2097408 | tf_op jit(solution)/shard_map/convert_element_type | solution.py:108
  73.6 2.2 %fusion.31 = bf16[128,1,2,640]{0,3,2,1:T(8,128)(2,1)} fusion(bf16[128,1,2,640]{0,3,2,1:T(8,128)(2,1)} %collective-permute-done.2, bf16[128,1,2,640]{0,3,2,1:T(8,128)(2,1)} %collective-permute-done.1, bf16[128,1,2,640]{0,3,2,1:T(8,128)(2,1)} %collective-permute-done, bf16[4,128,1,2,640]{1,4,0,3,2:T(8,128)(2,1)} %copy-done.4, s32[]{:T(128)S(6)} %select_n.143), kind=kLoop, calls=%fused_computation.75 | loop fusion | flops 1310720 | bytes 1638404 | tf_op jit(solution)/shard_map/convert_element_type | solution.py:98
  75.8 38.0 %all-gather.2.cloned.1.call-done = bf16[512,1,2,640]{0,3,2,1:T(8,128)(2,1)} async-done(((bf16[128,1,2,640]{0,3,2,1:T(8,128)(2,1)}), bf16[512,1,2,640]{0,3,2,1:T(8,128)(2,1)}) %all-gather.2.cloned.1.call-update) | async-done | bytes 1310736 | tf_op jit(solution)/shard_map/all_gather | solution.py:115
  113.8 1.7 %copy.43 = bf16[512,1,2,640]{3,0,2,1:T(8,128)(2,1)S(1)} copy(bf16[512,1,2,640]{0,3,2,1:T(8,128)(2,1)} %all-gather.2.cloned.1.call-done) | data formatting | bytes 2621440 | tf_op jit(solution)/shard_map/reshape | solution.py:116
  115.6 4.3 %fusion.1 = pred[1024,1024]{1,0:T(8,128)(4,1)} fusion(s32[1024]{0:T(1024)S(1)} %get-tuple-element.55, s32[1024]{0:T(1024)S(1)} %get-tuple-element.56, pred[1024]{0:T(1024)(128)(4,1)S(1)} %fusion.79), kind=kLoop, calls=%fused_computation.21 | loop fusion | flops 15728640 | bytes 1057792 | tf_op jit(solution)/shard_map/le | solution.py:63
  121.0 1.8 %collective-permute-start.5 = (bf16[64,1,2,1024]{3,0,1,2:T(8,128)(2,1)}, bf16[64,1,2,1024]{3,0,1,2:T(8,128)(2,1)S(1)}, u32[]{:S(2)}, u32[]{:S(2)}) collective-permute-start(bf16[64,1,2,1024]{3,0,1,2:T(8,128)(2,1)} %get-tuple-element.45), channel_id=1, source_target_pairs={{0,12},{4,0},{8,4},{12,8},{1,13},{5,1},{9,5},{13,9},{2,14},{6,2},{... | collective-permute-start | bytes 786440 | tf_op jit(solution)/shard_map/ppermute | solution.py:73
  126.5 2.4 %copy.40 = bf16[2,1,8,128,1024]{4,3,2,0,1:T(8,128)(2,1)} copy(bf16[2,1,8,128,1024]{4,3,0,1,2:T(8,128)(2,1)S(1)} %bitcast.236) | data formatting | bytes 8388608 | tf_op jit(solution)/shard_map/transpose | solution.py:58
  128.9 6.3 %copy.41 = bf16[2,1,1024,1024]{2,3,0,1:T(8,128)(2,1)} copy(bf16[2,1,1024,1024]{3,2,0,1:T(8,128)(2,1)} %bitcast.227) | data formatting | bytes 8388608 | tf_op jit(solution)/shard_map/reshape | solution.py:58
  135.2 2.6 %fusion.90 = (bf16[1,1,1024,1024]{3,2,0,1:T(8,128)(2,1)S(1)}, bf16[1,1,1024,1024]{3,2,0,1:T(8,128)(2,1)S(1)}) fusion(bf16[2,1,1024,1024]{3,2,0,1:T(8,128)(2,1)} %bitcast.228), kind=kLoop, calls=%fused_computation.177 | loop fusion | flops 1048576 | bytes 8388608 | tf_op jit(solution)/shard_map/slice | solution.py:60
  138.9 2.5 %divide_convert_fusion = bf16[2,1,1024,1024]{3,2,0,1:T(8,128)(2,1)S(1)} fusion(bf16[1,1,1024,1024]{3,2,0,1:T(8,128)(2,1)S(1)} %get-tuple-element.18, bf16[1,1,1024,1024]{3,2,0,1:T(8,128)(2,1)S(1)} %get-tuple-element.17, f32[]{:T(128)} %bitcast.33, pred[1024,1024]{1,0:T(8,128)(4,1)S(1)} %copy-done.5, bf16[2,1,8,128,1024]{4,3,2,0,1:T(8,128)(2,1)S(1)} %copy-done), kind=kLoop, calls=%fused_computation.1 | loop fusion | flops 10485760 | bytes 13631492 | tf_op jit(solution)/shard_map/convert_element_type | solution.py:130
  142.4 5.2 %collective-permute-done.4 = bf16[64,1,2,1024]{3,0,1,2:T(8,128)(2,1)S(1)} collective-permute-done((bf16[64,1,2,1024]{3,0,1,2:T(8,128)(2,1)S(1)}, bf16[64,1,2,1024]{3,0,1,2:T(8,128)(2,1)S(1)}, u32[]{:S(2)}, u32[]{:S(2)}) %collective-permute-start.4) | collective-permute-done | bytes 262176 | tf_op jit(solution)/shard_map/ppermute | solution.py:73
  (94 shorter events, 32.6 us)
Async XLA Ops:
  6.5 107.3 %all-gather.2.cloned.1.call-start = ((), (), s32[]{:S(2)}) async-start(), calls=%async_computation | async-start | bytes 1638400 | tf_op jit(solution)/shard_map/all_gather | solution.py:115
  11.1 2.0 %copy-start.3 = (bf16[1,1,768,1024]{2,3,1,0:T(8,128)(2,1)S(1)}, bf16[1,1,768,1024]{2,3,1,0:T(8,128)(2,1)}, u32[]{:S(2)}) copy-start(bf16[1,1,768,1024]{2,3,1,0:T(8,128)(2,1)} %copy.45) | copy-start | bytes 4718596
  19.0 1.3 copy-start.2
  24.8 9.9 %copy-start.1 = (bf16[2,1,768,1024]{3,2,1,0:T(8,128)(2,1)S(1)}, bf16[2,1,768,1024]{3,2,1,0:T(8,128)(2,1)}, u32[]{:S(2)}) copy-start(bf16[2,1,768,1024]{3,2,1,0:T(8,128)(2,1)} %param.3) | copy-start | bytes 9437188
  26.5 1.1 copy-start.4
  27.6 9.3 %copy-start.6 = (bf16[2,1,768,512]{3,2,1,0:T(8,128)(2,1)S(1)}, bf16[2,1,768,512]{3,2,1,0:T(8,128)(2,1)}, u32[]{:S(2)}) copy-start(bf16[2,1,768,512]{3,2,1,0:T(8,128)(2,1)} %param.4) | copy-start | bytes 4718596
  28.6 45.0 %collective-permute-start.2 = (bf16[128,1,2,640]{0,3,2,1:T(8,128)(2,1)}, bf16[128,1,2,640]{0,3,2,1:T(8,128)(2,1)}, u32[]{:S(2)}, u32[]{:S(2)}) collective-permute-start(bf16[128,1,2,640]{0,3,2,1:T(8,128)(2,1)} %get-tuple-element.42), channel_id=1, source_target_pairs={{0,12},{4,0},{8,4},{12,8},{1,13},{5,1},{9,5},{13,9},{2,14},{6,2},{... | collective-permute-start | bytes 983048 | tf_op jit(solution)/shard_map/ppermute | solution.py:73
  33.7 39.9 %collective-permute-start.1 = (bf16[128,1,2,640]{0,3,2,1:T(8,128)(2,1)}, bf16[128,1,2,640]{0,3,2,1:T(8,128)(2,1)}, u32[]{:S(2)}, u32[]{:S(2)}) collective-permute-start(bf16[128,1,2,640]{0,3,2,1:T(8,128)(2,1)} %get-tuple-element.43), channel_id=1, source_target_pairs={{0,8},{4,12},{8,0},{12,4},{1,9},{5,13},{9,1},{13,5},{2,10},{6,14},... | collective-permute-start | bytes 983048 | tf_op jit(solution)/shard_map/ppermute | solution.py:73
  33.7 40.0 %collective-permute-start = (bf16[128,1,2,640]{0,3,2,1:T(8,128)(2,1)}, bf16[128,1,2,640]{0,3,2,1:T(8,128)(2,1)}, u32[]{:S(2)}, u32[]{:S(2)}) collective-permute-start(bf16[128,1,2,640]{0,3,2,1:T(8,128)(2,1)} %get-tuple-element.41), channel_id=1, source_target_pairs={{0,4},{4,8},{8,12},{12,0},{1,5},{5,9},{9,13},{13,1},{2,6},{6,10},{... | collective-permute-start | bytes 983048 | tf_op jit(solution)/shard_map/ppermute | solution.py:73
  37.0 2.2 %copy-start.7 = (s32[512]{0:T(512)S(1)}, s32[512]{0:T(512)}, u32[]{:S(2)}) copy-start(s32[512]{0:T(512)} %param.5) | copy-start | bytes 6148
  115.5 8.3 %collective-permute-start.6 = (bf16[4,128,1,2,640]{4,1,0,3,2:T(8,128)(2,1)S(1)}, bf16[4,128,1,2,640]{4,1,0,3,2:T(8,128)(2,1)}, u32[]{:S(2)}, u32[]{:S(2)}) collective-permute-start(bf16[4,128,1,2,640]{4,1,0,3,2:T(8,128)(2,1)S(1)} %bitcast.237), channel_id=1, source_target_pairs={{0,1},{1,0},{2,3},{3,2},{4,5},{5,4},{6,7},{7,6},{8,9},{9,8},{10,11... | collective-permute-start | bytes 3932168 | tf_op jit(solution)/shard_map/ppermute | solution.py:119
  121.0 21.4 %collective-permute-start.5 = (bf16[64,1,2,1024]{3,0,1,2:T(8,128)(2,1)}, bf16[64,1,2,1024]{3,0,1,2:T(8,128)(2,1)S(1)}, u32[]{:S(2)}, u32[]{:S(2)}) collective-permute-start(bf16[64,1,2,1024]{3,0,1,2:T(8,128)(2,1)} %get-tuple-element.45), channel_id=1, source_target_pairs={{0,12},{4,0},{8,4},{12,8},{1,13},{5,1},{9,5},{13,9},{2,14},{6,2},{... | collective-permute-start | bytes 786440 | tf_op jit(solution)/shard_map/ppermute | solution.py:73
  122.8 24.8 %collective-permute-start.4 = (bf16[64,1,2,1024]{3,0,1,2:T(8,128)(2,1)S(1)}, bf16[64,1,2,1024]{3,0,1,2:T(8,128)(2,1)S(1)}, u32[]{:S(2)}, u32[]{:S(2)}) collective-permute-start(bf16[64,1,2,1024]{3,0,1,2:T(8,128)(2,1)S(1)} %get-tuple-element.46), channel_id=1, source_target_pairs={{0,8},{4,12},{8,0},{12,4},{1,9},{5,13},{9,1},{13,5},{2,10},{6,14},... | collective-permute-start | bytes 786440 | tf_op jit(solution)/shard_map/ppermute | solution.py:73
  123.8 23.7 %collective-permute-start.3 = (bf16[64,1,2,1024]{3,0,1,2:T(8,128)(2,1)S(1)}, bf16[64,1,2,1024]{3,0,1,2:T(8,128)(2,1)}, u32[]{:S(2)}, u32[]{:S(2)}) collective-permute-start(bf16[64,1,2,1024]{3,0,1,2:T(8,128)(2,1)S(1)} %get-tuple-element.44), channel_id=1, source_target_pairs={{0,4},{4,8},{8,12},{12,0},{1,5},{5,9},{9,13},{13,1},{2,6},{6,10},{... | collective-permute-start | bytes 786440 | tf_op jit(solution)/shard_map/ppermute | solution.py:73
  135.2 3.4 %copy-start = (bf16[2,1,8,128,1024]{4,3,2,0,1:T(8,128)(2,1)S(1)}, bf16[2,1,8,128,1024]{4,3,2,0,1:T(8,128)(2,1)}, u32[]{:S(2)}) copy-start(bf16[2,1,8,128,1024]{4,3,2,0,1:T(8,128)(2,1)} %copy.40) | copy-start | bytes 12582916
  135.2 3.7 %copy-start.5 = (pred[1024,1024]{1,0:T(8,128)(4,1)S(1)}, pred[1024,1024]{1,0:T(8,128)(4,1)}, u32[]{:S(2)}) copy-start(pred[1024,1024]{1,0:T(8,128)(4,1)} %fusion.1) | copy-start | bytes 3145732
Sparse Core Ops, SparseCore 0:
  76.0 37.8 all-gather.1

commit v11 on v7

--- a/solution.py
+++ b/solution.py
@@ -58,10 +58,12 @@
     upper = jnp.transpose(upper, (3, 2, 0, 1, 4)).reshape(2, freq_local, receivers, receivers)
     mirror = jnp.swapaxes(upper, 2, 3)
     mirror = jnp.stack([mirror[0], -mirror[1]])
-    row_tile = lax.broadcasted_iota(jnp.int32, (receivers, receivers), 0) // tile
-    col_tile = lax.broadcasted_iota(jnp.int32, (receivers, receivers), 1) // tile
+    row_tile = lax.broadcasted_iota(jnp.int32, (tiles, 1, tiles, 1), 0)
+    col_tile = lax.broadcasted_iota(jnp.int32, (tiles, 1, tiles, 1), 2)
     direct = (col_tile - row_tile) % tiles <= tiles // 2
-    return jnp.where(direct, upper, mirror)
+    shape6 = (2, freq_local, tiles, tile, tiles, tile)
+    whole = jnp.where(direct, upper.reshape(shape6), mirror.reshape(shape6))
+    return whole.reshape(upper.shape)
 
 
 def per_device(downgoing, upgoing, source_order):

time: 149 us -> 146 us (0.980)
  other arithmetic: 27.6 us -> 24.4 us
    another operation x0 -> x1, local copies, waits for them, and re-layouts: none -> 6.24 us  [rebuild_gram(): whole = jnp.where(direct, upper.reshape(shape6), mirror.reshape(shape6))]
    reshape x1 -> x0, local copies, waits for them, and re-layouts: 6.24 us -> none  [rebuild_gram(): jnp.transpose(upper, (3, 2, 0, 1, 4))]
    le x1, other arithmetic: 3.56 us -> 0.01 us  [rebuild_gram(): direct = (col_tile - row_tile) % tiles <= tiles // 2]
    unnamed x16 -> x15, local copies, waits for them, and re-layouts: 5.37 us -> 5.91 us
  transfers between devices with their start and end apart: 6 -> 6, of which waited for: 2 -> 2; matrix products, arithmetic and copies ran while one was open for 30% -> 29% of each run, Pallas kernels for 0% -> 0%
where the time goes in v11:
time: 146 us; the launch traced here: 145 us
  waiting for transfers between devices  35 us (24%)
  local copies, waits for them, and re-layouts  34.3 us (23%)
  other arithmetic  24.4 us (17%)
  matrix products  18.9 us (13%)
  between operations  14.6 us (10%)
  blocking collectives  14.4 us (10%)
  starting transfers between devices  3.49 us (2%)
    all_gather x1, waiting for transfers between devices, per_device(): across = lax.all_gather(gram_strip, 'shot', axis=0, tiled=True)  31 us
    psum x1, blocking collectives, per_device(): power = lax.psum(local_power, 'shot') / receivers  14.4 us
    another operation x1, local copies, waits for them, and re-layouts, rebuild_gram(): whole = jnp.where(direct, upper.reshape(shape6), mirror.reshape(shape6))  6.24 us
    unnamed x15, local copies, waits for them, and re-layouts  5.91 us
    transpose x1, local copies, waits for them, and re-layouts, per_device(): jnp.einsum('qtpu,qto->uqpo', stacked_left(upgoing), right, preferred_elem...  5.05 us
    dot_general x1, matrix products, per_device(): jnp.einsum('qtpu,qto->uqpo', stacked_left(upgoing), right, preferred_elem...  4.58 us
    reduce_sum x1, other arithmetic, per_device(): jnp.sum(jnp.square(downgoing.astype(jnp.float32)), axis=(0, 2, 3))  4.11 us
    ppermute x3, waiting for transfers between devices, per_device(): corr = corr + lax.ppermute(outgoing, 'shot', perm=pairs).astype(jnp.float32)  3.94 us
  transfers between devices with their start and end apart: 6, of which 2 were waited for; matrix products, arithmetic and copies ran while one was open for 29% of the time, Pallas kernels for 0%

profile of v11, /device:TPU:0, one launch (start us, length us, event | category | flops | bytes accessed | tf_op | source)
XLA Modules:
  0.0 145.0 jit_solution(6541168669168774255)
XLA Ops:
  6.5 2.2 %fusion.88 = (bf16[1,1,768,1024]{3,2,1,0:T(8,128)(2,1)S(1)}, bf16[1,1,768,1024]{3,2,1,0:T(8,128)(2,1)S(1)}) fusion(bf16[2,1,768,1024]{3,2,1,0:T(8,128)(2,1)} %param.3), kind=kLoop, calls=%fused_computation.168 | loop fusion | bytes 6291456 | tf_op jit(solution)/shard_map/slice | solution.py:26
  8.7 1.6 %copy.40 = bf16[1,1,768,1024]{2,3,1,0:T(8,128)(2,1)} copy(bf16[1,1,768,1024]{3,2,1,0:T(8,128)(2,1)S(1)} %get-tuple-element.19) | data formatting | bytes 3145728
  13.0 1.7 %fusion.26 = (bf16[1,1,1536,1024]{2,3,1,0:T(8,128)(2,1)S(1)}, bf16[1,1,1536,1024]{2,3,1,0:T(8,128)(2,1)S(1)}) fusion(bf16[1,768,1024]{1,2,0:T(8,128)(2,1)S(1)} %bitcast.230, bf16[1,768,1024]{1,2,0:T(8,128)(2,1)S(1)} %bitcast.226, bf16[1,768,1024]{1,2,0:T(8,128)(2,1)} %bitcast_negate_fusion), kind=kLoop, calls=%fused_computation.65 | loop fusion | flops 12582912 | bytes 11010048 | tf_op jit(solution)/shard_map/stack | solution.py:16
  15.3 3.7 %convert_bitcast_fusion = bf16[4,128,1,2,1024]{1,4,0,3,2:T(8,128)(2,1)S(1)} fusion(bf16[1,2,4,2,128,1536]{5,4,3,2,1,0:T(8,128)(2,1)S(1)} %bitcast.229, s32[]{:T(128)S(6)} %select_n.120, bf16[1,768,1024]{1,2,0:T(8,128)(2,1)S(1)} %bitcast.231, bf16[1,768,1024]{1,2,0:T(8,128)(2,1)S(1)} %bitcast.227), kind=kOutput, calls=%fused_computation.37 | convolution fusion | flops 3228565504 | bytes 8388612 | tf_op jit(solution)/shard_map/qpkit,qto->kiqpo/dot_general | solution.py:87
  19.0 1.3 copy-done.1
  20.3 2.8 %pad_slice_fusion.11 = (bf16[1,128,1,2,2048]{1,4,0,3,2:T(8,128)(2,1)}, bf16[1,128,1,2,2048]{1,4,0,3,2:T(8,128)(2,1)}, bf16[1,128,1,2,2048]{1,4,0,3,2:T(8,128)(2,...) fusion(bf16[4,128,1,2,1024]{1,4,0,3,2:T(8,128)(2,1)S(1)} %conve, ...), kind=kLoop, calls=%fused_computation.15 | loop fusion | bytes 8388608 | tf_op jit(solution)/shard_map/slice | solution.py:47
  23.1 1.5 %fusion.54 = (bf16[1,128,1,2,640]{1,4,0,3,2:T(8,128)(2,1)S(1)}, bf16[1,128,1,2,640]{1,4,0,3,2:T(8,128)(2,1)S(1)}) fusion(s32[]{:T(128)S(6)} %select_n.128, bf16[4,128,1,2,1024]{1,4,0,3,2:T(8,128)(2,1)} %copy-done.1, bf16[1,128,1,2,2048]{1,4,0,3,2:T(8,128)(2,1)} %get-tuple-element.33, s32[]{:T(128)S(6)} %select_n.122, ...), kind=kLoop, calls=%fused_computation.109 | loop fusion | flops 1310720 | bytes 3407880 | tf_op jit(solution)/shard_map/concatenate | solution.py:43
  24.6 1.5 %dynamic-slice_maximum_fusion = (bf16[1,128,1,2,640]{1,4,0,3,2:T(8,128)(2,1)S(1)}, bf16[1,128,1,2,640]{1,4,0,3,2:T(8,128)(2,1)S(1)}) fusion(bf16[1,128,1,2,2048]{1,4,0,3,2:T(8,128)(2,1)} %get-tuple-element.36, s32[]{:T(128)S(6)} %select_n.126, bf16[1,128,1,2,2048]{1,4,0,3,2:T(8,128)(2,1)} %get-tuple-element.35, ...), kind=kLoop, calls=%fused_computation.110 | loop fusion | flops 1310720 | bytes 1966088 | tf_op jit(solution)/shard_map/concatenate | solution.py:43
  27.3 2.4 %copy.31 = bf16[4,128,1,2,640]{4,1,0,3,2:T(8,128)(2,1)} copy(bf16[4,128,1,2,640]{1,4,0,3,2:T(8,128)(2,1)} %pad_maximum_fusion.3) | data formatting | bytes 2621440 | tf_op jit(solution)/shard_map/stack | solution.py:48
  29.8 4.1 %multiply_reduce_fusion = f32[]{:T(128)} fusion(bf16[2,1,768,1024]{3,2,1,0:T(8,128)(2,1)} %param.3), kind=kLoop, calls=%fused_computation.3 | loop fusion | flops 4718591 | bytes 3145732 | tf_op jit(solution)/shard_map/reduce_sum | solution.py:91
  34.0 14.4 %psum.7 = f32[1]{0:T(128)} all-reduce(f32[1]{0:T(128)} %bitcast.13), channel_id=1, replica_groups=mesh['grp'=2,'shot'=4,'freq'=2,'sub'=2] {'shot'}, use_global_device_ids=true, to_apply=%region_2.3 | all-reduce | flops 1 | bytes 8 | tf_op jit(solution)/shard_map/psum | solution.py:92
  49.6 1.5 %slice_bitcast_fusion.3 = (bf16[1,768,512]{2,1,0:T(8,128)(2,1)S(1)}, bf16[1,768,512]{2,1,0:T(8,128)(2,1)S(1)}) fusion(bf16[2,1,768,512]{3,2,1,0:T(8,128)(2,1)} %param.4), kind=kLoop, calls=%fused_computation.67 | loop fusion | bytes 3145728 | tf_op jit(solution)/shard_map/squeeze | solution.py:20
  51.4 4.6 %fusion.8 = bf16[512,2,1024]{0,2,1:T(8,128)(2,1)} fusion(bf16[1,1536,1,512]{3,1,2,0:T(8,128)(2,1)S(1)} %get-tuple-element.45, bf16[1,1536,1,512]{3,1,2,0:T(8,128)(2,1)S(1)} %get-tuple-element.44, bf16[1,768,1024]{1,2,0:T(8,128)(2,1)S(1)} %bitcast.232, bf16[1,768,1024]{1,2,0:T(8,128)(2,1)S(1)} %bitcast.228), kind=kOutput, calls=%fused_computation.31 | convolution fusion | flops 3233808384 | bytes 8388608 | tf_op jit(solution)/shard_map/qtpu,qto->uqpo/dot_general | solution.py:94
  55.9 5.0 %copy.32 = bf16[512,2,1024]{2,1,0:T(2,128)(2,1)S(1)} copy(bf16[512,2,1024]{0,2,1:T(8,128)(2,1)} %fusion.8) | data formatting | bytes 4194304 | tf_op jit(solution)/shard_map/qtpu,qto->uqpo/transpose | solution.py:94
  63.0 2.8 %gather_fusion = bf16[256,2,1024]{2,1,0:T(2,128)(2,1)S(1)} fusion(bf16[512,2,1024]{2,1,0:T(2,128)(2,1)S(1)} %copy.32, s32[1024]{0:T(1024)S(1)} %pad_clamp_fusion), kind=kCustom, calls=%fused_computation | custom fusion | bytes 2098176 | tf_op jit(solution)/shard_map/jit(_take)/gather | solution.py:99
  65.8 1.5 %fusion.11 = bf16[256,1,2,1024]{3,2,0,1:T(2,128)(2,1)S(1)} fusion(bf16[256,2,1024]{2,1,0:T(2,128)(2,1)S(1)} %gather_fusion, pred[256]{0:T(512)(128)(4,1)S(1)} %compare_and_fusion), kind=kLoop, calls=%fused_computation.36 | loop fusion | flops 524288 | bytes 2097408 | tf_op jit(solution)/shard_map/convert_element_type | solution.py:99
  67.4 31.0 %all-gather.2.cloned.1.call-done = bf16[512,1,2,640]{3,0,2,1:T(8,128)(2,1)} async-done(((bf16[128,1,2,640]{3,0,2,1:T(8,128)(2,1)}), bf16[512,1,2,640]{3,0,2,1:T(8,128)(2,1)}) %all-gather.2.cloned.1.call-update) | async-done | bytes 1310736 | tf_op jit(solution)/shard_map/all_gather | solution.py:112
  100.3 1.4 collective-permute-start.2
  103.8 2.0 %select_bitcast_fusion.1 = (bf16[4,1,128,1,2,640]{5,2,1,0,4,3:T(8,128)(2,1)S(1)}, bf16[4,1,128,1,2,640]{5,2,1,0,4,3:T(8,128)(2,1)S(1)}) fusion(bf16[4,128,1,2,640]{4,1,0,3,2:T(8,128)(2,1)} %bitcast.240, bf16[4,128,1,2,640]{4,1,0,3,2:T(8,128)(2,1)} %collective-permute-done.3, pred[]{:T(512)S(6)} %eq.10), kind=kLoop, calls=%fused_computation.42 | loop fusion | flops 1310720 | bytes 5242881 | tf_op jit(solution)/shard_map/stack | solution.py:119
  106.8 2.4 %copy.36 = bf16[2,1,8,128,1024]{4,3,2,0,1:T(8,128)(2,1)} copy(bf16[2,1,8,128,1024]{4,3,0,1,2:T(8,128)(2,1)S(1)} %bitcast.233) | data formatting | bytes 8388608 | tf_op jit(solution)/shard_map/transpose | solution.py:58
  109.2 6.2 %copy.37 = bf16[2,1,1024,1024]{2,3,0,1:T(8,128)(2,1)} copy(bf16[2,1,1024,1024]{3,2,0,1:T(8,128)(2,1)} %bitcast.224) | data formatting | bytes 8388608 | tf_op jit(solution)/shard_map/reshape;reshape | solution.py:65
  115.5 2.6 %fusion.87 = (bf16[1,1,1024,1024]{3,2,0,1:T(8,128)(2,1)S(1)}, bf16[1,1,1024,1024]{3,2,0,1:T(8,128)(2,1)S(1)}) fusion(bf16[2,1,1024,1024]{3,2,0,1:T(8,128)(2,1)} %bitcast.225), kind=kLoop, calls=%fused_computation.167 | loop fusion | flops 1048576 | bytes 8388608 | tf_op jit(solution)/shard_map/slice | solution.py:60
  118.9 2.5 %divide_convert_fusion = bf16[2,1,1024,1024]{3,2,0,1:T(8,128)(2,1)S(1)} fusion(bf16[1,1,1024,1024]{3,2,0,1:T(8,128)(2,1)S(1)} %get-tuple-element.18, bf16[1,1,1024,1024]{3,2,0,1:T(8,128)(2,1)S(1)} %get-tuple-element.17, f32[]{:T(128)} %bitcast.30, pred[1024,1024]{1,0:T(8,128)(4,1)S(1)} %bitcast.238, bf16[2,1,8,128,1024]{4,3,2,0,1:T(8,128)(2,1)S(1)} %copy-done), kind=kLoop, calls=%fused_computation.1 | loop fusion | flops 10485760 | bytes 13631492 | tf_op jit(solution)/shard_map/convert_element_type | solution.py:127
  122.4 3.9 %collective-permute-done.1 = bf16[64,1,2,1024]{3,0,1,2:T(8,128)(2,1)S(1)} collective-permute-done((bf16[64,1,2,1024]{3,0,1,2:T(8,128)(2,1)S(1)}, bf16[64,1,2,1024]{3,0,1,2:T(8,128)(2,1)S(1)}, u32[]{:S(2)}, u32[]{:S(2)}) %collective-permute-start.1) | collective-permute-done | bytes 262176 | tf_op jit(solution)/shard_map/ppermute | solution.py:110
  (81 shorter events, 25.8 us)
Async XLA Ops:
  6.5 60.8 %reduce-scatter.2.cloned.1.call-start = ((), (), s32[]{:S(2)}) async-start(), calls=%async_computation.1 | async-start | bytes 1638400 | tf_op jit(solution)/shard_map/reduce_scatter | solution.py:89
  11.0 2.0 %copy-start.2 = (bf16[1,1,768,1024]{2,3,1,0:T(8,128)(2,1)S(1)}, bf16[1,1,768,1024]{2,3,1,0:T(8,128)(2,1)}, u32[]{:S(2)}) copy-start(bf16[1,1,768,1024]{2,3,1,0:T(8,128)(2,1)} %copy.40) | copy-start | bytes 4718596
  19.0 1.3 copy-start.1
  29.8 68.5 %all-gather.2.cloned.1.call-start = ((), (), s32[]{:S(2)}) async-start(), calls=%async_computation.2 | async-start | bytes 1638400 | tf_op jit(solution)/shard_map/all_gather | solution.py:112
  55.9 5.1 %copy-start.3 = (s32[512]{0:T(512)S(1)}, s32[512]{0:T(512)}, u32[]{:S(2)}) copy-start(s32[512]{0:T(512)} %param.5) | copy-start | bytes 6148
  98.3 5.4 %collective-permute-start.3 = (bf16[4,128,1,2,640]{4,1,0,3,2:T(8,128)(2,1)}, bf16[4,128,1,2,640]{4,1,0,3,2:T(8,128)(2,1)}, u32[]{:S(2)}, u32[]{:S(2)}) collective-permute-start(bf16[4,128,1,2,640]{4,1,0,3,2:T(8,128)(2,1)} %bitcast.239), channel_id=1, source_target_pairs={{0,1},{1,0},{2,3},{3,2},{4,5},{5,4},{6,7},{7,6},{8,9},{9,8},{10,11... | collective-permute-start | bytes 3932168 | tf_op jit(solution)/shard_map/ppermute | solution.py:116
  100.3 22.0 %collective-permute-start.2 = (bf16[64,1,2,1024]{3,0,1,2:T(8,128)(2,1)}, bf16[64,1,2,1024]{3,0,1,2:T(8,128)(2,1)S(1)}, u32[]{:S(2)}, u32[]{:S(2)}) collective-permute-start(bf16[64,1,2,1024]{3,0,1,2:T(8,128)(2,1)} %get-tuple-element.42), channel_id=1, source_target_pairs={{0,12},{4,0},{8,4},{12,8},{1,13},{5,1},{9,5},{13,9},{2,14},{6,2},{... | collective-permute-start | bytes 786440 | tf_op jit(solution)/shard_map/ppermute | solution.py:110
  101.7 24.6 %collective-permute-start.1 = (bf16[64,1,2,1024]{3,0,1,2:T(8,128)(2,1)S(1)}, bf16[64,1,2,1024]{3,0,1,2:T(8,128)(2,1)S(1)}, u32[]{:S(2)}, u32[]{:S(2)}) collective-permute-start(bf16[64,1,2,1024]{3,0,1,2:T(8,128)(2,1)S(1)} %get-tuple-element.43), channel_id=1, source_target_pairs={{0,8},{4,12},{8,0},{12,4},{1,9},{5,13},{9,1},{13,5},{2,10},{6,14},... | collective-permute-start | bytes 786440 | tf_op jit(solution)/shard_map/ppermute | solution.py:110
  102.6 23.8 %collective-permute-start = (bf16[64,1,2,1024]{3,0,1,2:T(8,128)(2,1)S(1)}, bf16[64,1,2,1024]{3,0,1,2:T(8,128)(2,1)S(1)}, u32[]{:S(2)}, u32[]{:S(2)}) collective-permute-start(bf16[64,1,2,1024]{3,0,1,2:T(8,128)(2,1)S(1)} %get-tuple-element.41), channel_id=1, source_target_pairs={{0,4},{4,8},{8,12},{12,0},{1,5},{5,9},{9,13},{13,1},{2,6},{6,10},{... | collective-permute-start | bytes 786440 | tf_op jit(solution)/shard_map/ppermute | solution.py:110
  115.5 3.4 %copy-start = (bf16[2,1,8,128,1024]{4,3,2,0,1:T(8,128)(2,1)S(1)}, bf16[2,1,8,128,1024]{4,3,2,0,1:T(8,128)(2,1)}, u32[]{:S(2)}) copy-start(bf16[2,1,8,128,1024]{4,3,2,0,1:T(8,128)(2,1)} %copy.36) | copy-start | bytes 12582916
Sparse Core Ops, SparseCore 0:
  29.9 34.0 reduce-scatter.1
  67.5 30.8 all-gather.1

commit v12 on v11

--- a/solution.py
+++ b/solution.py
@@ -27,7 +27,8 @@
 
 
 def sweep_whole(scaled, solution, target):
-    for sweep in range(SWEEPS):
+    solution = solution + relaxation * (target - damping * solution)
+    for sweep in range(1, SWEEPS):
         narrow = solution.astype(jnp.bfloat16)
         real_real = jnp.einsum("qjc,qcr->qjr", narrow[0], scaled[0], preferred_element_type=jnp.float32)
         imag_imag = jnp.einsum("qjc,qcr->qjr", narrow[1], scaled[1], preferred_element_type=jnp.float32)

time: 146 us -> 163 us (1.12)
  waiting for transfers between devices: 35 us -> 52.5 us
    ppermute x3, waiting for transfers between devices: 3.94 us -> 21.4 us  [per_device(): corr = corr + lax.ppermute(outgoing, 'shot', perm=pairs).astype(jnp.float32)]
    unnamed x15 -> x17, local copies, waits for them, and re-layouts: 5.91 us -> 6.61 us
  transfers between devices with their start and end apart: 6 -> 6, of which waited for: 2 -> 3; matrix products, arithmetic and copies ran while one was open for 29% -> 15% of each run, Pallas kernels for 0% -> 0%
where the time goes in v12:
time: 163 us
  waiting for transfers between devices  52.5 us (32%)
  local copies, waits for them, and re-layouts  34.3 us (21%)
  other arithmetic  25.3 us (16%)
  matrix products  18 us (11%)
  between operations  14.6 us (9%)
  blocking collectives  14.4 us (9%)
  starting transfers between devices  3.54 us (2%)
    all_gather x1, waiting for transfers between devices, per_device(): across = lax.all_gather(gram_strip, 'shot', axis=0, tiled=True)  31 us
    ppermute x3, waiting for transfers between devices, per_device(): corr = corr + lax.ppermute(outgoing, 'shot', perm=pairs).astype(jnp.float32)  21.4 us
    psum x1, blocking collectives, per_device(): power = lax.psum(local_power, 'shot') / receivers  14.4 us
    unnamed x17, local copies, waits for them, and re-layouts  6.61 us
    another operation x1, local copies, waits for them, and re-layouts, rebuild_gram(): whole = jnp.where(direct, upper.reshape(shape6), mirror.reshape(shape6))  6.24 us
    transpose x1, local copies, waits for them, and re-layouts, per_device(): jnp.einsum('qtpu,qto->uqpo', stacked_left(upgoing), right, preferred_elem...  5.05 us
    dot_general x1, matrix products, per_device(): jnp.einsum('qtpu,qto->uqpo', stacked_left(upgoing), right, preferred_elem...  4.58 us
    reduce_sum x1, other arithmetic, per_device(): jnp.sum(jnp.square(downgoing.astype(jnp.float32)), axis=(0, 2, 3))  4.11 us
  transfers between devices with their start and end apart: 6, of which 3 were waited for; matrix products, arithmetic and copies ran while one was open for 15% of the time, Pallas kernels for 0%

profile of v12, /device:TPU:0, one launch (start us, length us, event | category | flops | bytes accessed | tf_op | source)
XLA Modules:
  0.0 162.6 jit_solution(18321033068724083155)
XLA Ops:
  6.5 2.2 %fusion.80 = (bf16[1,1,768,1024]{3,2,1,0:T(8,128)(2,1)S(1)}, bf16[1,1,768,1024]{3,2,1,0:T(8,128)(2,1)S(1)}) fusion(bf16[2,1,768,1024]{3,2,1,0:T(8,128)(2,1)} %param.3), kind=kLoop, calls=%fused_computation.158 | loop fusion | bytes 6291456 | tf_op jit(solution)/shard_map/slice | solution.py:26
  8.7 1.6 copy.40
  13.0 1.7 %fusion.26 = (bf16[1,1,1536,1024]{2,3,1,0:T(8,128)(2,1)S(1)}, bf16[1,1,1536,1024]{2,3,1,0:T(8,128)(2,1)S(1)}) fusion(bf16[1,768,1024]{1,2,0:T(8,128)(2,1)S(1)} %bitcast.222, bf16[1,768,1024]{1,2,0:T(8,128)(2,1)S(1)} %bitcast.218, bf16[1,768,1024]{1,2,0:T(8,128)(2,1)} %bitcast_negate_fusion), kind=kLoop, calls=%fused_computation.65 | loop fusion | flops 12582912 | bytes 11010048 | tf_op jit(solution)/shard_map/stack | solution.py:16
  15.3 3.7 %convert_bitcast_fusion = bf16[4,128,1,2,1024]{1,4,0,3,2:T(8,128)(2,1)S(1)} fusion(bf16[1,2,4,2,128,1536]{5,4,3,2,1,0:T(8,128)(2,1)S(1)} %bitcast.221, s32[]{:T(128)S(6)} %select_n.120, bf16[1,768,1024]{1,2,0:T(8,128)(2,1)S(1)} %bitcast.223, bf16[1,768,1024]{1,2,0:T(8,128)(2,1)S(1)} %bitcast.219), kind=kOutput, calls=%fused_computation.37 | convolution fusion | flops 3228565504 | bytes 8388612 | tf_op jit(solution)/shard_map/qpkit,qto->kiqpo/dot_general | solution.py:88
  20.3 2.8 %pad_slice_fusion.11 = (bf16[1,128,1,2,2048]{1,4,0,3,2:T(8,128)(2,1)}, bf16[1,128,1,2,2048]{1,4,0,3,2:T(8,128)(2,1)}, bf16[1,128,1,2,2048]{1,4,0,3,2:T(8,128)(2,...) fusion(bf16[4,128,1,2,1024]{1,4,0,3,2:T(8,128)(2,1)S(1)} %conve, ...), kind=kLoop, calls=%fused_computation.15 | loop fusion | bytes 8388608 | tf_op jit(solution)/shard_map/slice | solution.py:48
  23.1 1.5 fusion.52
  24.6 1.5 dynamic-slice_maximum_fusion
  27.3 2.4 %copy.31 = bf16[4,128,1,2,640]{4,1,0,3,2:T(8,128)(2,1)} copy(bf16[4,128,1,2,640]{1,4,0,3,2:T(8,128)(2,1)} %pad_maximum_fusion.3) | data formatting | bytes 2621440 | tf_op jit(solution)/shard_map/stack | solution.py:49
  29.8 4.1 %multiply_reduce_fusion = f32[]{:T(128)} fusion(bf16[2,1,768,1024]{3,2,1,0:T(8,128)(2,1)} %param.3), kind=kLoop, calls=%fused_computation.3 | loop fusion | flops 4718591 | bytes 3145732 | tf_op jit(solution)/shard_map/reduce_sum | solution.py:92
  34.0 14.4 %psum.7 = f32[1]{0:T(128)} all-reduce(f32[1]{0:T(128)} %bitcast.13), channel_id=1, replica_groups=mesh['grp'=2,'shot'=4,'freq'=2,'sub'=2] {'shot'}, use_global_device_ids=true, to_apply=%region_2.3 | all-reduce | flops 1 | bytes 8 | tf_op jit(solution)/shard_map/psum | solution.py:93
  49.6 1.5 slice_bitcast_fusion.3
  51.4 4.6 %fusion.8 = bf16[512,2,1024]{0,2,1:T(8,128)(2,1)} fusion(bf16[1,1536,1,512]{3,1,2,0:T(8,128)(2,1)S(1)} %get-tuple-element.45, bf16[1,1536,1,512]{3,1,2,0:T(8,128)(2,1)S(1)} %get-tuple-element.44, bf16[1,768,1024]{1,2,0:T(8,128)(2,1)S(1)} %bitcast.224, bf16[1,768,1024]{1,2,0:T(8,128)(2,1)S(1)} %bitcast.220), kind=kOutput, calls=%fused_computation.31 | convolution fusion | flops 3233808384 | bytes 8388608 | tf_op jit(solution)/shard_map/qtpu,qto->uqpo/dot_general | solution.py:95
  55.9 5.0 %copy.32 = bf16[512,2,1024]{2,1,0:T(2,128)(2,1)S(1)} copy(bf16[512,2,1024]{0,2,1:T(8,128)(2,1)} %fusion.8) | data formatting | bytes 4194304 | tf_op jit(solution)/shard_map/qtpu,qto->uqpo/transpose | solution.py:95
  63.0 2.8 %gather_fusion = bf16[256,2,1024]{2,1,0:T(2,128)(2,1)S(1)} fusion(bf16[512,2,1024]{2,1,0:T(2,128)(2,1)S(1)} %copy.32, s32[1024]{0:T(1024)S(1)} %pad_clamp_fusion), kind=kCustom, calls=%fused_computation | custom fusion | bytes 2098176 | tf_op jit(solution)/shard_map/jit(_take)/gather | solution.py:100
  65.8 1.5 fusion.11
  67.4 31.0 %all-gather.2.cloned.1.call-done = bf16[512,1,2,640]{3,0,2,1:T(8,128)(2,1)} async-done(((bf16[128,1,2,640]{3,0,2,1:T(8,128)(2,1)}), bf16[512,1,2,640]{3,0,2,1:T(8,128)(2,1)}) %all-gather.2.cloned.1.call-update) | async-done | bytes 1310736 | tf_op jit(solution)/shard_map/all_gather | solution.py:113
  98.7 1.5 collective-permute-start.2
  103.1 4.5 %collective-permute-done.2 = bf16[64,1,2,1024]{3,0,1,2:T(8,128)(2,1)S(1)} collective-permute-done((bf16[64,1,2,1024]{3,0,1,2:T(8,128)(2,1)S(1)}, bf16[64,1,2,1024]{3,0,1,2:T(8,128)(2,1)S(1)}, u32[]{:S(2)}, u32[]{:S(2)}) %collective-permute-start.2) | collective-permute-done | bytes 262176 | tf_op jit(solution)/shard_map/ppermute | solution.py:111
  107.6 16.9 %collective-permute-done.1 = bf16[64,1,2,1024]{3,0,1,2:T(8,128)(2,1)S(1)} collective-permute-done((bf16[64,1,2,1024]{3,0,1,2:T(8,128)(2,1)S(1)}, bf16[64,1,2,1024]{3,0,1,2:T(8,128)(2,1)S(1)}, u32[]{:S(2)}, u32[]{:S(2)}) %collective-permute-start.1) | collective-permute-done | bytes 262176 | tf_op jit(solution)/shard_map/ppermute | solution.py:111
  126.5 2.0 %select_bitcast_fusion.1 = (bf16[4,1,128,1,2,640]{5,2,1,0,4,3:T(8,128)(2,1)S(1)}, bf16[4,1,128,1,2,640]{5,2,1,0,4,3:T(8,128)(2,1)S(1)}) fusion(bf16[4,128,1,2,640]{4,1,0,3,2:T(8,128)(2,1)} %bitcast.232, bf16[4,128,1,2,640]{4,1,0,3,2:T(8,128)(2,1)} %collective-permute-done.3, pred[]{:T(512)S(6)} %eq.10), kind=kLoop, calls=%fused_computation.42 | loop fusion | flops 1310720 | bytes 5242881 | tf_op jit(solution)/shard_map/stack | solution.py:120
  129.5 2.4 %copy.36 = bf16[2,1,8,128,1024]{4,3,2,0,1:T(8,128)(2,1)} copy(bf16[2,1,8,128,1024]{4,3,0,1,2:T(8,128)(2,1)S(1)} %bitcast.225) | data formatting | bytes 8388608 | tf_op jit(solution)/shard_map/transpose | solution.py:59
  131.9 6.2 %copy.37 = bf16[2,1,1024,1024]{2,3,0,1:T(8,128)(2,1)} copy(bf16[2,1,1024,1024]{3,2,0,1:T(8,128)(2,1)} %bitcast.216) | data formatting | bytes 8388608 | tf_op jit(solution)/shard_map/reshape;reshape | solution.py:66
  138.2 2.6 %fusion.79 = (bf16[1,1,1024,1024]{3,2,0,1:T(8,128)(2,1)S(1)}, bf16[1,1,1024,1024]{3,2,0,1:T(8,128)(2,1)S(1)}) fusion(bf16[2,1,1024,1024]{3,2,0,1:T(8,128)(2,1)} %bitcast.217), kind=kLoop, calls=%fused_computation.157 | loop fusion | flops 1048576 | bytes 8388608 | tf_op jit(solution)/shard_map/slice | solution.py:61
  141.6 2.5 %divide_convert_fusion = bf16[2,1,1024,1024]{3,2,0,1:T(8,128)(2,1)S(1)} fusion(bf16[1,1,1024,1024]{3,2,0,1:T(8,128)(2,1)S(1)} %get-tuple-element.18, bf16[1,1,1024,1024]{3,2,0,1:T(8,128)(2,1)S(1)} %get-tuple-element.17, f32[]{:T(128)} %bitcast.30, pred[1024,1024]{1,0:T(8,128)(4,1)S(1)} %bitcast.230, bf16[2,1,8,128,1024]{4,3,2,0,1:T(8,128)(2,1)S(1)} %copy-done), kind=kLoop, calls=%fused_computation.1 | loop fusion | flops 10485760 | bytes 13631492 | tf_op jit(solution)/shard_map/convert_element_type | solution.py:128
  (81 shorter events, 27.2 us)
Async XLA Ops:
  6.5 60.8 %reduce-scatter.2.cloned.1.call-start = ((), (), s32[]{:S(2)}) async-start(), calls=%async_computation.1 | async-start | bytes 1638400 | tf_op jit(solution)/shard_map/reduce_scatter | solution.py:90
  11.0 2.0 %copy-start.2 = (bf16[1,1,768,1024]{2,3,1,0:T(8,128)(2,1)S(1)}, bf16[1,1,768,1024]{2,3,1,0:T(8,128)(2,1)}, u32[]{:S(2)}) copy-start(bf16[1,1,768,1024]{2,3,1,0:T(8,128)(2,1)} %copy.40) | copy-start | bytes 4718596
  19.0 1.3 copy-start.1
  29.8 68.5 %all-gather.2.cloned.1.call-start = ((), (), s32[]{:S(2)}) async-start(), calls=%async_computation.2 | async-start | bytes 1638400 | tf_op jit(solution)/shard_map/all_gather | solution.py:113
  55.9 5.1 %copy-start.4 = (s32[512]{0:T(512)S(1)}, s32[512]{0:T(512)}, u32[]{:S(2)}) copy-start(s32[512]{0:T(512)} %param.5) | copy-start | bytes 6148
  98.3 28.1 %collective-permute-start.3 = (bf16[4,128,1,2,640]{4,1,0,3,2:T(8,128)(2,1)}, bf16[4,128,1,2,640]{4,1,0,3,2:T(8,128)(2,1)}, u32[]{:S(2)}, u32[]{:S(2)}) collective-permute-start(bf16[4,128,1,2,640]{4,1,0,3,2:T(8,128)(2,1)} %bitcast.231), channel_id=1, source_target_pairs={{0,1},{1,0},{2,3},{3,2},{4,5},{5,4},{6,7},{7,6},{8,9},{9,8},{10,11... | collective-permute-start | bytes 3932168 | tf_op jit(solution)/shard_map/ppermute | solution.py:117
  98.7 8.9 %collective-permute-start.2 = (bf16[64,1,2,1024]{3,0,1,2:T(8,128)(2,1)S(1)}, bf16[64,1,2,1024]{3,0,1,2:T(8,128)(2,1)S(1)}, u32[]{:S(2)}, u32[]{:S(2)}) collective-permute-start(bf16[64,1,2,1024]{3,0,1,2:T(8,128)(2,1)S(1)} %get-tuple-element.42), channel_id=1, source_target_pairs={{0,12},{4,0},{8,4},{12,8},{1,13},{5,1},{9,5},{13,9},{2,14},{6,2},{... | collective-permute-start | bytes 786440 | tf_op jit(solution)/shard_map/ppermute | solution.py:111
  100.2 24.4 %collective-permute-start.1 = (bf16[64,1,2,1024]{3,0,1,2:T(8,128)(2,1)S(1)}, bf16[64,1,2,1024]{3,0,1,2:T(8,128)(2,1)S(1)}, u32[]{:S(2)}, u32[]{:S(2)}) collective-permute-start(bf16[64,1,2,1024]{3,0,1,2:T(8,128)(2,1)S(1)} %get-tuple-element.43), channel_id=1, source_target_pairs={{0,8},{4,12},{8,0},{12,4},{1,9},{5,13},{9,1},{13,5},{2,10},{6,14},... | collective-permute-start | bytes 786440 | tf_op jit(solution)/shard_map/ppermute | solution.py:111
  101.0 23.5 %collective-permute-start = (bf16[64,1,2,1024]{3,0,1,2:T(8,128)(2,1)S(1)}, bf16[64,1,2,1024]{3,0,1,2:T(8,128)(2,1)}, u32[]{:S(2)}, u32[]{:S(2)}) collective-permute-start(bf16[64,1,2,1024]{3,0,1,2:T(8,128)(2,1)S(1)} %get-tuple-element.41), channel_id=1, source_target_pairs={{0,4},{4,8},{8,12},{12,0},{1,5},{5,9},{9,13},{13,1},{2,6},{6,10},{... | collective-permute-start | bytes 786440 | tf_op jit(solution)/shard_map/ppermute | solution.py:111
  124.5 0.7 copy-start.3
  138.2 3.4 %copy-start = (bf16[2,1,8,128,1024]{4,3,2,0,1:T(8,128)(2,1)S(1)}, bf16[2,1,8,128,1024]{4,3,2,0,1:T(8,128)(2,1)}, u32[]{:S(2)}) copy-start(bf16[2,1,8,128,1024]{4,3,2,0,1:T(8,128)(2,1)} %copy.36) | copy-start | bytes 12582916
Sparse Core Ops, SparseCore 0:
  29.9 34.0 reduce-scatter.1
  67.5 30.8 all-gather.1

commit v13 on v11

--- a/solution.py
+++ b/solution.py
@@ -66,6 +66,25 @@
     return whole.reshape(upper.shape)
 
 
+def line_gather(block, shot_count, shot_index):
+    rightward = [(k, k + 1) for k in range(shot_count - 1)]
+    leftward = [(k + 1, k) for k in range(shot_count - 1)]
+    from_below, from_above = [], []
+    moving_up, moving_down = block, block
+    for step in range(1, shot_count):
+        moving_up = lax.ppermute(moving_up, "shot", perm=rightward)
+        moving_down = lax.ppermute(moving_down, "shot", perm=leftward)
+        from_below.append(moving_up)
+        from_above.append(moving_down)
+    arrivals = jnp.stack(from_below[::-1] + [block] + from_above)
+    return jnp.stack(
+        [
+            lax.dynamic_index_in_dim(arrivals, k + shot_count - 1 - shot_index, 0, keepdims=False)
+            for k in range(shot_count)
+        ]
+    )
+
+
 def per_device(downgoing, upgoing, source_order):
     shot_count = lax.axis_size("shot")
     core_count = lax.axis_size("sub")
@@ -109,8 +128,7 @@
         pairs = [(k, (k + shift) % shot_count) for k in range(shot_count)]
         corr = corr + lax.ppermute(outgoing, "shot", perm=pairs).astype(jnp.float32)
 
-    across = lax.all_gather(gram_strip, "shot", axis=0, tiled=True)
-    across = across.reshape(shot_count, rows_each, freq_local, 2, span)
+    across = line_gather(gram_strip, shot_count, shot_index)
 
     if core_count == 2:
         other = lax.ppermute(across, "sub", perm=[(0, 1), (1, 0)])

time: 146 us -> 149 us (1.021)
  waiting for transfers between devices: 35 us -> 19.5 us
  starting transfers between devices: 3.49 us -> 17 us
  local copies, waits for them, and re-layouts: 34.3 us -> 37.8 us
  other arithmetic: 24.4 us -> 26.2 us
    all_gather x1 -> x0, waiting for transfers between devices: 31 us -> none  [per_device(): across = lax.all_gather(gram_strip, 'shot', axis=0, tiled=True)]
    ppermute x0 -> x6, starting transfers between devices: none -> 14 us  [the longest x3 9.98 us: line_gather(): moving_up = lax.ppermute(moving_up, 'shot', perm=rightward)]
    ppermute x0 -> x6, waiting for transfers between devices: none -> 13.8 us  [the longest x3 10.6 us: line_gather(): moving_up = lax.ppermute(moving_up, 'shot', perm=rightward)]
    unnamed x15 -> x27, local copies, waits for them, and re-layouts: 5.91 us -> 8.78 us
    ppermute x3, waiting for transfers between devices: 3.94 us -> 5.63 us  [per_device(): corr = corr + lax.ppermute(outgoing, 'shot', perm=pairs).astype(jnp.float32)]
  transfers between devices with their start and end apart: 6 -> 11, of which waited for: 2 -> 5; matrix products, arithmetic and copies ran while one was open for 29% -> 30% of each run, Pallas kernels for 0% -> 0%
where the time goes in v13:
time: 149 us; the launch traced here: 148 us
  local copies, waits for them, and re-layouts  37.8 us (25%)
  other arithmetic  26.2 us (18%)
  waiting for transfers between devices  19.5 us (13%)
  matrix products  18.9 us (13%)
  starting transfers between devices  17 us (11%)
  between operations  14.7 us (10%)
  blocking collectives  14.3 us (10%)
    psum x1, blocking collectives, per_device(): power = lax.psum(local_power, 'shot') / receivers  14.3 us
    ppermute x3, waiting for transfers between devices, line_gather(): moving_up = lax.ppermute(moving_up, 'shot', perm=rightward)  10.6 us
    ppermute x3, starting transfers between devices, line_gather(): moving_up = lax.ppermute(moving_up, 'shot', perm=rightward)  9.98 us
    unnamed x27, local copies, waits for them, and re-layouts  8.78 us
    another operation x1, local copies, waits for them, and re-layouts, rebuild_gram(): whole = jnp.where(direct, upper.reshape(shape6), mirror.reshape(shape6))  6.26 us
    ppermute x3, waiting for transfers between devices, per_device(): corr = corr + lax.ppermute(outgoing, 'shot', perm=pairs).astype(jnp.float32)  5.63 us
    transpose x1, local copies, waits for them, and re-layouts, per_device(): jnp.einsum('qtpu,qto->uqpo', stacked_left(upgoing), right, preferred_elem...  5.05 us
    dot_general x1, matrix products, per_device(): jnp.einsum('qtpu,qto->uqpo', stacked_left(upgoing), right, preferred_elem...  4.61 us
  transfers between devices with their start and end apart: 11, of which 5 were waited for; matrix products, arithmetic and copies ran while one was open for 30% of the time, Pallas kernels for 0%

profile of v13, /device:TPU:0, one launch (start us, length us, event | category | flops | bytes accessed | tf_op | source)
XLA Modules:
  0.0 148.4 jit_solution(14016180568291337130)
XLA Ops:
  6.5 2.2 %fusion.90 = (bf16[1,1,768,1024]{3,2,1,0:T(8,128)(2,1)S(1)}, bf16[1,1,768,1024]{3,2,1,0:T(8,128)(2,1)S(1)}) fusion(bf16[2,1,768,1024]{3,2,1,0:T(8,128)(2,1)} %param.3), kind=kLoop, calls=%fused_computation.182 | loop fusion | bytes 6291456 | tf_op jit(solution)/shard_map/slice | solution.py:26
  8.7 1.6 %copy.53 = bf16[1,1,768,1024]{2,3,1,0:T(8,128)(2,1)} copy(bf16[1,1,768,1024]{3,2,1,0:T(8,128)(2,1)S(1)} %get-tuple-element.19) | data formatting | bytes 3145728
  13.0 1.7 %fusion.27 = (bf16[1,1,1536,1024]{2,3,1,0:T(8,128)(2,1)S(1)}, bf16[1,1,1536,1024]{2,3,1,0:T(8,128)(2,1)S(1)}) fusion(bf16[1,768,1024]{1,2,0:T(8,128)(2,1)S(1)} %bitcast.252, bf16[1,768,1024]{1,2,0:T(8,128)(2,1)S(1)} %bitcast.248, bf16[1,768,1024]{1,2,0:T(8,128)(2,1)} %bitcast_negate_fusion), kind=kLoop, calls=%fused_computation.67 | loop fusion | flops 12582912 | bytes 11010048 | tf_op jit(solution)/shard_map/stack | solution.py:16
  15.3 3.7 %convert_bitcast_fusion = bf16[4,128,1,2,1024]{1,4,0,3,2:T(8,128)(2,1)S(1)} fusion(bf16[1,2,4,2,128,1536]{5,4,3,2,1,0:T(8,128)(2,1)S(1)} %bitcast.251, s32[]{:T(128)S(6)} %select_n.133, bf16[1,768,1024]{1,2,0:T(8,128)(2,1)S(1)} %bitcast.253, bf16[1,768,1024]{1,2,0:T(8,128)(2,1)S(1)} %bitcast.249), kind=kOutput, calls=%fused_computation.38 | convolution fusion | flops 3228565504 | bytes 8388612 | tf_op jit(solution)/shard_map/qpkit,qto->kiqpo/dot_general | solution.py:106
  20.3 2.9 %pad_slice_fusion.11 = (bf16[1,128,1,2,2048]{1,4,0,3,2:T(8,128)(2,1)}, bf16[1,128,1,2,2048]{1,4,0,3,2:T(8,128)(2,1)}, bf16[1,128,1,2,2048]{1,4,0,3,2:T(8,128)(2,...) fusion(bf16[4,128,1,2,1024]{1,4,0,3,2:T(8,128)(2,1)S(1)} %conve, ...), kind=kLoop, calls=%fused_computation.15 | loop fusion | bytes 8388608 | tf_op jit(solution)/shard_map/slice | solution.py:47
  27.4 2.4 %copy.40 = bf16[4,128,1,2,640]{4,1,0,3,2:T(8,128)(2,1)} copy(bf16[4,128,1,2,640]{1,4,0,3,2:T(8,128)(2,1)} %pad_maximum_fusion.3) | data formatting | bytes 2621440 | tf_op jit(solution)/shard_map/stack | solution.py:48
  29.9 4.1 %multiply_reduce_fusion = f32[]{:T(128)} fusion(bf16[2,1,768,1024]{3,2,1,0:T(8,128)(2,1)} %param.3), kind=kLoop, calls=%fused_computation.3 | loop fusion | flops 4718591 | bytes 3145732 | tf_op jit(solution)/shard_map/reduce_sum | solution.py:110
  34.0 14.3 %psum.7 = f32[1]{0:T(128)} all-reduce(f32[1]{0:T(128)} %bitcast.13), channel_id=1, replica_groups=mesh['grp'=2,'shot'=4,'freq'=2,'sub'=2] {'shot'}, use_global_device_ids=true, to_apply=%region_2.3 | all-reduce | flops 1 | bytes 8 | tf_op jit(solution)/shard_map/psum | solution.py:111
  50.4 4.6 %fusion.8 = bf16[512,2,1024]{0,2,1:T(8,128)(2,1)} fusion(bf16[1,1536,1,512]{3,1,2,0:T(8,128)(2,1)S(1)} %get-tuple-element.47, bf16[1,1536,1,512]{3,1,2,0:T(8,128)(2,1)S(1)} %get-tuple-element.46, bf16[1,768,1024]{1,2,0:T(8,128)(2,1)S(1)} %bitcast.254, bf16[1,768,1024]{1,2,0:T(8,128)(2,1)S(1)} %bitcast.250), kind=kOutput, calls=%fused_computation.32 | convolution fusion | flops 3233808384 | bytes 8388608 | tf_op jit(solution)/shard_map/qtpu,qto->uqpo/dot_general | solution.py:113
  55.0 5.0 %copy.41 = bf16[512,2,1024]{2,1,0:T(2,128)(2,1)S(1)} copy(bf16[512,2,1024]{0,2,1:T(8,128)(2,1)} %fusion.8) | data formatting | bytes 4194304 | tf_op jit(solution)/shard_map/qtpu,qto->uqpo/transpose | solution.py:113
  62.1 2.8 %gather_fusion = bf16[256,2,1024]{2,1,0:T(2,128)(2,1)S(1)} fusion(bf16[512,2,1024]{2,1,0:T(2,128)(2,1)S(1)} %copy.41, s32[1024]{0:T(1024)S(1)} %pad_clamp_fusion), kind=kCustom, calls=%fused_computation | custom fusion | bytes 2098176 | tf_op jit(solution)/shard_map/jit(_take)/gather | solution.py:118
  64.8 2.3 %fusion.11 = bf16[256,1,2,1024]{3,2,0,1:T(2,128)(2,1)} fusion(bf16[256,2,1024]{2,1,0:T(2,128)(2,1)S(1)} %gather_fusion, pred[256]{0:T(512)(128)(4,1)S(1)} %compare_and_fusion), kind=kLoop, calls=%fused_computation.37 | loop fusion | flops 524288 | bytes 2097408 | tf_op jit(solution)/shard_map/convert_element_type | solution.py:118
  69.7 4.3 %collective-permute-done.3 = bf16[128,1,2,640]{3,0,2,1:T(8,128)(2,1)S(1)} collective-permute-done((bf16[128,1,2,640]{3,0,2,1:T(8,128)(2,1)}, bf16[128,1,2,640]{3,0,2,1:T(8,128)(2,1)S(1)}, u32[]{:S(2)}, u32[]{:S(2)}) %collective-permute-start.3) | collective-permute-done | bytes 327712 | tf_op jit(solution)/shard_map/ppermute | solution.py:75
  74.1 4.3 %collective-permute-start.4 = (bf16[128,1,2,640]{3,0,2,1:T(8,128)(2,1)S(1)}, bf16[128,1,2,640]{3,0,2,1:T(8,128)(2,1)S(1)}, u32[]{:S(2)}, u32[]{:S(2)}) collective-permute-start(bf16[128,1,2,640]{3,0,2,1:T(8,128)(2,1)S(1)} %collective-permute-done.3), channel_id=1, source_target_pairs={{0,4},{4,8},{8,12},{1,5},{5,9},{9,13},{2,6},{6,10},{10,14},{3,7},{... | collective-permute-start | bytes 983048 | tf_op jit(solution)/shard_map/ppermute | solution.py:75
  79.7 3.2 %collective-permute-done.4 = bf16[128,1,2,640]{3,0,2,1:T(8,128)(2,1)S(1)} collective-permute-done((bf16[128,1,2,640]{3,0,2,1:T(8,128)(2,1)S(1)}, bf16[128,1,2,640]{3,0,2,1:T(8,128)(2,1)S(1)}, u32[]{:S(2)}, u32[]{:S(2)}) %collective-permute-start.4) | collective-permute-done | bytes 327712 | tf_op jit(solution)/shard_map/ppermute | solution.py:75
  82.9 4.4 %collective-permute-start.5 = (bf16[128,1,2,640]{3,0,2,1:T(8,128)(2,1)S(1)}, bf16[128,1,2,640]{3,0,2,1:T(8,128)(2,1)S(1)}, u32[]{:S(2)}, u32[]{:S(2)}) collective-permute-start(bf16[128,1,2,640]{3,0,2,1:T(8,128)(2,1)S(1)} %collective-permute-done.4), channel_id=1, source_target_pairs={{0,4},{4,8},{8,12},{1,5},{5,9},{9,13},{2,6},{6,10},{10,14},{3,7},{... | collective-permute-start | bytes 983048 | tf_op jit(solution)/shard_map/ppermute | solution.py:75
  88.8 3.1 %collective-permute-done.5 = bf16[128,1,2,640]{3,0,2,1:T(8,128)(2,1)S(1)} collective-permute-done((bf16[128,1,2,640]{3,0,2,1:T(8,128)(2,1)S(1)}, bf16[128,1,2,640]{3,0,2,1:T(8,128)(2,1)S(1)}, u32[]{:S(2)}, u32[]{:S(2)}) %collective-permute-start.5) | collective-permute-done | bytes 327712 | tf_op jit(solution)/shard_map/ppermute | solution.py:75
  93.1 3.2 %collective-permute-done.8 = bf16[128,1,2,640]{3,0,2,1:T(8,128)(2,1)S(1)} collective-permute-done((bf16[128,1,2,640]{3,0,2,1:T(8,128)(2,1)S(1)}, bf16[128,1,2,640]{3,0,2,1:T(8,128)(2,1)S(1)}, u32[]{:S(2)}, u32[]{:S(2)}) %collective-permute-start.8) | collective-permute-done | bytes 327712 | tf_op jit(solution)/shard_map/ppermute | solution.py:76
  102.2 2.7 %collective-permute-start.1 = (bf16[64,1,2,1024]{3,0,1,2:T(8,128)(2,1)}, bf16[64,1,2,1024]{3,0,1,2:T(8,128)(2,1)S(1)}, u32[]{:S(2)}, u32[]{:S(2)}) collective-permute-start(bf16[64,1,2,1024]{3,0,1,2:T(8,128)(2,1)} %get-tuple-element.45), channel_id=1, source_target_pairs={{0,8},{4,12},{8,0},{12,4},{1,9},{5,13},{9,1},{13,5},{2,10},{6,14},... | collective-permute-start | bytes 786440 | tf_op jit(solution)/shard_map/ppermute | solution.py:129
  107.1 2.4 %copy.49 = bf16[2,1,8,128,1024]{4,3,2,0,1:T(8,128)(2,1)} copy(bf16[2,1,8,128,1024]{4,3,0,1,2:T(8,128)(2,1)S(1)} %bitcast.255) | data formatting | bytes 8388608 | tf_op jit(solution)/shard_map/transpose | solution.py:58
  109.5 6.3 %copy.50 = bf16[2,1,1024,1024]{2,3,0,1:T(8,128)(2,1)} copy(bf16[2,1,1024,1024]{3,2,0,1:T(8,128)(2,1)} %bitcast.246) | data formatting | bytes 8388608 | tf_op jit(solution)/shard_map/reshape;reshape | solution.py:65
  115.8 2.6 %fusion.89 = (bf16[1,1,1024,1024]{3,2,0,1:T(8,128)(2,1)S(1)}, bf16[1,1,1024,1024]{3,2,0,1:T(8,128)(2,1)S(1)}) fusion(bf16[2,1,1024,1024]{3,2,0,1:T(8,128)(2,1)} %bitcast.247), kind=kLoop, calls=%fused_computation.181 | loop fusion | flops 1048576 | bytes 8388608 | tf_op jit(solution)/shard_map/slice | solution.py:60
  119.5 2.5 %divide_convert_fusion = bf16[2,1,1024,1024]{3,2,0,1:T(8,128)(2,1)S(1)} fusion(bf16[1,1,1024,1024]{3,2,0,1:T(8,128)(2,1)S(1)} %get-tuple-element.18, bf16[1,1,1024,1024]{3,2,0,1:T(8,128)(2,1)S(1)} %get-tuple-element.17, f32[]{:T(128)} %bitcast.30, pred[1024,1024]{1,0:T(8,128)(4,1)S(1)} %bitcast.260, bf16[2,1,8,128,1024]{4,3,2,0,1:T(8,128)(2,1)S(1)} %copy-done), kind=kLoop, calls=%fused_computation.1 | loop fusion | flops 10485760 | bytes 13631492 | tf_op jit(solution)/shard_map/convert_element_type | solution.py:145
  123.0 5.6 %collective-permute-done.1 = bf16[64,1,2,1024]{3,0,1,2:T(8,128)(2,1)S(1)} collective-permute-done((bf16[64,1,2,1024]{3,0,1,2:T(8,128)(2,1)}, bf16[64,1,2,1024]{3,0,1,2:T(8,128)(2,1)S(1)}, u32[]{:S(2)}, u32[]{:S(2)}) %collective-permute-start.1) | collective-permute-done | bytes 262176 | tf_op jit(solution)/shard_map/ppermute | solution.py:129
  (107 shorter events, 41.5 us)
Async XLA Ops:
  6.5 60.6 %reduce-scatter.2.cloned.1.call-start = ((), (), s32[]{:S(2)}) async-start(), calls=%async_computation.1 | async-start | bytes 1638400 | tf_op jit(solution)/shard_map/reduce_scatter | solution.py:108
  11.1 2.0 %copy-start.2 = (bf16[1,1,768,1024]{2,3,1,0:T(8,128)(2,1)S(1)}, bf16[1,1,768,1024]{2,3,1,0:T(8,128)(2,1)}, u32[]{:S(2)}) copy-start(bf16[1,1,768,1024]{2,3,1,0:T(8,128)(2,1)} %copy.53) | copy-start | bytes 4718596
  19.0 1.3 copy-start.1
  48.3 1.6 %copy-start.5 = (bf16[2,1,768,512]{3,2,1,0:T(8,128)(2,1)S(1)}, bf16[2,1,768,512]{3,2,1,0:T(8,128)(2,1)}, u32[]{:S(2)}) copy-start(bf16[2,1,768,512]{3,2,1,0:T(8,128)(2,1)} %param.4) | copy-start | bytes 4718596
  55.0 5.1 %copy-start.6 = (s32[512]{0:T(512)S(1)}, s32[512]{0:T(512)}, u32[]{:S(2)}) copy-start(s32[512]{0:T(512)} %param.5) | copy-start | bytes 6148
  67.1 6.9 %collective-permute-start.3 = (bf16[128,1,2,640]{3,0,2,1:T(8,128)(2,1)}, bf16[128,1,2,640]{3,0,2,1:T(8,128)(2,1)S(1)}, u32[]{:S(2)}, u32[]{:S(2)}) collective-permute-start(bf16[128,1,2,640]{3,0,2,1:T(8,128)(2,1)} %reduce-scatter.2.cloned.1.call-done), channel_id=1, source_target_pairs={{0,4},{4,8},{8,12},{1,5},{5,9},{9,13},{2,6},{6,10},{10,14},{3,7},{... | collective-permute-start | bytes 983048 | tf_op jit(solution)/shard_map/ppermute | solution.py:75
  68.4 9.9 %collective-permute-start.6 = (bf16[128,1,2,640]{3,0,2,1:T(8,128)(2,1)}, bf16[128,1,2,640]{3,0,2,1:T(8,128)(2,1)S(1)}, u32[]{:S(2)}, u32[]{:S(2)}) collective-permute-start(bf16[128,1,2,640]{3,0,2,1:T(8,128)(2,1)} %reduce-scatter.2.cloned.1.call-done), channel_id=1, source_target_pairs={{4,0},{8,4},{12,8},{5,1},{9,5},{13,9},{6,2},{10,6},{14,10},{7,3},{... | collective-permute-start | bytes 983048 | tf_op jit(solution)/shard_map/ppermute | solution.py:76
  74.1 8.9 %collective-permute-start.4 = (bf16[128,1,2,640]{3,0,2,1:T(8,128)(2,1)S(1)}, bf16[128,1,2,640]{3,0,2,1:T(8,128)(2,1)S(1)}, u32[]{:S(2)}, u32[]{:S(2)}) collective-permute-start(bf16[128,1,2,640]{3,0,2,1:T(8,128)(2,1)S(1)} %collective-permute-done.3), channel_id=1, source_target_pairs={{0,4},{4,8},{8,12},{1,5},{5,9},{9,13},{2,6},{6,10},{10,14},{3,7},{... | collective-permute-start | bytes 983048 | tf_op jit(solution)/shard_map/ppermute | solution.py:75
  78.4 9.0 %collective-permute-start.7 = (bf16[128,1,2,640]{3,0,2,1:T(8,128)(2,1)S(1)}, bf16[128,1,2,640]{3,0,2,1:T(8,128)(2,1)S(1)}, u32[]{:S(2)}, u32[]{:S(2)}) collective-permute-start(bf16[128,1,2,640]{3,0,2,1:T(8,128)(2,1)S(1)} %collective-permute-done.6), channel_id=1, source_target_pairs={{4,0},{8,4},{12,8},{5,1},{9,5},{13,9},{6,2},{10,6},{14,10},{7,3},{... | collective-permute-start | bytes 983048 | tf_op jit(solution)/shard_map/ppermute | solution.py:76
  82.9 9.0 %collective-permute-start.5 = (bf16[128,1,2,640]{3,0,2,1:T(8,128)(2,1)S(1)}, bf16[128,1,2,640]{3,0,2,1:T(8,128)(2,1)S(1)}, u32[]{:S(2)}, u32[]{:S(2)}) collective-permute-start(bf16[128,1,2,640]{3,0,2,1:T(8,128)(2,1)S(1)} %collective-permute-done.4), channel_id=1, source_target_pairs={{0,4},{4,8},{8,12},{1,5},{5,9},{9,13},{2,6},{6,10},{10,14},{3,7},{... | collective-permute-start | bytes 983048 | tf_op jit(solution)/shard_map/ppermute | solution.py:75
  87.3 9.0 %collective-permute-start.8 = (bf16[128,1,2,640]{3,0,2,1:T(8,128)(2,1)S(1)}, bf16[128,1,2,640]{3,0,2,1:T(8,128)(2,1)S(1)}, u32[]{:S(2)}, u32[]{:S(2)}) collective-permute-start(bf16[128,1,2,640]{3,0,2,1:T(8,128)(2,1)S(1)} %collective-permute-done.7), channel_id=1, source_target_pairs={{4,0},{8,4},{12,8},{5,1},{9,5},{13,9},{6,2},{10,6},{14,10},{7,3},{... | collective-permute-start | bytes 983048 | tf_op jit(solution)/shard_map/ppermute | solution.py:76
  97.8 7.4 %collective-permute-start.9 = (bf16[4,128,1,2,640]{4,1,3,0,2:T(8,128)(2,1)}, bf16[4,128,1,2,640]{4,1,3,0,2:T(8,128)(2,1)S(1)}, u32[]{:S(2)}, u32[]{:S(2)}) collective-permute-start(bf16[4,128,1,2,640]{4,1,3,0,2:T(8,128)(2,1)} %fusion.56), channel_id=1, source_target_pairs={{0,1},{1,0},{2,3},{3,2},{4,5},{5,4},{6,7},{7,6},{8,9},{9,8},{10,11... | collective-permute-start | bytes 3932168 | tf_op jit(solution)/shard_map/ppermute | solution.py:134
  101.2 4.0 %copy-start.3 = (bf16[256,1,2,1024]{3,0,2,1:T(8,128)(2,1)}, bf16[256,1,2,1024]{3,0,2,1:T(8,128)(2,1)S(1)}, u32[]{:S(2)}) copy-start(bf16[256,1,2,1024]{3,0,2,1:T(8,128)(2,1)S(1)} %copy.42) | copy-start | bytes 3145732
  102.2 20.8 %collective-permute-start.2 = (bf16[64,1,2,1024]{3,0,1,2:T(8,128)(2,1)}, bf16[64,1,2,1024]{3,0,1,2:T(8,128)(2,1)S(1)}, u32[]{:S(2)}, u32[]{:S(2)}) collective-permute-start(bf16[64,1,2,1024]{3,0,1,2:T(8,128)(2,1)} %get-tuple-element.44), channel_id=1, source_target_pairs={{0,12},{4,0},{8,4},{12,8},{1,13},{5,1},{9,5},{13,9},{2,14},{6,2},{... | collective-permute-start | bytes 786440 | tf_op jit(solution)/shard_map/ppermute | solution.py:129
  102.2 26.5 %collective-permute-start.1 = (bf16[64,1,2,1024]{3,0,1,2:T(8,128)(2,1)}, bf16[64,1,2,1024]{3,0,1,2:T(8,128)(2,1)S(1)}, u32[]{:S(2)}, u32[]{:S(2)}) collective-permute-start(bf16[64,1,2,1024]{3,0,1,2:T(8,128)(2,1)} %get-tuple-element.45), channel_id=1, source_target_pairs={{0,8},{4,12},{8,0},{12,4},{1,9},{5,13},{9,1},{13,5},{2,10},{6,14},... | collective-permute-start | bytes 786440 | tf_op jit(solution)/shard_map/ppermute | solution.py:129
  104.9 23.8 %collective-permute-start = (bf16[64,1,2,1024]{3,0,1,2:T(8,128)(2,1)S(1)}, bf16[64,1,2,1024]{3,0,1,2:T(8,128)(2,1)}, u32[]{:S(2)}, u32[]{:S(2)}) collective-permute-start(bf16[64,1,2,1024]{3,0,1,2:T(8,128)(2,1)S(1)} %get-tuple-element.43), channel_id=1, source_target_pairs={{0,4},{4,8},{8,12},{12,0},{1,5},{5,9},{9,13},{13,1},{2,6},{6,10},{... | collective-permute-start | bytes 786440 | tf_op jit(solution)/shard_map/ppermute | solution.py:129
  115.8 3.4 %copy-start = (bf16[2,1,8,128,1024]{4,3,2,0,1:T(8,128)(2,1)S(1)}, bf16[2,1,8,128,1024]{4,3,2,0,1:T(8,128)(2,1)}, u32[]{:S(2)}) copy-start(bf16[2,1,8,128,1024]{4,3,2,0,1:T(8,128)(2,1)} %copy.49) | copy-start | bytes 12582916
  115.8 3.7 %copy-start.4 = (pred[128,8,8,128]{3,1,2,0:T(8,128)(4,1)S(1)}, pred[128,8,8,128]{3,1,2,0:T(8,128)(4,1)}, u32[]{:S(2)}) copy-start(pred[128,8,8,128]{3,1,2,0:T(8,128)(4,1)} %copy.58) | copy-start | bytes 3145732
Sparse Core Ops, SparseCore 0:
  30.0 34.0 reduce-scatter.1

commit v14 on v11

--- a/solution.py
+++ b/solution.py
@@ -88,9 +88,6 @@
     gram_part = strip_partials(gram_rows, shot_count, core_count, core_index, rows_each, tile, span)
     gram_strip = lax.psum_scatter(gram_part, "shot", scatter_dimension=0, tiled=True)
 
-    local_power = jnp.sum(jnp.square(downgoing.astype(jnp.float32)), axis=(0, 2, 3))
-    power = lax.psum(local_power, "shot") / receivers
-
     corr_all = jnp.einsum(
         "qtpu,qto->uqpo", stacked_left(upgoing), right, preferred_element_type=jnp.float32
     )
@@ -98,8 +95,7 @@
     own_order = lax.dynamic_slice_in_dim(order_table, core_index, 1, 1).reshape(-1)
     corr_part = jnp.take(corr_all, own_order, axis=0).astype(jnp.bfloat16)
 
-    gram_strip, power, corr_part = lax.optimization_barrier((gram_strip, power, corr_part))
-    power_wide = power[None, :, None, None]
+    gram_strip, corr_part, power_trace = lax.optimization_barrier((gram_strip, corr_part, downgoing))
 
     shot_index = lax.axis_index("shot")
     corr_blocks = corr_part.reshape(shot_count, source_local, *corr_part.shape[1:])
@@ -111,6 +107,10 @@
 
     across = lax.all_gather(gram_strip, "shot", axis=0, tiled=True)
     across = across.reshape(shot_count, rows_each, freq_local, 2, span)
+    local_power = jnp.sum(jnp.square(power_trace.astype(jnp.float32)), axis=(0, 2, 3))
+    power = lax.psum(local_power, "shot") / receivers
+    across, power = lax.optimization_barrier((across, power))
+    power_wide = power[None, :, None, None]
 
     if core_count == 2:
         other = lax.ppermute(across, "sub", perm=[(0, 1), (1, 0)])

time: 146 us -> 144 us (0.986)
  local copies, waits for them, and re-layouts: 34.3 us -> 38.4 us
  blocking collectives: 14.4 us -> 10.4 us
    all_gather x1, waiting for transfers between devices: 31 us -> 19.9 us  [per_device(): across = lax.all_gather(gram_strip, 'shot', axis=0, tiled=True)]
    reduce_scatter x1, waiting for transfers between devices: 0.02 us -> 9.92 us  [per_device(): lax.psum_scatter(gram_part, 'shot', scatter_dimension=0, tiled=True)]
    psum x1, blocking collectives: 14.4 us -> 10.4 us  [per_device(): power = lax.psum(local_power, 'shot') / receivers]
    gather x1, local copies, waits for them, and re-layouts: 2.75 us -> 5.26 us  [per_device(): corr_part = jnp.take(corr_all, own_order, axis=0).astype(jnp.bfloat16)]
    reduce_sum x1, other arithmetic: 4.11 us -> 2.22 us  [per_device(): jnp.sum(jnp.square(power_trace.astype(jnp.float32)), axis=(0, 2, 3))]
    convert_element_type x1, other arithmetic: 1.5 us -> 3.25 us  [per_device(): corr_part = jnp.take(corr_all, own_order, axis=0).astype(jnp.bfloat16)]
    unnamed x15 -> x19, local copies, waits for them, and re-layouts: 5.91 us -> 5.9 us
  transfers between devices with their start and end apart: 6 -> 6, of which waited for: 2 -> 3; matrix products, arithmetic and copies ran while one was open for 29% -> 32% of each run, Pallas kernels for 0% -> 0%
where the time goes in v14:
time: 144 us
  local copies, waits for them, and re-layouts  38.4 us (27%)
  waiting for transfers between devices  33.8 us (23%)
  other arithmetic  24.3 us (17%)
  matrix products  18.9 us (13%)
  between operations  14.6 us (10%)
  blocking collectives  10.4 us (7%)
  starting transfers between devices  3.4 us (2%)
    all_gather x1, waiting for transfers between devices, per_device(): across = lax.all_gather(gram_strip, 'shot', axis=0, tiled=True)  19.9 us
    psum x1, blocking collectives, per_device(): power = lax.psum(local_power, 'shot') / receivers  10.4 us
    reduce_scatter x1, waiting for transfers between devices, per_device(): lax.psum_scatter(gram_part, 'shot', scatter_dimension=0, tiled=True)  9.92 us
    transpose x1, local copies, waits for them, and re-layouts, per_device(): jnp.einsum('qtpu,qto->uqpo', stacked_left(upgoing), right, preferred_elem...  6.29 us
    another operation x1, local copies, waits for them, and re-layouts, rebuild_gram(): whole = jnp.where(direct, upper.reshape(shape6), mirror.reshape(shape6))  6.24 us
    unnamed x19, local copies, waits for them, and re-layouts  5.9 us
    gather x1, local copies, waits for them, and re-layouts, per_device(): corr_part = jnp.take(corr_all, own_order, axis=0).astype(jnp.bfloat16)  5.26 us
    dot_general x1, matrix products, per_device(): jnp.einsum('qtpu,qto->uqpo', stacked_left(upgoing), right, preferred_elem...  4.57 us
  transfers between devices with their start and end apart: 6, of which 3 were waited for; matrix products, arithmetic and copies ran while one was open for 32% of the time, Pallas kernels for 0%

profile of v14, /device:TPU:0, one launch (start us, length us, event | category | flops | bytes accessed | tf_op | source)
XLA Modules:
  0.0 143.6 jit_solution(1805498605549089845)
XLA Ops:
  6.5 2.2 %fusion.88 = (bf16[1,1,768,1024]{3,2,1,0:T(8,128)(2,1)S(1)}, bf16[1,1,768,1024]{3,2,1,0:T(8,128)(2,1)S(1)}) fusion(bf16[2,1,768,1024]{3,2,1,0:T(8,128)(2,1)} %param.3), kind=kLoop, calls=%fused_computation.168 | loop fusion | bytes 6291456 | tf_op jit(solution)/shard_map/slice | solution.py:26
  8.7 1.6 %copy.40 = bf16[1,1,768,1024]{2,3,1,0:T(8,128)(2,1)} copy(bf16[1,1,768,1024]{3,2,1,0:T(8,128)(2,1)S(1)} %get-tuple-element.23) | data formatting | bytes 3145728
  13.0 1.7 %fusion.26 = (bf16[1,1,1536,1024]{2,3,1,0:T(8,128)(2,1)S(1)}, bf16[1,1,1536,1024]{2,3,1,0:T(8,128)(2,1)S(1)}) fusion(bf16[1,768,1024]{1,2,0:T(8,128)(2,1)S(1)} %bitcast.230, bf16[1,768,1024]{1,2,0:T(8,128)(2,1)S(1)} %bitcast.226, bf16[1,768,1024]{1,2,0:T(8,128)(2,1)} %bitcast_negate_fusion), kind=kLoop, calls=%fused_computation.65 | loop fusion | flops 12582912 | bytes 11010048 | tf_op jit(solution)/shard_map/stack | solution.py:16
  15.3 3.7 %convert_bitcast_fusion = bf16[4,128,1,2,1024]{1,4,0,3,2:T(8,128)(2,1)S(1)} fusion(bf16[1,2,4,2,128,1536]{5,4,3,2,1,0:T(8,128)(2,1)S(1)} %bitcast.229, s32[]{:T(128)S(6)} %select_n.120, bf16[1,768,1024]{1,2,0:T(8,128)(2,1)S(1)} %bitcast.231, bf16[1,768,1024]{1,2,0:T(8,128)(2,1)S(1)} %bitcast.227), kind=kOutput, calls=%fused_computation.37 | convolution fusion | flops 3228565504 | bytes 8388612 | tf_op jit(solution)/shard_map/qpkit,qto->kiqpo/dot_general | solution.py:87
  20.3 2.8 %pad_slice_fusion.11 = (bf16[1,128,1,2,2048]{1,4,0,3,2:T(8,128)(2,1)}, bf16[1,128,1,2,2048]{1,4,0,3,2:T(8,128)(2,1)}, bf16[1,128,1,2,2048]{1,4,0,3,2:T(8,128)(2,...) fusion(bf16[4,128,1,2,1024]{1,4,0,3,2:T(8,128)(2,1)S(1)} %conve, ...), kind=kLoop, calls=%fused_computation.15 | loop fusion | bytes 8388608 | tf_op jit(solution)/shard_map/slice | solution.py:47
  23.1 1.5 %fusion.54 = (bf16[1,128,1,2,640]{1,4,0,3,2:T(8,128)(2,1)S(1)}, bf16[1,128,1,2,640]{1,4,0,3,2:T(8,128)(2,1)S(1)}) fusion(s32[]{:T(128)S(6)} %select_n.128, bf16[4,128,1,2,1024]{1,4,0,3,2:T(8,128)(2,1)} %copy-done.2, bf16[1,128,1,2,2048]{1,4,0,3,2:T(8,128)(2,1)} %get-tuple-element.37, s32[]{:T(128)S(6)} %select_n.122, ...), kind=kLoop, calls=%fused_computation.109 | loop fusion | flops 1310720 | bytes 3407880 | tf_op jit(solution)/shard_map/concatenate | solution.py:43
  24.6 1.5 %dynamic-slice_maximum_fusion = (bf16[1,128,1,2,640]{1,4,0,3,2:T(8,128)(2,1)S(1)}, bf16[1,128,1,2,640]{1,4,0,3,2:T(8,128)(2,1)S(1)}) fusion(bf16[1,128,1,2,2048]{1,4,0,3,2:T(8,128)(2,1)} %get-tuple-element.40, s32[]{:T(128)S(6)} %select_n.126, bf16[1,128,1,2,2048]{1,4,0,3,2:T(8,128)(2,1)} %get-tuple-element.39, ...), kind=kLoop, calls=%fused_computation.110 | loop fusion | flops 1310720 | bytes 1966088 | tf_op jit(solution)/shard_map/concatenate | solution.py:43
  27.3 2.4 %copy.31 = bf16[4,128,1,2,640]{4,1,0,3,2:T(8,128)(2,1)} copy(bf16[4,128,1,2,640]{1,4,0,3,2:T(8,128)(2,1)} %pad_maximum_fusion.3) | data formatting | bytes 2621440 | tf_op jit(solution)/shard_map/stack | solution.py:48
  31.0 1.5 %slice_bitcast_fusion.3 = (bf16[1,768,512]{2,1,0:T(8,128)(2,1)S(1)}, bf16[1,768,512]{2,1,0:T(8,128)(2,1)S(1)}) fusion(bf16[2,1,768,512]{3,2,1,0:T(8,128)(2,1)} %param.4), kind=kLoop, calls=%fused_computation.67 | loop fusion | bytes 3145728 | tf_op jit(solution)/shard_map/squeeze | solution.py:20
  32.8 4.6 %fusion.8 = bf16[512,2,1024]{0,2,1:T(8,128)(2,1)} fusion(bf16[1,1536,1,512]{3,1,2,0:T(8,128)(2,1)S(1)} %get-tuple-element.49, bf16[1,1536,1,512]{3,1,2,0:T(8,128)(2,1)S(1)} %get-tuple-element.48, bf16[1,768,1024]{1,2,0:T(8,128)(2,1)S(1)} %bitcast.232, bf16[1,768,1024]{1,2,0:T(8,128)(2,1)S(1)} %bitcast.228), kind=kOutput, calls=%fused_computation.31 | convolution fusion | flops 3233808384 | bytes 8388608 | tf_op jit(solution)/shard_map/qtpu,qto->uqpo/dot_general | solution.py:91
  37.4 6.3 %copy.32 = bf16[512,2,1024]{2,1,0:T(2,128)(2,1)} copy(bf16[512,2,1024]{0,2,1:T(8,128)(2,1)} %fusion.8) | data formatting | bytes 4194304 | tf_op jit(solution)/shard_map/qtpu,qto->uqpo/transpose | solution.py:91
  45.4 5.3 %gather_fusion = bf16[256,2,1024]{2,1,0:T(2,128)(2,1)} fusion(bf16[512,2,1024]{2,1,0:T(2,128)(2,1)} %copy.32, s32[1024]{0:T(1024)S(1)} %pad_clamp_fusion), kind=kCustom, calls=%fused_computation | custom fusion | bytes 2098176 | tf_op jit(solution)/shard_map/jit(_take)/gather | solution.py:96
  50.7 3.2 %fusion.11 = bf16[256,1,2,1024]{3,2,0,1:T(2,128)(2,1)} fusion(bf16[256,2,1024]{2,1,0:T(2,128)(2,1)} %gather_fusion, pred[256]{0:T(512)(128)(4,1)S(1)} %compare_and_fusion), kind=kLoop, calls=%fused_computation.36 | loop fusion | flops 524288 | bytes 2097408 | tf_op jit(solution)/shard_map/convert_element_type | solution.py:96
  54.0 9.9 %reduce-scatter.2.cloned.1.call-done = bf16[128,1,2,640]{3,0,2,1:T(8,128)(2,1)} async-done(((bf16[512,1,2,640]{3,0,2,1:T(8,128)(2,1)}), bf16[128,1,2,640]{3,0,2,1:T(8,128)(2,1)}) %reduce-scatter.2.cloned.1.call-update) | async-done | bytes 327696 | tf_op jit(solution)/shard_map/reduce_scatter | solution.py:89
  63.9 2.2 %multiply_reduce_fusion = f32[]{:T(128)} fusion(bf16[2,1,768,1024]{3,2,1,0:T(8,128)(2,1)S(1)} %copy-done.1), kind=kLoop, calls=%fused_computation.3 | loop fusion | flops 4718591 | bytes 3145732 | tf_op jit(solution)/shard_map/reduce_sum | solution.py:110
  66.1 10.4 %psum.7 = f32[1]{0:T(128)} all-reduce(f32[1]{0:T(128)} %bitcast.30), channel_id=1, replica_groups=mesh['grp'=2,'shot'=4,'freq'=2,'sub'=2] {'shot'}, use_global_device_ids=true, to_apply=%region_2.3 | all-reduce | flops 1 | bytes 8 | tf_op jit(solution)/shard_map/psum | solution.py:111
  77.1 19.9 %all-gather.2.cloned.1.call-done = bf16[512,1,2,640]{3,0,2,1:T(8,128)(2,1)} async-done(((bf16[128,1,2,640]{3,0,2,1:T(8,128)(2,1)}), bf16[512,1,2,640]{3,0,2,1:T(8,128)(2,1)}) %all-gather.2.cloned.1.call-update) | async-done | bytes 1310736 | tf_op jit(solution)/shard_map/all_gather | solution.py:108
  99.0 1.3 collective-permute-start.2
  102.4 2.0 %select_bitcast_fusion.1 = (bf16[4,1,128,1,2,640]{5,2,1,0,4,3:T(8,128)(2,1)S(1)}, bf16[4,1,128,1,2,640]{5,2,1,0,4,3:T(8,128)(2,1)S(1)}) fusion(bf16[4,128,1,2,640]{4,1,0,3,2:T(8,128)(2,1)} %bitcast.240, bf16[4,128,1,2,640]{4,1,0,3,2:T(8,128)(2,1)} %collective-permute-done.3, pred[]{:T(512)S(6)} %eq.10), kind=kLoop, calls=%fused_computation.42 | loop fusion | flops 1310720 | bytes 5242881 | tf_op jit(solution)/shard_map/stack | solution.py:119
  105.5 2.4 %copy.36 = bf16[2,1,8,128,1024]{4,3,2,0,1:T(8,128)(2,1)} copy(bf16[2,1,8,128,1024]{4,3,0,1,2:T(8,128)(2,1)S(1)} %bitcast.233) | data formatting | bytes 8388608 | tf_op jit(solution)/shard_map/transpose | solution.py:58
  107.8 6.2 %copy.37 = bf16[2,1,1024,1024]{2,3,0,1:T(8,128)(2,1)} copy(bf16[2,1,1024,1024]{3,2,0,1:T(8,128)(2,1)} %bitcast.224) | data formatting | bytes 8388608 | tf_op jit(solution)/shard_map/reshape;reshape | solution.py:65
  114.1 2.6 %fusion.87 = (bf16[1,1,1024,1024]{3,2,0,1:T(8,128)(2,1)S(1)}, bf16[1,1,1024,1024]{3,2,0,1:T(8,128)(2,1)S(1)}) fusion(bf16[2,1,1024,1024]{3,2,0,1:T(8,128)(2,1)} %bitcast.225), kind=kLoop, calls=%fused_computation.167 | loop fusion | flops 1048576 | bytes 8388608 | tf_op jit(solution)/shard_map/slice | solution.py:60
  117.5 2.5 %divide_convert_fusion = bf16[2,1,1024,1024]{3,2,0,1:T(8,128)(2,1)S(1)} fusion(bf16[1,1,1024,1024]{3,2,0,1:T(8,128)(2,1)S(1)} %get-tuple-element.22, bf16[1,1,1024,1024]{3,2,0,1:T(8,128)(2,1)S(1)} %get-tuple-element.21, f32[]{:T(128)} %bitcast.31, pred[1024,1024]{1,0:T(8,128)(4,1)S(1)} %bitcast.238, bf16[2,1,8,128,1024]{4,3,2,0,1:T(8,128)(2,1)S(1)} %copy-done), kind=kLoop, calls=%fused_computation.1 | loop fusion | flops 10485760 | bytes 13631492 | tf_op jit(solution)/shard_map/convert_element_type | solution.py:127
  121.0 4.0 %collective-permute-done.1 = bf16[64,1,2,1024]{3,0,1,2:T(8,128)(2,1)S(1)} collective-permute-done((bf16[64,1,2,1024]{3,0,1,2:T(8,128)(2,1)S(1)}, bf16[64,1,2,1024]{3,0,1,2:T(8,128)(2,1)S(1)}, u32[]{:S(2)}, u32[]{:S(2)}) %collective-permute-start.1) | collective-permute-done | bytes 262176 | tf_op jit(solution)/shard_map/ppermute | solution.py:106
  (85 shorter events, 27.5 us)
Async XLA Ops:
  6.5 57.3 %reduce-scatter.2.cloned.1.call-start = ((), (), s32[]{:S(2)}) async-start(), calls=%async_computation.1 | async-start | bytes 1638400 | tf_op jit(solution)/shard_map/reduce_scatter | solution.py:89
  11.0 2.0 %copy-start.3 = (bf16[1,1,768,1024]{2,3,1,0:T(8,128)(2,1)S(1)}, bf16[1,1,768,1024]{2,3,1,0:T(8,128)(2,1)}, u32[]{:S(2)}) copy-start(bf16[1,1,768,1024]{2,3,1,0:T(8,128)(2,1)} %copy.40) | copy-start | bytes 4718596
  19.0 1.3 copy-start.2
  29.8 67.3 %all-gather.2.cloned.1.call-start = ((), (), s32[]{:S(2)}) async-start(), calls=%async_computation.2 | async-start | bytes 1638400 | tf_op jit(solution)/shard_map/all_gather | solution.py:108
  37.4 6.3 %copy-start.5 = (s32[512]{0:T(512)S(1)}, s32[512]{0:T(512)}, u32[]{:S(2)}) copy-start(s32[512]{0:T(512)} %param.5) | copy-start | bytes 6148
  43.7 20.2 %copy-start.1 = (bf16[2,1,768,1024]{3,2,1,0:T(8,128)(2,1)S(1)}, bf16[2,1,768,1024]{3,2,1,0:T(8,128)(2,1)}, u32[]{:S(2)}) copy-start(bf16[2,1,768,1024]{3,2,1,0:T(8,128)(2,1)} %param.3) | copy-start | bytes 9437188
  66.1 31.8 %copy-start.4 = (bf16[256,1,2,1024]{3,2,0,1:T(2,128)(2,1)S(1)}, bf16[256,1,2,1024]{3,2,0,1:T(2,128)(2,1)}, u32[]{:S(2)}) copy-start(bf16[256,1,2,1024]{3,2,0,1:T(2,128)(2,1)} %fusion.11) | copy-start | bytes 3145732
  97.0 5.3 %collective-permute-start.3 = (bf16[4,128,1,2,640]{4,1,0,3,2:T(8,128)(2,1)}, bf16[4,128,1,2,640]{4,1,0,3,2:T(8,128)(2,1)}, u32[]{:S(2)}, u32[]{:S(2)}) collective-permute-start(bf16[4,128,1,2,640]{4,1,0,3,2:T(8,128)(2,1)} %bitcast.239), channel_id=1, source_target_pairs={{0,1},{1,0},{2,3},{3,2},{4,5},{5,4},{6,7},{7,6},{8,9},{9,8},{10,11... | collective-permute-start | bytes 3932168 | tf_op jit(solution)/shard_map/ppermute | solution.py:116
  99.0 21.9 %collective-permute-start.2 = (bf16[64,1,2,1024]{3,0,1,2:T(8,128)(2,1)}, bf16[64,1,2,1024]{3,0,1,2:T(8,128)(2,1)S(1)}, u32[]{:S(2)}, u32[]{:S(2)}) collective-permute-start(bf16[64,1,2,1024]{3,0,1,2:T(8,128)(2,1)} %get-tuple-element.46), channel_id=1, source_target_pairs={{0,12},{4,0},{8,4},{12,8},{1,13},{5,1},{9,5},{13,9},{2,14},{6,2},{... | collective-permute-start | bytes 786440 | tf_op jit(solution)/shard_map/ppermute | solution.py:106
  100.4 24.6 %collective-permute-start.1 = (bf16[64,1,2,1024]{3,0,1,2:T(8,128)(2,1)S(1)}, bf16[64,1,2,1024]{3,0,1,2:T(8,128)(2,1)S(1)}, u32[]{:S(2)}, u32[]{:S(2)}) collective-permute-start(bf16[64,1,2,1024]{3,0,1,2:T(8,128)(2,1)S(1)} %get-tuple-element.47), channel_id=1, source_target_pairs={{0,8},{4,12},{8,0},{12,4},{1,9},{5,13},{9,1},{13,5},{2,10},{6,14},... | collective-permute-start | bytes 786440 | tf_op jit(solution)/shard_map/ppermute | solution.py:106
  101.2 23.8 %collective-permute-start = (bf16[64,1,2,1024]{3,0,1,2:T(8,128)(2,1)S(1)}, bf16[64,1,2,1024]{3,0,1,2:T(8,128)(2,1)S(1)}, u32[]{:S(2)}, u32[]{:S(2)}) collective-permute-start(bf16[64,1,2,1024]{3,0,1,2:T(8,128)(2,1)S(1)} %get-tuple-element.45), channel_id=1, source_target_pairs={{0,4},{4,8},{8,12},{12,0},{1,5},{5,9},{9,13},{13,1},{2,6},{6,10},{... | collective-permute-start | bytes 786440 | tf_op jit(solution)/shard_map/ppermute | solution.py:106
  114.1 3.4 %copy-start = (bf16[2,1,8,128,1024]{4,3,2,0,1:T(8,128)(2,1)S(1)}, bf16[2,1,8,128,1024]{4,3,2,0,1:T(8,128)(2,1)}, u32[]{:S(2)}) copy-start(bf16[2,1,8,128,1024]{4,3,2,0,1:T(8,128)(2,1)} %copy.36) | copy-start | bytes 12582916
Sparse Core Ops, SparseCore 0:
  29.9 33.9 reduce-scatter.1
  65.4 31.5 all-gather.1

commit v15 on v14

--- a/solution.py
+++ b/solution.py
@@ -27,12 +27,17 @@
 
 
 def sweep_whole(scaled, solution, target):
+    freq_local, receivers = scaled.shape[1], scaled.shape[-1]
+    sources = target.shape[2]
+    wide = jnp.transpose(scaled, (1, 2, 0, 3)).reshape(freq_local, receivers, 2 * receivers)
     for sweep in range(SWEEPS):
         narrow = solution.astype(jnp.bfloat16)
-        real_real = jnp.einsum("qjc,qcr->qjr", narrow[0], scaled[0], preferred_element_type=jnp.float32)
-        imag_imag = jnp.einsum("qjc,qcr->qjr", narrow[1], scaled[1], preferred_element_type=jnp.float32)
-        real_imag = jnp.einsum("qjc,qcr->qjr", narrow[0], scaled[1], preferred_element_type=jnp.float32)
-        imag_real = jnp.einsum("qjc,qcr->qjr", narrow[1], scaled[0], preferred_element_type=jnp.float32)
+        stacked = jnp.concatenate([narrow[0], narrow[1]], axis=1)
+        products = jnp.einsum("qjc,qcr->qjr", stacked, wide, preferred_element_type=jnp.float32)
+        real_real = products[:, :sources, :receivers]
+        real_imag = products[:, :sources, receivers:]
+        imag_real = products[:, sources:, :receivers]
+        imag_imag = products[:, sources:, receivers:]
         image = jnp.stack([real_real - imag_imag, real_imag + imag_real])
         solution = solution + relaxation * (target - image - damping * solution)
     return solution

time: 144 us -> 151 us (1.049)
  local copies, waits for them, and re-layouts: 38.4 us -> 46.8 us
  waiting for transfers between devices: 33.8 us -> 29.8 us
  other arithmetic: 24.3 us -> 26.1 us
    transpose x0 -> x1, local copies, waits for them, and re-layouts: none -> 6.22 us  [sweep_whole(): jnp.transpose(scaled, (1, 2, 0, 3))]
    ppermute x3, waiting for transfers between devices: 3.96 us -> 0.01 us  [per_device(): corr = corr + lax.ppermute(outgoing, 'shot', perm=pairs).astype(jnp.float32)]
    transpose x0 -> x1, other arithmetic: none -> 3.89 us  [sweep_whole(): jnp.transpose(scaled, (1, 2, 0, 3))]
    convert_element_type x1 -> x0, other arithmetic: 2.47 us -> none  [per_device(): scaled = (whole.astype(jnp.float32) / power_wide).astype(jnp.bfloat16)]
    unnamed x19 -> x21, local copies, waits for them, and re-layouts: 5.9 us -> 7.78 us
    dot_general x22 -> x6, matrix products: 10.6 us -> 11.3 us  [sweep_whole(): jnp.einsum('qjc,qcr->qjr', stacked, wide, preferred_element_type=jnp.floa...]
  transfers between devices with their start and end apart: 6 -> 6, of which waited for: 3 -> 2; matrix products, arithmetic and copies ran while one was open for 32% -> 37% of each run, Pallas kernels for 0% -> 0%
where the time goes in v15:
time: 151 us
  local copies, waits for them, and re-layouts  46.8 us (31%)
  waiting for transfers between devices  29.8 us (20%)
  other arithmetic  26.1 us (17%)
  matrix products  19.5 us (13%)
  between operations  14.5 us (10%)
  blocking collectives  10.4 us (7%)
  starting transfers between devices  3.4 us (2%)
    all_gather x1, waiting for transfers between devices, per_device(): across = lax.all_gather(gram_strip, 'shot', axis=0, tiled=True)  19.9 us
    dot_general x6, matrix products, sweep_whole(): jnp.einsum('qjc,qcr->qjr', stacked, wide, preferred_element_type=jnp.floa...  11.3 us
    psum x1, blocking collectives, per_device(): power = lax.psum(local_power, 'shot') / receivers  10.4 us
    reduce_scatter x1, waiting for transfers between devices, per_device(): lax.psum_scatter(gram_part, 'shot', scatter_dimension=0, tiled=True)  9.91 us
    unnamed x21, local copies, waits for them, and re-layouts  7.78 us
    transpose x1, local copies, waits for them, and re-layouts, per_device(): jnp.einsum('qtpu,qto->uqpo', stacked_left(upgoing), right, preferred_elem...  6.29 us
    another operation x1, local copies, waits for them, and re-layouts, rebuild_gram(): whole = jnp.where(direct, upper.reshape(shape6), mirror.reshape(shape6))  6.26 us
    transpose x1, local copies, waits for them, and re-layouts, sweep_whole(): jnp.transpose(scaled, (1, 2, 0, 3))  6.22 us
  transfers between devices with their start and end apart: 6, of which 2 were waited for; matrix products, arithmetic and copies ran while one was open for 37% of the time, Pallas kernels for 0%

profile of v15, /device:TPU:0, one launch (start us, length us, event | category | flops | bytes accessed | tf_op | source)
XLA Modules:
  0.0 150.5 jit_solution(10901118086951663343)
XLA Ops:
  6.5 2.2 %fusion.91 = (bf16[1,1,768,1024]{3,2,1,0:T(8,128)(2,1)S(1)}, bf16[1,1,768,1024]{3,2,1,0:T(8,128)(2,1)S(1)}) fusion(bf16[2,1,768,1024]{3,2,1,0:T(8,128)(2,1)} %param.3), kind=kLoop, calls=%fused_computation.180 | loop fusion | bytes 6291456 | tf_op jit(solution)/shard_map/slice | solution.py:26
  8.7 1.6 %copy.41 = bf16[1,1,768,1024]{2,3,1,0:T(8,128)(2,1)} copy(bf16[1,1,768,1024]{3,2,1,0:T(8,128)(2,1)S(1)} %get-tuple-element.23) | data formatting | bytes 3145728
  13.0 1.7 %fusion.17 = (bf16[1,1,1536,1024]{2,3,1,0:T(8,128)(2,1)S(1)}, bf16[1,1,1536,1024]{2,3,1,0:T(8,128)(2,1)S(1)}) fusion(bf16[1,768,1024]{1,2,0:T(8,128)(2,1)S(1)} %bitcast.224, bf16[1,768,1024]{1,2,0:T(8,128)(2,1)S(1)} %bitcast.220, bf16[1,768,1024]{1,2,0:T(8,128)(2,1)} %bitcast_negate_fusion), kind=kLoop, calls=%fused_computation.50 | loop fusion | flops 12582912 | bytes 11010048 | tf_op jit(solution)/shard_map/stack | solution.py:16
  15.3 3.7 %convert_bitcast_fusion = bf16[4,128,1,2,1024]{1,4,0,3,2:T(8,128)(2,1)S(1)} fusion(bf16[1,2,4,2,128,1536]{5,4,3,2,1,0:T(8,128)(2,1)S(1)} %bitcast.223, s32[]{:T(128)S(6)} %select_n.120, bf16[1,768,1024]{1,2,0:T(8,128)(2,1)S(1)} %bitcast.225, bf16[1,768,1024]{1,2,0:T(8,128)(2,1)S(1)} %bitcast.221), kind=kOutput, calls=%fused_computation.42 | convolution fusion | flops 3228565504 | bytes 8388612 | tf_op jit(solution)/shard_map/qpkit,qto->kiqpo/dot_general | solution.py:92
  20.3 2.9 %pad_slice_fusion.11 = (bf16[1,128,1,2,2048]{1,4,0,3,2:T(8,128)(2,1)}, bf16[1,128,1,2,2048]{1,4,0,3,2:T(8,128)(2,1)}, bf16[1,128,1,2,2048]{1,4,0,3,2:T(8,128)(2,...) fusion(bf16[4,128,1,2,1024]{1,4,0,3,2:T(8,128)(2,1)S(1)} %conve, ...), kind=kLoop, calls=%fused_computation.15 | loop fusion | bytes 8388608 | tf_op jit(solution)/shard_map/slice | solution.py:52
  27.5 2.5 %copy.31 = bf16[4,128,1,2,640]{4,1,0,3,2:T(8,128)(2,1)} copy(bf16[4,128,1,2,640]{1,4,0,3,2:T(8,128)(2,1)} %pad_maximum_fusion.3) | data formatting | bytes 2621440 | tf_op jit(solution)/shard_map/stack | solution.py:53
  33.0 4.6 %fusion.9 = bf16[512,2,1024]{0,2,1:T(8,128)(2,1)} fusion(bf16[1,1536,1,512]{3,1,2,0:T(8,128)(2,1)S(1)} %get-tuple-element.61, bf16[1,1536,1,512]{3,1,2,0:T(8,128)(2,1)S(1)} %get-tuple-element.60, bf16[1,768,1024]{1,2,0:T(8,128)(2,1)S(1)} %bitcast.226, bf16[1,768,1024]{1,2,0:T(8,128)(2,1)S(1)} %bitcast.222), kind=kOutput, calls=%fused_computation.38 | convolution fusion | flops 3233808384 | bytes 8388608 | tf_op jit(solution)/shard_map/qtpu,qto->uqpo/dot_general | solution.py:96
  37.6 6.3 %copy.32 = bf16[512,2,1024]{2,1,0:T(2,128)(2,1)} copy(bf16[512,2,1024]{0,2,1:T(8,128)(2,1)} %fusion.9) | data formatting | bytes 4194304 | tf_op jit(solution)/shard_map/qtpu,qto->uqpo/transpose | solution.py:96
  45.6 5.3 %gather_fusion = bf16[256,2,1024]{2,1,0:T(2,128)(2,1)} fusion(bf16[512,2,1024]{2,1,0:T(2,128)(2,1)} %copy.32, s32[1024]{0:T(1024)S(1)} %pad_clamp_fusion), kind=kCustom, calls=%fused_computation | custom fusion | bytes 2098176 | tf_op jit(solution)/shard_map/jit(_take)/gather | solution.py:101
  50.9 3.3 %fusion.12 = bf16[256,1,2,1024]{3,2,0,1:T(2,128)(2,1)} fusion(bf16[256,2,1024]{2,1,0:T(2,128)(2,1)} %gather_fusion, pred[256]{0:T(512)(128)(4,1)S(1)} %compare_and_fusion), kind=kLoop, calls=%fused_computation.41 | loop fusion | flops 524288 | bytes 2097408 | tf_op jit(solution)/shard_map/convert_element_type | solution.py:101
  54.1 9.9 %reduce-scatter.2.cloned.1.call-done = bf16[128,1,2,640]{3,0,2,1:T(8,128)(2,1)} async-done(((bf16[512,1,2,640]{3,0,2,1:T(8,128)(2,1)}), bf16[128,1,2,640]{3,0,2,1:T(8,128)(2,1)}) %reduce-scatter.2.cloned.1.call-update) | async-done | bytes 327696 | tf_op jit(solution)/shard_map/reduce_scatter | solution.py:94
  64.1 2.2 %multiply_reduce_fusion = f32[]{:T(128)} fusion(bf16[2,1,768,1024]{3,2,1,0:T(8,128)(2,1)S(1)} %copy-done.2), kind=kLoop, calls=%fused_computation.3 | loop fusion | flops 4718591 | bytes 3145732 | tf_op jit(solution)/shard_map/reduce_sum | solution.py:115
  66.3 10.4 %psum.7 = f32[1]{0:T(128)} all-reduce(f32[1]{0:T(128)} %bitcast.30), channel_id=1, replica_groups=mesh['grp'=2,'shot'=4,'freq'=2,'sub'=2] {'shot'}, use_global_device_ids=true, to_apply=%region_2.3 | all-reduce | flops 1 | bytes 8 | tf_op jit(solution)/shard_map/psum | solution.py:116
  77.3 19.9 %all-gather.2.cloned.1.call-done = bf16[512,1,2,640]{3,0,2,1:T(8,128)(2,1)} async-done(((bf16[128,1,2,640]{3,0,2,1:T(8,128)(2,1)}), bf16[512,1,2,640]{3,0,2,1:T(8,128)(2,1)}) %all-gather.2.cloned.1.call-update) | async-done | bytes 1310736 | tf_op jit(solution)/shard_map/all_gather | solution.py:113
  102.6 2.0 %select_bitcast_fusion.1 = (bf16[4,1,128,1,2,640]{5,2,1,0,4,3:T(8,128)(2,1)S(1)}, bf16[4,1,128,1,2,640]{5,2,1,0,4,3:T(8,128)(2,1)S(1)}) fusion(bf16[4,128,1,2,640]{4,1,0,3,2:T(8,128)(2,1)} %bitcast.234, bf16[4,128,1,2,640]{4,1,0,3,2:T(8,128)(2,1)} %collective-permute-done.3, pred[]{:T(512)S(6)} %eq.10), kind=kLoop, calls=%fused_computation.47 | loop fusion | flops 1310720 | bytes 5242881 | tf_op jit(solution)/shard_map/stack | solution.py:124
  105.7 2.4 %copy.36 = bf16[2,1,8,128,1024]{4,3,2,0,1:T(8,128)(2,1)} copy(bf16[2,1,8,128,1024]{4,3,0,1,2:T(8,128)(2,1)S(1)} %bitcast.227) | data formatting | bytes 8388608 | tf_op jit(solution)/shard_map/transpose | solution.py:63
  108.1 6.3 %copy.37 = bf16[2,1,1024,1024]{2,3,0,1:T(8,128)(2,1)} copy(bf16[2,1,1024,1024]{3,2,0,1:T(8,128)(2,1)} %bitcast.218) | data formatting | bytes 8388608 | tf_op jit(solution)/shard_map/reshape;reshape | solution.py:70
  114.3 2.6 %fusion.90 = (bf16[1,1,1024,1024]{3,2,0,1:T(8,128)(2,1)S(1)}, bf16[1,1,1024,1024]{3,2,0,1:T(8,128)(2,1)S(1)}) fusion(bf16[2,1,1024,1024]{3,2,0,1:T(8,128)(2,1)} %bitcast.219), kind=kLoop, calls=%fused_computation.179 | loop fusion | flops 1048576 | bytes 8388608 | tf_op jit(solution)/shard_map/slice | solution.py:65
  117.8 3.9 %fusion = bf16[1,1024,2,1024]{3,1,2,0:T(8,128)(2,1)} fusion(bf16[1,1,1024,1024]{3,2,0,1:T(8,128)(2,1)S(1)} %get-tuple-element.22, bf16[1,1,1024,1024]{3,2,0,1:T(8,128)(2,1)S(1)} %get-tuple-element.21, f32[]{:T(128)} %bitcast.31, pred[1024,1024]{1,0:T(8,128)(4,1)S(1)} %bitcast.232, bf16[2,1,8,128,1024]{4,3,2,0,1:T(8,128)(2,1)S(1)} %copy-done.1), kind=kLoop, calls=%fused_computation.17 | loop fusion | flops 10485760 | bytes 13631492 | tf_op jit(solution)/shard_map/transpose | solution.py:32
  121.7 6.2 %copy.38 = bf16[1,1024,2,1024]{1,3,2,0:T(8,128)(2,1)} copy(bf16[1,1024,2,1024]{3,1,2,0:T(8,128)(2,1)} %fusion) | data formatting | bytes 8388608 | tf_op jit(solution)/shard_map/transpose | solution.py:32
  127.9 3.7 %convolution_bitcast_fusion.5 = f32[1,128,2048]{2,1,0:T(8,128)S(1)} fusion(bf16[1024,2048]{0,1:T(8,128)(2,1)} %bitcast.204, bf16[128]{0:T(256)(128)(2,1)S(1)} %concatenate.77), kind=kOutput, calls=%fused_computation.37 | convolution fusion | flops 536870912 | bytes 5243136 | tf_op jit(solution)/shard_map/qjc,qcr->qjr/dot_general | solution.py:36
  132.0 1.8 %copy-done = bf16[1,1024,2,1024]{1,3,2,0:T(8,128)(2,1)S(1)} copy-done((bf16[1,1024,2,1024]{1,3,2,0:T(8,128)(2,1)S(1)}, bf16[1,1024,2,1024]{1,3,2,0:T(8,128)(2,1)}, u32[]{:S(2)}) %copy-start) | copy-done | bytes 4194328
  137.4 1.5 %convolution_bitcast_fusion.2 = f32[1,128,2048]{2,1,0:T(8,128)S(1)} fusion(bf16[1024,2048]{0,1:T(8,128)(2,1)S(1)} %bitcast.207, bf16[1,64,1024]{2,1,0:T(8,128)(2,1)S(1)} %get-tuple-element.67, bf16[1,64,1024]{2,1,0:T(8,128)(2,1)S(1)} %get-tuple-element.66), kind=kOutput, calls=%fused_computation.34 | convolution fusion | flops 537395200 | bytes 5505024 | tf_op jit(solution)/shard_map/qjc,qcr->qjr/dot_general | solution.py:36
  139.3 1.5 %convolution_bitcast_fusion.1 = f32[1,128,2048]{2,1,0:T(8,128)S(1)} fusion(bf16[1024,2048]{0,1:T(8,128)(2,1)S(1)} %bitcast.208, bf16[1,64,1024]{2,1,0:T(8,128)(2,1)S(1)} %get-tuple-element.65, bf16[1,64,1024]{2,1,0:T(8,128)(2,1)S(1)} %get-tuple-element.64), kind=kOutput, calls=%fused_computation.33 | convolution fusion | flops 537395200 | bytes 5505024 | tf_op jit(solution)/shard_map/qjc,qcr->qjr/dot_general | solution.py:36
  (85 shorter events, 27.7 us)
Async XLA Ops:
  6.5 57.5 %reduce-scatter.2.cloned.1.call-start = ((), (), s32[]{:S(2)}) async-start(), calls=%async_computation.1 | async-start | bytes 1638400 | tf_op jit(solution)/shard_map/reduce_scatter | solution.py:94
  11.0 2.0 %copy-start.4 = (bf16[1,1,768,1024]{2,3,1,0:T(8,128)(2,1)S(1)}, bf16[1,1,768,1024]{2,3,1,0:T(8,128)(2,1)}, u32[]{:S(2)}) copy-start(bf16[1,1,768,1024]{2,3,1,0:T(8,128)(2,1)} %copy.41) | copy-start | bytes 4718596
  19.0 1.4 copy-start.3
  30.0 67.2 %all-gather.2.cloned.1.call-start = ((), (), s32[]{:S(2)}) async-start(), calls=%async_computation.2 | async-start | bytes 1638400 | tf_op jit(solution)/shard_map/all_gather | solution.py:113
  37.6 6.3 %copy-start.6 = (s32[512]{0:T(512)S(1)}, s32[512]{0:T(512)}, u32[]{:S(2)}) copy-start(s32[512]{0:T(512)} %param.5) | copy-start | bytes 6148
  43.9 20.2 %copy-start.2 = (bf16[2,1,768,1024]{3,2,1,0:T(8,128)(2,1)S(1)}, bf16[2,1,768,1024]{3,2,1,0:T(8,128)(2,1)}, u32[]{:S(2)}) copy-start(bf16[2,1,768,1024]{3,2,1,0:T(8,128)(2,1)} %param.3) | copy-start | bytes 9437188
  66.3 31.9 %copy-start.5 = (bf16[256,1,2,1024]{3,2,0,1:T(2,128)(2,1)S(1)}, bf16[256,1,2,1024]{3,2,0,1:T(2,128)(2,1)}, u32[]{:S(2)}) copy-start(bf16[256,1,2,1024]{3,2,0,1:T(2,128)(2,1)} %fusion.12) | copy-start | bytes 3145732
  97.2 5.4 %collective-permute-start.3 = (bf16[4,128,1,2,640]{4,1,0,3,2:T(8,128)(2,1)}, bf16[4,128,1,2,640]{4,1,0,3,2:T(8,128)(2,1)}, u32[]{:S(2)}, u32[]{:S(2)}) collective-permute-start(bf16[4,128,1,2,640]{4,1,0,3,2:T(8,128)(2,1)} %bitcast.233), channel_id=1, source_target_pairs={{0,1},{1,0},{2,3},{3,2},{4,5},{5,4},{6,7},{7,6},{8,9},{9,8},{10,11... | collective-permute-start | bytes 3932168 | tf_op jit(solution)/shard_map/ppermute | solution.py:121
  99.2 32.4 %collective-permute-start.2 = (bf16[64,1,2,1024]{3,0,1,2:T(8,128)(2,1)}, bf16[64,1,2,1024]{3,0,1,2:T(8,128)(2,1)S(1)}, u32[]{:S(2)}, u32[]{:S(2)}) collective-permute-start(bf16[64,1,2,1024]{3,0,1,2:T(8,128)(2,1)} %get-tuple-element.56), channel_id=1, source_target_pairs={{0,12},{4,0},{8,4},{12,8},{1,13},{5,1},{9,5},{13,9},{2,14},{6,2},{... | collective-permute-start | bytes 786440 | tf_op jit(solution)/shard_map/ppermute | solution.py:111
  100.6 31.1 %collective-permute-start.1 = (bf16[64,1,2,1024]{3,0,1,2:T(8,128)(2,1)S(1)}, bf16[64,1,2,1024]{3,0,1,2:T(8,128)(2,1)S(1)}, u32[]{:S(2)}, u32[]{:S(2)}) collective-permute-start(bf16[64,1,2,1024]{3,0,1,2:T(8,128)(2,1)S(1)} %get-tuple-element.57), channel_id=1, source_target_pairs={{0,8},{4,12},{8,0},{12,4},{1,9},{5,13},{9,1},{13,5},{2,10},{6,14},... | collective-permute-start | bytes 786440 | tf_op jit(solution)/shard_map/ppermute | solution.py:111
  101.4 30.3 %collective-permute-start = (bf16[64,1,2,1024]{3,0,1,2:T(8,128)(2,1)S(1)}, bf16[64,1,2,1024]{3,0,1,2:T(8,128)(2,1)S(1)}, u32[]{:S(2)}, u32[]{:S(2)}) collective-permute-start(bf16[64,1,2,1024]{3,0,1,2:T(8,128)(2,1)S(1)} %get-tuple-element.55), channel_id=1, source_target_pairs={{0,4},{4,8},{8,12},{12,0},{1,5},{5,9},{9,13},{13,1},{2,6},{6,10},{... | collective-permute-start | bytes 786440 | tf_op jit(solution)/shard_map/ppermute | solution.py:111
  114.3 3.4 %copy-start.1 = (bf16[2,1,8,128,1024]{4,3,2,0,1:T(8,128)(2,1)S(1)}, bf16[2,1,8,128,1024]{4,3,2,0,1:T(8,128)(2,1)}, u32[]{:S(2)}) copy-start(bf16[2,1,8,128,1024]{4,3,2,0,1:T(8,128)(2,1)} %copy.36) | copy-start | bytes 12582916
  131.6 2.2 %copy-start = (bf16[1,1024,2,1024]{1,3,2,0:T(8,128)(2,1)S(1)}, bf16[1,1024,2,1024]{1,3,2,0:T(8,128)(2,1)}, u32[]{:S(2)}) copy-start(bf16[1,1024,2,1024]{1,3,2,0:T(8,128)(2,1)} %copy.38) | copy-start | bytes 12582916
Sparse Core Ops, SparseCore 0:
  30.1 33.9 reduce-scatter.1
  65.6 31.5 all-gather.1

commit v16 on v15

--- a/solution.py
+++ b/solution.py
@@ -26,10 +26,9 @@
     return jnp.concatenate([trace[0], trace[1]], axis=1)
 
 
-def sweep_whole(scaled, solution, target):
-    freq_local, receivers = scaled.shape[1], scaled.shape[-1]
+def sweep_whole(wide, solution, target):
+    receivers = target.shape[-1]
     sources = target.shape[2]
-    wide = jnp.transpose(scaled, (1, 2, 0, 3)).reshape(freq_local, receivers, 2 * receivers)
     for sweep in range(SWEEPS):
         narrow = solution.astype(jnp.bfloat16)
         stacked = jnp.concatenate([narrow[0], narrow[1]], axis=1)
@@ -60,13 +59,13 @@
     padded = jnp.pad(strips, [(0, 0)] * 3 + [(0, receivers - span)])
     padded = padded.reshape(tiles, tile, freq_local, 2, receivers)
     upper = jnp.stack([jnp.roll(padded[a], a * tile, axis=-1) for a in range(tiles)])
-    upper = jnp.transpose(upper, (3, 2, 0, 1, 4)).reshape(2, freq_local, receivers, receivers)
-    mirror = jnp.swapaxes(upper, 2, 3)
-    mirror = jnp.stack([mirror[0], -mirror[1]])
-    row_tile = lax.broadcasted_iota(jnp.int32, (tiles, 1, tiles, 1), 0)
-    col_tile = lax.broadcasted_iota(jnp.int32, (tiles, 1, tiles, 1), 2)
+    upper = jnp.transpose(upper, (2, 0, 1, 3, 4)).reshape(freq_local, receivers, 2, receivers)
+    mirror = jnp.transpose(upper, (0, 3, 2, 1))
+    mirror = jnp.stack([mirror[:, :, 0], -mirror[:, :, 1]], axis=2)
+    row_tile = lax.broadcasted_iota(jnp.int32, (tiles, 1, 1, tiles, 1), 0)
+    col_tile = lax.broadcasted_iota(jnp.int32, (tiles, 1, 1, tiles, 1), 3)
     direct = (col_tile - row_tile) % tiles <= tiles // 2
-    shape6 = (2, freq_local, tiles, tile, tiles, tile)
+    shape6 = (freq_local, tiles, tile, 2, tiles, tile)
     whole = jnp.where(direct, upper.reshape(shape6), mirror.reshape(shape6))
     return whole.reshape(upper.shape)
 
@@ -129,7 +128,8 @@
 
     target = jnp.transpose(corr, (2, 1, 0, 3)) / power_wide
 
-    scaled = (whole.astype(jnp.float32) / power_wide).astype(jnp.bfloat16)
+    scaled = (whole.astype(jnp.float32) / power[:, None, None, None]).astype(jnp.bfloat16)
+    scaled = scaled.reshape(freq_local, receivers, 2 * receivers)
     solution = jnp.zeros((2, freq_local, source_local, receivers), jnp.float32)
     return sweep_whole(scaled, solution, target)
 

time: 151 us -> 217 us (1.44); the launches traced: 151 us -> 213 us
  local copies, waits for them, and re-layouts: 46.8 us -> 102 us
  other arithmetic: 26.1 us -> 33.2 us
    another operation x1 -> x11, local copies, waits for them, and re-layouts: 6.26 us -> 51.8 us  [rebuild_gram(): jnp.stack([jnp.roll(padded[a], a * tile, axis=-1) for a in range(tiles)])]
    unnamed x21 -> x31, local copies, waits for them, and re-layouts: 7.78 us -> 20 us
    transpose x2 -> x0, local copies, waits for them, and re-layouts: 8.62 us -> none  [the longest x1 6.22 us: sweep_whole(): jnp.transpose(scaled, (1, 2, 0, 3))]
    convert_element_type x0 -> x2, other arithmetic: none -> 6.4 us  [per_device(): (whole.astype(jnp.float32) / power[:, None, None, None]).astype(jnp.bfloa...]
    another operation x0 -> x1, other arithmetic: none -> 4.14 us  [rebuild_gram(): mirror = jnp.stack([mirror[:, :, 0], -mirror[:, :, 1]], axis=2)]
    transpose x1 -> x0, other arithmetic: 3.89 us -> none  [sweep_whole(): jnp.transpose(scaled, (1, 2, 0, 3))]
    concatenate x0 -> x4, other arithmetic: none -> 2.68 us  [rebuild_gram(): jnp.roll(padded[a], a * tile, axis=-1)]
    concatenate x0 -> x3, local copies, waits for them, and re-layouts: none -> 2.6 us  [rebuild_gram(): jnp.roll(padded[a], a * tile, axis=-1)]
  transfers between devices with their start and end apart: 6 -> 6, of which waited for: 2 -> 2; matrix products, arithmetic and copies ran while one was open for 37% -> 55% of each run, Pallas kernels for 0% -> 0%
where the time goes in v16:
time: 217 us; the launch traced here: 213 us
  local copies, waits for them, and re-layouts  102 us (47%)
  other arithmetic  33.2 us (15%)
  waiting for transfers between devices  30 us (14%)
  matrix products  18.3 us (8%)
  between operations  14.6 us (7%)
  blocking collectives  10.4 us (5%)
  starting transfers between devices  4.3 us (2%)
    another operation x11, local copies, waits for them, and re-layouts, rebuild_gram(): jnp.stack([jnp.roll(padded[a], a * tile, axis=-1) for a in range(tiles)])  51.8 us
    unnamed x31, local copies, waits for them, and re-layouts  20 us
    all_gather x1, waiting for transfers between devices, per_device(): across = lax.all_gather(gram_strip, 'shot', axis=0, tiled=True)  19.9 us
    psum x1, blocking collectives, per_device(): power = lax.psum(local_power, 'shot') / receivers  10.4 us
    reduce_scatter x1, waiting for transfers between devices, per_device(): lax.psum_scatter(gram_part, 'shot', scatter_dimension=0, tiled=True)  10.1 us
    dot_general x6, matrix products, sweep_whole(): jnp.einsum('qjc,qcr->qjr', stacked, wide, preferred_element_type=jnp.floa...  9.09 us
    convert_element_type x2, other arithmetic, per_device(): (whole.astype(jnp.float32) / power[:, None, None, None]).astype(jnp.bfloa...  6.4 us
    transpose x1, local copies, waits for them, and re-layouts, per_device(): jnp.einsum('qtpu,qto->uqpo', stacked_left(upgoing), right, preferred_elem...  6.28 us
  transfers between devices with their start and end apart: 6, of which 2 were waited for; matrix products, arithmetic and copies ran while one was open for 55% of the time, Pallas kernels for 0%

profile of v16, /device:TPU:0, one launch (start us, length us, event | category | flops | bytes accessed | tf_op | source)
XLA Modules:
  0.0 213.2 jit_solution(12088547131687888519)
XLA Ops:
  6.5 3.4 %fusion.84 = (bf16[1,1,768,1024]{3,2,1,0:T(8,128)(2,1)S(1)}, bf16[1,1,768,1024]{3,2,1,0:T(8,128)(2,1)}) fusion(bf16[2,1,768,1024]{3,2,1,0:T(8,128)(2,1)} %param.3), kind=kLoop, calls=%fused_computation.181 | loop fusion | bytes 6291456 | tf_op jit(solution)/shard_map/slice | solution.py:26
  15.7 4.6 %convert_bitcast_fusion = bf16[4,128,1,2,1024]{1,4,0,3,2:T(8,128)(2,1)} fusion(bf16[1,2,4,2,128,1536]{5,4,3,2,1,0:T(8,128)(2,1)S(1)} %bitcast.290, s32[]{:T(128)S(6)} %select_n.148, bf16[1,768,1024]{1,2,0:T(8,128)(2,1)S(1)} %bitcast.292, bf16[1,768,1024]{1,2,0:T(8,128)(2,1)S(1)} %bitcast.286), kind=kOutput, calls=%fused_computation.44 | convolution fusion | flops 3228565504 | bytes 8388612 | tf_op jit(solution)/shard_map/qpkit,qto->kiqpo/dot_general | solution.py:91
  20.4 4.8 %pad_slice_fusion.11 = (bf16[1,128,1,2,2048]{1,4,0,3,2:T(8,128)(2,1)}, bf16[1,128,1,2,2048]{1,4,0,3,2:T(8,128)(2,1)}, bf16[1,128,1,2,2048]{1,4,0,3,2:T(8,128)(2,...) fusion(bf16[4,128,1,2,1024]{1,4,0,3,2:T(8,128)(2,1)} %convert_b, ...), kind=kLoop, calls=%fused_computation.17 | loop fusion | bytes 8388608 | tf_op jit(solution)/shard_map/slice | solution.py:51
  29.5 2.5 %copy.29 = bf16[4,128,1,2,640]{4,1,0,3,2:T(8,128)(2,1)} copy(bf16[4,128,1,2,640]{1,4,0,3,2:T(8,128)(2,1)} %pad_maximum_fusion.4) | data formatting | bytes 2621440 | tf_op jit(solution)/shard_map/stack | solution.py:52
  36.3 4.6 %fusion.8 = bf16[512,2,1024]{0,2,1:T(8,128)(2,1)} fusion(bf16[1,1536,1,512]{3,1,2,0:T(8,128)(2,1)S(1)} %get-tuple-element.61, bf16[1,1536,1,512]{3,1,2,0:T(8,128)(2,1)S(1)} %get-tuple-element.60, bf16[1,768,1024]{1,2,0:T(8,128)(2,1)S(1)} %bitcast.293, bf16[1,768,1024]{1,2,0:T(8,128)(2,1)S(1)} %bitcast.287), kind=kOutput, calls=%fused_computation.40 | convolution fusion | flops 3233808384 | bytes 8388608 | tf_op jit(solution)/shard_map/qtpu,qto->uqpo/dot_general | solution.py:95
  40.9 6.3 %copy.30 = bf16[512,2,1024]{2,1,0:T(2,128)(2,1)} copy(bf16[512,2,1024]{0,2,1:T(8,128)(2,1)} %fusion.8) | data formatting | bytes 4194304 | tf_op jit(solution)/shard_map/qtpu,qto->uqpo/transpose | solution.py:95
  47.3 5.4 %gather_fusion = bf16[256,2,1024]{2,1,0:T(2,128)(2,1)} fusion(bf16[512,2,1024]{2,1,0:T(2,128)(2,1)} %copy.30, s32[1024]{0:T(1024)S(1)} %pad_clamp_fusion), kind=kCustom, calls=%fused_computation | custom fusion | bytes 2098176 | tf_op jit(solution)/shard_map/jit(_take)/gather | solution.py:100
  52.7 3.3 %fusion.11 = bf16[256,1,2,1024]{3,2,0,1:T(2,128)(2,1)} fusion(bf16[256,2,1024]{2,1,0:T(2,128)(2,1)} %gather_fusion, pred[256]{0:T(512)(128)(4,1)S(1)} %compare_and_fusion), kind=kLoop, calls=%fused_computation.43 | loop fusion | flops 524288 | bytes 2097408 | tf_op jit(solution)/shard_map/convert_element_type | solution.py:100
  55.9 10.1 %reduce-scatter.2.cloned.1.call-done = bf16[128,1,2,640]{3,0,2,1:T(8,128)(2,1)} async-done(((bf16[512,1,2,640]{3,0,2,1:T(8,128)(2,1)}), bf16[128,1,2,640]{3,0,2,1:T(8,128)(2,1)}) %reduce-scatter.2.cloned.1.call-update) | async-done | bytes 327696 | tf_op jit(solution)/shard_map/reduce_scatter | solution.py:93
  68.3 10.4 %psum.7 = f32[1]{0:T(128)} all-reduce(f32[1]{0:T(128)} %bitcast.30), channel_id=1, replica_groups=mesh['grp'=2,'shot'=4,'freq'=2,'sub'=2] {'shot'}, use_global_device_ids=true, to_apply=%region_2.3 | all-reduce | flops 1 | bytes 8 | tf_op jit(solution)/shard_map/psum | solution.py:115
  79.3 19.9 %all-gather.2.cloned.1.call-done = bf16[512,1,2,640]{3,0,2,1:T(8,128)(2,1)} async-done(((bf16[128,1,2,640]{3,0,2,1:T(8,128)(2,1)}), bf16[512,1,2,640]{3,0,2,1:T(8,128)(2,1)}) %all-gather.2.cloned.1.call-update) | async-done | bytes 1310736 | tf_op jit(solution)/shard_map/all_gather | solution.py:112
  103.3 2.4 %collective-permute-start.2 = (bf16[64,1,2,1024]{3,0,1,2:T(8,128)(2,1)}, bf16[64,1,2,1024]{3,0,1,2:T(8,128)(2,1)}, u32[]{:S(2)}, u32[]{:S(2)}) collective-permute-start(bf16[64,1,2,1024]{3,0,1,2:T(8,128)(2,1)} %get-tuple-element.56), channel_id=1, source_target_pairs={{0,12},{4,0},{8,4},{12,8},{1,13},{5,1},{9,5},{13,9},{2,14},{6,2},{... | collective-permute-start | bytes 786440 | tf_op jit(solution)/shard_map/ppermute | solution.py:110
  117.9 2.7 %copy.41 = bf16[1,1,128,2,8,128]{2,1,5,4,3,0:T(2,128)(2,1)} copy(bf16[1,1,128,2,8,128]{5,4,2,3,1,0:T(8,128)(2,1)} %bitcast.298) | data formatting | bytes 1048576 | tf_op jit(solution)/shard_map/stack | solution.py:61
  122.6 2.7 %copy.40 = bf16[1,1,128,2,8,128]{2,1,5,4,3,0:T(2,128)(2,1)} copy(bf16[1,1,128,2,8,128]{5,4,2,3,1,0:T(8,128)(2,1)} %bitcast.299) | data formatting | bytes 1048576 | tf_op jit(solution)/shard_map/stack | solution.py:61
  127.3 2.7 %copy.39 = bf16[1,1,128,2,8,128]{2,1,5,4,3,0:T(2,128)(2,1)} copy(bf16[1,1,128,2,8,128]{5,4,2,3,1,0:T(8,128)(2,1)} %bitcast.300) | data formatting | bytes 1048576 | tf_op jit(solution)/shard_map/stack | solution.py:61
  131.9 2.7 %copy.38 = bf16[1,1,128,2,8,128]{2,1,5,4,3,0:T(2,128)(2,1)} copy(bf16[1,1,128,2,8,128]{5,4,2,3,1,0:T(8,128)(2,1)} %bitcast.301) | data formatting | bytes 1048576 | tf_op jit(solution)/shard_map/stack | solution.py:61
  136.6 2.7 %copy.35 = bf16[1,1,128,2,8,128]{2,1,5,4,3,0:T(2,128)(2,1)} copy(bf16[1,1,128,2,8,128]{5,4,2,3,1,0:T(8,128)(2,1)} %bitcast.302) | data formatting | bytes 1048576 | tf_op jit(solution)/shard_map/stack | solution.py:61
  141.2 2.7 %copy.36 = bf16[1,1,128,2,8,128]{2,1,5,4,3,0:T(2,128)(2,1)} copy(bf16[1,1,128,2,8,128]{5,4,2,3,1,0:T(8,128)(2,1)} %bitcast.303) | data formatting | bytes 1048576 | tf_op jit(solution)/shard_map/stack | solution.py:61
  145.8 2.7 %copy.37 = bf16[1,1,128,2,8,128]{2,1,5,4,3,0:T(2,128)(2,1)} copy(bf16[1,1,128,2,8,128]{5,4,2,3,1,0:T(8,128)(2,1)} %bitcast.304) | data formatting | bytes 1048576 | tf_op jit(solution)/shard_map/stack | solution.py:61
  150.5 2.7 %copy.34 = bf16[1,1,128,2,8,128]{2,1,5,4,3,0:T(2,128)(2,1)} copy(bf16[1,1,128,2,8,128]{5,4,2,3,1,0:T(8,128)(2,1)} %bitcast.305) | data formatting | bytes 1048576 | tf_op jit(solution)/shard_map/stack | solution.py:61
  153.2 22.3 %stack.161 = bf16[1,8,128,2,8,128]{2,1,5,4,3,0:T(8,128)(2,1)} concatenate(bf16[1,1,128,2,8,128]{2,1,5,4,3,0:T(2,128)(2,1)} %copy.34, bf16[1,1,128,2,8,128]{2,1,5,4,3,0:T(2,128)(2,1)} %copy.35, bf16[1,1,128,2,8,128]{2,1,5,4,3,0:T(2,128)(2,1)} %copy.36, bf16[1,1,128,2,8,128]{2,1,5,4,3,0:T(2,128)(2,1)} %copy.37, bf16[1,1,128,2,8,128]{2,1,5,4,3,0:T(2,128)(2,1)} %copy.38, ...), dimensions={1} | concatenate | bytes 8388608 | tf_op jit(solution)/shard_map/stack | solution.py:61
  175.5 7.3 %stack.176 = bf16[1024,2,1024]{0,2,1:T(8,128)(2,1)} reshape(bf16[1,8,128,2,8,128]{2,1,5,4,3,0:T(8,128)(2,1)} %stack.161) | data formatting | bytes 8388608 | tf_op jit(solution)/shard_map/stack | solution.py:61
  182.8 4.1 %pad_maximum_fusion.1 = bf16[1,1024,2,1024]{1,3,2,0:T(8,128)(2,1)} fusion(bf16[1,1024,1,1024]{1,3,2,0:T(8,128)(2,1)} %get-tuple-element.22, bf16[1,1024,1,1024]{1,3,2,0:T(8,128)(2,1)S(1)} %get-tuple-element.21), kind=kLoop, calls=%fused_computation.19 | loop fusion | flops 2097152 | bytes 8388608 | tf_op jit(solution)/shard_map/stack | solution.py:64
  189.2 4.2 %divide_convert_fusion.1 = bf16[1024,2048]{0,1:T(8,128)(2,1)S(1)} fusion(bf16[256,8,8,128]{3,2,1,0:T(8,128)(2,1)S(1)} %bitcast.283, bf16[1,1024,2,1024]{1,3,2,0:T(8,128)(2,1)} %pad_maximum_fusion.1, f32[]{:T(128)} %bitcast.31, pred[1024,1024]{0,1:T(8,128)(4,1)S(1)} %bitcast.289), kind=kLoop, calls=%fused_computation.2 | loop fusion | flops 8388608 | bytes 13631492 | tf_op jit(solution)/shard_map/convert_element_type | solution.py:131
  (113 shorter events, 61.5 us)
Async XLA Ops:
  6.5 59.5 %reduce-scatter.2.cloned.1.call-start = ((), (), s32[]{:S(2)}) async-start(), calls=%async_computation.1 | async-start | bytes 1638400 | tf_op jit(solution)/shard_map/reduce_scatter | solution.py:93
  13.2 1.4 copy-start.4
  28.2 3.8 %copy-start.7 = (s32[512]{0:T(512)S(1)}, s32[512]{0:T(512)}, u32[]{:S(2)}) copy-start(s32[512]{0:T(512)} %param.5) | copy-start | bytes 6148
  31.9 67.3 %all-gather.2.cloned.1.call-start = ((), (), s32[]{:S(2)}) async-start(), calls=%async_computation.2 | async-start | bytes 1638400 | tf_op jit(solution)/shard_map/all_gather | solution.py:112
  47.2 18.9 %copy-start.3 = (bf16[2,1,768,1024]{3,2,1,0:T(8,128)(2,1)S(1)}, bf16[2,1,768,1024]{3,2,1,0:T(8,128)(2,1)}, u32[]{:S(2)}) copy-start(bf16[2,1,768,1024]{3,2,1,0:T(8,128)(2,1)} %param.3) | copy-start | bytes 9437188
  68.3 31.9 %copy-start.6 = (bf16[256,1,2,1024]{3,2,0,1:T(2,128)(2,1)S(1)}, bf16[256,1,2,1024]{3,2,0,1:T(2,128)(2,1)}, u32[]{:S(2)}) copy-start(bf16[256,1,2,1024]{3,2,0,1:T(2,128)(2,1)} %fusion.11) | copy-start | bytes 3145732
  99.2 6.5 %collective-permute-start.3 = (bf16[4,128,1,2,640]{4,1,0,3,2:T(8,128)(2,1)}, bf16[4,128,1,2,640]{4,1,0,3,2:T(8,128)(2,1)}, u32[]{:S(2)}, u32[]{:S(2)}) collective-permute-start(bf16[4,128,1,2,640]{4,1,0,3,2:T(8,128)(2,1)} %bitcast.314), channel_id=1, source_target_pairs={{0,1},{1,0},{2,3},{3,2},{4,5},{5,4},{6,7},{7,6},{8,9},{9,8},{10,11... | collective-permute-start | bytes 3932168 | tf_op jit(solution)/shard_map/ppermute | solution.py:120
  100.4 5.2 %copy-start.5 = (bf16[256,1,2,1024]{3,0,2,1:T(8,128)(2,1)}, bf16[256,1,2,1024]{3,0,2,1:T(8,128)(2,1)S(1)}, u32[]{:S(2)}) copy-start(bf16[256,1,2,1024]{3,0,2,1:T(8,128)(2,1)S(1)} %copy.31) | copy-start | bytes 3145732
  101.4 93.6 %collective-permute-start = (bf16[64,1,2,1024]{3,0,1,2:T(8,128)(2,1)}, bf16[64,1,2,1024]{3,0,1,2:T(8,128)(2,1)S(1)}, u32[]{:S(2)}, u32[]{:S(2)}) collective-permute-start(bf16[64,1,2,1024]{3,0,1,2:T(8,128)(2,1)} %get-tuple-element.55), channel_id=1, source_target_pairs={{0,4},{4,8},{8,12},{12,0},{1,5},{5,9},{9,13},{13,1},{2,6},{6,10},{... | collective-permute-start | bytes 786440 | tf_op jit(solution)/shard_map/ppermute | solution.py:110
  102.1 93.0 %collective-permute-start.1 = (bf16[64,1,2,1024]{3,0,1,2:T(8,128)(2,1)}, bf16[64,1,2,1024]{3,0,1,2:T(8,128)(2,1)}, u32[]{:S(2)}, u32[]{:S(2)}) collective-permute-start(bf16[64,1,2,1024]{3,0,1,2:T(8,128)(2,1)} %get-tuple-element.57), channel_id=1, source_target_pairs={{0,8},{4,12},{8,0},{12,4},{1,9},{5,13},{9,1},{13,5},{2,10},{6,14},... | collective-permute-start | bytes 786440 | tf_op jit(solution)/shard_map/ppermute | solution.py:110
  103.3 91.8 %collective-permute-start.2 = (bf16[64,1,2,1024]{3,0,1,2:T(8,128)(2,1)}, bf16[64,1,2,1024]{3,0,1,2:T(8,128)(2,1)}, u32[]{:S(2)}, u32[]{:S(2)}) collective-permute-start(bf16[64,1,2,1024]{3,0,1,2:T(8,128)(2,1)} %get-tuple-element.56), channel_id=1, source_target_pairs={{0,12},{4,0},{8,4},{12,8},{1,13},{5,1},{9,5},{13,9},{2,14},{6,2},{... | collective-permute-start | bytes 786440 | tf_op jit(solution)/shard_map/ppermute | solution.py:110
  182.8 4.2 %copy-start.1 = (bf16[1,1024,1,1024]{1,3,2,0:T(8,128)(2,1)S(1)}, bf16[1,1024,1,1024]{1,3,2,0:T(8,128)(2,1)}, u32[]{:S(2)}) copy-start(bf16[1,1024,1,1024]{1,3,2,0:T(8,128)(2,1)} %get-tuple-element.22) | copy-start | bytes 6291460
  182.8 4.3 %copy-start.2 = (bf16[1024,2,1024]{0,2,1:T(8,128)(2,1)S(1)}, bf16[1024,2,1024]{0,2,1:T(8,128)(2,1)}, u32[]{:S(2)}) copy-start(bf16[1024,2,1024]{0,2,1:T(8,128)(2,1)} %stack.176) | copy-start | bytes 12582916
  187.0 2.2 %copy-start = (bf16[1,8,128,2,8,128]{2,1,5,4,3,0:T(8,128)(2,1)S(1)}, bf16[1,8,128,2,8,128]{2,1,5,4,3,0:T(8,128)(2,1)}, u32[]{:S(2)}) copy-start(bf16[1,8,128,2,8,128]{2,1,5,4,3,0:T(8,128)(2,1)} %stack.161) | copy-start | bytes 12582916
Sparse Core Ops, SparseCore 0:
  32.1 33.9 reduce-scatter.1
  67.6 31.5 all-gather.1

commit v17 on v15

--- a/solution.py
+++ b/solution.py
@@ -27,9 +27,9 @@
 
 
 def sweep_whole(scaled, solution, target):
-    freq_local, receivers = scaled.shape[1], scaled.shape[-1]
+    receivers = target.shape[-1]
     sources = target.shape[2]
-    wide = jnp.transpose(scaled, (1, 2, 0, 3)).reshape(freq_local, receivers, 2 * receivers)
+    wide = jnp.concatenate([scaled[0], scaled[1]], axis=-1)
     for sweep in range(SWEEPS):
         narrow = solution.astype(jnp.bfloat16)
         stacked = jnp.concatenate([narrow[0], narrow[1]], axis=1)

time: 151 us -> 139 us (0.921)
  local copies, waits for them, and re-layouts: 46.8 us -> 39.1 us
  matrix products: 19.5 us -> 12.6 us
  waiting for transfers between devices: 29.8 us -> 33.5 us
    dot_general x6, matrix products: 11.3 us -> 4.35 us  [sweep_whole(): jnp.einsum('qjc,qcr->qjr', stacked, wide, preferred_element_type=jnp.floa...]
    transpose x1 -> x0, local copies, waits for them, and re-layouts: 6.22 us -> none  [sweep_whole(): jnp.transpose(scaled, (1, 2, 0, 3))]
    transpose x1 -> x0, other arithmetic: 3.89 us -> none  [sweep_whole(): jnp.transpose(scaled, (1, 2, 0, 3))]
    ppermute x3, waiting for transfers between devices: 0.01 us -> 3.68 us  [per_device(): corr = corr + lax.ppermute(outgoing, 'shot', perm=pairs).astype(jnp.float32)]
    convert_element_type x0 -> x1, other arithmetic: none -> 2.47 us  [per_device(): scaled = (whole.astype(jnp.float32) / power_wide).astype(jnp.bfloat16)]
    unnamed x21 -> x19, local copies, waits for them, and re-layouts: 7.78 us -> 5.95 us
  transfers between devices with their start and end apart: 6 -> 6, of which waited for: 2 -> 3; matrix products, arithmetic and copies ran while one was open for 37% -> 33% of each run, Pallas kernels for 0% -> 0%
where the time goes in v17:
time: 139 us; the launch traced here: 138 us
  local copies, waits for them, and re-layouts  39.1 us (28%)
  waiting for transfers between devices  33.5 us (24%)
  other arithmetic  24.7 us (18%)
  between operations  14.5 us (10%)
  matrix products  12.6 us (9%)
  blocking collectives  10.4 us (7%)
  starting transfers between devices  3.4 us (2%)
    all_gather x1, waiting for transfers between devices, per_device(): across = lax.all_gather(gram_strip, 'shot', axis=0, tiled=True)  19.9 us
    psum x1, blocking collectives, per_device(): power = lax.psum(local_power, 'shot') / receivers  10.4 us
    reduce_scatter x1, waiting for transfers between devices, per_device(): lax.psum_scatter(gram_part, 'shot', scatter_dimension=0, tiled=True)  9.86 us
    transpose x1, local copies, waits for them, and re-layouts, per_device(): jnp.einsum('qtpu,qto->uqpo', stacked_left(upgoing), right, preferred_elem...  6.31 us
    another operation x1, local copies, waits for them, and re-layouts, rebuild_gram(): whole = jnp.where(direct, upper.reshape(shape6), mirror.reshape(shape6))  6.27 us
    unnamed x19, local copies, waits for them, and re-layouts  5.95 us
    gather x1, local copies, waits for them, and re-layouts, per_device(): corr_part = jnp.take(corr_all, own_order, axis=0).astype(jnp.bfloat16)  5.28 us
    dot_general x1, matrix products, per_device(): jnp.einsum('qtpu,qto->uqpo', stacked_left(upgoing), right, preferred_elem...  4.58 us
  transfers between devices with their start and end apart: 6, of which 3 were waited for; matrix products, arithmetic and copies ran while one was open for 33% of the time, Pallas kernels for 0%

profile of v17, /device:TPU:0, one launch (start us, length us, event | category | flops | bytes accessed | tf_op | source)
XLA Modules:
  0.0 138.1 jit_solution(3189843580643648292)
XLA Ops:
  6.5 2.2 %fusion.90 = (bf16[1,1,768,1024]{3,2,1,0:T(8,128)(2,1)S(1)}, bf16[1,1,768,1024]{3,2,1,0:T(8,128)(2,1)S(1)}) fusion(bf16[2,1,768,1024]{3,2,1,0:T(8,128)(2,1)} %param.3), kind=kLoop, calls=%fused_computation.182 | loop fusion | bytes 6291456 | tf_op jit(solution)/shard_map/slice | solution.py:26
  8.7 1.6 %copy.41 = bf16[1,1,768,1024]{2,3,1,0:T(8,128)(2,1)} copy(bf16[1,1,768,1024]{3,2,1,0:T(8,128)(2,1)S(1)} %get-tuple-element.23) | data formatting | bytes 3145728
  13.0 1.7 %fusion.16 = (bf16[1,1,1536,1024]{2,3,1,0:T(8,128)(2,1)S(1)}, bf16[1,1,1536,1024]{2,3,1,0:T(8,128)(2,1)S(1)}) fusion(bf16[1,768,1024]{1,2,0:T(8,128)(2,1)S(1)} %bitcast.223, bf16[1,768,1024]{1,2,0:T(8,128)(2,1)S(1)} %bitcast.219, bf16[1,768,1024]{1,2,0:T(8,128)(2,1)} %bitcast_negate_fusion), kind=kLoop, calls=%fused_computation.52 | loop fusion | flops 12582912 | bytes 11010048 | tf_op jit(solution)/shard_map/stack | solution.py:16
  15.3 3.7 %convert_bitcast_fusion = bf16[4,128,1,2,1024]{1,4,0,3,2:T(8,128)(2,1)S(1)} fusion(bf16[1,2,4,2,128,1536]{5,4,3,2,1,0:T(8,128)(2,1)S(1)} %bitcast.222, s32[]{:T(128)S(6)} %select_n.120, bf16[1,768,1024]{1,2,0:T(8,128)(2,1)S(1)} %bitcast.224, bf16[1,768,1024]{1,2,0:T(8,128)(2,1)S(1)} %bitcast.220), kind=kOutput, calls=%fused_computation.44 | convolution fusion | flops 3228565504 | bytes 8388612 | tf_op jit(solution)/shard_map/qpkit,qto->kiqpo/dot_general | solution.py:92
  19.0 1.4 copy-done.2
  20.3 3.0 %pad_slice_fusion.11 = (bf16[1,128,1,2,2048]{1,4,0,3,2:T(8,128)(2,1)}, bf16[1,128,1,2,2048]{1,4,0,3,2:T(8,128)(2,1)}, bf16[1,128,1,2,2048]{1,4,0,3,2:T(8,128)(2,...) fusion(bf16[4,128,1,2,1024]{1,4,0,3,2:T(8,128)(2,1)S(1)} %conve, ...), kind=kLoop, calls=%fused_computation.15 | loop fusion | bytes 8388608 | tf_op jit(solution)/shard_map/slice | solution.py:52
  23.3 1.5 %fusion.44 = (bf16[1,128,1,2,640]{1,4,0,3,2:T(8,128)(2,1)S(1)}, bf16[1,128,1,2,640]{1,4,0,3,2:T(8,128)(2,1)S(1)}) fusion(s32[]{:T(128)S(6)} %select_n.128, bf16[4,128,1,2,1024]{1,4,0,3,2:T(8,128)(2,1)} %copy-done.2, bf16[1,128,1,2,2048]{1,4,0,3,2:T(8,128)(2,1)} %get-tuple-element.37, s32[]{:T(128)S(6)} %select_n.122, ...), kind=kLoop, calls=%fused_computation.96 | loop fusion | flops 1310720 | bytes 3407880 | tf_op jit(solution)/shard_map/concatenate | solution.py:48
  24.8 1.5 %dynamic-slice_maximum_fusion = (bf16[1,128,1,2,640]{1,4,0,3,2:T(8,128)(2,1)S(1)}, bf16[1,128,1,2,640]{1,4,0,3,2:T(8,128)(2,1)S(1)}) fusion(bf16[1,128,1,2,2048]{1,4,0,3,2:T(8,128)(2,1)} %get-tuple-element.40, s32[]{:T(128)S(6)} %select_n.126, bf16[1,128,1,2,2048]{1,4,0,3,2:T(8,128)(2,1)} %get-tuple-element.39, ...), kind=kLoop, calls=%fused_computation.97 | loop fusion | flops 1310720 | bytes 1966088 | tf_op jit(solution)/shard_map/concatenate | solution.py:48
  27.5 2.5 %copy.31 = bf16[4,128,1,2,640]{4,1,0,3,2:T(8,128)(2,1)} copy(bf16[4,128,1,2,640]{1,4,0,3,2:T(8,128)(2,1)} %pad_maximum_fusion.3) | data formatting | bytes 2621440 | tf_op jit(solution)/shard_map/stack | solution.py:53
  31.2 1.5 %slice_bitcast_fusion.3 = (bf16[1,768,512]{2,1,0:T(8,128)(2,1)S(1)}, bf16[1,768,512]{2,1,0:T(8,128)(2,1)S(1)}) fusion(bf16[2,1,768,512]{3,2,1,0:T(8,128)(2,1)} %param.4), kind=kLoop, calls=%fused_computation.54 | loop fusion | bytes 3145728 | tf_op jit(solution)/shard_map/squeeze | solution.py:20
  33.0 4.6 %fusion.8 = bf16[512,2,1024]{0,2,1:T(8,128)(2,1)} fusion(bf16[1,1536,1,512]{3,1,2,0:T(8,128)(2,1)S(1)} %get-tuple-element.61, bf16[1,1536,1,512]{3,1,2,0:T(8,128)(2,1)S(1)} %get-tuple-element.60, bf16[1,768,1024]{1,2,0:T(8,128)(2,1)S(1)} %bitcast.225, bf16[1,768,1024]{1,2,0:T(8,128)(2,1)S(1)} %bitcast.221), kind=kOutput, calls=%fused_computation.38 | convolution fusion | flops 3233808384 | bytes 8388608 | tf_op jit(solution)/shard_map/qtpu,qto->uqpo/dot_general | solution.py:96
  37.6 6.3 %copy.32 = bf16[512,2,1024]{2,1,0:T(2,128)(2,1)} copy(bf16[512,2,1024]{0,2,1:T(8,128)(2,1)} %fusion.8) | data formatting | bytes 4194304 | tf_op jit(solution)/shard_map/qtpu,qto->uqpo/transpose | solution.py:96
  45.7 5.3 %gather_fusion = bf16[256,2,1024]{2,1,0:T(2,128)(2,1)} fusion(bf16[512,2,1024]{2,1,0:T(2,128)(2,1)} %copy.32, s32[1024]{0:T(1024)S(1)} %pad_clamp_fusion), kind=kCustom, calls=%fused_computation | custom fusion | bytes 2098176 | tf_op jit(solution)/shard_map/jit(_take)/gather | solution.py:101
  50.9 3.3 %fusion.11 = bf16[256,1,2,1024]{3,2,0,1:T(2,128)(2,1)} fusion(bf16[256,2,1024]{2,1,0:T(2,128)(2,1)} %gather_fusion, pred[256]{0:T(512)(128)(4,1)S(1)} %compare_and_fusion), kind=kLoop, calls=%fused_computation.43 | loop fusion | flops 524288 | bytes 2097408 | tf_op jit(solution)/shard_map/convert_element_type | solution.py:101
  54.2 9.9 %reduce-scatter.2.cloned.1.call-done = bf16[128,1,2,640]{3,0,2,1:T(8,128)(2,1)} async-done(((bf16[512,1,2,640]{3,0,2,1:T(8,128)(2,1)}), bf16[128,1,2,640]{3,0,2,1:T(8,128)(2,1)}) %reduce-scatter.2.cloned.1.call-update) | async-done | bytes 327696 | tf_op jit(solution)/shard_map/reduce_scatter | solution.py:94
  64.1 2.2 %multiply_reduce_fusion = f32[]{:T(128)} fusion(bf16[2,1,768,1024]{3,2,1,0:T(8,128)(2,1)S(1)} %copy-done.1), kind=kLoop, calls=%fused_computation.3 | loop fusion | flops 4718591 | bytes 3145732 | tf_op jit(solution)/shard_map/reduce_sum | solution.py:115
  66.3 10.4 %psum.7 = f32[1]{0:T(128)} all-reduce(f32[1]{0:T(128)} %bitcast.30), channel_id=1, replica_groups=mesh['grp'=2,'shot'=4,'freq'=2,'sub'=2] {'shot'}, use_global_device_ids=true, to_apply=%region_2.3 | all-reduce | flops 1 | bytes 8 | tf_op jit(solution)/shard_map/psum | solution.py:116
  77.3 19.9 %all-gather.2.cloned.1.call-done = bf16[512,1,2,640]{3,0,2,1:T(8,128)(2,1)} async-done(((bf16[128,1,2,640]{3,0,2,1:T(8,128)(2,1)}), bf16[512,1,2,640]{3,0,2,1:T(8,128)(2,1)}) %all-gather.2.cloned.1.call-update) | async-done | bytes 1310736 | tf_op jit(solution)/shard_map/all_gather | solution.py:113
  102.6 2.0 %select_bitcast_fusion.1 = (bf16[4,1,128,1,2,640]{5,2,1,0,4,3:T(8,128)(2,1)S(1)}, bf16[4,1,128,1,2,640]{5,2,1,0,4,3:T(8,128)(2,1)S(1)}) fusion(bf16[4,128,1,2,640]{4,1,0,3,2:T(8,128)(2,1)} %bitcast.233, bf16[4,128,1,2,640]{4,1,0,3,2:T(8,128)(2,1)} %collective-permute-done.3, pred[]{:T(512)S(6)} %eq.10), kind=kLoop, calls=%fused_computation.49 | loop fusion | flops 1310720 | bytes 5242881 | tf_op jit(solution)/shard_map/stack | solution.py:124
  105.7 2.4 %copy.36 = bf16[2,1,8,128,1024]{4,3,2,0,1:T(8,128)(2,1)} copy(bf16[2,1,8,128,1024]{4,3,0,1,2:T(8,128)(2,1)S(1)} %bitcast.226) | data formatting | bytes 8388608 | tf_op jit(solution)/shard_map/transpose | solution.py:63
  108.1 6.3 %copy.37 = bf16[2,1,1024,1024]{2,3,0,1:T(8,128)(2,1)} copy(bf16[2,1,1024,1024]{3,2,0,1:T(8,128)(2,1)} %bitcast.216) | data formatting | bytes 8388608 | tf_op jit(solution)/shard_map/reshape;reshape | solution.py:70
  114.3 2.6 %fusion.89 = (bf16[1,1,1024,1024]{3,2,0,1:T(8,128)(2,1)S(1)}, bf16[1,1,1024,1024]{3,2,0,1:T(8,128)(2,1)S(1)}) fusion(bf16[2,1,1024,1024]{3,2,0,1:T(8,128)(2,1)} %bitcast.217), kind=kLoop, calls=%fused_computation.181 | loop fusion | flops 1048576 | bytes 8388608 | tf_op jit(solution)/shard_map/slice | solution.py:65
  117.8 2.5 %divide_convert_fusion = bf16[2,1,1024,1024]{3,2,0,1:T(8,128)(2,1)S(1)} fusion(bf16[1,1,1024,1024]{3,2,0,1:T(8,128)(2,1)S(1)} %get-tuple-element.22, bf16[1,1,1024,1024]{3,2,0,1:T(8,128)(2,1)S(1)} %get-tuple-element.21, f32[]{:T(128)} %bitcast.31, pred[1024,1024]{1,0:T(8,128)(4,1)S(1)} %bitcast.231, bf16[2,1,8,128,1024]{4,3,2,0,1:T(8,128)(2,1)S(1)} %copy-done), kind=kLoop, calls=%fused_computation.1 | loop fusion | flops 10485760 | bytes 13631492 | tf_op jit(solution)/shard_map/convert_element_type | solution.py:132
  121.5 3.7 %collective-permute-done.1 = bf16[64,1,2,1024]{3,0,1,2:T(8,128)(2,1)S(1)} collective-permute-done((bf16[64,1,2,1024]{3,0,1,2:T(8,128)(2,1)S(1)}, bf16[64,1,2,1024]{3,0,1,2:T(8,128)(2,1)S(1)}, u32[]{:S(2)}, u32[]{:S(2)}) %collective-permute-start.1) | collective-permute-done | bytes 262176 | tf_op jit(solution)/shard_map/ppermute | solution.py:111
  (84 shorter events, 22.1 us)
Async XLA Ops:
  6.5 57.5 %reduce-scatter.2.cloned.1.call-start = ((), (), s32[]{:S(2)}) async-start(), calls=%async_computation.1 | async-start | bytes 1638400 | tf_op jit(solution)/shard_map/reduce_scatter | solution.py:94
  11.1 2.0 %copy-start.3 = (bf16[1,1,768,1024]{2,3,1,0:T(8,128)(2,1)S(1)}, bf16[1,1,768,1024]{2,3,1,0:T(8,128)(2,1)}, u32[]{:S(2)}) copy-start(bf16[1,1,768,1024]{2,3,1,0:T(8,128)(2,1)} %copy.41) | copy-start | bytes 4718596
  19.0 1.4 copy-start.2
  30.0 67.2 %all-gather.2.cloned.1.call-start = ((), (), s32[]{:S(2)}) async-start(), calls=%async_computation.2 | async-start | bytes 1638400 | tf_op jit(solution)/shard_map/all_gather | solution.py:113
  37.6 6.3 %copy-start.5 = (s32[512]{0:T(512)S(1)}, s32[512]{0:T(512)}, u32[]{:S(2)}) copy-start(s32[512]{0:T(512)} %param.5) | copy-start | bytes 6148
  43.9 20.2 %copy-start.1 = (bf16[2,1,768,1024]{3,2,1,0:T(8,128)(2,1)S(1)}, bf16[2,1,768,1024]{3,2,1,0:T(8,128)(2,1)}, u32[]{:S(2)}) copy-start(bf16[2,1,768,1024]{3,2,1,0:T(8,128)(2,1)} %param.3) | copy-start | bytes 9437188
  66.3 31.8 %copy-start.4 = (bf16[256,1,2,1024]{3,2,0,1:T(2,128)(2,1)S(1)}, bf16[256,1,2,1024]{3,2,0,1:T(2,128)(2,1)}, u32[]{:S(2)}) copy-start(bf16[256,1,2,1024]{3,2,0,1:T(2,128)(2,1)} %fusion.11) | copy-start | bytes 3145732
  97.2 5.4 %collective-permute-start.3 = (bf16[4,128,1,2,640]{4,1,0,3,2:T(8,128)(2,1)}, bf16[4,128,1,2,640]{4,1,0,3,2:T(8,128)(2,1)}, u32[]{:S(2)}, u32[]{:S(2)}) collective-permute-start(bf16[4,128,1,2,640]{4,1,0,3,2:T(8,128)(2,1)} %bitcast.232), channel_id=1, source_target_pairs={{0,1},{1,0},{2,3},{3,2},{4,5},{5,4},{6,7},{7,6},{8,9},{9,8},{10,11... | collective-permute-start | bytes 3932168 | tf_op jit(solution)/shard_map/ppermute | solution.py:121
  99.2 22.2 %collective-permute-start.2 = (bf16[64,1,2,1024]{3,0,1,2:T(8,128)(2,1)}, bf16[64,1,2,1024]{3,0,1,2:T(8,128)(2,1)S(1)}, u32[]{:S(2)}, u32[]{:S(2)}) collective-permute-start(bf16[64,1,2,1024]{3,0,1,2:T(8,128)(2,1)} %get-tuple-element.56), channel_id=1, source_target_pairs={{0,12},{4,0},{8,4},{12,8},{1,13},{5,1},{9,5},{13,9},{2,14},{6,2},{... | collective-permute-start | bytes 786440 | tf_op jit(solution)/shard_map/ppermute | solution.py:111
  100.6 24.6 %collective-permute-start.1 = (bf16[64,1,2,1024]{3,0,1,2:T(8,128)(2,1)S(1)}, bf16[64,1,2,1024]{3,0,1,2:T(8,128)(2,1)S(1)}, u32[]{:S(2)}, u32[]{:S(2)}) collective-permute-start(bf16[64,1,2,1024]{3,0,1,2:T(8,128)(2,1)S(1)} %get-tuple-element.57), channel_id=1, source_target_pairs={{0,8},{4,12},{8,0},{12,4},{1,9},{5,13},{9,1},{13,5},{2,10},{6,14},... | collective-permute-start | bytes 786440 | tf_op jit(solution)/shard_map/ppermute | solution.py:111
  101.4 23.8 %collective-permute-start = (bf16[64,1,2,1024]{3,0,1,2:T(8,128)(2,1)S(1)}, bf16[64,1,2,1024]{3,0,1,2:T(8,128)(2,1)S(1)}, u32[]{:S(2)}, u32[]{:S(2)}) collective-permute-start(bf16[64,1,2,1024]{3,0,1,2:T(8,128)(2,1)S(1)} %get-tuple-element.55), channel_id=1, source_target_pairs={{0,4},{4,8},{8,12},{12,0},{1,5},{5,9},{9,13},{13,1},{2,6},{6,10},{... | collective-permute-start | bytes 786440 | tf_op jit(solution)/shard_map/ppermute | solution.py:111
  114.3 3.4 %copy-start = (bf16[2,1,8,128,1024]{4,3,2,0,1:T(8,128)(2,1)S(1)}, bf16[2,1,8,128,1024]{4,3,2,0,1:T(8,128)(2,1)}, u32[]{:S(2)}) copy-start(bf16[2,1,8,128,1024]{4,3,2,0,1:T(8,128)(2,1)} %copy.36) | copy-start | bytes 12582916
Sparse Core Ops, SparseCore 0:
  30.1 33.9 reduce-scatter.1
  65.6 31.5 all-gather.1

commit v18 on v17

--- a/solution.py
+++ b/solution.py
@@ -110,20 +110,11 @@
         pairs = [(k, (k + shift) % shot_count) for k in range(shot_count)]
         corr = corr + lax.ppermute(outgoing, "shot", perm=pairs).astype(jnp.float32)
 
-    across = lax.all_gather(gram_strip, "shot", axis=0, tiled=True)
-    across = across.reshape(shot_count, rows_each, freq_local, 2, span)
+    strips = lax.all_gather(gram_strip, ("shot", "sub"), axis=0, tiled=True)
     local_power = jnp.sum(jnp.square(power_trace.astype(jnp.float32)), axis=(0, 2, 3))
     power = lax.psum(local_power, "shot") / receivers
-    across, power = lax.optimization_barrier((across, power))
+    strips, power = lax.optimization_barrier((strips, power))
     power_wide = power[None, :, None, None]
-
-    if core_count == 2:
-        other = lax.ppermute(across, "sub", perm=[(0, 1), (1, 0)])
-        first = jnp.where(core_index == 0, across, other)
-        second = jnp.where(core_index == 0, other, across)
-        strips = jnp.stack([first, second], axis=1)
-    else:
-        strips = lax.all_gather(across, "sub", axis=1, tiled=False)
     strips = strips.reshape(receivers, freq_local, 2, span)
     whole = rebuild_gram(strips, tiles, tile)
 

time: 139 us -> 149 us (1.072)
  waiting for transfers between devices: 33.5 us -> 46.5 us
  other arithmetic: 24.7 us -> 22.6 us
    all_gather x1, waiting for transfers between devices: 19.9 us -> 33.5 us  [per_device(): strips = lax.all_gather(gram_strip, ('shot', 'sub'), axis=0, tiled=True)]
    ppermute x3, waiting for transfers between devices: 3.68 us -> 0.01 us  [per_device(): corr = corr + lax.ppermute(outgoing, 'shot', perm=pairs).astype(jnp.float32)]
    unnamed x19 -> x21, local copies, waits for them, and re-layouts: 5.95 us -> 9.06 us
    reduce_scatter x1, waiting for transfers between devices: 9.86 us -> 12.9 us  [per_device(): lax.psum_scatter(gram_part, 'shot', scatter_dimension=0, tiled=True)]
    another operation x2 -> x0, other arithmetic: 2.23 us -> none  [per_device(): strips = jnp.stack([first, second], axis=1)]
    gather x1, local copies, waits for them, and re-layouts: 5.28 us -> 3.66 us  [per_device(): corr_part = jnp.take(corr_all, own_order, axis=0).astype(jnp.bfloat16)]
  transfers between devices with their start and end apart: 6 -> 5, of which waited for: 3 -> 2; matrix products, arithmetic and copies ran while one was open for 33% -> 29% of each run, Pallas kernels for 0% -> 0%
where the time goes in v18:
time: 149 us
  waiting for transfers between devices  46.5 us (31%)
  local copies, waits for them, and re-layouts  39.6 us (27%)
  other arithmetic  22.6 us (15%)
  between operations  14.6 us (10%)
  matrix products  12.7 us (9%)
  blocking collectives  10.3 us (7%)
  starting transfers between devices  2.57 us (2%)
    all_gather x1, waiting for transfers between devices, per_device(): strips = lax.all_gather(gram_strip, ('shot', 'sub'), axis=0, tiled=True)  33.5 us
    reduce_scatter x1, waiting for transfers between devices, per_device(): lax.psum_scatter(gram_part, 'shot', scatter_dimension=0, tiled=True)  12.9 us
    psum x1, blocking collectives, per_device(): power = lax.psum(local_power, 'shot') / receivers  10.3 us
    unnamed x21, local copies, waits for them, and re-layouts  9.06 us
    another operation x1, local copies, waits for them, and re-layouts, rebuild_gram(): whole = jnp.where(direct, upper.reshape(shape6), mirror.reshape(shape6))  6.27 us
    transpose x1, local copies, waits for them, and re-layouts, per_device(): jnp.einsum('qtpu,qto->uqpo', stacked_left(upgoing), right, preferred_elem...  5.05 us
    dot_general x1, matrix products, per_device(): jnp.einsum('qtpu,qto->uqpo', stacked_left(upgoing), right, preferred_elem...  4.6 us
    dot_general x6, matrix products, sweep_whole(): jnp.einsum('qjc,qcr->qjr', stacked, wide, preferred_element_type=jnp.floa...  4.43 us
  transfers between devices with their start and end apart: 5, of which 2 were waited for; matrix products, arithmetic and copies ran while one was open for 29% of the time, Pallas kernels for 0%

profile of v18, /device:TPU:0, one launch (start us, length us, event | category | flops | bytes accessed | tf_op | source)
XLA Modules:
  0.0 148.8 jit_solution(862947173422040371)
XLA Ops:
  6.5 2.2 %fusion.90 = (bf16[1,1,768,1024]{3,2,1,0:T(8,128)(2,1)S(1)}, bf16[1,1,768,1024]{3,2,1,0:T(8,128)(2,1)S(1)}) fusion(bf16[2,1,768,1024]{3,2,1,0:T(8,128)(2,1)} %param.3), kind=kLoop, calls=%fused_computation.179 | loop fusion | bytes 6291456 | tf_op jit(solution)/shard_map/slice | solution.py:26
  8.7 1.6 %copy.38 = bf16[1,1,768,1024]{2,3,1,0:T(8,128)(2,1)} copy(bf16[1,1,768,1024]{3,2,1,0:T(8,128)(2,1)S(1)} %get-tuple-element.25) | data formatting | bytes 3145728
  13.0 1.7 %fusion.16 = (bf16[1,1,1536,1024]{2,3,1,0:T(8,128)(2,1)S(1)}, bf16[1,1,1536,1024]{2,3,1,0:T(8,128)(2,1)S(1)}) fusion(bf16[1,768,1024]{1,2,0:T(8,128)(2,1)S(1)} %bitcast.205, bf16[1,768,1024]{1,2,0:T(8,128)(2,1)S(1)} %bitcast.201, bf16[1,768,1024]{1,2,0:T(8,128)(2,1)} %bitcast_negate_fusion), kind=kLoop, calls=%fused_computation.49 | loop fusion | flops 12582912 | bytes 11010048 | tf_op jit(solution)/shard_map/stack | solution.py:16
  15.3 3.7 %convert_bitcast_fusion = bf16[4,128,1,2,1024]{1,4,0,3,2:T(8,128)(2,1)S(1)} fusion(bf16[1,2,4,2,128,1536]{5,4,3,2,1,0:T(8,128)(2,1)S(1)} %bitcast.204, s32[]{:T(128)S(6)} %select_n.108, bf16[1,768,1024]{1,2,0:T(8,128)(2,1)S(1)} %bitcast.206, bf16[1,768,1024]{1,2,0:T(8,128)(2,1)S(1)} %bitcast.202), kind=kOutput, calls=%fused_computation.43 | convolution fusion | flops 3228565504 | bytes 8388612 | tf_op jit(solution)/shard_map/qpkit,qto->kiqpo/dot_general | solution.py:92
  20.3 3.0 %pad_slice_fusion.11 = (bf16[1,128,1,2,2048]{1,4,0,3,2:T(8,128)(2,1)}, bf16[1,128,1,2,2048]{1,4,0,3,2:T(8,128)(2,1)}, bf16[1,128,1,2,2048]{1,4,0,3,2:T(8,128)(2,...) fusion(bf16[4,128,1,2,1024]{1,4,0,3,2:T(8,128)(2,1)S(1)} %conve, ...), kind=kLoop, calls=%fused_computation.15 | loop fusion | bytes 8388608 | tf_op jit(solution)/shard_map/slice | solution.py:52
  23.3 1.5 %fusion.44 = (bf16[1,128,1,2,640]{1,4,0,3,2:T(8,128)(2,1)S(1)}, bf16[1,128,1,2,640]{1,4,0,3,2:T(8,128)(2,1)S(1)}) fusion(s32[]{:T(128)S(6)} %select_n.116, bf16[4,128,1,2,1024]{1,4,0,3,2:T(8,128)(2,1)} %copy-done.3, bf16[1,128,1,2,2048]{1,4,0,3,2:T(8,128)(2,1)} %get-tuple-element.37, s32[]{:T(128)S(6)} %select_n.110, ...), kind=kLoop, calls=%fused_computation.93 | loop fusion | flops 1310720 | bytes 3407880 | tf_op jit(solution)/shard_map/concatenate | solution.py:48
  24.8 1.5 dynamic-slice_maximum_fusion
  27.5 2.4 %copy.30 = bf16[4,128,1,2,640]{4,1,0,3,2:T(8,128)(2,1)} copy(bf16[4,128,1,2,640]{1,4,0,3,2:T(8,128)(2,1)} %pad_maximum_fusion.2) | data formatting | bytes 2621440 | tf_op jit(solution)/shard_map/stack | solution.py:53
  31.2 1.5 slice_bitcast_fusion.3
  33.0 4.6 %fusion.8 = bf16[512,2,1024]{0,2,1:T(8,128)(2,1)} fusion(bf16[1,1536,1,512]{3,1,2,0:T(8,128)(2,1)S(1)} %get-tuple-element.61, bf16[1,1536,1,512]{3,1,2,0:T(8,128)(2,1)S(1)} %get-tuple-element.60, bf16[1,768,1024]{1,2,0:T(8,128)(2,1)S(1)} %bitcast.207, bf16[1,768,1024]{1,2,0:T(8,128)(2,1)S(1)} %bitcast.203), kind=kOutput, calls=%fused_computation.37 | convolution fusion | flops 3233808384 | bytes 8388608 | tf_op jit(solution)/shard_map/qtpu,qto->uqpo/dot_general | solution.py:96
  37.6 5.0 %copy.31 = bf16[512,2,1024]{2,1,0:T(2,128)(2,1)S(1)} copy(bf16[512,2,1024]{0,2,1:T(8,128)(2,1)} %fusion.8) | data formatting | bytes 4194304 | tf_op jit(solution)/shard_map/qtpu,qto->uqpo/transpose | solution.py:96
  44.1 3.7 %gather_fusion = bf16[256,2,1024]{2,1,0:T(2,128)(2,1)} fusion(bf16[512,2,1024]{2,1,0:T(2,128)(2,1)S(1)} %copy.31, s32[1024]{0:T(1024)S(1)} %pad_clamp_fusion), kind=kCustom, calls=%fused_computation | custom fusion | bytes 2098176 | tf_op jit(solution)/shard_map/jit(_take)/gather | solution.py:101
  47.7 3.4 %fusion.11 = bf16[256,1,2,1024]{3,2,0,1:T(2,128)(2,1)} fusion(bf16[256,2,1024]{2,1,0:T(2,128)(2,1)} %gather_fusion, pred[256]{0:T(512)(128)(4,1)S(1)} %compare_and_fusion), kind=kLoop, calls=%fused_computation.42 | loop fusion | flops 524288 | bytes 2097408 | tf_op jit(solution)/shard_map/convert_element_type | solution.py:101
  51.2 12.9 %reduce-scatter.2.cloned.1.call-done = bf16[128,1,2,640]{3,0,2,1:T(8,128)(2,1)} async-done(((bf16[512,1,2,640]{3,0,2,1:T(8,128)(2,1)}), bf16[128,1,2,640]{3,0,2,1:T(8,128)(2,1)}) %reduce-scatter.2.cloned.1.call-update) | async-done | bytes 327696 | tf_op jit(solution)/shard_map/reduce_scatter | solution.py:94
  64.5 1.6 %copy.43 = pred[128,8,8,128]{3,1,2,0:T(8,128)(4,1)} copy(pred[128,8,8,128]{3,2,1,0:T(8,128)(4,1)S(1)} %bitcast.212) | data formatting | bytes 2097152
  66.1 2.2 %multiply_reduce_fusion = f32[]{:T(128)} fusion(bf16[2,1,768,1024]{3,2,1,0:T(8,128)(2,1)S(1)} %copy-done.2), kind=kLoop, calls=%fused_computation.3 | loop fusion | flops 4718591 | bytes 3145732 | tf_op jit(solution)/shard_map/reduce_sum | solution.py:114
  68.3 10.3 %psum.7 = f32[1]{0:T(128)} all-reduce(f32[1]{0:T(128)} %bitcast.29), channel_id=1, replica_groups=mesh['grp'=2,'shot'=4,'freq'=2,'sub'=2] {'shot'}, use_global_device_ids=true, to_apply=%region_2.3 | all-reduce | flops 1 | bytes 8 | tf_op jit(solution)/shard_map/psum | solution.py:115
  78.5 1.5 %copy.32 = bf16[256,1,2,1024]{3,0,2,1:T(8,128)(2,1)S(1)} copy(bf16[256,1,2,1024]{3,2,0,1:T(2,128)(2,1)} %fusion.11) | data formatting | bytes 2097152 | tf_op jit(solution)/shard_map/optimization_barrier | solution.py:103
  81.2 1.4 collective-permute-start.1
  83.3 33.5 %all-gather.2.cloned.1.call-done = bf16[1024,1,2,640]{3,0,2,1:T(8,128)(2,1)} async-done(((bf16[128,1,2,640]{3,0,2,1:T(8,128)(2,1)}), bf16[1024,1,2,640]{3,0,2,1:T(8,128)(2,1)}) %all-gather.2.cloned.1.call-update) | async-done | bytes 2621456 | tf_op jit(solution)/shard_map/all_gather | solution.py:113
  119.5 2.4 %copy.34 = bf16[2,1,8,128,1024]{4,3,2,0,1:T(8,128)(2,1)} copy(bf16[2,1,8,128,1024]{4,3,0,1,2:T(8,128)(2,1)S(1)} %bitcast.208) | data formatting | bytes 8388608 | tf_op jit(solution)/shard_map/transpose | solution.py:63
  121.9 6.3 %copy.35 = bf16[2,1,1024,1024]{2,3,0,1:T(8,128)(2,1)} copy(bf16[2,1,1024,1024]{3,2,0,1:T(8,128)(2,1)} %bitcast.199) | data formatting | bytes 8388608 | tf_op jit(solution)/shard_map/reshape;reshape | solution.py:70
  128.2 2.6 %fusion.89 = (bf16[1,1,1024,1024]{3,2,0,1:T(8,128)(2,1)S(1)}, bf16[1,1,1024,1024]{3,2,0,1:T(8,128)(2,1)S(1)}) fusion(bf16[2,1,1024,1024]{3,2,0,1:T(8,128)(2,1)} %bitcast.200), kind=kLoop, calls=%fused_computation.178 | loop fusion | flops 1048576 | bytes 8388608 | tf_op jit(solution)/shard_map/slice | solution.py:65
  131.9 2.5 %divide_convert_fusion = bf16[2,1,1024,1024]{3,2,0,1:T(8,128)(2,1)S(1)} fusion(bf16[1,1,1024,1024]{3,2,0,1:T(8,128)(2,1)S(1)} %get-tuple-element.24, bf16[1,1,1024,1024]{3,2,0,1:T(8,128)(2,1)S(1)} %get-tuple-element.23, f32[]{:T(128)} %bitcast.30, pred[1024,1024]{1,0:T(8,128)(4,1)S(1)} %bitcast.213, bf16[2,1,8,128,1024]{4,3,2,0,1:T(8,128)(2,1)S(1)} %copy-done.1), kind=kLoop, calls=%fused_computation.1 | loop fusion | flops 10485760 | bytes 13631492 | tf_op jit(solution)/shard_map/convert_element_type | solution.py:123
  (81 shorter events, 21.4 us)
Async XLA Ops:
  6.5 57.5 %reduce-scatter.2.cloned.1.call-start = ((), (), s32[]{:S(2)}) async-start(), calls=%async_computation.1 | async-start | bytes 1638400 | tf_op jit(solution)/shard_map/reduce_scatter | solution.py:94
  11.1 2.0 %copy-start.4 = (bf16[1,1,768,1024]{2,3,1,0:T(8,128)(2,1)S(1)}, bf16[1,1,768,1024]{2,3,1,0:T(8,128)(2,1)}, u32[]{:S(2)}) copy-start(bf16[1,1,768,1024]{2,3,1,0:T(8,128)(2,1)} %copy.38) | copy-start | bytes 4718596
  19.0 1.4 copy-start.3
  29.9 86.9 %all-gather.2.cloned.1.call-start = ((), (), s32[]{:S(2)}) async-start(), calls=%async_computation.2 | async-start | bytes 2949120 | tf_op jit(solution)/shard_map/all_gather | solution.py:113
  37.6 5.1 %copy-start.6 = (s32[512]{0:T(512)S(1)}, s32[512]{0:T(512)}, u32[]{:S(2)}) copy-start(s32[512]{0:T(512)} %param.5) | copy-start | bytes 6148
  47.7 18.3 %copy-start.2 = (bf16[2,1,768,1024]{3,2,1,0:T(8,128)(2,1)S(1)}, bf16[2,1,768,1024]{3,2,1,0:T(8,128)(2,1)}, u32[]{:S(2)}) copy-start(bf16[2,1,768,1024]{3,2,1,0:T(8,128)(2,1)} %param.3) | copy-start | bytes 9437188
  80.1 55.6 %collective-permute-start.2 = (bf16[64,1,2,1024]{3,0,1,2:T(8,128)(2,1)S(1)}, bf16[64,1,2,1024]{3,0,1,2:T(8,128)(2,1)S(1)}, u32[]{:S(2)}, u32[]{:S(2)}) collective-permute-start(bf16[64,1,2,1024]{3,0,1,2:T(8,128)(2,1)S(1)} %get-tuple-element.56), channel_id=1, source_target_pairs={{0,12},{4,0},{8,4},{12,8},{1,13},{5,1},{9,5},{13,9},{2,14},{6,2},{... | collective-permute-start | bytes 786440 | tf_op jit(solution)/shard_map/ppermute | solution.py:111
  81.2 54.5 %collective-permute-start.1 = (bf16[64,1,2,1024]{3,0,1,2:T(8,128)(2,1)S(1)}, bf16[64,1,2,1024]{3,0,1,2:T(8,128)(2,1)S(1)}, u32[]{:S(2)}, u32[]{:S(2)}) collective-permute-start(bf16[64,1,2,1024]{3,0,1,2:T(8,128)(2,1)S(1)} %get-tuple-element.57), channel_id=1, source_target_pairs={{0,8},{4,12},{8,0},{12,4},{1,9},{5,13},{9,1},{13,5},{2,10},{6,14},... | collective-permute-start | bytes 786440 | tf_op jit(solution)/shard_map/ppermute | solution.py:111
  82.7 53.1 %collective-permute-start = (bf16[64,1,2,1024]{3,0,1,2:T(8,128)(2,1)S(1)}, bf16[64,1,2,1024]{3,0,1,2:T(8,128)(2,1)S(1)}, u32[]{:S(2)}, u32[]{:S(2)}) collective-permute-start(bf16[64,1,2,1024]{3,0,1,2:T(8,128)(2,1)S(1)} %get-tuple-element.55), channel_id=1, source_target_pairs={{0,4},{4,8},{8,12},{12,0},{1,5},{5,9},{9,13},{13,1},{2,6},{6,10},{... | collective-permute-start | bytes 786440 | tf_op jit(solution)/shard_map/ppermute | solution.py:111
  116.9 1.8 %copy-start = (bf16[1024,1,2,640]{3,0,2,1:T(8,128)(2,1)S(1)}, bf16[1024,1,2,640]{3,0,2,1:T(8,128)(2,1)}, u32[]{:S(2)}) copy-start(bf16[1024,1,2,640]{3,0,2,1:T(8,128)(2,1)} %all-gather.2.cloned.1.call-done) | copy-start | bytes 7864324
  128.1 3.4 %copy-start.1 = (bf16[2,1,8,128,1024]{4,3,2,0,1:T(8,128)(2,1)S(1)}, bf16[2,1,8,128,1024]{4,3,2,0,1:T(8,128)(2,1)}, u32[]{:S(2)}) copy-start(bf16[2,1,8,128,1024]{4,3,2,0,1:T(8,128)(2,1)} %copy.34) | copy-start | bytes 12582916
  128.1 3.7 %copy-start.5 = (pred[128,8,8,128]{3,1,2,0:T(8,128)(4,1)S(1)}, pred[128,8,8,128]{3,1,2,0:T(8,128)(4,1)}, u32[]{:S(2)}) copy-start(pred[128,8,8,128]{3,1,2,0:T(8,128)(4,1)} %copy.43) | copy-start | bytes 3145732
Sparse Core Ops, SparseCore 0:
  30.1 33.9 reduce-scatter.1
  65.6 51.1 all-gather.1

commit v19 on v17

--- a/solution.py
+++ b/solution.py
@@ -44,12 +44,21 @@
 
 
 def strip_partials(rows, shot_count, core_count, core_index, rows_each, tile, span):
+    receivers = rows.shape[-1]
     rows = rows.astype(jnp.bfloat16)
-    doubled = jnp.concatenate([rows, rows], axis=-1)
+
+    def window(k, start):
+        if start + span <= receivers:
+            return rows[k, ..., start : start + span]
+        return jnp.concatenate([rows[k, ..., start:], rows[k, ..., : start + span - receivers]], axis=-1)
+
     windows = []
     for k in range(shot_count):
-        start = ((k * core_count + core_index) * rows_each // tile) * tile
-        windows.append(lax.dynamic_slice_in_dim(doubled[k], start, span, axis=-1))
+        chosen = window(k, (k * core_count * rows_each // tile) * tile)
+        for position in range(1, core_count):
+            start = ((k * core_count + position) * rows_each // tile) * tile
+            chosen = jnp.where(core_index == position, window(k, start), chosen)
+        windows.append(chosen)
     return jnp.stack(windows).reshape(shot_count * rows_each, *rows.shape[2:4], span)
 
 

time: 139 us -> 175 us (1.26); the launches traced: 138 us -> 172 us
  local copies, waits for them, and re-layouts: 39.1 us -> 70.3 us
  waiting for transfers between devices: 33.5 us -> 28.4 us
  other arithmetic: 24.7 us -> 28.8 us
  matrix products: 12.6 us -> 15.3 us
    unnamed x19 -> x20, local copies, waits for them, and re-layouts: 5.95 us -> 18.5 us
    reshape x0 -> x1, local copies, waits for them, and re-layouts: none -> 11 us  [per_device(): stacked_rows(downgoing)]
    dynamic_slice x0 -> x1, local copies, waits for them, and re-layouts: none -> 8.58 us  [per_device(): left = lax.dynamic_slice_in_dim(left, core_index, 1, 3)[:, :, :, 0]]
    squeeze x0 -> x1, local copies, waits for them, and re-layouts: none -> 3.99 us  [stacked_right(): return jnp.concatenate([trace[0], trace[1]], axis=1)]
    ppermute x3, waiting for transfers between devices: 3.68 us -> 0.01 us  [per_device(): corr = corr + lax.ppermute(outgoing, 'shot', perm=pairs).astype(jnp.float32)]
    transpose x0 -> x1, other arithmetic: none -> 3.17 us  [stacked_rows(): return jnp.swapaxes(jnp.stack([real_left, imag_left], axis=1), 2, 3)]
    concatenate x2 -> x0, other arithmetic: 2.95 us -> none  [strip_partials(): doubled = jnp.concatenate([rows, rows], axis=-1)]
    select_n x0 -> x2, other arithmetic: none -> 2.76 us  [strip_partials(): chosen = jnp.where(core_index == position, window(k, start), chosen)]
  transfers between devices with their start and end apart: 6 -> 6, of which waited for: 3 -> 2; matrix products, arithmetic and copies ran while one was open for 33% -> 27% of each run, Pallas kernels for 0% -> 0%
where the time goes in v19:
time: 175 us; the launch traced here: 172 us
  local copies, waits for them, and re-layouts  70.3 us (40%)
  other arithmetic  28.8 us (16%)
  waiting for transfers between devices  28.4 us (16%)
  matrix products  15.3 us (9%)
  between operations  14.5 us (8%)
  blocking collectives  10.4 us (6%)
  starting transfers between devices  4.48 us (3%)
    all_gather x1, waiting for transfers between devices, per_device(): across = lax.all_gather(gram_strip, 'shot', axis=0, tiled=True)  19.9 us
    unnamed x20, local copies, waits for them, and re-layouts  18.5 us
    reshape x1, local copies, waits for them, and re-layouts, per_device(): stacked_rows(downgoing)  11 us
    psum x1, blocking collectives, per_device(): power = lax.psum(local_power, 'shot') / receivers  10.4 us
    dynamic_slice x1, local copies, waits for them, and re-layouts, per_device(): left = lax.dynamic_slice_in_dim(left, core_index, 1, 3)[:, :, :, 0]  8.58 us
    reduce_scatter x1, waiting for transfers between devices, per_device(): lax.psum_scatter(gram_part, 'shot', scatter_dimension=0, tiled=True)  8.41 us
    another operation x1, local copies, waits for them, and re-layouts, rebuild_gram(): whole = jnp.where(direct, upper.reshape(shape6), mirror.reshape(shape6))  6.27 us
    dot_general x1, matrix products, per_device(): jnp.einsum('qpkit,qto->kiqpo', left, right, preferred_element_type=jnp.fl...  6.26 us
  transfers between devices with their start and end apart: 6, of which 2 were waited for; matrix products, arithmetic and copies ran while one was open for 27% of the time, Pallas kernels for 0%

profile of v19, /device:TPU:0, one launch (start us, length us, event | category | flops | bytes accessed | tf_op | source)
XLA Modules:
  0.0 172.1 jit_solution(9817465955597093917)
XLA Ops:
  6.5 4.0 %slice_bitcast_fusion.3 = (bf16[1,768,1024]{2,1,0:T(8,128)(2,1)}, bf16[1,768,1024]{2,1,0:T(8,128)(2,1)}) fusion(bf16[2,1,768,1024]{3,2,1,0:T(8,128)(2,1)} %param.3), kind=kLoop, calls=%fused_computation.41 | loop fusion | bytes 6291456 | tf_op jit(solution)/shard_map/squeeze | solution.py:26
  11.8 3.3 %fusion.15 = (bf16[1,1,1536,1024]{3,2,1,0:T(8,128)(2,1)S(1)}, bf16[1,1,1536,1024]{3,2,1,0:T(8,128)(2,1)S(1)}) fusion(bf16[1,768,1024]{2,1,0:T(8,128)(2,1)} %get-tuple-element.24, bf16[1,768,1024]{2,1,0:T(8,128)(2,1)} %get-tuple-element.23, bf16[1,768,1024]{2,1,0:T(8,128)(2,1)} %fusion.81), kind=kLoop, calls=%fused_computation.45 | loop fusion | flops 12582912 | bytes 11010048 | tf_op jit(solution)/shard_map/stack | solution.py:16
  15.1 3.2 %maximum_bitcast_fusion = bf16[1,2,1024,1536]{2,3,1,0:T(8,128)(2,1)} fusion(bf16[1,1,1536,1024]{3,2,1,0:T(8,128)(2,1)S(1)} %get-tuple-element.48, bf16[1,1,1536,1024]{3,2,1,0:T(8,128)(2,1)S(1)} %get-tuple-element.47), kind=kLoop, calls=%fused_computation.2 | loop fusion | flops 3145728 | bytes 12582912 | tf_op jit(solution)/shard_map/transpose | solution.py:16
  18.3 11.0 %reshape.391 = bf16[1,2,4,2,128,1536]{4,3,2,5,1,0:T(2,128)(2,1)} reshape(bf16[1,2,1024,1536]{2,3,1,0:T(8,128)(2,1)} %maximum_bitcast_fusion) | data formatting | bytes 12582912 | tf_op jit(solution)/shard_map/reshape | solution.py:99
  29.3 8.6 %constant_dynamic-slice_fusion.1 = bf16[1,2,4,1,128,1536]{4,3,2,5,1,0:T(2,128)(2,1)} fusion(bf16[1,2,4,2,128,1536]{4,3,2,5,1,0:T(2,128)(2,1)} %reshape.391, s32[]{:T(128)S(6)} %select_n.140), kind=kLoop, calls=%fused_computation.161 | loop fusion | bytes 6291460 | tf_op jit(solution)/shard_map/dynamic_slice | solution.py:100
  37.9 15.4 %copy.37 = bf16[1,2,4,1,128,1536]{5,4,2,1,3,0:T(8,128)(2,1)} copy(bf16[1,2,4,1,128,1536]{4,3,2,5,1,0:T(2,128)(2,1)} %constant_dynamic-slice_fusion.1) | data formatting | bytes 6291456
  53.2 6.3 %convert_bitcast_fusion = bf16[4,128,1,2,1024]{4,1,0,3,2:T(8,128)(2,1)S(1)} fusion(bf16[1,2,4,1,128,1536]{5,4,2,1,3,0:T(8,128)(2,1)} %copy.37, bf16[1,768,1024]{2,1,0:T(8,128)(2,1)} %get-tuple-element.24, bf16[1,768,1024]{2,1,0:T(8,128)(2,1)} %get-tuple-element.23), kind=kOutput, calls=%fused_computation.37 | convolution fusion | flops 3228565504 | bytes 8388608 | tf_op jit(solution)/shard_map/qpkit,qto->kiqpo/dot_general | solution.py:101
  62.5 1.4 slice_select_fusion.1
  63.9 1.4 maximum_select_fusion.1
  69.4 1.5 slice_bitcast_fusion.5
  72.8 4.7 %fusion.7 = bf16[512,2,1024]{0,2,1:T(8,128)(2,1)} fusion(bf16[1,1536,1,512]{3,1,2,0:T(8,128)(2,1)S(1)} %get-tuple-element.65, bf16[1,1536,1,512]{3,1,2,0:T(8,128)(2,1)S(1)} %get-tuple-element.64, bf16[1,768,1024]{2,1,0:T(8,128)(2,1)S(1)} %copy-done.3, bf16[1,768,1024]{2,1,0:T(8,128)(2,1)S(1)} %copy-done.2), kind=kOutput, calls=%fused_computation.31 | convolution fusion | flops 3233808384 | bytes 8388608 | tf_op jit(solution)/shard_map/qtpu,qto->uqpo/dot_general | solution.py:105
  77.4 6.2 %copy.27 = bf16[512,2,1024]{2,1,0:T(2,128)(2,1)} copy(bf16[512,2,1024]{0,2,1:T(8,128)(2,1)} %fusion.7) | data formatting | bytes 4194304 | tf_op jit(solution)/shard_map/qtpu,qto->uqpo/transpose | solution.py:105
  83.8 5.3 %gather_fusion = bf16[256,2,1024]{2,1,0:T(2,128)(2,1)} fusion(bf16[512,2,1024]{2,1,0:T(2,128)(2,1)} %copy.27, s32[1024]{0:T(1024)S(1)} %pad_clamp_fusion), kind=kCustom, calls=%fused_computation | custom fusion | bytes 2098176 | tf_op jit(solution)/shard_map/jit(_take)/gather | solution.py:110
  89.1 3.2 %fusion.10 = bf16[256,1,2,1024]{3,2,0,1:T(2,128)(2,1)} fusion(bf16[256,2,1024]{2,1,0:T(2,128)(2,1)} %gather_fusion, pred[256]{0:T(512)(128)(4,1)S(1)} %compare_and_fusion), kind=kLoop, calls=%fused_computation.36 | loop fusion | flops 524288 | bytes 2097408 | tf_op jit(solution)/shard_map/convert_element_type | solution.py:110
  92.3 8.4 %reduce-scatter.2.cloned.1.call-done = bf16[128,1,2,640]{3,0,2,1:T(8,128)(2,1)} async-done(((bf16[512,1,2,640]{3,0,2,1:T(8,128)(2,1)}), bf16[128,1,2,640]{3,0,2,1:T(8,128)(2,1)}) %reduce-scatter.2.cloned.1.call-update) | async-done | bytes 327696 | tf_op jit(solution)/shard_map/reduce_scatter | solution.py:103
  100.7 2.2 %multiply_reduce_fusion = f32[]{:T(128)} fusion(bf16[2,1,768,1024]{3,2,1,0:T(8,128)(2,1)S(1)} %copy-done.1), kind=kLoop, calls=%fused_computation.3 | loop fusion | flops 4718591 | bytes 3145732 | tf_op jit(solution)/shard_map/reduce_sum | solution.py:124
  103.0 10.4 %psum.7 = f32[1]{0:T(128)} all-reduce(f32[1]{0:T(128)} %bitcast.30), channel_id=1, replica_groups=mesh['grp'=2,'shot'=4,'freq'=2,'sub'=2] {'shot'}, use_global_device_ids=true, to_apply=%region_2.3 | all-reduce | flops 1 | bytes 8 | tf_op jit(solution)/shard_map/psum | solution.py:125
  114.0 19.9 %all-gather.2.cloned.1.call-done = bf16[512,1,2,640]{3,0,2,1:T(8,128)(2,1)} async-done(((bf16[128,1,2,640]{3,0,2,1:T(8,128)(2,1)}), bf16[512,1,2,640]{3,0,2,1:T(8,128)(2,1)}) %all-gather.2.cloned.1.call-update) | async-done | bytes 1310736 | tf_op jit(solution)/shard_map/all_gather | solution.py:122
  137.8 2.4 %collective-permute-start.2 = (bf16[64,1,2,1024]{3,0,1,2:T(8,128)(2,1)S(1)}, bf16[64,1,2,1024]{3,0,1,2:T(8,128)(2,1)S(1)}, u32[]{:S(2)}, u32[]{:S(2)}) collective-permute-start(bf16[64,1,2,1024]{3,0,1,2:T(8,128)(2,1)S(1)} %get-tuple-element.60), channel_id=1, source_target_pairs={{0,12},{4,0},{8,4},{12,8},{1,13},{5,1},{9,5},{13,9},{2,14},{6,2},{... | collective-permute-start | bytes 786440 | tf_op jit(solution)/shard_map/ppermute | solution.py:120
  140.2 2.0 %select_bitcast_fusion.1 = (bf16[4,1,128,1,2,640]{5,2,1,0,4,3:T(8,128)(2,1)S(1)}, bf16[4,1,128,1,2,640]{5,2,1,0,4,3:T(8,128)(2,1)S(1)}) fusion(bf16[4,128,1,2,640]{4,1,0,3,2:T(8,128)(2,1)} %bitcast.231, bf16[4,128,1,2,640]{4,1,0,3,2:T(8,128)(2,1)} %collective-permute-done.3, pred[]{:T(512)S(6)} %eq.17), kind=kLoop, calls=%fused_computation.44 | loop fusion | flops 1310720 | bytes 5242881 | tf_op jit(solution)/shard_map/stack | solution.py:133
  143.2 2.4 %copy.31 = bf16[2,1,8,128,1024]{4,3,2,0,1:T(8,128)(2,1)} copy(bf16[2,1,8,128,1024]{4,3,0,1,2:T(8,128)(2,1)S(1)} %bitcast.224) | data formatting | bytes 8388608 | tf_op jit(solution)/shard_map/transpose | solution.py:72
  145.6 6.3 %copy.32 = bf16[2,1,1024,1024]{2,3,0,1:T(8,128)(2,1)} copy(bf16[2,1,1024,1024]{3,2,0,1:T(8,128)(2,1)} %bitcast.221) | data formatting | bytes 8388608 | tf_op jit(solution)/shard_map/reshape;reshape | solution.py:79
  151.9 2.6 %fusion.87 = (bf16[1,1,1024,1024]{3,2,0,1:T(8,128)(2,1)S(1)}, bf16[1,1,1024,1024]{3,2,0,1:T(8,128)(2,1)S(1)}) fusion(bf16[2,1,1024,1024]{3,2,0,1:T(8,128)(2,1)} %bitcast.222), kind=kLoop, calls=%fused_computation.174 | loop fusion | flops 1048576 | bytes 8388608 | tf_op jit(solution)/shard_map/slice | solution.py:74
  155.3 2.5 %divide_convert_fusion = bf16[2,1,1024,1024]{3,2,0,1:T(8,128)(2,1)S(1)} fusion(bf16[1,1,1024,1024]{3,2,0,1:T(8,128)(2,1)S(1)} %get-tuple-element.22, bf16[1,1,1024,1024]{3,2,0,1:T(8,128)(2,1)S(1)} %get-tuple-element.21, f32[]{:T(128)} %bitcast.31, pred[1024,1024]{1,0:T(8,128)(4,1)S(1)} %bitcast.229, bf16[2,1,8,128,1024]{4,3,2,0,1:T(8,128)(2,1)S(1)} %copy-done), kind=kLoop, calls=%fused_computation.1 | loop fusion | flops 10485760 | bytes 13631492 | tf_op jit(solution)/shard_map/convert_element_type | solution.py:141
  (89 shorter events, 23.2 us)
Async XLA Ops:
  6.5 94.2 %reduce-scatter.2.cloned.1.call-start = ((), (), s32[]{:S(2)}) async-start(), calls=%async_computation.1 | async-start | bytes 1638400 | tf_op jit(solution)/shard_map/reduce_scatter | solution.py:103
  6.5 4.0 %copy-start.1 = (bf16[2,1,768,1024]{3,2,1,0:T(8,128)(2,1)S(1)}, bf16[2,1,768,1024]{3,2,1,0:T(8,128)(2,1)}, u32[]{:S(2)}) copy-start(bf16[2,1,768,1024]{3,2,1,0:T(8,128)(2,1)} %param.3) | copy-start | bytes 9437188
  59.5 2.3 %copy-start.5 = (bf16[4,128,1,2,1024]{4,1,0,3,2:T(8,128)(2,1)}, bf16[4,128,1,2,1024]{4,1,0,3,2:T(8,128)(2,1)S(1)}, u32[]{:S(2)}) copy-start(bf16[4,128,1,2,1024]{4,1,0,3,2:T(8,128)(2,1)S(1)} %convert_bitcast_fusion) | copy-start | bytes 6291460
  63.9 3.0 %copy-start.6 = (s32[512]{0:T(512)S(1)}, s32[512]{0:T(512)}, u32[]{:S(2)}) copy-start(s32[512]{0:T(512)} %param.5) | copy-start | bytes 6148
  66.6 67.2 %all-gather.2.cloned.1.call-start = ((), (), s32[]{:S(2)}) async-start(), calls=%async_computation.2 | async-start | bytes 1638400 | tf_op jit(solution)/shard_map/all_gather | solution.py:122
  70.9 1.4 copy-start.2
  70.9 1.9 %copy-start.3 = (bf16[1,768,1024]{2,1,0:T(8,128)(2,1)S(1)}, bf16[1,768,1024]{2,1,0:T(8,128)(2,1)}, u32[]{:S(2)}) copy-start(bf16[1,768,1024]{2,1,0:T(8,128)(2,1)} %get-tuple-element.24) | copy-start | bytes 4718596
  103.0 31.9 %copy-start.4 = (bf16[256,1,2,1024]{3,2,0,1:T(2,128)(2,1)S(1)}, bf16[256,1,2,1024]{3,2,0,1:T(2,128)(2,1)}, u32[]{:S(2)}) copy-start(bf16[256,1,2,1024]{3,2,0,1:T(2,128)(2,1)} %fusion.10) | copy-start | bytes 3145732
  133.9 6.3 %collective-permute-start.3 = (bf16[4,128,1,2,640]{4,1,0,3,2:T(8,128)(2,1)}, bf16[4,128,1,2,640]{4,1,0,3,2:T(8,128)(2,1)}, u32[]{:S(2)}, u32[]{:S(2)}) collective-permute-start(bf16[4,128,1,2,640]{4,1,0,3,2:T(8,128)(2,1)} %bitcast.230), channel_id=1, source_target_pairs={{0,1},{1,0},{2,3},{3,2},{4,5},{5,4},{6,7},{7,6},{8,9},{9,8},{10,11... | collective-permute-start | bytes 3932168 | tf_op jit(solution)/shard_map/ppermute | solution.py:130
  135.9 23.1 %collective-permute-start = (bf16[64,1,2,1024]{3,0,1,2:T(8,128)(2,1)}, bf16[64,1,2,1024]{3,0,1,2:T(8,128)(2,1)S(1)}, u32[]{:S(2)}, u32[]{:S(2)}) collective-permute-start(bf16[64,1,2,1024]{3,0,1,2:T(8,128)(2,1)} %get-tuple-element.59), channel_id=1, source_target_pairs={{0,4},{4,8},{8,12},{12,0},{1,5},{5,9},{9,13},{13,1},{2,6},{6,10},{... | collective-permute-start | bytes 786440 | tf_op jit(solution)/shard_map/ppermute | solution.py:120
  136.6 22.5 %collective-permute-start.1 = (bf16[64,1,2,1024]{3,0,1,2:T(8,128)(2,1)S(1)}, bf16[64,1,2,1024]{3,0,1,2:T(8,128)(2,1)S(1)}, u32[]{:S(2)}, u32[]{:S(2)}) collective-permute-start(bf16[64,1,2,1024]{3,0,1,2:T(8,128)(2,1)S(1)} %get-tuple-element.61), channel_id=1, source_target_pairs={{0,8},{4,12},{8,0},{12,4},{1,9},{5,13},{9,1},{13,5},{2,10},{6,14},... | collective-permute-start | bytes 786440 | tf_op jit(solution)/shard_map/ppermute | solution.py:120
  137.8 21.3 %collective-permute-start.2 = (bf16[64,1,2,1024]{3,0,1,2:T(8,128)(2,1)S(1)}, bf16[64,1,2,1024]{3,0,1,2:T(8,128)(2,1)S(1)}, u32[]{:S(2)}, u32[]{:S(2)}) collective-permute-start(bf16[64,1,2,1024]{3,0,1,2:T(8,128)(2,1)S(1)} %get-tuple-element.60), channel_id=1, source_target_pairs={{0,12},{4,0},{8,4},{12,8},{1,13},{5,1},{9,5},{13,9},{2,14},{6,2},{... | collective-permute-start | bytes 786440 | tf_op jit(solution)/shard_map/ppermute | solution.py:120
  151.9 3.4 %copy-start = (bf16[2,1,8,128,1024]{4,3,2,0,1:T(8,128)(2,1)S(1)}, bf16[2,1,8,128,1024]{4,3,2,0,1:T(8,128)(2,1)}, u32[]{:S(2)}) copy-start(bf16[2,1,8,128,1024]{4,3,2,0,1:T(8,128)(2,1)} %copy.31) | copy-start | bytes 12582916
Sparse Core Ops, SparseCore 0:
  66.8 33.9 reduce-scatter.1
  102.3 31.5 all-gather.1

commit v20 on v17

--- a/solution.py
+++ b/solution.py
@@ -50,7 +50,7 @@
     for k in range(shot_count):
         start = ((k * core_count + core_index) * rows_each // tile) * tile
         windows.append(lax.dynamic_slice_in_dim(doubled[k], start, span, axis=-1))
-    return jnp.stack(windows).reshape(shot_count * rows_each, *rows.shape[2:4], span)
+    return jnp.stack(windows).reshape(shot_count * rows.shape[1], *rows.shape[2:4], span)
 
 
 def rebuild_gram(strips, tiles, tile):
@@ -89,9 +89,15 @@
 
     left = stacked_rows(downgoing).reshape(freq_local, 2, shot_count, core_count, rows_each, -1)
     left = lax.dynamic_slice_in_dim(left, core_index, 1, 3)[:, :, :, 0]
-    gram_rows = jnp.einsum("qpkit,qto->kiqpo", left, right, preferred_element_type=jnp.float32)
-    gram_part = strip_partials(gram_rows, shot_count, core_count, core_index, rows_each, tile, span)
-    gram_strip = lax.psum_scatter(gram_part, "shot", scatter_dimension=0, tiled=True)
+    half = rows_each // 2 if rows_each % 16 == 0 else rows_each
+    chunks = []
+    for low in range(0, rows_each, half):
+        chunk_rows = jnp.einsum(
+            "qpkit,qto->kiqpo", left[:, :, :, low : low + half], right, preferred_element_type=jnp.float32
+        )
+        chunk_part = strip_partials(chunk_rows, shot_count, core_count, core_index, rows_each, tile, span)
+        chunks.append(lax.psum_scatter(chunk_part, "shot", scatter_dimension=0, tiled=True))
+    gram_strip = jnp.concatenate(chunks, axis=0)
 
     corr_all = jnp.einsum(
         "qtpu,qto->uqpo", stacked_left(upgoing), right, preferred_element_type=jnp.float32

time: 139 us -> 195 us (1.40)
  local copies, waits for them, and re-layouts: 39.1 us -> 72.9 us
  other arithmetic: 24.7 us -> 36.7 us
  matrix products: 12.6 us -> 17.1 us
  waiting for transfers between devices: 33.5 us -> 37 us
    unnamed x19 -> x28, local copies, waits for them, and re-layouts: 5.95 us -> 17.6 us
    reshape x0 -> x1, local copies, waits for them, and re-layouts: none -> 11 us  [per_device(): stacked_rows(downgoing)]
    dynamic_slice x0 -> x1, local copies, waits for them, and re-layouts: none -> 8.59 us  [per_device(): left = lax.dynamic_slice_in_dim(left, core_index, 1, 3)[:, :, :, 0]]
    reduce_scatter x1 -> x2, waiting for transfers between devices: 9.86 us -> 18.4 us  [per_device(): lax.psum_scatter(chunk_part, 'shot', scatter_dimension=0, tiled=True)]
    dot_general x1 -> x2, matrix products: 3.69 us -> 8.09 us  [per_device(): jnp.einsum('qpkit,qto->kiqpo', left[:, :, :, low:low + half], right, pref...]
    squeeze x0 -> x1, local copies, waits for them, and re-layouts: none -> 3.99 us  [stacked_right(): return jnp.concatenate([trace[0], trace[1]], axis=1)]
    ppermute x3, waiting for transfers between devices: 3.68 us -> 0.01 us  [per_device(): corr = corr + lax.ppermute(outgoing, 'shot', perm=pairs).astype(jnp.float32)]
    transpose x0 -> x1, other arithmetic: none -> 3.19 us  [stacked_rows(): return jnp.swapaxes(jnp.stack([real_left, imag_left], axis=1), 2, 3)]
  transfers between devices with their start and end apart: 6 -> 7, of which waited for: 3 -> 2; matrix products, arithmetic and copies ran while one was open for 33% -> 27% of each run, Pallas kernels for 0% -> 0%
where the time goes in v20:
time: 195 us; the launch traced here: 193 us
  local copies, waits for them, and re-layouts  72.9 us (37%)
  waiting for transfers between devices  37 us (19%)
  other arithmetic  36.7 us (19%)
  matrix products  17.1 us (9%)
  between operations  14.1 us (7%)
  blocking collectives  10.4 us (5%)
  starting transfers between devices  4.61 us (2%)
    all_gather x1, waiting for transfers between devices, per_device(): across = lax.all_gather(gram_strip, 'shot', axis=0, tiled=True)  18.6 us
    reduce_scatter x2, waiting for transfers between devices, per_device(): lax.psum_scatter(chunk_part, 'shot', scatter_dimension=0, tiled=True)  18.4 us
    unnamed x28, local copies, waits for them, and re-layouts  17.6 us
    reshape x1, local copies, waits for them, and re-layouts, per_device(): stacked_rows(downgoing)  11 us
    psum x1, blocking collectives, per_device(): power = lax.psum(local_power, 'shot') / receivers  10.4 us
    dynamic_slice x1, local copies, waits for them, and re-layouts, per_device(): left = lax.dynamic_slice_in_dim(left, core_index, 1, 3)[:, :, :, 0]  8.59 us
    dot_general x2, matrix products, per_device(): jnp.einsum('qpkit,qto->kiqpo', left[:, :, :, low:low + half], right, pref...  8.09 us
    transpose x1, local copies, waits for them, and re-layouts, per_device(): jnp.einsum('qtpu,qto->uqpo', stacked_left(upgoing), right, preferred_elem...  6.29 us
  transfers between devices with their start and end apart: 7, of which 2 were waited for; matrix products, arithmetic and copies ran while one was open for 27% of the time, Pallas kernels for 0%

profile of v20, /device:TPU:0, one launch (start us, length us, event | category | flops | bytes accessed | tf_op | source)
XLA Modules:
  0.0 192.8 jit_solution(11698379435499295979)
XLA Ops:
  6.5 4.0 %slice_bitcast_fusion.7 = (bf16[1,768,1024]{2,1,0:T(8,128)(2,1)}, bf16[1,768,1024]{2,1,0:T(8,128)(2,1)}) fusion(bf16[2,1,768,1024]{3,2,1,0:T(8,128)(2,1)} %param.3), kind=kLoop, calls=%fused_computation.55 | loop fusion | bytes 6291456 | tf_op jit(solution)/shard_map/squeeze | solution.py:26
  11.8 3.3 %fusion.91 = (bf16[1,1,1536,1024]{3,2,1,0:T(8,128)(2,1)S(1)}, bf16[1,1,1536,1024]{3,2,1,0:T(8,128)(2,1)S(1)}) fusion(bf16[1,768,1024]{2,1,0:T(8,128)(2,1)} %get-tuple-element.24, bf16[1,768,1024]{2,1,0:T(8,128)(2,1)} %get-tuple-element.23, bf16[1,768,1024]{2,1,0:T(8,128)(2,1)} %fusion.90), kind=kLoop, calls=%fused_computation.197 | loop fusion | flops 12582912 | bytes 11010048 | tf_op jit(solution)/shard_map/stack | solution.py:16
  15.1 3.2 %maximum_bitcast_fusion = bf16[1,2,1024,1536]{2,3,1,0:T(8,128)(2,1)} fusion(bf16[1,1,1536,1024]{3,2,1,0:T(8,128)(2,1)S(1)} %get-tuple-element.38, bf16[1,1,1536,1024]{3,2,1,0:T(8,128)(2,1)S(1)} %get-tuple-element.37), kind=kLoop, calls=%fused_computation.2 | loop fusion | flops 3145728 | bytes 12582912 | tf_op jit(solution)/shard_map/transpose | solution.py:16
  18.3 11.0 %reshape.277 = bf16[1,2,4,2,128,1536]{4,3,2,5,1,0:T(2,128)(2,1)} reshape(bf16[1,2,1024,1536]{2,3,1,0:T(8,128)(2,1)} %maximum_bitcast_fusion) | data formatting | bytes 12582912 | tf_op jit(solution)/shard_map/reshape | solution.py:90
  29.3 8.6 %constant_dynamic-slice_fusion.1 = bf16[1,2,4,1,128,1536]{4,3,2,5,1,0:T(2,128)(2,1)} fusion(bf16[1,2,4,2,128,1536]{4,3,2,5,1,0:T(2,128)(2,1)} %reshape.277, s32[]{:T(128)S(6)} %select_n.128), kind=kLoop, calls=%fused_computation.180 | loop fusion | bytes 6291460 | tf_op jit(solution)/shard_map/dynamic_slice | solution.py:91
  37.9 15.3 %copy.37 = bf16[1,2,4,1,128,1536]{5,4,2,1,3,0:T(8,128)(2,1)} copy(bf16[1,2,4,1,128,1536]{4,3,2,5,1,0:T(2,128)(2,1)} %constant_dynamic-slice_fusion.1) | data formatting | bytes 6291456
  53.2 5.3 %fusion.21 = bf16[4,64,1,2,1024]{4,1,0,3,2:T(8,128)(2,1)} fusion(bf16[1,2,4,128,1536]{4,3,2,1,0:T(8,128)(2,1)} %bitcast.252, bf16[1,768,1024]{2,1,0:T(8,128)(2,1)} %get-tuple-element.24, bf16[1,768,1024]{2,1,0:T(8,128)(2,1)} %get-tuple-element.23), kind=kOutput, calls=%fused_computation.59 | convolution fusion | flops 1617428480 | bytes 5767168 | tf_op jit(solution)/shard_map/qpkit,qto->kiqpo/dot_general | solution.py:95
  58.6 2.8 %fusion.18 = bf16[4,64,1,2,1024]{4,1,0,3,2:T(8,128)(2,1)} fusion(bf16[1,2,4,128,1536]{4,3,2,1,0:T(8,128)(2,1)S(1)} %bitcast.253, bf16[1,768,1024]{2,1,0:T(8,128)(2,1)S(1)} %copy-done.4, bf16[1,768,1024]{2,1,0:T(8,128)(2,1)S(1)} %copy-done.2), kind=kOutput, calls=%fused_computation.58 | convolution fusion | flops 1617428480 | bytes 5767168 | tf_op jit(solution)/shard_map/qpkit,qto->kiqpo/dot_general | solution.py:95
  61.3 3.3 %pad_slice_fusion.11 = (bf16[1,64,1,2,2048]{4,1,0,3,2:T(8,128)(2,1)}, bf16[1,64,1,2,2048]{4,1,0,3,2:T(8,128)(2,1)}, bf16[1,64,1,2,2048]{4,1,0,3,2:T(8,128)(2,1)}...) fusion(bf16[4,64,1,2,1024]{4,1,0,3,2:T(8,128)(2,1)} %fusion.21), kind=kLoop, calls=%fused_computation.29 | loop fusion | bytes 4194304 | tf_op jit(solution)/shard_map/slice | solution.py:52
  75.2 2.8 %slice_bitcast_fusion.17 = (bf16[1,768,512]{2,1,0:T(8,128)(2,1)}, bf16[1,768,512]{2,1,0:T(8,128)(2,1)}) fusion(bf16[2,1,768,512]{3,2,1,0:T(8,128)(2,1)} %param.4), kind=kLoop, calls=%fused_computation.63 | loop fusion | bytes 3145728 | tf_op jit(solution)/shard_map/squeeze | solution.py:20
  80.3 2.3 %maximum_bitcast_fusion.7 = (bf16[1,1536,1,512]{3,1,2,0:T(8,128)(2,1)S(1)}, bf16[1,1536,1,512]{3,1,2,0:T(8,128)(2,1)S(1)}) fusion(bf16[1,768,512]{2,1,0:T(8,128)(2,1)} %get-tuple-element.36, bf16[1,768,512]{2,1,0:T(8,128)(2,1)} %get-tuple-element.35, bf16[1,768,512]{2,1,0:T(8,128)(2,1)} %fusion.89), kind=kLoop, calls=%fused_computation.52 | loop fusion | flops 6291456 | bytes 5505024 | tf_op jit(solution)/shard_map/stack | solution.py:22
  83.3 4.7 %fusion.8 = bf16[512,2,1024]{0,2,1:T(8,128)(2,1)} fusion(bf16[1,1536,1,512]{3,1,2,0:T(8,128)(2,1)S(1)} %get-tuple-element.67, bf16[1,1536,1,512]{3,1,2,0:T(8,128)(2,1)S(1)} %get-tuple-element.66, bf16[1,768,1024]{2,1,0:T(8,128)(2,1)S(1)} %copy-done.5, bf16[1,768,1024]{2,1,0:T(8,128)(2,1)S(1)} %copy-done.3), kind=kOutput, calls=%fused_computation.44 | convolution fusion | flops 3233808384 | bytes 8388608 | tf_op jit(solution)/shard_map/qtpu,qto->uqpo/dot_general | solution.py:102
  87.9 6.3 %copy.27 = bf16[512,2,1024]{2,1,0:T(2,128)(2,1)} copy(bf16[512,2,1024]{0,2,1:T(8,128)(2,1)} %fusion.8) | data formatting | bytes 4194304 | tf_op jit(solution)/shard_map/qtpu,qto->uqpo/transpose | solution.py:102
  94.3 5.3 %gather_fusion = bf16[256,2,1024]{2,1,0:T(2,128)(2,1)} fusion(bf16[512,2,1024]{2,1,0:T(2,128)(2,1)} %copy.27, s32[1024]{0:T(1024)S(1)} %pad_clamp_fusion), kind=kCustom, calls=%fused_computation | custom fusion | bytes 2098176 | tf_op jit(solution)/shard_map/jit(_take)/gather | solution.py:107
  99.6 3.2 %fusion.11 = bf16[256,1,2,1024]{3,2,0,1:T(2,128)(2,1)} fusion(bf16[256,2,1024]{2,1,0:T(2,128)(2,1)} %gather_fusion, pred[256]{0:T(512)(128)(4,1)S(1)} %compare_and_fusion), kind=kLoop, calls=%fused_computation.49 | loop fusion | flops 524288 | bytes 2097408 | tf_op jit(solution)/shard_map/convert_element_type | solution.py:107
  102.9 18.4 %reduce-scatter.5.cloned.1.call-done = bf16[64,1,2,640]{3,0,2,1:T(8,128)(2,1)} async-done(((bf16[256,1,2,640]{3,0,2,1:T(8,128)(2,1)}), bf16[64,1,2,640]{3,0,2,1:T(8,128)(2,1)}) %reduce-scatter.5.cloned.1.call-update) | async-done | bytes 163856 | tf_op jit(solution)/shard_map/reduce_scatter | solution.py:99
  123.0 2.3 %multiply_reduce_fusion = f32[]{:T(128)} fusion(bf16[2,1,768,1024]{3,2,1,0:T(8,128)(2,1)S(1)} %copy-done.1), kind=kLoop, calls=%fused_computation.3 | loop fusion | flops 4718591 | bytes 3145732 | tf_op jit(solution)/shard_map/reduce_sum | solution.py:121
  125.3 10.4 %psum.7 = f32[1]{0:T(128)} all-reduce(f32[1]{0:T(128)} %bitcast.36), channel_id=1, replica_groups=mesh['grp'=2,'shot'=4,'freq'=2,'sub'=2] {'shot'}, use_global_device_ids=true, to_apply=%region_3.4 | all-reduce | flops 1 | bytes 8 | tf_op jit(solution)/shard_map/psum | solution.py:122
  136.2 18.6 %all-gather.2.cloned.1.call-done = bf16[512,1,2,640]{3,0,2,1:T(8,128)(2,1)} async-done(((bf16[128,1,2,640]{3,0,2,1:T(8,128)(2,1)}), bf16[512,1,2,640]{3,0,2,1:T(8,128)(2,1)}) %all-gather.2.cloned.1.call-update) | async-done | bytes 1310736 | tf_op jit(solution)/shard_map/all_gather | solution.py:119
  158.8 2.4 %collective-permute-start.2 = (bf16[64,1,2,1024]{3,0,1,2:T(8,128)(2,1)S(1)}, bf16[64,1,2,1024]{3,0,1,2:T(8,128)(2,1)S(1)}, u32[]{:S(2)}, u32[]{:S(2)}) collective-permute-start(bf16[64,1,2,1024]{3,0,1,2:T(8,128)(2,1)S(1)} %get-tuple-element.50), channel_id=1, source_target_pairs={{0,12},{4,0},{8,4},{12,8},{1,13},{5,1},{9,5},{13,9},{2,14},{6,2},{... | collective-permute-start | bytes 786440 | tf_op jit(solution)/shard_map/ppermute | solution.py:117
  164.2 2.4 %copy.31 = bf16[2,1,8,128,1024]{4,3,2,0,1:T(8,128)(2,1)} copy(bf16[2,1,8,128,1024]{4,3,0,1,2:T(8,128)(2,1)S(1)} %bitcast.247) | data formatting | bytes 8388608 | tf_op jit(solution)/shard_map/transpose | solution.py:63
  166.7 6.3 %copy.32 = bf16[2,1,1024,1024]{2,3,0,1:T(8,128)(2,1)} copy(bf16[2,1,1024,1024]{3,2,0,1:T(8,128)(2,1)} %bitcast.244) | data formatting | bytes 8388608 | tf_op jit(solution)/shard_map/reshape;reshape | solution.py:70
  172.9 2.6 %fusion.97 = (bf16[1,1,1024,1024]{3,2,0,1:T(8,128)(2,1)S(1)}, bf16[1,1,1024,1024]{3,2,0,1:T(8,128)(2,1)S(1)}) fusion(bf16[2,1,1024,1024]{3,2,0,1:T(8,128)(2,1)} %bitcast.245), kind=kLoop, calls=%fused_computation.201 | loop fusion | flops 1048576 | bytes 8388608 | tf_op jit(solution)/shard_map/slice | solution.py:65
  176.4 2.5 %divide_convert_fusion = bf16[2,1,1024,1024]{3,2,0,1:T(8,128)(2,1)S(1)} fusion(bf16[1,1,1024,1024]{3,2,0,1:T(8,128)(2,1)S(1)} %get-tuple-element.22, bf16[1,1,1024,1024]{3,2,0,1:T(8,128)(2,1)S(1)} %get-tuple-element.21, f32[]{:T(128)} %bitcast.37, pred[1024,1024]{1,0:T(8,128)(4,1)S(1)} %bitcast.251, bf16[2,1,8,128,1024]{4,3,2,0,1:T(8,128)(2,1)S(1)} %copy-done), kind=kLoop, calls=%fused_computation.1 | loop fusion | flops 10485760 | bytes 13631492 | tf_op jit(solution)/shard_map/convert_element_type | solution.py:138
  (103 shorter events, 31.5 us)
Async XLA Ops:
  6.5 96.3 %reduce-scatter.3.cloned.1.call-start = ((), (), s32[]{:S(2)}) async-start(), calls=%async_computation.2 | async-start | bytes 819200 | tf_op jit(solution)/shard_map/reduce_scatter | solution.py:99
  6.5 4.0 %copy-start.1 = (bf16[2,1,768,1024]{3,2,1,0:T(8,128)(2,1)S(1)}, bf16[2,1,768,1024]{3,2,1,0:T(8,128)(2,1)}, u32[]{:S(2)}) copy-start(bf16[2,1,768,1024]{3,2,1,0:T(8,128)(2,1)} %param.3) | copy-start | bytes 9437188
  53.2 5.3 %copy-start.2 = (bf16[1,768,1024]{2,1,0:T(8,128)(2,1)S(1)}, bf16[1,768,1024]{2,1,0:T(8,128)(2,1)}, u32[]{:S(2)}) copy-start(bf16[1,768,1024]{2,1,0:T(8,128)(2,1)} %get-tuple-element.23) | copy-start | bytes 4718596
  53.2 5.3 %copy-start.4 = (bf16[1,768,1024]{2,1,0:T(8,128)(2,1)S(1)}, bf16[1,768,1024]{2,1,0:T(8,128)(2,1)}, u32[]{:S(2)}) copy-start(bf16[1,768,1024]{2,1,0:T(8,128)(2,1)} %get-tuple-element.24) | copy-start | bytes 4718596
  53.2 5.3 %copy-start.9 = (bf16[1,2,4,1,128,1536]{5,4,2,1,3,0:T(8,128)(2,1)S(1)}, bf16[1,2,4,1,128,1536]{5,4,2,1,3,0:T(8,128)(2,1)}, u32[]{:S(2)}) copy-start(bf16[1,2,4,1,128,1536]{5,4,2,1,3,0:T(8,128)(2,1)} %copy.37) | copy-start | bytes 9437188
  61.3 3.3 %copy-start.7 = (bf16[4,64,1,2,1024]{4,1,0,3,2:T(8,128)(2,1)S(1)}, bf16[4,64,1,2,1024]{4,1,0,3,2:T(8,128)(2,1)}, u32[]{:S(2)}) copy-start(bf16[4,64,1,2,1024]{4,1,0,3,2:T(8,128)(2,1)} %fusion.18) | copy-start | bytes 3145732
  72.7 48.6 %reduce-scatter.5.cloned.1.call-start = ((), (), s32[]{:S(2)}) async-start(), calls=%async_computation.3 | async-start | bytes 819200 | tf_op jit(solution)/shard_map/reduce_scatter | solution.py:99
  74.0 5.0 %copy-start.10 = (s32[512]{0:T(512)S(1)}, s32[512]{0:T(512)}, u32[]{:S(2)}) copy-start(s32[512]{0:T(512)} %param.5) | copy-start | bytes 6148
  75.0 79.8 %all-gather.2.cloned.1.call-start = ((), (), s32[]{:S(2)}) async-start(), calls=%async_computation.4 | async-start | bytes 1638400 | tf_op jit(solution)/shard_map/all_gather | solution.py:119
  75.2 2.8 %copy-start.8 = (bf16[2,1,768,512]{3,2,1,0:T(8,128)(2,1)S(1)}, bf16[2,1,768,512]{3,2,1,0:T(8,128)(2,1)}, u32[]{:S(2)}) copy-start(bf16[2,1,768,512]{3,2,1,0:T(8,128)(2,1)} %param.4) | copy-start | bytes 4718596
  80.3 2.5 %copy-start.3 = (bf16[1,768,1024]{2,1,0:T(8,128)(2,1)S(1)}, bf16[1,768,1024]{2,1,0:T(8,128)(2,1)}, u32[]{:S(2)}) copy-start(bf16[1,768,1024]{2,1,0:T(8,128)(2,1)} %get-tuple-element.23) | copy-start | bytes 4718596
  80.3 3.0 %copy-start.5 = (bf16[1,768,1024]{2,1,0:T(8,128)(2,1)S(1)}, bf16[1,768,1024]{2,1,0:T(8,128)(2,1)}, u32[]{:S(2)}) copy-start(bf16[1,768,1024]{2,1,0:T(8,128)(2,1)} %get-tuple-element.24) | copy-start | bytes 4718596
  125.3 30.5 %copy-start.6 = (bf16[256,1,2,1024]{3,2,0,1:T(2,128)(2,1)S(1)}, bf16[256,1,2,1024]{3,2,0,1:T(2,128)(2,1)}, u32[]{:S(2)}) copy-start(bf16[256,1,2,1024]{3,2,0,1:T(2,128)(2,1)} %fusion.11) | copy-start | bytes 3145732
  154.8 6.4 %collective-permute-start.3 = (bf16[4,128,1,2,640]{4,1,0,3,2:T(8,128)(2,1)}, bf16[4,128,1,2,640]{4,1,0,3,2:T(8,128)(2,1)}, u32[]{:S(2)}, u32[]{:S(2)}) collective-permute-start(bf16[4,128,1,2,640]{4,1,0,3,2:T(8,128)(2,1)} %bitcast.256), channel_id=1, source_target_pairs={{0,1},{1,0},{2,3},{3,2},{4,5},{5,4},{6,7},{7,6},{8,9},{9,8},{10,11... | collective-permute-start | bytes 3932168 | tf_op jit(solution)/shard_map/ppermute | solution.py:127
  156.8 23.2 %collective-permute-start = (bf16[64,1,2,1024]{3,0,1,2:T(8,128)(2,1)}, bf16[64,1,2,1024]{3,0,1,2:T(8,128)(2,1)S(1)}, u32[]{:S(2)}, u32[]{:S(2)}) collective-permute-start(bf16[64,1,2,1024]{3,0,1,2:T(8,128)(2,1)} %get-tuple-element.49), channel_id=1, source_target_pairs={{0,4},{4,8},{8,12},{12,0},{1,5},{5,9},{9,13},{13,1},{2,6},{6,10},{... | collective-permute-start | bytes 786440 | tf_op jit(solution)/shard_map/ppermute | solution.py:117
  157.6 22.5 %collective-permute-start.1 = (bf16[64,1,2,1024]{3,0,1,2:T(8,128)(2,1)S(1)}, bf16[64,1,2,1024]{3,0,1,2:T(8,128)(2,1)S(1)}, u32[]{:S(2)}, u32[]{:S(2)}) collective-permute-start(bf16[64,1,2,1024]{3,0,1,2:T(8,128)(2,1)S(1)} %get-tuple-element.51), channel_id=1, source_target_pairs={{0,8},{4,12},{8,0},{12,4},{1,9},{5,13},{9,1},{13,5},{2,10},{6,14},... | collective-permute-start | bytes 786440 | tf_op jit(solution)/shard_map/ppermute | solution.py:117
  158.8 21.3 %collective-permute-start.2 = (bf16[64,1,2,1024]{3,0,1,2:T(8,128)(2,1)S(1)}, bf16[64,1,2,1024]{3,0,1,2:T(8,128)(2,1)S(1)}, u32[]{:S(2)}, u32[]{:S(2)}) collective-permute-start(bf16[64,1,2,1024]{3,0,1,2:T(8,128)(2,1)S(1)} %get-tuple-element.50), channel_id=1, source_target_pairs={{0,12},{4,0},{8,4},{12,8},{1,13},{5,1},{9,5},{13,9},{2,14},{6,2},{... | collective-permute-start | bytes 786440 | tf_op jit(solution)/shard_map/ppermute | solution.py:117
  172.9 3.4 %copy-start = (bf16[2,1,8,128,1024]{4,3,2,0,1:T(8,128)(2,1)S(1)}, bf16[2,1,8,128,1024]{4,3,2,0,1:T(8,128)(2,1)}, u32[]{:S(2)}) copy-start(bf16[2,1,8,128,1024]{4,3,2,0,1:T(8,128)(2,1)} %copy.31) | copy-start | bytes 12582916
Sparse Core Ops, SparseCore 0:
  72.8 25.1 reduce-scatter.2
  100.3 20.9 reduce-scatter.4
  123.1 31.6 all-gather.1

commit v21 on v17

--- a/solution.py
+++ b/solution.py
@@ -100,7 +100,8 @@
     own_order = lax.dynamic_slice_in_dim(order_table, core_index, 1, 1).reshape(-1)
     corr_part = jnp.take(corr_all, own_order, axis=0).astype(jnp.bfloat16)
 
-    gram_strip, corr_part, power_trace = lax.optimization_barrier((gram_strip, corr_part, downgoing))
+    local_power = jnp.sum(jnp.square(downgoing.astype(jnp.float32)), axis=(0, 2, 3))
+    gram_strip, corr_part, local_power = lax.optimization_barrier((gram_strip, corr_part, local_power))
 
     shot_index = lax.axis_index("shot")
     corr_blocks = corr_part.reshape(shot_count, source_local, *corr_part.shape[1:])
@@ -112,7 +113,6 @@
 
     across = lax.all_gather(gram_strip, "shot", axis=0, tiled=True)
     across = across.reshape(shot_count, rows_each, freq_local, 2, span)
-    local_power = jnp.sum(jnp.square(power_trace.astype(jnp.float32)), axis=(0, 2, 3))
     power = lax.psum(local_power, "shot") / receivers
     across, power = lax.optimization_barrier((across, power))
     power_wide = power[None, :, None, None]

time: 139 us -> 139 us (level)
  waiting for transfers between devices: 33.5 us -> 35.4 us
  other arithmetic: 24.7 us -> 22.9 us
    all_gather x1, waiting for transfers between devices: 19.9 us -> 22.2 us  [per_device(): across = lax.all_gather(gram_strip, 'shot', axis=0, tiled=True)]
    convert_element_type x1, other arithmetic: 3.27 us -> 1.47 us  [per_device(): corr_part = jnp.take(corr_all, own_order, axis=0).astype(jnp.bfloat16)]
  transfers between devices with their start and end apart: 6 -> 6, of which waited for: 3 -> 3; matrix products, arithmetic and copies ran while one was open for 33% -> 32% of each run, Pallas kernels for 0% -> 0%
where the time goes in v21:
time: 139 us; the launch traced here: 138 us
  local copies, waits for them, and re-layouts  39.1 us (28%)
  waiting for transfers between devices  35.4 us (25%)
  other arithmetic  22.9 us (16%)
  between operations  14.5 us (10%)
  matrix products  12.6 us (9%)
  blocking collectives  10.2 us (7%)
  starting transfers between devices  3.49 us (3%)
    all_gather x1, waiting for transfers between devices, per_device(): across = lax.all_gather(gram_strip, 'shot', axis=0, tiled=True)  22.2 us
    psum x1, blocking collectives, per_device(): power = lax.psum(local_power, 'shot') / receivers  10.2 us
    reduce_scatter x1, waiting for transfers between devices, per_device(): lax.psum_scatter(gram_part, 'shot', scatter_dimension=0, tiled=True)  9.43 us
    transpose x1, local copies, waits for them, and re-layouts, per_device(): jnp.einsum('qtpu,qto->uqpo', stacked_left(upgoing), right, preferred_elem...  6.61 us
    another operation x1, local copies, waits for them, and re-layouts, rebuild_gram(): whole = jnp.where(direct, upper.reshape(shape6), mirror.reshape(shape6))  6.27 us
    unnamed x19, local copies, waits for them, and re-layouts  5.95 us
    gather x1, local copies, waits for them, and re-layouts, per_device(): corr_part = jnp.take(corr_all, own_order, axis=0).astype(jnp.bfloat16)  5.28 us
    dot_general x1, matrix products, per_device(): jnp.einsum('qtpu,qto->uqpo', stacked_left(upgoing), right, preferred_elem...  4.58 us
  transfers between devices with their start and end apart: 6, of which 3 were waited for; matrix products, arithmetic and copies ran while one was open for 32% of the time, Pallas kernels for 0%

profile of v21, /device:TPU:0, one launch (start us, length us, event | category | flops | bytes accessed | tf_op | source)
XLA Modules:
  0.0 138.1 jit_solution(11540533351473334212)
XLA Ops:
  6.5 2.2 %fusion.90 = (bf16[1,1,768,1024]{3,2,1,0:T(8,128)(2,1)S(1)}, bf16[1,1,768,1024]{3,2,1,0:T(8,128)(2,1)S(1)}) fusion(bf16[2,1,768,1024]{3,2,1,0:T(8,128)(2,1)} %param.3), kind=kLoop, calls=%fused_computation.182 | loop fusion | bytes 6291456 | tf_op jit(solution)/shard_map/slice | solution.py:26
  8.7 1.6 %copy.41 = bf16[1,1,768,1024]{2,3,1,0:T(8,128)(2,1)} copy(bf16[1,1,768,1024]{3,2,1,0:T(8,128)(2,1)S(1)} %get-tuple-element.23) | data formatting | bytes 3145728
  13.0 1.7 %fusion.16 = (bf16[1,1,1536,1024]{2,3,1,0:T(8,128)(2,1)S(1)}, bf16[1,1,1536,1024]{2,3,1,0:T(8,128)(2,1)S(1)}) fusion(bf16[1,768,1024]{1,2,0:T(8,128)(2,1)S(1)} %bitcast.223, bf16[1,768,1024]{1,2,0:T(8,128)(2,1)S(1)} %bitcast.219, bf16[1,768,1024]{1,2,0:T(8,128)(2,1)} %bitcast_negate_fusion), kind=kLoop, calls=%fused_computation.52 | loop fusion | flops 12582912 | bytes 11010048 | tf_op jit(solution)/shard_map/stack | solution.py:16
  15.3 3.7 %convert_bitcast_fusion = bf16[4,128,1,2,1024]{1,4,0,3,2:T(8,128)(2,1)S(1)} fusion(bf16[1,2,4,2,128,1536]{5,4,3,2,1,0:T(8,128)(2,1)S(1)} %bitcast.222, s32[]{:T(128)S(6)} %select_n.120, bf16[1,768,1024]{1,2,0:T(8,128)(2,1)S(1)} %bitcast.224, bf16[1,768,1024]{1,2,0:T(8,128)(2,1)S(1)} %bitcast.220), kind=kOutput, calls=%fused_computation.44 | convolution fusion | flops 3228565504 | bytes 8388612 | tf_op jit(solution)/shard_map/qpkit,qto->kiqpo/dot_general | solution.py:92
  20.3 3.0 %pad_slice_fusion.11 = (bf16[1,128,1,2,2048]{1,4,0,3,2:T(8,128)(2,1)}, bf16[1,128,1,2,2048]{1,4,0,3,2:T(8,128)(2,1)}, bf16[1,128,1,2,2048]{1,4,0,3,2:T(8,128)(2,...) fusion(bf16[4,128,1,2,1024]{1,4,0,3,2:T(8,128)(2,1)S(1)} %conve, ...), kind=kLoop, calls=%fused_computation.15 | loop fusion | bytes 8388608 | tf_op jit(solution)/shard_map/slice | solution.py:52
  23.3 1.5 %fusion.44 = (bf16[1,128,1,2,640]{1,4,0,3,2:T(8,128)(2,1)S(1)}, bf16[1,128,1,2,640]{1,4,0,3,2:T(8,128)(2,1)S(1)}) fusion(s32[]{:T(128)S(6)} %select_n.128, bf16[4,128,1,2,1024]{1,4,0,3,2:T(8,128)(2,1)} %copy-done.2, bf16[1,128,1,2,2048]{1,4,0,3,2:T(8,128)(2,1)} %get-tuple-element.37, s32[]{:T(128)S(6)} %select_n.122, ...), kind=kLoop, calls=%fused_computation.96 | loop fusion | flops 1310720 | bytes 3407880 | tf_op jit(solution)/shard_map/concatenate | solution.py:48
  24.8 1.5 %dynamic-slice_maximum_fusion = (bf16[1,128,1,2,640]{1,4,0,3,2:T(8,128)(2,1)S(1)}, bf16[1,128,1,2,640]{1,4,0,3,2:T(8,128)(2,1)S(1)}) fusion(bf16[1,128,1,2,2048]{1,4,0,3,2:T(8,128)(2,1)} %get-tuple-element.40, s32[]{:T(128)S(6)} %select_n.126, bf16[1,128,1,2,2048]{1,4,0,3,2:T(8,128)(2,1)} %get-tuple-element.39, ...), kind=kLoop, calls=%fused_computation.97 | loop fusion | flops 1310720 | bytes 1966088 | tf_op jit(solution)/shard_map/concatenate | solution.py:48
  27.5 2.5 %copy.31 = bf16[4,128,1,2,640]{4,1,0,3,2:T(8,128)(2,1)} copy(bf16[4,128,1,2,640]{1,4,0,3,2:T(8,128)(2,1)} %pad_maximum_fusion.3) | data formatting | bytes 2621440 | tf_op jit(solution)/shard_map/stack | solution.py:53
  31.2 1.5 %slice_bitcast_fusion.3 = (bf16[1,768,512]{2,1,0:T(8,128)(2,1)S(1)}, bf16[1,768,512]{2,1,0:T(8,128)(2,1)S(1)}) fusion(bf16[2,1,768,512]{3,2,1,0:T(8,128)(2,1)} %param.4), kind=kLoop, calls=%fused_computation.54 | loop fusion | bytes 3145728 | tf_op jit(solution)/shard_map/squeeze | solution.py:20
  33.0 4.6 %fusion.8 = bf16[512,2,1024]{0,2,1:T(8,128)(2,1)} fusion(bf16[1,1536,1,512]{3,1,2,0:T(8,128)(2,1)S(1)} %get-tuple-element.61, bf16[1,1536,1,512]{3,1,2,0:T(8,128)(2,1)S(1)} %get-tuple-element.60, bf16[1,768,1024]{1,2,0:T(8,128)(2,1)S(1)} %bitcast.225, bf16[1,768,1024]{1,2,0:T(8,128)(2,1)S(1)} %bitcast.221), kind=kOutput, calls=%fused_computation.38 | convolution fusion | flops 3233808384 | bytes 8388608 | tf_op jit(solution)/shard_map/qtpu,qto->uqpo/dot_general | solution.py:96
  37.6 6.6 %copy.32 = bf16[512,2,1024]{2,1,0:T(2,128)(2,1)} copy(bf16[512,2,1024]{0,2,1:T(8,128)(2,1)} %fusion.8) | data formatting | bytes 4194304 | tf_op jit(solution)/shard_map/qtpu,qto->uqpo/transpose | solution.py:96
  45.6 5.3 %gather_fusion = bf16[256,2,1024]{2,1,0:T(2,128)(2,1)} fusion(bf16[512,2,1024]{2,1,0:T(2,128)(2,1)} %copy.32, s32[1024]{0:T(1024)S(1)} %pad_clamp_fusion), kind=kCustom, calls=%fused_computation | custom fusion | bytes 2098176 | tf_op jit(solution)/shard_map/jit(_take)/gather | solution.py:101
  50.9 2.2 %multiply_reduce_fusion = f32[]{:T(128)} fusion(bf16[2,1,768,1024]{3,2,1,0:T(8,128)(2,1)S(1)} %copy-done.1), kind=kLoop, calls=%fused_computation.3 | loop fusion | flops 4718591 | bytes 3145732 | tf_op jit(solution)/shard_map/reduce_sum | solution.py:103
  53.2 1.5 %fusion.11 = bf16[256,1,2,1024]{3,2,0,1:T(2,128)(2,1)S(1)} fusion(bf16[256,2,1024]{2,1,0:T(2,128)(2,1)S(1)} %copy-done.4, pred[256]{0:T(512)(128)(4,1)S(1)} %compare_and_fusion), kind=kLoop, calls=%fused_computation.43 | loop fusion | flops 524288 | bytes 2097408 | tf_op jit(solution)/shard_map/convert_element_type | solution.py:101
  54.6 9.4 %reduce-scatter.2.cloned.1.call-done = bf16[128,1,2,640]{3,0,2,1:T(8,128)(2,1)} async-done(((bf16[512,1,2,640]{3,0,2,1:T(8,128)(2,1)}), bf16[128,1,2,640]{3,0,2,1:T(8,128)(2,1)}) %reduce-scatter.2.cloned.1.call-update) | async-done | bytes 327696 | tf_op jit(solution)/shard_map/reduce_scatter | solution.py:94
  64.1 10.2 %psum.7 = f32[1]{0:T(128)} all-reduce(f32[1]{0:T(128)} %bitcast.24), channel_id=1, replica_groups=mesh['grp'=2,'shot'=4,'freq'=2,'sub'=2] {'shot'}, use_global_device_ids=true, to_apply=%region_2.3 | all-reduce | flops 1 | bytes 8 | tf_op jit(solution)/shard_map/psum | solution.py:116
  74.9 22.2 %all-gather.2.cloned.1.call-done = bf16[512,1,2,640]{3,0,2,1:T(8,128)(2,1)} async-done(((bf16[128,1,2,640]{3,0,2,1:T(8,128)(2,1)}), bf16[512,1,2,640]{3,0,2,1:T(8,128)(2,1)}) %all-gather.2.cloned.1.call-update) | async-done | bytes 1310736 | tf_op jit(solution)/shard_map/all_gather | solution.py:114
  99.1 1.4 %collective-permute-start.2 = (bf16[64,1,2,1024]{3,0,1,2:T(8,128)(2,1)}, bf16[64,1,2,1024]{3,0,1,2:T(8,128)(2,1)S(1)}, u32[]{:S(2)}, u32[]{:S(2)}) collective-permute-start(bf16[64,1,2,1024]{3,0,1,2:T(8,128)(2,1)} %get-tuple-element.56), channel_id=1, source_target_pairs={{0,12},{4,0},{8,4},{12,8},{1,13},{5,1},{9,5},{13,9},{2,14},{6,2},{... | collective-permute-start | bytes 786440 | tf_op jit(solution)/shard_map/ppermute | solution.py:112
  102.6 2.0 %select_bitcast_fusion.1 = (bf16[4,1,128,1,2,640]{5,2,1,0,4,3:T(8,128)(2,1)S(1)}, bf16[4,1,128,1,2,640]{5,2,1,0,4,3:T(8,128)(2,1)S(1)}) fusion(bf16[4,128,1,2,640]{4,1,0,3,2:T(8,128)(2,1)} %bitcast.233, bf16[4,128,1,2,640]{4,1,0,3,2:T(8,128)(2,1)} %collective-permute-done.3, pred[]{:T(512)S(6)} %eq.10), kind=kLoop, calls=%fused_computation.49 | loop fusion | flops 1310720 | bytes 5242881 | tf_op jit(solution)/shard_map/stack | solution.py:124
  105.6 2.4 %copy.36 = bf16[2,1,8,128,1024]{4,3,2,0,1:T(8,128)(2,1)} copy(bf16[2,1,8,128,1024]{4,3,0,1,2:T(8,128)(2,1)S(1)} %bitcast.226) | data formatting | bytes 8388608 | tf_op jit(solution)/shard_map/transpose | solution.py:63
  108.1 6.3 %copy.37 = bf16[2,1,1024,1024]{2,3,0,1:T(8,128)(2,1)} copy(bf16[2,1,1024,1024]{3,2,0,1:T(8,128)(2,1)} %bitcast.216) | data formatting | bytes 8388608 | tf_op jit(solution)/shard_map/reshape;reshape | solution.py:70
  114.3 2.6 %fusion.89 = (bf16[1,1,1024,1024]{3,2,0,1:T(8,128)(2,1)S(1)}, bf16[1,1,1024,1024]{3,2,0,1:T(8,128)(2,1)S(1)}) fusion(bf16[2,1,1024,1024]{3,2,0,1:T(8,128)(2,1)} %bitcast.217), kind=kLoop, calls=%fused_computation.181 | loop fusion | flops 1048576 | bytes 8388608 | tf_op jit(solution)/shard_map/slice | solution.py:65
  117.8 2.5 %divide_convert_fusion = bf16[2,1,1024,1024]{3,2,0,1:T(8,128)(2,1)S(1)} fusion(bf16[1,1,1024,1024]{3,2,0,1:T(8,128)(2,1)S(1)} %get-tuple-element.22, bf16[1,1,1024,1024]{3,2,0,1:T(8,128)(2,1)S(1)} %get-tuple-element.21, f32[]{:T(128)} %bitcast.31, pred[1024,1024]{1,0:T(8,128)(4,1)S(1)} %bitcast.231, bf16[2,1,8,128,1024]{4,3,2,0,1:T(8,128)(2,1)S(1)} %copy-done), kind=kLoop, calls=%fused_computation.1 | loop fusion | flops 10485760 | bytes 13631492 | tf_op jit(solution)/shard_map/convert_element_type | solution.py:132
  121.5 3.7 %collective-permute-done.1 = bf16[64,1,2,1024]{3,0,1,2:T(8,128)(2,1)S(1)} collective-permute-done((bf16[64,1,2,1024]{3,0,1,2:T(8,128)(2,1)S(1)}, bf16[64,1,2,1024]{3,0,1,2:T(8,128)(2,1)S(1)}, u32[]{:S(2)}, u32[]{:S(2)}) %collective-permute-start.1) | collective-permute-done | bytes 262176 | tf_op jit(solution)/shard_map/ppermute | solution.py:112
  (84 shorter events, 21.8 us)
Async XLA Ops:
  6.5 57.5 %reduce-scatter.2.cloned.1.call-start = ((), (), s32[]{:S(2)}) async-start(), calls=%async_computation.1 | async-start | bytes 1638400 | tf_op jit(solution)/shard_map/reduce_scatter | solution.py:94
  11.1 2.0 %copy-start.3 = (bf16[1,1,768,1024]{2,3,1,0:T(8,128)(2,1)S(1)}, bf16[1,1,768,1024]{2,3,1,0:T(8,128)(2,1)}, u32[]{:S(2)}) copy-start(bf16[1,1,768,1024]{2,3,1,0:T(8,128)(2,1)} %copy.41) | copy-start | bytes 4718596
  19.0 1.4 copy-start.2
  30.0 67.2 %all-gather.2.cloned.1.call-start = ((), (), s32[]{:S(2)}) async-start(), calls=%async_computation.2 | async-start | bytes 1638400 | tf_op jit(solution)/shard_map/all_gather | solution.py:114
  37.6 6.6 %copy-start.5 = (s32[512]{0:T(512)S(1)}, s32[512]{0:T(512)}, u32[]{:S(2)}) copy-start(s32[512]{0:T(512)} %param.5) | copy-start | bytes 6148
  37.6 13.3 %copy-start.1 = (bf16[2,1,768,1024]{3,2,1,0:T(8,128)(2,1)S(1)}, bf16[2,1,768,1024]{3,2,1,0:T(8,128)(2,1)}, u32[]{:S(2)}) copy-start(bf16[2,1,768,1024]{3,2,1,0:T(8,128)(2,1)} %param.3) | copy-start | bytes 9437188
  50.9 2.2 %copy-start.4 = (bf16[256,2,1024]{2,1,0:T(2,128)(2,1)S(1)}, bf16[256,2,1024]{2,1,0:T(2,128)(2,1)}, u32[]{:S(2)}) copy-start(bf16[256,2,1024]{2,1,0:T(2,128)(2,1)} %gather_fusion) | copy-start | bytes 3145732
  97.1 5.4 %collective-permute-start.3 = (bf16[4,128,1,2,640]{4,1,0,3,2:T(8,128)(2,1)}, bf16[4,128,1,2,640]{4,1,0,3,2:T(8,128)(2,1)}, u32[]{:S(2)}, u32[]{:S(2)}) collective-permute-start(bf16[4,128,1,2,640]{4,1,0,3,2:T(8,128)(2,1)} %bitcast.232), channel_id=1, source_target_pairs={{0,1},{1,0},{2,3},{3,2},{4,5},{5,4},{6,7},{7,6},{8,9},{9,8},{10,11... | collective-permute-start | bytes 3932168 | tf_op jit(solution)/shard_map/ppermute | solution.py:121
  99.1 22.3 %collective-permute-start.2 = (bf16[64,1,2,1024]{3,0,1,2:T(8,128)(2,1)}, bf16[64,1,2,1024]{3,0,1,2:T(8,128)(2,1)S(1)}, u32[]{:S(2)}, u32[]{:S(2)}) collective-permute-start(bf16[64,1,2,1024]{3,0,1,2:T(8,128)(2,1)} %get-tuple-element.56), channel_id=1, source_target_pairs={{0,12},{4,0},{8,4},{12,8},{1,13},{5,1},{9,5},{13,9},{2,14},{6,2},{... | collective-permute-start | bytes 786440 | tf_op jit(solution)/shard_map/ppermute | solution.py:112
  100.5 24.6 %collective-permute-start.1 = (bf16[64,1,2,1024]{3,0,1,2:T(8,128)(2,1)S(1)}, bf16[64,1,2,1024]{3,0,1,2:T(8,128)(2,1)S(1)}, u32[]{:S(2)}, u32[]{:S(2)}) collective-permute-start(bf16[64,1,2,1024]{3,0,1,2:T(8,128)(2,1)S(1)} %get-tuple-element.57), channel_id=1, source_target_pairs={{0,8},{4,12},{8,0},{12,4},{1,9},{5,13},{9,1},{13,5},{2,10},{6,14},... | collective-permute-start | bytes 786440 | tf_op jit(solution)/shard_map/ppermute | solution.py:112
  101.4 23.8 %collective-permute-start = (bf16[64,1,2,1024]{3,0,1,2:T(8,128)(2,1)S(1)}, bf16[64,1,2,1024]{3,0,1,2:T(8,128)(2,1)S(1)}, u32[]{:S(2)}, u32[]{:S(2)}) collective-permute-start(bf16[64,1,2,1024]{3,0,1,2:T(8,128)(2,1)S(1)} %get-tuple-element.55), channel_id=1, source_target_pairs={{0,4},{4,8},{8,12},{12,0},{1,5},{5,9},{9,13},{13,1},{2,6},{6,10},{... | collective-permute-start | bytes 786440 | tf_op jit(solution)/shard_map/ppermute | solution.py:112
  114.3 3.4 %copy-start = (bf16[2,1,8,128,1024]{4,3,2,0,1:T(8,128)(2,1)S(1)}, bf16[2,1,8,128,1024]{4,3,2,0,1:T(8,128)(2,1)}, u32[]{:S(2)}) copy-start(bf16[2,1,8,128,1024]{4,3,2,0,1:T(8,128)(2,1)} %copy.36) | copy-start | bytes 12582916
Sparse Core Ops, SparseCore 0:
  30.1 33.9 reduce-scatter.1
  65.6 31.4 all-gather.1

commit v22 on v17

--- a/solution.py
+++ b/solution.py
@@ -113,7 +113,11 @@
     across = lax.all_gather(gram_strip, "shot", axis=0, tiled=True)
     across = across.reshape(shot_count, rows_each, freq_local, 2, span)
     local_power = jnp.sum(jnp.square(power_trace.astype(jnp.float32)), axis=(0, 2, 3))
-    power = lax.psum(local_power, "shot") / receivers
+    total_power = local_power
+    for shift in range(1, shot_count):
+        pairs = [(k, (k + shift) % shot_count) for k in range(shot_count)]
+        total_power = total_power + lax.ppermute(local_power, "shot", perm=pairs)
+    power = total_power / receivers
     across, power = lax.optimization_barrier((across, power))
     power_wide = power[None, :, None, None]
 

time: 139 us -> 139 us (level)
  blocking collectives: 10.4 us -> 0 us
  starting transfers between devices: 3.4 us -> 7.62 us
  waiting for transfers between devices: 33.5 us -> 37.7 us
  between operations: 14.5 us -> 16.4 us
    psum x1 -> x0, blocking collectives: 10.4 us -> none  [per_device(): power = lax.psum(local_power, 'shot') / receivers]
    ppermute x0 -> x3, starting transfers between devices: none -> 4.14 us  [per_device(): total_power = total_power + lax.ppermute(local_power, 'shot', perm=pairs)]
    all_gather x1, waiting for transfers between devices: 19.9 us -> 22.8 us  [per_device(): across = lax.all_gather(gram_strip, 'shot', axis=0, tiled=True)]
  transfers between devices with their start and end apart: 6 -> 9, of which waited for: 3 -> 4; matrix products, arithmetic and copies ran while one was open for 33% -> 33% of each run, Pallas kernels for 0% -> 0%
where the time goes in v22:
time: 139 us; the launch traced here: 138 us
  local copies, waits for them, and re-layouts  39 us (28%)
  waiting for transfers between devices  37.7 us (27%)
  other arithmetic  24.6 us (18%)
  between operations  16.4 us (12%)
  matrix products  12.6 us (9%)
  starting transfers between devices  7.62 us (5%)
    all_gather x1, waiting for transfers between devices, per_device(): across = lax.all_gather(gram_strip, 'shot', axis=0, tiled=True)  22.8 us
    reduce_scatter x1, waiting for transfers between devices, per_device(): lax.psum_scatter(gram_part, 'shot', scatter_dimension=0, tiled=True)  9.92 us
    transpose x1, local copies, waits for them, and re-layouts, per_device(): jnp.einsum('qtpu,qto->uqpo', stacked_left(upgoing), right, preferred_elem...  6.27 us
    another operation x1, local copies, waits for them, and re-layouts, rebuild_gram(): whole = jnp.where(direct, upper.reshape(shape6), mirror.reshape(shape6))  6.26 us
    unnamed x19, local copies, waits for them, and re-layouts  5.93 us
    gather x1, local copies, waits for them, and re-layouts, per_device(): corr_part = jnp.take(corr_all, own_order, axis=0).astype(jnp.bfloat16)  5.28 us
    dot_general x1, matrix products, per_device(): jnp.einsum('qtpu,qto->uqpo', stacked_left(upgoing), right, preferred_elem...  4.58 us
    dot_general x6, matrix products, sweep_whole(): jnp.einsum('qjc,qcr->qjr', stacked, wide, preferred_element_type=jnp.floa...  4.36 us
  transfers between devices with their start and end apart: 9, of which 4 were waited for; matrix products, arithmetic and copies ran while one was open for 33% of the time, Pallas kernels for 0%

profile of v22, /device:TPU:0, one launch (start us, length us, event | category | flops | bytes accessed | tf_op | source)
XLA Modules:
  0.0 138.1 jit_solution(4718407722957995708)
XLA Ops:
  6.5 2.2 %fusion.90 = (bf16[1,1,768,1024]{3,2,1,0:T(8,128)(2,1)S(1)}, bf16[1,1,768,1024]{3,2,1,0:T(8,128)(2,1)S(1)}) fusion(bf16[2,1,768,1024]{3,2,1,0:T(8,128)(2,1)} %param.3), kind=kLoop, calls=%fused_computation.182 | loop fusion | bytes 6291456 | tf_op jit(solution)/shard_map/slice | solution.py:26
  8.7 1.6 %copy.41 = bf16[1,1,768,1024]{2,3,1,0:T(8,128)(2,1)} copy(bf16[1,1,768,1024]{3,2,1,0:T(8,128)(2,1)S(1)} %get-tuple-element.23) | data formatting | bytes 3145728
  13.0 1.7 %fusion.16 = (bf16[1,1,1536,1024]{2,3,1,0:T(8,128)(2,1)S(1)}, bf16[1,1,1536,1024]{2,3,1,0:T(8,128)(2,1)S(1)}) fusion(bf16[1,768,1024]{1,2,0:T(8,128)(2,1)S(1)} %bitcast.223, bf16[1,768,1024]{1,2,0:T(8,128)(2,1)S(1)} %bitcast.219, bf16[1,768,1024]{1,2,0:T(8,128)(2,1)} %bitcast_negate_fusion), kind=kLoop, calls=%fused_computation.52 | loop fusion | flops 12582912 | bytes 11010048 | tf_op jit(solution)/shard_map/stack | solution.py:16
  15.3 3.7 %convert_bitcast_fusion = bf16[4,128,1,2,1024]{1,4,0,3,2:T(8,128)(2,1)S(1)} fusion(bf16[1,2,4,2,128,1536]{5,4,3,2,1,0:T(8,128)(2,1)S(1)} %bitcast.222, s32[]{:T(128)S(6)} %select_n.120, bf16[1,768,1024]{1,2,0:T(8,128)(2,1)S(1)} %bitcast.224, bf16[1,768,1024]{1,2,0:T(8,128)(2,1)S(1)} %bitcast.220), kind=kOutput, calls=%fused_computation.44 | convolution fusion | flops 3228565504 | bytes 8388612 | tf_op jit(solution)/shard_map/qpkit,qto->kiqpo/dot_general | solution.py:92
  20.3 2.9 %pad_slice_fusion.11 = (bf16[1,128,1,2,2048]{1,4,0,3,2:T(8,128)(2,1)}, bf16[1,128,1,2,2048]{1,4,0,3,2:T(8,128)(2,1)}, bf16[1,128,1,2,2048]{1,4,0,3,2:T(8,128)(2,...) fusion(bf16[4,128,1,2,1024]{1,4,0,3,2:T(8,128)(2,1)S(1)} %conve, ...), kind=kLoop, calls=%fused_computation.15 | loop fusion | bytes 8388608 | tf_op jit(solution)/shard_map/slice | solution.py:52
  23.2 1.5 %fusion.44 = (bf16[1,128,1,2,640]{1,4,0,3,2:T(8,128)(2,1)S(1)}, bf16[1,128,1,2,640]{1,4,0,3,2:T(8,128)(2,1)S(1)}) fusion(s32[]{:T(128)S(6)} %select_n.128, bf16[4,128,1,2,1024]{1,4,0,3,2:T(8,128)(2,1)} %copy-done.2, bf16[1,128,1,2,2048]{1,4,0,3,2:T(8,128)(2,1)} %get-tuple-element.37, s32[]{:T(128)S(6)} %select_n.122, ...), kind=kLoop, calls=%fused_computation.96 | loop fusion | flops 1310720 | bytes 3407880 | tf_op jit(solution)/shard_map/concatenate | solution.py:48
  24.7 1.5 %dynamic-slice_maximum_fusion = (bf16[1,128,1,2,640]{1,4,0,3,2:T(8,128)(2,1)S(1)}, bf16[1,128,1,2,640]{1,4,0,3,2:T(8,128)(2,1)S(1)}) fusion(bf16[1,128,1,2,2048]{1,4,0,3,2:T(8,128)(2,1)} %get-tuple-element.40, s32[]{:T(128)S(6)} %select_n.126, bf16[1,128,1,2,2048]{1,4,0,3,2:T(8,128)(2,1)} %get-tuple-element.39, ...), kind=kLoop, calls=%fused_computation.97 | loop fusion | flops 1310720 | bytes 1966088 | tf_op jit(solution)/shard_map/concatenate | solution.py:48
  27.4 2.4 %copy.31 = bf16[4,128,1,2,640]{4,1,0,3,2:T(8,128)(2,1)} copy(bf16[4,128,1,2,640]{1,4,0,3,2:T(8,128)(2,1)} %pad_maximum_fusion.3) | data formatting | bytes 2621440 | tf_op jit(solution)/shard_map/stack | solution.py:53
  31.1 1.5 %slice_bitcast_fusion.3 = (bf16[1,768,512]{2,1,0:T(8,128)(2,1)S(1)}, bf16[1,768,512]{2,1,0:T(8,128)(2,1)S(1)}) fusion(bf16[2,1,768,512]{3,2,1,0:T(8,128)(2,1)} %param.4), kind=kLoop, calls=%fused_computation.54 | loop fusion | bytes 3145728 | tf_op jit(solution)/shard_map/squeeze | solution.py:20
  32.9 4.6 %fusion.8 = bf16[512,2,1024]{0,2,1:T(8,128)(2,1)} fusion(bf16[1,1536,1,512]{3,1,2,0:T(8,128)(2,1)S(1)} %get-tuple-element.61, bf16[1,1536,1,512]{3,1,2,0:T(8,128)(2,1)S(1)} %get-tuple-element.60, bf16[1,768,1024]{1,2,0:T(8,128)(2,1)S(1)} %bitcast.225, bf16[1,768,1024]{1,2,0:T(8,128)(2,1)S(1)} %bitcast.221), kind=kOutput, calls=%fused_computation.38 | convolution fusion | flops 3233808384 | bytes 8388608 | tf_op jit(solution)/shard_map/qtpu,qto->uqpo/dot_general | solution.py:96
  37.5 6.3 %copy.32 = bf16[512,2,1024]{2,1,0:T(2,128)(2,1)} copy(bf16[512,2,1024]{0,2,1:T(8,128)(2,1)} %fusion.8) | data formatting | bytes 4194304 | tf_op jit(solution)/shard_map/qtpu,qto->uqpo/transpose | solution.py:96
  45.5 5.3 %gather_fusion = bf16[256,2,1024]{2,1,0:T(2,128)(2,1)} fusion(bf16[512,2,1024]{2,1,0:T(2,128)(2,1)} %copy.32, s32[1024]{0:T(1024)S(1)} %pad_clamp_fusion), kind=kCustom, calls=%fused_computation | custom fusion | bytes 2098176 | tf_op jit(solution)/shard_map/jit(_take)/gather | solution.py:101
  50.8 3.3 %fusion.11 = bf16[256,1,2,1024]{3,2,0,1:T(2,128)(2,1)} fusion(bf16[256,2,1024]{2,1,0:T(2,128)(2,1)} %gather_fusion, pred[256]{0:T(512)(128)(4,1)S(1)} %compare_and_fusion), kind=kLoop, calls=%fused_computation.43 | loop fusion | flops 524288 | bytes 2097408 | tf_op jit(solution)/shard_map/convert_element_type | solution.py:101
  54.1 9.9 %reduce-scatter.2.cloned.1.call-done = bf16[128,1,2,640]{3,0,2,1:T(8,128)(2,1)} async-done(((bf16[512,1,2,640]{3,0,2,1:T(8,128)(2,1)}), bf16[128,1,2,640]{3,0,2,1:T(8,128)(2,1)}) %reduce-scatter.2.cloned.1.call-update) | async-done | bytes 327696 | tf_op jit(solution)/shard_map/reduce_scatter | solution.py:94
  64.0 2.2 %multiply_reduce_fusion = f32[]{:T(128)} fusion(bf16[2,1,768,1024]{3,2,1,0:T(8,128)(2,1)S(1)} %copy-done.1), kind=kLoop, calls=%fused_computation.3 | loop fusion | flops 4718591 | bytes 3145732 | tf_op jit(solution)/shard_map/reduce_sum | solution.py:115
  66.2 1.8 %collective-permute-start.4 = (f32[1]{0:T(128)}, f32[1]{0:T(128)}, u32[]{:S(2)}, u32[]{:S(2)}) collective-permute-start(f32[1]{0:T(128)} %bitcast.30), channel_id=1, source_target_pairs={{0,8},{4,12},{8,0},{12,4},{1,9},{5,13},{9,1},{13,5},{2,10},{6,14},... | collective-permute-start | bytes 20 | tf_op jit(solution)/shard_map/ppermute | solution.py:119
  68.0 2.4 %collective-permute-start.5 = (f32[1]{0:T(128)}, f32[1]{0:T(128)}, u32[]{:S(2)}, u32[]{:S(2)}) collective-permute-start(f32[1]{0:T(128)} %bitcast.30), channel_id=1, source_target_pairs={{0,12},{4,0},{8,4},{12,8},{1,13},{5,1},{9,5},{13,9},{2,14},{6,2},{... | collective-permute-start | bytes 20 | tf_op jit(solution)/shard_map/ppermute | solution.py:119
  74.2 22.8 %all-gather.2.cloned.1.call-done = bf16[512,1,2,640]{3,0,2,1:T(8,128)(2,1)} async-done(((bf16[128,1,2,640]{3,0,2,1:T(8,128)(2,1)}), bf16[512,1,2,640]{3,0,2,1:T(8,128)(2,1)}) %all-gather.2.cloned.1.call-update) | async-done | bytes 1310736 | tf_op jit(solution)/shard_map/all_gather | solution.py:113
  102.5 2.0 %select_bitcast_fusion.1 = (bf16[4,1,128,1,2,640]{5,2,1,0,4,3:T(8,128)(2,1)S(1)}, bf16[4,1,128,1,2,640]{5,2,1,0,4,3:T(8,128)(2,1)S(1)}) fusion(bf16[4,128,1,2,640]{4,1,0,3,2:T(8,128)(2,1)} %bitcast.233, bf16[4,128,1,2,640]{4,1,0,3,2:T(8,128)(2,1)} %collective-permute-done.6, pred[]{:T(512)S(6)} %eq.10), kind=kLoop, calls=%fused_computation.49 | loop fusion | flops 1310720 | bytes 5242881 | tf_op jit(solution)/shard_map/stack | solution.py:128
  105.6 2.4 %copy.36 = bf16[2,1,8,128,1024]{4,3,2,0,1:T(8,128)(2,1)} copy(bf16[2,1,8,128,1024]{4,3,0,1,2:T(8,128)(2,1)S(1)} %bitcast.226) | data formatting | bytes 8388608 | tf_op jit(solution)/shard_map/transpose | solution.py:63
  108.0 6.3 %copy.37 = bf16[2,1,1024,1024]{2,3,0,1:T(8,128)(2,1)} copy(bf16[2,1,1024,1024]{3,2,0,1:T(8,128)(2,1)} %bitcast.216) | data formatting | bytes 8388608 | tf_op jit(solution)/shard_map/reshape;reshape | solution.py:70
  114.2 2.6 %fusion.89 = (bf16[1,1,1024,1024]{3,2,0,1:T(8,128)(2,1)S(1)}, bf16[1,1,1024,1024]{3,2,0,1:T(8,128)(2,1)S(1)}) fusion(bf16[2,1,1024,1024]{3,2,0,1:T(8,128)(2,1)} %bitcast.217), kind=kLoop, calls=%fused_computation.181 | loop fusion | flops 1048576 | bytes 8388608 | tf_op jit(solution)/shard_map/slice | solution.py:65
  117.7 2.5 %divide_convert_fusion = bf16[2,1,1024,1024]{3,2,0,1:T(8,128)(2,1)S(1)} fusion(bf16[1,1,1024,1024]{3,2,0,1:T(8,128)(2,1)S(1)} %get-tuple-element.22, bf16[1,1,1024,1024]{3,2,0,1:T(8,128)(2,1)S(1)} %get-tuple-element.21, f32[]{:T(128)} %bitcast.31, pred[1024,1024]{1,0:T(8,128)(4,1)S(1)} %bitcast.231, bf16[2,1,8,128,1024]{4,3,2,0,1:T(8,128)(2,1)S(1)} %copy-done), kind=kLoop, calls=%fused_computation.1 | loop fusion | flops 10485760 | bytes 13631492 | tf_op jit(solution)/shard_map/convert_element_type | solution.py:136
  121.4 3.7 %collective-permute-done.1 = bf16[64,1,2,1024]{3,0,1,2:T(8,128)(2,1)S(1)} collective-permute-done((bf16[64,1,2,1024]{3,0,1,2:T(8,128)(2,1)S(1)}, bf16[64,1,2,1024]{3,0,1,2:T(8,128)(2,1)S(1)}, u32[]{:S(2)}, u32[]{:S(2)}) %collective-permute-start.1) | collective-permute-done | bytes 262176 | tf_op jit(solution)/shard_map/ppermute | solution.py:111
  (89 shorter events, 24.8 us)
Async XLA Ops:
  6.5 57.4 %reduce-scatter.2.cloned.1.call-start = ((), (), s32[]{:S(2)}) async-start(), calls=%async_computation.1 | async-start | bytes 1638400 | tf_op jit(solution)/shard_map/reduce_scatter | solution.py:94
  11.0 2.0 %copy-start.3 = (bf16[1,1,768,1024]{2,3,1,0:T(8,128)(2,1)S(1)}, bf16[1,1,768,1024]{2,3,1,0:T(8,128)(2,1)}, u32[]{:S(2)}) copy-start(bf16[1,1,768,1024]{2,3,1,0:T(8,128)(2,1)} %copy.41) | copy-start | bytes 4718596
  19.0 1.4 copy-start.2
  29.9 67.2 %all-gather.2.cloned.1.call-start = ((), (), s32[]{:S(2)}) async-start(), calls=%async_computation.2 | async-start | bytes 1638400 | tf_op jit(solution)/shard_map/all_gather | solution.py:113
  37.5 6.3 %copy-start.5 = (s32[512]{0:T(512)S(1)}, s32[512]{0:T(512)}, u32[]{:S(2)}) copy-start(s32[512]{0:T(512)} %param.5) | copy-start | bytes 6148
  43.8 20.2 %copy-start.1 = (bf16[2,1,768,1024]{3,2,1,0:T(8,128)(2,1)S(1)}, bf16[2,1,768,1024]{3,2,1,0:T(8,128)(2,1)}, u32[]{:S(2)}) copy-start(bf16[2,1,768,1024]{3,2,1,0:T(8,128)(2,1)} %param.3) | copy-start | bytes 9437188
  66.2 31.8 %copy-start.4 = (bf16[256,1,2,1024]{3,2,0,1:T(2,128)(2,1)S(1)}, bf16[256,1,2,1024]{3,2,0,1:T(2,128)(2,1)}, u32[]{:S(2)}) copy-start(bf16[256,1,2,1024]{3,2,0,1:T(2,128)(2,1)} %fusion.11) | copy-start | bytes 3145732
  66.2 5.4 %collective-permute-start.3 = (f32[1]{0:T(128)}, f32[1]{0:T(128)}, u32[]{:S(2)}, u32[]{:S(2)}) collective-permute-start(f32[1]{0:T(128)} %bitcast.30), channel_id=1, source_target_pairs={{0,4},{4,8},{8,12},{12,0},{1,5},{5,9},{9,13},{13,1},{2,6},{6,10},{... | collective-permute-start | bytes 20 | tf_op jit(solution)/shard_map/ppermute | solution.py:119
  66.2 6.7 %collective-permute-start.4 = (f32[1]{0:T(128)}, f32[1]{0:T(128)}, u32[]{:S(2)}, u32[]{:S(2)}) collective-permute-start(f32[1]{0:T(128)} %bitcast.30), channel_id=1, source_target_pairs={{0,8},{4,12},{8,0},{12,4},{1,9},{5,13},{9,1},{13,5},{2,10},{6,14},... | collective-permute-start | bytes 20 | tf_op jit(solution)/shard_map/ppermute | solution.py:119
  68.0 5.6 %collective-permute-start.5 = (f32[1]{0:T(128)}, f32[1]{0:T(128)}, u32[]{:S(2)}, u32[]{:S(2)}) collective-permute-start(f32[1]{0:T(128)} %bitcast.30), channel_id=1, source_target_pairs={{0,12},{4,0},{8,4},{12,8},{1,13},{5,1},{9,5},{13,9},{2,14},{6,2},{... | collective-permute-start | bytes 20 | tf_op jit(solution)/shard_map/ppermute | solution.py:119
  97.1 5.4 %collective-permute-start.6 = (bf16[4,128,1,2,640]{4,1,0,3,2:T(8,128)(2,1)}, bf16[4,128,1,2,640]{4,1,0,3,2:T(8,128)(2,1)}, u32[]{:S(2)}, u32[]{:S(2)}) collective-permute-start(bf16[4,128,1,2,640]{4,1,0,3,2:T(8,128)(2,1)} %bitcast.232), channel_id=1, source_target_pairs={{0,1},{1,0},{2,3},{3,2},{4,5},{5,4},{6,7},{7,6},{8,9},{9,8},{10,11... | collective-permute-start | bytes 3932168 | tf_op jit(solution)/shard_map/ppermute | solution.py:125
  99.1 22.3 %collective-permute-start.2 = (bf16[64,1,2,1024]{3,0,1,2:T(8,128)(2,1)}, bf16[64,1,2,1024]{3,0,1,2:T(8,128)(2,1)S(1)}, u32[]{:S(2)}, u32[]{:S(2)}) collective-permute-start(bf16[64,1,2,1024]{3,0,1,2:T(8,128)(2,1)} %get-tuple-element.56), channel_id=1, source_target_pairs={{0,12},{4,0},{8,4},{12,8},{1,13},{5,1},{9,5},{13,9},{2,14},{6,2},{... | collective-permute-start | bytes 786440 | tf_op jit(solution)/shard_map/ppermute | solution.py:111
  100.5 24.6 %collective-permute-start.1 = (bf16[64,1,2,1024]{3,0,1,2:T(8,128)(2,1)S(1)}, bf16[64,1,2,1024]{3,0,1,2:T(8,128)(2,1)S(1)}, u32[]{:S(2)}, u32[]{:S(2)}) collective-permute-start(bf16[64,1,2,1024]{3,0,1,2:T(8,128)(2,1)S(1)} %get-tuple-element.57), channel_id=1, source_target_pairs={{0,8},{4,12},{8,0},{12,4},{1,9},{5,13},{9,1},{13,5},{2,10},{6,14},... | collective-permute-start | bytes 786440 | tf_op jit(solution)/shard_map/ppermute | solution.py:111
  101.3 23.8 %collective-permute-start = (bf16[64,1,2,1024]{3,0,1,2:T(8,128)(2,1)S(1)}, bf16[64,1,2,1024]{3,0,1,2:T(8,128)(2,1)S(1)}, u32[]{:S(2)}, u32[]{:S(2)}) collective-permute-start(bf16[64,1,2,1024]{3,0,1,2:T(8,128)(2,1)S(1)} %get-tuple-element.55), channel_id=1, source_target_pairs={{0,4},{4,8},{8,12},{12,0},{1,5},{5,9},{9,13},{13,1},{2,6},{6,10},{... | collective-permute-start | bytes 786440 | tf_op jit(solution)/shard_map/ppermute | solution.py:111
  114.2 3.4 %copy-start = (bf16[2,1,8,128,1024]{4,3,2,0,1:T(8,128)(2,1)S(1)}, bf16[2,1,8,128,1024]{4,3,2,0,1:T(8,128)(2,1)}, u32[]{:S(2)}) copy-start(bf16[2,1,8,128,1024]{4,3,2,0,1:T(8,128)(2,1)} %copy.36) | copy-start | bytes 12582916
Sparse Core Ops, SparseCore 0:
  30.0 33.9 reduce-scatter.1
  65.5 31.4 all-gather.1

commit v23 on v17

--- a/solution.py
+++ b/solution.py
@@ -105,16 +105,19 @@
     shot_index = lax.axis_index("shot")
     corr_blocks = corr_part.reshape(shot_count, source_local, *corr_part.shape[1:])
     corr = lax.dynamic_index_in_dim(corr_blocks, shot_index, 0, keepdims=False).astype(jnp.float32)
-    for shift in range(1, shot_count):
-        outgoing = lax.dynamic_index_in_dim(corr_blocks, (shot_index + shift) % shot_count, 0, keepdims=False)
-        pairs = [(k, (k + shift) % shot_count) for k in range(shot_count)]
-        corr = corr + lax.ppermute(outgoing, "shot", perm=pairs).astype(jnp.float32)
+    outgoing = [
+        lax.dynamic_index_in_dim(corr_blocks, (shot_index + shift) % shot_count, 0, keepdims=False)
+        for shift in range(1, shot_count)
+    ]
 
     across = lax.all_gather(gram_strip, "shot", axis=0, tiled=True)
     across = across.reshape(shot_count, rows_each, freq_local, 2, span)
     local_power = jnp.sum(jnp.square(power_trace.astype(jnp.float32)), axis=(0, 2, 3))
     power = lax.psum(local_power, "shot") / receivers
-    across, power = lax.optimization_barrier((across, power))
+    across, power, outgoing = lax.optimization_barrier((across, power, outgoing))
+    for shift in range(1, shot_count):
+        pairs = [(k, (k + shift) % shot_count) for k in range(shot_count)]
+        corr = corr + lax.ppermute(outgoing[shift - 1], "shot", perm=pairs).astype(jnp.float32)
     power_wide = power[None, :, None, None]
 
     if core_count == 2:

time: 139 us -> 139 us (level)
  waiting for transfers between devices: 33.5 us -> 31.5 us
  local copies, waits for them, and re-layouts: 39.1 us -> 40.5 us
    all_gather x1, waiting for transfers between devices: 19.9 us -> 17.4 us  [per_device(): across = lax.all_gather(gram_strip, 'shot', axis=0, tiled=True)]
  transfers between devices with their start and end apart: 6 -> 6, of which waited for: 3 -> 3; matrix products, arithmetic and copies ran while one was open for 33% -> 34% of each run, Pallas kernels for 0% -> 0%
where the time goes in v23:
time: 139 us
  local copies, waits for them, and re-layouts  40.5 us (29%)
  waiting for transfers between devices  31.5 us (23%)
  other arithmetic  25.4 us (18%)
  between operations  14.5 us (10%)
  matrix products  12.6 us (9%)
  blocking collectives  10.3 us (7%)
  starting transfers between devices  3.63 us (3%)
    all_gather x1, waiting for transfers between devices, per_device(): across = lax.all_gather(gram_strip, 'shot', axis=0, tiled=True)  17.4 us
    psum x1, blocking collectives, per_device(): power = lax.psum(local_power, 'shot') / receivers  10.3 us
    reduce_scatter x1, waiting for transfers between devices, per_device(): lax.psum_scatter(gram_part, 'shot', scatter_dimension=0, tiled=True)  9.87 us
    transpose x1, local copies, waits for them, and re-layouts, per_device(): jnp.einsum('qtpu,qto->uqpo', stacked_left(upgoing), right, preferred_elem...  6.31 us
    another operation x1, local copies, waits for them, and re-layouts, rebuild_gram(): whole = jnp.where(direct, upper.reshape(shape6), mirror.reshape(shape6))  6.27 us
    unnamed x19, local copies, waits for them, and re-layouts  5.95 us
    gather x1, local copies, waits for them, and re-layouts, per_device(): corr_part = jnp.take(corr_all, own_order, axis=0).astype(jnp.bfloat16)  5.28 us
    dot_general x1, matrix products, per_device(): jnp.einsum('qtpu,qto->uqpo', stacked_left(upgoing), right, preferred_elem...  4.58 us
  transfers between devices with their start and end apart: 6, of which 3 were waited for; matrix products, arithmetic and copies ran while one was open for 34% of the time, Pallas kernels for 0%

profile of v23, /device:TPU:0, one launch (start us, length us, event | category | flops | bytes accessed | tf_op | source)
XLA Modules:
  0.0 138.5 jit_solution(12941214513267232944)
XLA Ops:
  6.5 2.2 %fusion.90 = (bf16[1,1,768,1024]{3,2,1,0:T(8,128)(2,1)S(1)}, bf16[1,1,768,1024]{3,2,1,0:T(8,128)(2,1)S(1)}) fusion(bf16[2,1,768,1024]{3,2,1,0:T(8,128)(2,1)} %param.3), kind=kLoop, calls=%fused_computation.182 | loop fusion | bytes 6291456 | tf_op jit(solution)/shard_map/slice | solution.py:26
  8.7 1.6 %copy.41 = bf16[1,1,768,1024]{2,3,1,0:T(8,128)(2,1)} copy(bf16[1,1,768,1024]{3,2,1,0:T(8,128)(2,1)S(1)} %get-tuple-element.29) | data formatting | bytes 3145728
  13.0 1.7 %fusion.16 = (bf16[1,1,1536,1024]{2,3,1,0:T(8,128)(2,1)S(1)}, bf16[1,1,1536,1024]{2,3,1,0:T(8,128)(2,1)S(1)}) fusion(bf16[1,768,1024]{1,2,0:T(8,128)(2,1)S(1)} %bitcast.223, bf16[1,768,1024]{1,2,0:T(8,128)(2,1)S(1)} %bitcast.219, bf16[1,768,1024]{1,2,0:T(8,128)(2,1)} %bitcast_negate_fusion), kind=kLoop, calls=%fused_computation.52 | loop fusion | flops 12582912 | bytes 11010048 | tf_op jit(solution)/shard_map/stack | solution.py:16
  15.3 3.7 %convert_bitcast_fusion = bf16[4,128,1,2,1024]{1,4,0,3,2:T(8,128)(2,1)S(1)} fusion(bf16[1,2,4,2,128,1536]{5,4,3,2,1,0:T(8,128)(2,1)S(1)} %bitcast.222, s32[]{:T(128)S(6)} %select_n.120, bf16[1,768,1024]{1,2,0:T(8,128)(2,1)S(1)} %bitcast.224, bf16[1,768,1024]{1,2,0:T(8,128)(2,1)S(1)} %bitcast.220), kind=kOutput, calls=%fused_computation.44 | convolution fusion | flops 3228565504 | bytes 8388612 | tf_op jit(solution)/shard_map/qpkit,qto->kiqpo/dot_general | solution.py:92
  20.3 3.0 %pad_slice_fusion.11 = (bf16[1,128,1,2,2048]{1,4,0,3,2:T(8,128)(2,1)}, bf16[1,128,1,2,2048]{1,4,0,3,2:T(8,128)(2,1)}, bf16[1,128,1,2,2048]{1,4,0,3,2:T(8,128)(2,...) fusion(bf16[4,128,1,2,1024]{1,4,0,3,2:T(8,128)(2,1)S(1)} %conve, ...), kind=kLoop, calls=%fused_computation.15 | loop fusion | bytes 8388608 | tf_op jit(solution)/shard_map/slice | solution.py:52
  23.3 1.5 %fusion.44 = (bf16[1,128,1,2,640]{1,4,0,3,2:T(8,128)(2,1)S(1)}, bf16[1,128,1,2,640]{1,4,0,3,2:T(8,128)(2,1)S(1)}) fusion(s32[]{:T(128)S(6)} %select_n.128, bf16[4,128,1,2,1024]{1,4,0,3,2:T(8,128)(2,1)} %copy-done.2, bf16[1,128,1,2,2048]{1,4,0,3,2:T(8,128)(2,1)} %get-tuple-element.43, s32[]{:T(128)S(6)} %select_n.122, ...), kind=kLoop, calls=%fused_computation.96 | loop fusion | flops 1310720 | bytes 3407880 | tf_op jit(solution)/shard_map/concatenate | solution.py:48
  27.5 2.5 %copy.31 = bf16[4,128,1,2,640]{4,1,0,3,2:T(8,128)(2,1)} copy(bf16[4,128,1,2,640]{1,4,0,3,2:T(8,128)(2,1)} %pad_maximum_fusion.3) | data formatting | bytes 2621440 | tf_op jit(solution)/shard_map/stack | solution.py:53
  31.2 1.5 %slice_bitcast_fusion.3 = (bf16[1,768,512]{2,1,0:T(8,128)(2,1)S(1)}, bf16[1,768,512]{2,1,0:T(8,128)(2,1)S(1)}) fusion(bf16[2,1,768,512]{3,2,1,0:T(8,128)(2,1)} %param.4), kind=kLoop, calls=%fused_computation.54 | loop fusion | bytes 3145728 | tf_op jit(solution)/shard_map/squeeze | solution.py:20
  33.0 4.6 %fusion.8 = bf16[512,2,1024]{0,2,1:T(8,128)(2,1)} fusion(bf16[1,1536,1,512]{3,1,2,0:T(8,128)(2,1)S(1)} %get-tuple-element.67, bf16[1,1536,1,512]{3,1,2,0:T(8,128)(2,1)S(1)} %get-tuple-element.66, bf16[1,768,1024]{1,2,0:T(8,128)(2,1)S(1)} %bitcast.225, bf16[1,768,1024]{1,2,0:T(8,128)(2,1)S(1)} %bitcast.221), kind=kOutput, calls=%fused_computation.38 | convolution fusion | flops 3233808384 | bytes 8388608 | tf_op jit(solution)/shard_map/qtpu,qto->uqpo/dot_general | solution.py:96
  37.6 6.3 %copy.32 = bf16[512,2,1024]{2,1,0:T(2,128)(2,1)} copy(bf16[512,2,1024]{0,2,1:T(8,128)(2,1)} %fusion.8) | data formatting | bytes 4194304 | tf_op jit(solution)/shard_map/qtpu,qto->uqpo/transpose | solution.py:96
  45.7 5.3 %gather_fusion = bf16[256,2,1024]{2,1,0:T(2,128)(2,1)} fusion(bf16[512,2,1024]{2,1,0:T(2,128)(2,1)} %copy.32, s32[1024]{0:T(1024)S(1)} %pad_clamp_fusion), kind=kCustom, calls=%fused_computation | custom fusion | bytes 2098176 | tf_op jit(solution)/shard_map/jit(_take)/gather | solution.py:101
  50.9 3.2 %fusion.11 = bf16[256,1,2,1024]{3,2,0,1:T(2,128)(2,1)} fusion(bf16[256,2,1024]{2,1,0:T(2,128)(2,1)} %gather_fusion, pred[256]{0:T(512)(128)(4,1)S(1)} %compare_and_fusion), kind=kLoop, calls=%fused_computation.43 | loop fusion | flops 524288 | bytes 2097408 | tf_op jit(solution)/shard_map/convert_element_type | solution.py:101
  54.2 9.9 %reduce-scatter.2.cloned.1.call-done = bf16[128,1,2,640]{3,0,2,1:T(8,128)(2,1)} async-done(((bf16[512,1,2,640]{3,0,2,1:T(8,128)(2,1)}), bf16[128,1,2,640]{3,0,2,1:T(8,128)(2,1)}) %reduce-scatter.2.cloned.1.call-update) | async-done | bytes 327696 | tf_op jit(solution)/shard_map/reduce_scatter | solution.py:94
  64.1 2.2 %multiply_reduce_fusion = f32[]{:T(128)} fusion(bf16[2,1,768,1024]{3,2,1,0:T(8,128)(2,1)S(1)} %copy-done.1), kind=kLoop, calls=%fused_computation.3 | loop fusion | flops 4718591 | bytes 3145732 | tf_op jit(solution)/shard_map/reduce_sum | solution.py:115
  66.4 10.3 %psum.7 = f32[1]{0:T(128)} all-reduce(f32[1]{0:T(128)} %bitcast.27), channel_id=1, replica_groups=mesh['grp'=2,'shot'=4,'freq'=2,'sub'=2] {'shot'}, use_global_device_ids=true, to_apply=%region_2.3 | all-reduce | flops 1 | bytes 8 | tf_op jit(solution)/shard_map/psum | solution.py:116
  76.7 1.5 %copy.33 = bf16[256,1,2,1024]{3,0,2,1:T(8,128)(2,1)S(1)} copy(bf16[256,1,2,1024]{3,2,0,1:T(2,128)(2,1)} %fusion.11) | data formatting | bytes 2097152 | tf_op jit(solution)/shard_map/optimization_barrier | solution.py:103
  79.8 17.4 %all-gather.2.cloned.1.call-done = bf16[512,1,2,640]{3,0,2,1:T(8,128)(2,1)} async-done(((bf16[128,1,2,640]{3,0,2,1:T(8,128)(2,1)}), bf16[512,1,2,640]{3,0,2,1:T(8,128)(2,1)}) %all-gather.2.cloned.1.call-update) | async-done | bytes 1310736 | tf_op jit(solution)/shard_map/all_gather | solution.py:113
  98.2 1.6 %collective-permute-start.2 = (bf16[64,1,2,1024]{3,0,1,2:T(8,128)(2,1)}, bf16[64,1,2,1024]{3,0,1,2:T(8,128)(2,1)}, u32[]{:S(2)}, u32[]{:S(2)}) collective-permute-start(bf16[64,1,2,1024]{3,0,1,2:T(8,128)(2,1)} %get-tuple-element.18), channel_id=1, source_target_pairs={{0,12},{4,0},{8,4},{12,8},{1,13},{5,1},{9,5},{13,9},{2,14},{6,2},{... | collective-permute-start | bytes 786440 | tf_op jit(solution)/shard_map/ppermute | solution.py:120
  101.7 1.6 %select_bitcast_fusion.1 = (bf16[4,1,128,1,2,640]{5,2,1,0,4,3:T(8,128)(2,1)S(1)}, bf16[4,1,128,1,2,640]{5,2,1,0,4,3:T(8,128)(2,1)S(1)}) fusion(bf16[4,128,1,2,640]{4,1,0,3,2:T(8,128)(2,1)S(1)} %bitcast.233, bf16[4,128,1,2,640]{4,1,0,3,2:T(8,128)(2,1)} %collective-permute-done.3, pred[]{:T(512)S(6)} %eq.10), kind=kLoop, calls=%fused_computation.49 | loop fusion | flops 1310720 | bytes 5242881 | tf_op jit(solution)/shard_map/stack | solution.py:127
  104.4 2.4 %copy.36 = bf16[2,1,8,128,1024]{4,3,2,0,1:T(8,128)(2,1)} copy(bf16[2,1,8,128,1024]{4,3,0,1,2:T(8,128)(2,1)S(1)} %bitcast.226) | data formatting | bytes 8388608 | tf_op jit(solution)/shard_map/transpose | solution.py:63
  106.8 6.3 %copy.37 = bf16[2,1,1024,1024]{2,3,0,1:T(8,128)(2,1)} copy(bf16[2,1,1024,1024]{3,2,0,1:T(8,128)(2,1)} %bitcast.216) | data formatting | bytes 8388608 | tf_op jit(solution)/shard_map/reshape;reshape | solution.py:70
  113.1 2.6 %fusion.89 = (bf16[1,1,1024,1024]{3,2,0,1:T(8,128)(2,1)S(1)}, bf16[1,1,1024,1024]{3,2,0,1:T(8,128)(2,1)S(1)}) fusion(bf16[2,1,1024,1024]{3,2,0,1:T(8,128)(2,1)} %bitcast.217), kind=kLoop, calls=%fused_computation.181 | loop fusion | flops 1048576 | bytes 8388608 | tf_op jit(solution)/shard_map/slice | solution.py:65
  116.5 2.5 %divide_convert_fusion = bf16[2,1,1024,1024]{3,2,0,1:T(8,128)(2,1)S(1)} fusion(bf16[1,1,1024,1024]{3,2,0,1:T(8,128)(2,1)S(1)} %get-tuple-element.28, bf16[1,1,1024,1024]{3,2,0,1:T(8,128)(2,1)S(1)} %get-tuple-element.27, f32[]{:T(128)} %bitcast.31, pred[1024,1024]{1,0:T(8,128)(4,1)S(1)} %bitcast.231, bf16[2,1,8,128,1024]{4,3,2,0,1:T(8,128)(2,1)S(1)} %copy-done), kind=kLoop, calls=%fused_computation.1 | loop fusion | flops 10485760 | bytes 13631492 | tf_op jit(solution)/shard_map/convert_element_type | solution.py:135
  120.2 4.2 %collective-permute-done.1 = bf16[64,1,2,1024]{3,0,1,2:T(8,128)(2,1)} collective-permute-done((bf16[64,1,2,1024]{3,0,1,2:T(8,128)(2,1)}, bf16[64,1,2,1024]{3,0,1,2:T(8,128)(2,1)}, u32[]{:S(2)}, u32[]{:S(2)}) %collective-permute-start.1) | collective-permute-done | bytes 262176 | tf_op jit(solution)/shard_map/ppermute | solution.py:120
  (84 shorter events, 24.6 us)
Async XLA Ops:
  6.5 57.5 %reduce-scatter.2.cloned.1.call-start = ((), (), s32[]{:S(2)}) async-start(), calls=%async_computation.1 | async-start | bytes 1638400 | tf_op jit(solution)/shard_map/reduce_scatter | solution.py:94
  11.1 2.0 %copy-start.3 = (bf16[1,1,768,1024]{2,3,1,0:T(8,128)(2,1)S(1)}, bf16[1,1,768,1024]{2,3,1,0:T(8,128)(2,1)}, u32[]{:S(2)}) copy-start(bf16[1,1,768,1024]{2,3,1,0:T(8,128)(2,1)} %copy.41) | copy-start | bytes 4718596
  19.0 1.4 copy-start.2
  30.0 67.2 %all-gather.2.cloned.1.call-start = ((), (), s32[]{:S(2)}) async-start(), calls=%async_computation.2 | async-start | bytes 1638400 | tf_op jit(solution)/shard_map/all_gather | solution.py:113
  37.6 6.3 %copy-start.5 = (s32[512]{0:T(512)S(1)}, s32[512]{0:T(512)}, u32[]{:S(2)}) copy-start(s32[512]{0:T(512)} %param.5) | copy-start | bytes 6148
  43.9 20.2 %copy-start.1 = (bf16[2,1,768,1024]{3,2,1,0:T(8,128)(2,1)S(1)}, bf16[2,1,768,1024]{3,2,1,0:T(8,128)(2,1)}, u32[]{:S(2)}) copy-start(bf16[2,1,768,1024]{3,2,1,0:T(8,128)(2,1)} %param.3) | copy-start | bytes 9437188
  97.2 4.5 %copy-start.4 = (bf16[512,1,2,640]{3,0,2,1:T(8,128)(2,1)S(1)}, bf16[512,1,2,640]{3,0,2,1:T(8,128)(2,1)}, u32[]{:S(2)}) copy-start(bf16[512,1,2,640]{3,0,2,1:T(8,128)(2,1)} %all-gather.2.cloned.1.call-done) | copy-start | bytes 3932164
  97.2 4.5 %collective-permute-start.3 = (bf16[4,128,1,2,640]{4,1,0,3,2:T(8,128)(2,1)}, bf16[4,128,1,2,640]{4,1,0,3,2:T(8,128)(2,1)}, u32[]{:S(2)}, u32[]{:S(2)}) collective-permute-start(bf16[4,128,1,2,640]{4,1,0,3,2:T(8,128)(2,1)} %bitcast.232), channel_id=1, source_target_pairs={{0,1},{1,0},{2,3},{3,2},{4,5},{5,4},{6,7},{7,6},{8,9},{9,8},{10,11... | collective-permute-start | bytes 3932168 | tf_op jit(solution)/shard_map/ppermute | solution.py:124
  98.2 22.1 %collective-permute-start.2 = (bf16[64,1,2,1024]{3,0,1,2:T(8,128)(2,1)}, bf16[64,1,2,1024]{3,0,1,2:T(8,128)(2,1)}, u32[]{:S(2)}, u32[]{:S(2)}) collective-permute-start(bf16[64,1,2,1024]{3,0,1,2:T(8,128)(2,1)} %get-tuple-element.18), channel_id=1, source_target_pairs={{0,12},{4,0},{8,4},{12,8},{1,13},{5,1},{9,5},{13,9},{2,14},{6,2},{... | collective-permute-start | bytes 786440 | tf_op jit(solution)/shard_map/ppermute | solution.py:120
  99.7 24.7 %collective-permute-start.1 = (bf16[64,1,2,1024]{3,0,1,2:T(8,128)(2,1)}, bf16[64,1,2,1024]{3,0,1,2:T(8,128)(2,1)}, u32[]{:S(2)}, u32[]{:S(2)}) collective-permute-start(bf16[64,1,2,1024]{3,0,1,2:T(8,128)(2,1)} %get-tuple-element.17), channel_id=1, source_target_pairs={{0,8},{4,12},{8,0},{12,4},{1,9},{5,13},{9,1},{13,5},{2,10},{6,14},... | collective-permute-start | bytes 786440 | tf_op jit(solution)/shard_map/ppermute | solution.py:120
  100.5 23.9 %collective-permute-start = (bf16[64,1,2,1024]{3,0,1,2:T(8,128)(2,1)}, bf16[64,1,2,1024]{3,0,1,2:T(8,128)(2,1)}, u32[]{:S(2)}, u32[]{:S(2)}) collective-permute-start(bf16[64,1,2,1024]{3,0,1,2:T(8,128)(2,1)} %get-tuple-element.16), channel_id=1, source_target_pairs={{0,4},{4,8},{8,12},{12,0},{1,5},{5,9},{9,13},{13,1},{2,6},{6,10},{... | collective-permute-start | bytes 786440 | tf_op jit(solution)/shard_map/ppermute | solution.py:120
  113.1 3.4 %copy-start = (bf16[2,1,8,128,1024]{4,3,2,0,1:T(8,128)(2,1)S(1)}, bf16[2,1,8,128,1024]{4,3,2,0,1:T(8,128)(2,1)}, u32[]{:S(2)}) copy-start(bf16[2,1,8,128,1024]{4,3,2,0,1:T(8,128)(2,1)} %copy.36) | copy-start | bytes 12582916
Sparse Core Ops, SparseCore 0:
  30.1 33.9 reduce-scatter.1
  65.6 31.5 all-gather.1
